TPU v7x, 32 devices: a whole 2x2x4 slice. The times are simulated.
32 devices in a mesh: grp: 4 (over y, core), blk: 8 (over z, x).
Axes of the slice: x: 2, y: 2, z: 4, core: 2. Of those that a mesh axis runs over, the one named last changes fastest.
Arguments:
- fields: float32 [14, 512, 4096], P(None, 'grp', 'blk'), may hold values from -6 to 6
- react_rate: float32 [512, 4096], P('grp', 'blk'), may hold values from 0.05 to 0.8
- mix_matrix: float32 [14, 14], replicated, may hold values from -1.5 to 1.5
- activation: float32 [14], replicated, may hold values from 0.3 to 4
- inlet_ids: int32 [4, 4096], P(None, 'blk'), may hold values from 0 to 4095
- inlet_weights: float32 [4, 4096], P(None, 'blk'), may hold values from 0.1 to 0.45
- outlet_ids: int32 [4, 4096], P(None, 'blk'), may hold values from 0 to 4095
- outlet_weights: float32 [4, 4096], P(None, 'blk'), may hold values from 0.1 to 0.45
Outputs:
- advanced: float32 [14, 512, 4096], P(None, 'grp', 'blk')
Inputs may be any that keep to these rules, and one draw needn't show every extreme that they name: Every inlet_ids entry names a row of the combustor exit plane. Every outlet_ids entry names a row of the turbine inlet plane.
All inputs are finite; a program needn't handle non-finite values.
Results may differ from a plain program's by a relative error of at most 0.00005.
Values sent between devices are 32-bit elements; how exact they have to be, the bound alone decides.
No kernel may reach another device: no remote copies, remote signals or barrier semaphores. Data moves between devices by JAX's collectives and lax.ppermute only.
A program may use at most 128 MiB of HBM per device.

v0:
```python
import jax
import jax.numpy as jnp
from jax import lax
from jax.sharding import PartitionSpec as P

courant = 0.5
diffusion = 0.1
source_step = 0.5


def padded(cells, sides, width, closed):
    for axis, dim in sides:
        count = lax.axis_size(axis)
        ends = count if closed else count - 1
        head = lax.slice_in_dim(cells, 0, width, axis=dim)
        tail = lax.slice_in_dim(cells, cells.shape[dim] - width, cells.shape[dim], axis=dim)
        cells = jnp.concatenate(
            [
                lax.ppermute(tail, axis, [(i, (i + 1) % count) for i in range(ends)]),
                cells,
                lax.ppermute(head, axis, [((i + 1) % count, i) for i in range(ends)]),
            ],
            axis=dim,
        )
    return cells


def tendency(values, backward, forward, cycle_left, cycle_right, rates, mix_matrix, activation):
    heat = 1.0 + jax.nn.softplus(values[4])
    reaction = rates[None] * values * jnp.exp(-activation[:, None, None] / heat[None])
    source = jnp.einsum("fg,gxr->fxr", mix_matrix, reaction, precision=lax.Precision.HIGHEST)
    advect = -courant * (values - backward)
    spread = diffusion * (backward + forward + cycle_left + cycle_right - 4.0 * values)
    return advect + spread + source_step * source


def faces(values):
    axial_pad = padded(values, (("grp", 1),), 1, False)
    cycle_pad = padded(values, (("blk", 2),), 1, True)
    return (axial_pad, cycle_pad)


def shards(
    fields, react_rate, mix_matrix, activation, inlet_ids, inlet_weights, outlet_ids, outlet_weights
):
    group_count = lax.axis_size("grp")
    group_index = lax.axis_index("grp")
    at_turbine = group_index == group_count - 1
    at_exit = group_index == group_count - 2
    axial_pad, cycle_pad = faces(fields)
    low_row = axial_pad[:, 0, :]
    high_row = axial_pad[:, -1, :]
    donors = lax.all_gather(low_row, "blk", axis=1, tiled=True)
    row_count = donors.shape[1]
    inside = (inlet_ids >= 0) & (inlet_ids < row_count)
    picked = jnp.take(donors, jnp.clip(inlet_ids, 0, row_count - 1), axis=1)
    weight = jnp.where(inside, inlet_weights, 0.0)
    inlet_values = jnp.sum(picked * weight[None], axis=1)
    pressure = lax.all_gather(high_row[4], "blk", axis=0, tiled=True)
    back_pressure = jnp.sum(jnp.take(pressure, outlet_ids) * outlet_weights, axis=0)

    def rate_of(values, axial_pad, cycle_pad):
        last_layer = values[:, -1, :]
        exit_ghost = last_layer.at[4].set(back_pressure)
        low_ghost = jnp.where(at_turbine, inlet_values, axial_pad[:, 0, :])
        high_ghost = jnp.where(
            at_turbine, last_layer, jnp.where(at_exit, exit_ghost, axial_pad[:, -1, :])
        )
        backward = jnp.concatenate([low_ghost[:, None, :], values[:, :-1, :]], axis=1)
        forward = jnp.concatenate([values[:, 1:, :], high_ghost[:, None, :]], axis=1)
        return tendency(
            values,
            backward,
            forward,
            cycle_pad[:, :, :-2],
            cycle_pad[:, :, 2:],
            react_rate,
            mix_matrix,
            activation,
        )

    first_section = fields + rate_of(fields, axial_pad, cycle_pad)
    second_axial, second_cycle = faces(first_section)
    return 0.5 * (fields + first_section + rate_of(first_section, second_axial, second_cycle))


def solution(mesh):
    in_specs = (
        P(None, "grp", "blk"),
        P("grp", "blk"),
        P(),
        P(),
        P(None, "blk"),
        P(None, "blk"),
        P(None, "blk"),
        P(None, "blk"),
    )
    out_specs = P(None, "grp", "blk")
    return jax.shard_map(shards, mesh=mesh, in_specs=in_specs, out_specs=out_specs, check_vma=False)
```

profile of v0, /device:TPU:1, one launch (start us, length us, event | category | flops | bytes accessed | tf_op | source)
XLA Modules:
  0.0 159.8 jit_solution(1495912322812927714)
XLA Ops:
  0.0 0.0 copy-start
  0.0 1.8 %fusion.48 = (f32[14,128,1]{2,1,0:T(8,128)S(1)}, f32[14,128,1]{2,1,0:T(8,128)S(1)}) fusion(f32[14,128,512]{2,1,0:T(8,128)} %param.12), kind=kLoop, calls=%fused_computation.72 | loop fusion | bytes 28672 | tf_op jit(solution)/shard_map/slice | solution.py:16
  1.8 0.3 copy.67
  2.1 5.1 %collective-permute-start.3 = (f32[14,128,1]{1,2,0:T(1,128)S(1)}, f32[14,128,1]{1,2,0:T(1,128)S(1)}, u32[]{:S(2)}, u32[]{:S(2)}) collective-permute-start(f32[14,128,1]{1,2,0:T(1,128)S(1)} %copy.67), channel_id=1, source_target_pairs={{1,0},{2,1},{3,2},{4,3},{5,4},{6,5},{7,6},{0,7},{9,8},{10,9},{11,1... | collective-permute-start | bytes 21512 | tf_op jit(solution)/shard_map/ppermute | solution.py:21
  7.2 0.3 copy.66
  7.5 0.0 collective-permute-start.2
  7.5 4.2 %copy.58 = f32[14,128,512]{2,0,1:T(8,128)S(1)} copy(f32[14,128,512]{2,1,0:T(8,128)} %param.12) | data formatting | bytes 7340032 | tf_op args[0]
  11.7 0.0 copy-start.1
  11.8 4.0 %collective-permute-start = (f32[14,1,512]{2,0,1:T(8,128)S(1)}, f32[14,1,512]{2,0,1:T(8,128)S(1)}, u32[]{:S(2)}, u32[]{:S(2)}) collective-permute-start(f32[14,1,512]{2,0,1:T(8,128)S(1)} %get-tuple-element.36), channel_id=1, source_target_pairs={{0,8},{8,16},{16,24},{1,9},{9,17},{17,25},{2,10},{10,18},{18,26},{... | collective-permute-start | bytes 86024 | tf_op jit(solution)/shard_map/ppermute | solution.py:19
  15.8 1.9 %collective-permute-start.1 = (f32[14,1,512]{2,0,1:T(8,128)S(1)}, f32[14,1,512]{2,0,1:T(8,128)S(1)}, u32[]{:S(2)}, u32[]{:S(2)}) collective-permute-start(f32[14,1,512]{2,0,1:T(8,128)S(1)} %get-tuple-element.38), channel_id=1, source_target_pairs={{8,0},{16,8},{24,16},{9,1},{17,9},{25,17},{10,2},{18,10},{26,18},{... | collective-permute-start | bytes 86024 | tf_op jit(solution)/shard_map/ppermute | solution.py:21
  17.7 1.3 fusion.33
  19.0 0.0 copy-start.3
  19.0 0.0 copy-start.5
  19.0 0.0 copy-start.4
  19.0 0.0 copy-start.7
  19.0 4.3 %fusion.47 = (f32[14,127,512]{2,0,1:T(8,128)}, f32[14,127,512]{2,0,1:T(8,128)}) fusion(f32[14,128,512]{2,0,1:T(8,128)S(1)} %copy.58), kind=kLoop, calls=%fused_computation.71 | loop fusion | bytes 14565376 | tf_op jit(solution)/shard_map/slice | solution.py:69
  23.4 0.0 copy-done.1
  23.4 0.0 copy-done.3
  23.4 0.0 copy-done.5
  23.4 0.0 copy-done.4
  23.5 0.0 copy-done.7
  23.5 0.0 collective-permute-done.2
  23.6 1.5 copy.49
  25.1 0.0 collective-permute-done.3
  25.1 1.4 copy.53
  26.5 0.0 collective-permute-done.1
  26.5 21.7 %all-gather.1 = f32[1,1,4096]{2,0,1:T(1,128)S(1)} all-gather(f32[1,1,512]{2,0,1:T(1,128)S(1)} %slice.121), channel_id=3, replica_groups=mesh['grp'=4,'blk'=8] {'blk'}, dimensions={2}, use_global_device_ids=true | all-gather | bytes 18432 | tf_op jit(solution)/shard_map/all_gather | solution.py:59
  48.1 11.8 %gather_fusion.1 = f32[2048]{0:T(1024)S(1)} fusion(f32[4096]{0:T(1024)S(1)} %bitcast.52, s32[2048]{0:T(1024)S(1)} %broadcast_clamp_fusion), kind=kCustom, calls=%fused_computation.1 | custom fusion | bytes 24576 | tf_op jit(solution)/shard_map/jit(_take)/gather | solution.py:60
  59.9 0.0 collective-permute-done
  59.9 24.8 %all-gather = f32[14,1,4096]{2,0,1:T(8,128)S(1)} all-gather(f32[14,1,512]{2,0,1:T(8,128)S(1)} %collective-permute-done), channel_id=2, replica_groups=mesh['grp'=4,'blk'=8] {'blk'}, dimensions={2}, use_global_device_ids=true | all-gather | bytes 258048 | tf_op jit(solution)/shard_map/all_gather | solution.py:53
  84.7 0.6 copy.42
  85.4 5.5 %gather_fusion = f32[2048,14]{1,0:T(8,128)S(1)} fusion(f32[14,4096]{0,1:T(8,128)S(1)} %copy.42, s32[2048]{0:T(1024)S(1)} %broadcast_clamp_fusion.1), kind=kCustom, calls=%fused_computation | custom fusion | bytes 237568 | tf_op jit(solution)/shard_map/jit(_take)/gather | solution.py:56
  90.9 0.7 multiply_reduce_fusion
  91.6 0.1 copy.43
  91.7 0.7 multiply_reduce_fusion.1
  92.4 0.2 scatter.6
  92.7 0.8 fusion.38
  93.5 0.0 copy-done
  93.5 14.2 %fusion.19 = f32[14,128,512]{2,0,1:T(8,128)S(1)} fusion(f32[14,128,512]{2,0,1:T(8,128)} %copy-done.1, f32[14,128,1]{2,0,1:T(8,128)} %copy.53, f32[14,128,1]{2,0,1:T(8,128)} %copy.49, f32[14,1,512]{2,0,1:T(8,128)S(1)} %fusion.38, f32[14,127,512]{2,0,1:T(8,128)} %get-tuple-element.40, f32[14,127,512]{2,0,1:T(8,128)} %get-tuple-element.39, ...), kind=kOutput, calls=%fused_computation.24 | convolution fusion | flops 171573248 | bytes 15219528 | tf_op jit(solution)/shard_map/fg,gxr->fxr/dot_general | solution.py:31
  107.7 0.0 copy-start.2
  107.7 0.4 fusion.45
  108.1 4.3 %fusion.44 = (f32[14,127,512]{2,0,1:T(8,128)}, f32[14,127,512]{2,0,1:T(8,128)}) fusion(f32[14,128,512]{2,0,1:T(8,128)S(1)} %fusion.19), kind=kLoop, calls=%fused_computation.68 | loop fusion | bytes 14565376 | tf_op jit(solution)/shard_map/slice | solution.py:69
  112.4 0.0 copy-done.2
  112.4 0.0 copy-start.6
  112.4 14.1 %collective-permute-start.4 = (f32[14,1,512]{2,0,1:T(8,128)S(1)}, f32[14,1,512]{2,0,1:T(8,128)S(1)}, u32[]{:S(2)}, u32[]{:S(2)}) collective-permute-start(f32[14,1,512]{2,0,1:T(8,128)S(1)} %get-tuple-element.29), channel_id=1, source_target_pairs={{0,8},{8,16},{16,24},{1,9},{9,17},{17,25},{2,10},{10,18},{18,26},{... | collective-permute-start | bytes 86024 | tf_op jit(solution)/shard_map/ppermute | solution.py:19
  126.5 0.4 copy.59
  126.9 0.4 copy.61
  127.3 3.2 %collective-permute-start.7 = (f32[14,128,1]{1,2,0:T(1,128)S(1)}, f32[14,128,1]{1,2,0:T(1,128)S(1)}, u32[]{:S(2)}, u32[]{:S(2)}) collective-permute-start(f32[14,128,1]{1,2,0:T(1,128)S(1)} %copy.61), channel_id=1, source_target_pairs={{1,0},{2,1},{3,2},{4,3},{5,4},{6,5},{7,6},{0,7},{9,8},{10,9},{11,1... | collective-permute-start | bytes 21512 | tf_op jit(solution)/shard_map/ppermute | solution.py:21
  130.5 0.0 collective-permute-start.6
  130.5 2.9 %fusion.34 = f32[1,128,512]{2,0,1:T(1,128)S(1)} fusion(f32[14,128,512]{2,0,1:T(8,128)} %copy-done.2), kind=kLoop, calls=%fused_computation.43 | loop fusion | flops 458752 | bytes 524288 | tf_op jit(solution)/shard_map/add | solution.py:29
  133.4 0.1 scatter.9
  133.4 2.1 %collective-permute-start.5 = (f32[14,1,512]{2,0,1:T(8,128)S(1)}, f32[14,1,512]{2,0,1:T(8,128)S(1)}, u32[]{:S(2)}, u32[]{:S(2)}) collective-permute-start(f32[14,1,512]{2,0,1:T(8,128)S(1)} %get-tuple-element.31), channel_id=1, source_target_pairs={{8,0},{16,8},{24,16},{9,1},{17,9},{25,17},{10,2},{18,10},{26,18},{... | collective-permute-start | bytes 86024 | tf_op jit(solution)/shard_map/ppermute | solution.py:21
  135.6 0.1 collective-permute-done.6
  135.7 0.5 copy.60
  136.2 0.0 collective-permute-done.7
  136.2 0.5 copy.62
  136.7 0.0 collective-permute-done.4
  136.8 1.9 %collective-permute-done.5 = f32[14,1,512]{2,0,1:T(8,128)S(1)} collective-permute-done((f32[14,1,512]{2,0,1:T(8,128)S(1)}, f32[14,1,512]{2,0,1:T(8,128)S(1)}, u32[]{:S(2)}, u32[]{:S(2)}) %collective-permute-start.5) | collective-permute-done | bytes 28704 | tf_op jit(solution)/shard_map/ppermute | solution.py:21
  138.7 0.8 fusion.36
  139.4 0.0 copy-done.6
  139.4 16.4 %fusion.12 = f32[14,128,512]{2,0,1:T(8,128)S(1)} fusion(f32[14,128,1]{2,0,1:T(8,128)S(1)} %copy.62, f32[14,128,512]{2,0,1:T(8,128)} %copy-done.2, f32[14,128,1]{2,0,1:T(8,128)S(1)} %copy.60, f32[14,1,512]{2,0,1:T(8,128)S(1)} %fusion.36, f32[14,127,512]{2,0,1:T(8,128)} %get-tuple-element.33, f32[14,127,512]{2,0,1:T(8,128)} %get-tuple-element.32, ...), kind=kOutput, calls=%fused_computation.15 | convolution fusion | flops 173408256 | bytes 18889544 | tf_op jit(solution)/shard_map/fg,gxr->fxr/dot_general | solution.py:31
  155.8 4.0 %copy.63 = f32[14,128,512]{2,1,0:T(8,128)} copy(f32[14,128,512]{2,0,1:T(8,128)S(1)} %fusion.12) | data formatting | bytes 7340032 | tf_op jit(solution)/shard_map/mul | solution.py:84
  (17 shorter events, 0.1 us)
Async XLA Ops:
  0.0 93.5 %copy-start = (f32[14,14]{1,0:T(8,128)S(1)}, f32[14,14]{1,0:T(8,128)}, u32[]{:S(2)}) copy-start(f32[14,14]{1,0:T(8,128)} %param.14) | copy-start | bytes 2356
  2.1 22.9 %collective-permute-start.3 = (f32[14,128,1]{1,2,0:T(1,128)S(1)}, f32[14,128,1]{1,2,0:T(1,128)S(1)}, u32[]{:S(2)}, u32[]{:S(2)}) collective-permute-start(f32[14,128,1]{1,2,0:T(1,128)S(1)} %copy.67), channel_id=1, source_target_pairs={{1,0},{2,1},{3,2},{4,3},{5,4},{6,5},{7,6},{0,7},{9,8},{10,9},{11,1... | collective-permute-start | bytes 21512 | tf_op jit(solution)/shard_map/ppermute | solution.py:21
  7.5 16.0 %collective-permute-start.2 = (f32[14,128,1]{1,2,0:T(1,128)S(1)}, f32[14,128,1]{1,2,0:T(1,128)S(1)}, u32[]{:S(2)}, u32[]{:S(2)}) collective-permute-start(f32[14,128,1]{1,2,0:T(1,128)S(1)} %copy.66), channel_id=1, source_target_pairs={{0,1},{1,2},{2,3},{3,4},{4,5},{5,6},{6,7},{7,0},{8,9},{9,10},{10,1... | collective-permute-start | bytes 21512 | tf_op jit(solution)/shard_map/ppermute | solution.py:19
  11.7 11.6 %copy-start.1 = (f32[14,128,512]{2,0,1:T(8,128)}, f32[14,128,512]{2,0,1:T(8,128)S(1)}, u32[]{:S(2)}) copy-start(f32[14,128,512]{2,0,1:T(8,128)S(1)} %copy.58) | copy-start | bytes 11010052
  11.8 48.2 %collective-permute-start = (f32[14,1,512]{2,0,1:T(8,128)S(1)}, f32[14,1,512]{2,0,1:T(8,128)S(1)}, u32[]{:S(2)}, u32[]{:S(2)}) collective-permute-start(f32[14,1,512]{2,0,1:T(8,128)S(1)} %get-tuple-element.36), channel_id=1, source_target_pairs={{0,8},{8,16},{16,24},{1,9},{9,17},{17,25},{2,10},{10,18},{18,26},{... | collective-permute-start | bytes 86024 | tf_op jit(solution)/shard_map/ppermute | solution.py:19
  15.8 10.7 %collective-permute-start.1 = (f32[14,1,512]{2,0,1:T(8,128)S(1)}, f32[14,1,512]{2,0,1:T(8,128)S(1)}, u32[]{:S(2)}, u32[]{:S(2)}) collective-permute-start(f32[14,1,512]{2,0,1:T(8,128)S(1)} %get-tuple-element.38), channel_id=1, source_target_pairs={{8,0},{16,8},{24,16},{9,1},{17,9},{25,17},{10,2},{18,10},{26,18},{... | collective-permute-start | bytes 86024 | tf_op jit(solution)/shard_map/ppermute | solution.py:21
  19.0 4.4 %copy-start.3 = (s32[4,512]{1,0:T(4,128)S(1)}, s32[4,512]{1,0:T(4,128)}, u32[]{:S(2)}) copy-start(s32[4,512]{1,0:T(4,128)} %param.16) | copy-start | bytes 24580
  19.0 4.4 %copy-start.5 = (f32[4,512]{1,0:T(4,128)S(1)}, f32[4,512]{1,0:T(4,128)}, u32[]{:S(2)}) copy-start(f32[4,512]{1,0:T(4,128)} %param.17) | copy-start | bytes 24580
  19.0 4.4 %copy-start.4 = (s32[4,512]{1,0:T(4,128)S(1)}, s32[4,512]{1,0:T(4,128)}, u32[]{:S(2)}) copy-start(s32[4,512]{1,0:T(4,128)} %param.18) | copy-start | bytes 24580
  19.0 4.5 %copy-start.7 = (f32[14]{0:T(128)S(1)}, f32[14]{0:T(128)}, u32[]{:S(2)}) copy-start(f32[14]{0:T(128)} %param.15) | copy-start | bytes 172
  107.7 4.7 %copy-start.2 = (f32[14,128,512]{2,0,1:T(8,128)}, f32[14,128,512]{2,0,1:T(8,128)S(1)}, u32[]{:S(2)}) copy-start(f32[14,128,512]{2,0,1:T(8,128)S(1)} %fusion.19) | copy-start | bytes 11010052
  112.4 27.0 %copy-start.6 = (f32[128,512]{1,0:T(8,128)S(1)}, f32[128,512]{1,0:T(8,128)}, u32[]{:S(2)}) copy-start(f32[128,512]{1,0:T(8,128)} %param.13) | copy-start | bytes 786436
  112.4 24.3 %collective-permute-start.4 = (f32[14,1,512]{2,0,1:T(8,128)S(1)}, f32[14,1,512]{2,0,1:T(8,128)S(1)}, u32[]{:S(2)}, u32[]{:S(2)}) collective-permute-start(f32[14,1,512]{2,0,1:T(8,128)S(1)} %get-tuple-element.29), channel_id=1, source_target_pairs={{0,8},{8,16},{16,24},{1,9},{9,17},{17,25},{2,10},{10,18},{18,26},{... | collective-permute-start | bytes 86024 | tf_op jit(solution)/shard_map/ppermute | solution.py:19
  127.3 8.9 %collective-permute-start.7 = (f32[14,128,1]{1,2,0:T(1,128)S(1)}, f32[14,128,1]{1,2,0:T(1,128)S(1)}, u32[]{:S(2)}, u32[]{:S(2)}) collective-permute-start(f32[14,128,1]{1,2,0:T(1,128)S(1)} %copy.61), channel_id=1, source_target_pairs={{1,0},{2,1},{3,2},{4,3},{5,4},{6,5},{7,6},{0,7},{9,8},{10,9},{11,1... | collective-permute-start | bytes 21512 | tf_op jit(solution)/shard_map/ppermute | solution.py:21
  130.5 5.2 %collective-permute-start.6 = (f32[14,128,1]{1,2,0:T(1,128)S(1)}, f32[14,128,1]{1,2,0:T(1,128)S(1)}, u32[]{:S(2)}, u32[]{:S(2)}) collective-permute-start(f32[14,128,1]{1,2,0:T(1,128)S(1)} %copy.59), channel_id=1, source_target_pairs={{0,1},{1,2},{2,3},{3,4},{4,5},{5,6},{6,7},{7,0},{8,9},{9,10},{10,1... | collective-permute-start | bytes 21512 | tf_op jit(solution)/shard_map/ppermute | solution.py:19
  133.4 5.2 %collective-permute-start.5 = (f32[14,1,512]{2,0,1:T(8,128)S(1)}, f32[14,1,512]{2,0,1:T(8,128)S(1)}, u32[]{:S(2)}, u32[]{:S(2)}) collective-permute-start(f32[14,1,512]{2,0,1:T(8,128)S(1)} %get-tuple-element.31), channel_id=1, source_target_pairs={{8,0},{16,8},{24,16},{9,1},{17,9},{25,17},{10,2},{18,10},{26,18},{... | collective-permute-start | bytes 86024 | tf_op jit(solution)/shard_map/ppermute | solution.py:21
where the time goes:
time: 160 us
  blocking collectives  46.5 us (29%)
  local copies, waits for them, and re-layouts  42.7 us (27%)
  matrix products  30.6 us (19%)
  starting transfers between devices  30.4 us (19%)
  other arithmetic  7.22 us (5%)
  waiting for transfers between devices  1.97 us (1%)
    dot_general x2, matrix products, tendency(): jnp.einsum('fg,gxr->fxr', mix_matrix, reaction, precision=lax.Precision.H...  30.6 us
    all_gather x1, blocking collectives, shards(): donors = lax.all_gather(low_row, 'blk', axis=1, tiled=True)  24.8 us
    all_gather x1, blocking collectives, shards(): pressure = lax.all_gather(high_row[4], 'blk', axis=0, tiled=True)  21.7 us
    ppermute x4, starting transfers between devices, padded(): lax.ppermute(tail, axis, [(i, (i + 1) % count) for i in range(ends)])  18.1 us
    ppermute x4, starting transfers between devices, padded(): lax.ppermute(head, axis, [((i + 1) % count, i) for i in range(ends)])  12.3 us
    gather x2, local copies, waits for them, and re-layouts, shards(): jnp.take(pressure, outlet_ids) * outlet_weights  11.8 us
    slice x2, local copies, waits for them, and re-layouts, rate_of(): values[:, :-1, :]  8.64 us
    gather x1, local copies, waits for them, and re-layouts, shards(): picked = jnp.take(donors, jnp.clip(inlet_ids, 0, row_count - 1), axis=1)  5.48 us
  transfers between devices with their start and end apart: 8, of which 2 were waited for; matrix products, arithmetic and copies ran while one was open for 19% of the time, Pallas kernels for 0%

commit v1 on v0

v1 whole, which is shorter than its diff:
```python
import functools

import jax
import jax.numpy as jnp
from jax import lax
from jax.experimental import pallas as pl
from jax.experimental.pallas import tpu as pltpu
from jax.sharding import PartitionSpec as P

courant = 0.5
diffusion = 0.1
source_step = 0.5

SUB = 8
LANE = 128


def shift_from(axis, count, step, pairs_of):
    return [(i, (i + step) % count) for i in pairs_of]


def step_kernel(nf, rows, lanes, mix_s, act_s, ahi_s, f_hbm, rate_ref, lo1_ref, lo2_ref, hi1_ref,
                hi2_ref, lft_ref, rgt_ref, out_ref, edge_rows_ref, col0_ref, col1_ref, ext1, ext2, sem):
    n_i = rows // SUB
    n_j = lanes // LANE
    top = SUB + rows
    right = LANE + lanes

    copy = pltpu.make_async_copy(f_hbm, ext1.at[:, SUB:top, LANE:right], sem.at[0])
    copy.start()
    ext1[:, SUB - 1:SUB, LANE:right] = lo1_ref[...]
    ext2[:, SUB - 1:SUB, LANE:right] = lo2_ref[...]
    ext1[:, SUB:top, 0:LANE] = jnp.broadcast_to(lft_ref[...], (nf, rows, LANE))
    ext1[:, SUB:top, right:right + LANE] = jnp.broadcast_to(rgt_ref[...], (nf, rows, LANE))
    zeros = jnp.zeros((nf, rows, LANE), jnp.float32)
    ext2[:, SUB:top, 0:LANE] = zeros
    ext2[:, SUB:top, right:right + LANE] = zeros
    copy.wait()
    for f in range(nf):
        ext1[f, top:top + 1, LANE:right] = ahi_s[f] * ext1[f, top - 1:top, LANE:right] + hi1_ref[f]

    sub_id = lax.broadcasted_iota(jnp.int32, (SUB, LANE), 0)
    lane_id = lax.broadcasted_iota(jnp.int32, (SUB, LANE), 1)
    first_sub = sub_id == 0
    last_sub = sub_id == SUB - 1
    first_lane = lane_id == 0
    last_lane = lane_id == LANE - 1

    def tendency_tile(src, r, c, rate_t):
        v4 = src[4, pl.ds(r, SUB), pl.ds(c, LANE)]
        heat = 1.0 + (jnp.maximum(v4, 0.0) + jnp.log1p(jnp.exp(-jnp.abs(v4))))
        inv_heat = 1.0 / heat
        vals = []
        react = []
        for f in range(nf):
            v = src[f, pl.ds(r, SUB), pl.ds(c, LANE)]
            vals.append(v)
            react.append(rate_t * v * jnp.exp(-act_s[f] * inv_heat))
        tends = []
        for f in range(nf):
            v = vals[f]
            up = src[f, pl.ds(r - SUB, SUB), pl.ds(c, LANE)]
            down = src[f, pl.ds(r + SUB, SUB), pl.ds(c, LANE)]
            west = src[f, pl.ds(r, SUB), pl.ds(c - LANE, LANE)]
            east = src[f, pl.ds(r, SUB), pl.ds(c + LANE, LANE)]
            backward = jnp.where(first_sub, pltpu.roll(up, 1, 0), pltpu.roll(v, 1, 0))
            forward = jnp.where(last_sub, pltpu.roll(down, SUB - 1, 0), pltpu.roll(v, SUB - 1, 0))
            left = jnp.where(first_lane, pltpu.roll(west, 1, 1), pltpu.roll(v, 1, 1))
            rgt = jnp.where(last_lane, pltpu.roll(east, LANE - 1, 1), pltpu.roll(v, LANE - 1, 1))
            acc = mix_s[f, 0] * react[0]
            for g in range(1, nf):
                acc = acc + mix_s[f, g] * react[g]
            advect = -courant * (v - backward)
            spread = diffusion * (backward + forward + left + rgt - 4.0 * v)
            tends.append(advect + spread + source_step * acc)
        return vals, tends

    def tile_offsets(t):
        i = t // n_j
        j = t % n_j
        r0 = pl.multiple_of(i * SUB, SUB)
        c0 = pl.multiple_of(j * LANE, LANE)
        return r0, c0

    def stage_one(t, carry):
        r0, c0 = tile_offsets(t)
        rate_t = rate_ref[pl.ds(r0, SUB), pl.ds(c0, LANE)]
        vals, tends = tendency_tile(ext1, r0 + SUB, c0 + LANE, rate_t)
        for f in range(nf):
            ext2[f, pl.ds(r0 + SUB, SUB), pl.ds(c0 + LANE, LANE)] = vals[f] + tends[f]
        return carry

    lax.fori_loop(0, n_i * n_j, stage_one, 0)

    for f in range(nf):
        ext2[f, top:top + 1, LANE:right] = ahi_s[f] * ext2[f, top - 1:top, LANE:right] + hi2_ref[f]

    def stage_two(t, carry):
        r0, c0 = tile_offsets(t)
        rate_t = rate_ref[pl.ds(r0, SUB), pl.ds(c0, LANE)]
        vals, tends = tendency_tile(ext2, r0 + SUB, c0 + LANE, rate_t)
        for f in range(nf):
            base = ext1[f, pl.ds(r0 + SUB, SUB), pl.ds(c0 + LANE, LANE)]
            out_ref[f, pl.ds(r0, SUB), pl.ds(c0, LANE)] = 0.5 * (base + vals[f] + tends[f])
        return carry

    lax.fori_loop(0, n_i * n_j, stage_two, 0)

    edge_rows_ref[:, 0:1, :] = ext2[:, SUB:SUB + 1, LANE:right]
    edge_rows_ref[:, 1:2, :] = ext2[:, top - 1:top, LANE:right]
    col0_ref[...] = ext2[:, SUB:top, LANE:LANE + 1]
    col1_ref[...] = ext2[:, SUB:top, right - 1:right]


def fused_step(fields, rate, mix, act, ahi, lo1, lo2, hi1, hi2, lft, rgt):
    nf, rows, lanes = fields.shape
    vmem = pltpu.VMEM
    smem = pl.BlockSpec(memory_space=pltpu.SMEM)
    vspec = pl.BlockSpec(memory_space=vmem)
    cells = rows * lanes
    cost = pl.CostEstimate(
        flops=2 * cells * nf * (2 * nf + 24),
        transcendentals=2 * cells * (nf + 3),
        bytes_accessed=4 * cells * (2 * nf + 1),
    )
    return pl.pallas_call(
        functools.partial(step_kernel, nf, rows, lanes),
        out_shape=(
            jax.ShapeDtypeStruct((nf, rows, lanes), jnp.float32),
            jax.ShapeDtypeStruct((nf, 2, lanes), jnp.float32),
            jax.ShapeDtypeStruct((nf, rows, 1), jnp.float32),
            jax.ShapeDtypeStruct((nf, rows, 1), jnp.float32),
        ),
        in_specs=[smem, smem, smem, pl.BlockSpec(memory_space=pl.ANY)] + [vspec] * 7,
        out_specs=(vspec, vspec, vspec, vspec),
        scratch_shapes=[
            vmem((nf, rows + 2 * SUB, lanes + 2 * LANE), jnp.float32),
            vmem((nf, rows + 2 * SUB, lanes + 2 * LANE), jnp.float32),
            pltpu.SemaphoreType.DMA((1,)),
        ],
        compiler_params=pltpu.CompilerParams(vmem_limit_bytes=60 * 1024 * 1024),
        cost_estimate=cost,
    )(mix, act, ahi, fields, rate, lo1, lo2, hi1, hi2, lft, rgt)


def shards(
    fields, react_rate, mix_matrix, activation, inlet_ids, inlet_weights, outlet_ids, outlet_weights
):
    nf, rows, lanes = fields.shape
    n_grp = lax.axis_size("grp")
    n_blk = lax.axis_size("blk")
    g = lax.axis_index("grp")
    exit_grp = n_grp - 2
    turb_grp = n_grp - 1
    at_exit = g == exit_grp
    at_turb = g == turb_grp

    last_row = fields[:, -1, :]
    first_row = fields[:, 0, :]
    payload = jnp.concatenate([last_row, first_row[4:5]], axis=0)
    planes = lax.all_gather(payload, "blk", axis=0, tiled=False)
    table = jnp.transpose(planes, (0, 2, 1)).reshape(n_blk * lanes, nf + 1)
    ids = jnp.concatenate([inlet_ids, outlet_ids], axis=0)
    picked = jnp.take(table, ids, axis=0, mode="clip")
    ks = inlet_ids.shape[0]
    inlet = jnp.sum(picked[:ks, :, :nf] * inlet_weights[:, :, None], axis=0)
    back = jnp.sum(picked[ks:, :, nf] * outlet_weights, axis=0)
    swap = jnp.concatenate([jnp.transpose(inlet), back[None]], axis=0)
    swapped = lax.ppermute(swap, "grp", [(exit_grp, turb_grp), (turb_grp, exit_grp)])
    inlet_values = swapped[:nf]
    back_pressure = swapped[nf]

    halo_lo = lax.ppermute(last_row, "grp", [(i, i + 1) for i in range(n_grp - 2)])
    halo_hi = lax.ppermute(first_row, "grp", [(i + 1, i) for i in range(n_grp - 2)])
    lft = lax.ppermute(fields[:, :, -1:], "blk", [(i, (i + 1) % n_blk) for i in range(n_blk)])
    rgt = lax.ppermute(fields[:, :, :1], "blk", [((i + 1) % n_blk, i) for i in range(n_blk)])

    field_id = jnp.arange(nf)
    bp_term = jnp.where((field_id[:, None] == 4) & at_exit, back_pressure[None, :], 0.0)
    lo1 = jnp.where(at_turb, inlet_values, halo_lo)
    lo2 = jnp.where(at_turb, inlet_values, 0.0)
    hi1 = halo_hi + bp_term
    hi2 = bp_term
    ahi = jnp.where(at_turb, 1.0, jnp.where(at_exit & (field_id != 4), 1.0, 0.0)).astype(jnp.float32)

    out, edge_rows, col0, col1 = fused_step(
        fields, react_rate, mix_matrix, activation, ahi,
        lo1[:, None, :], lo2[:, None, :], hi1[:, None, :], hi2[:, None, :], lft, rgt,
    )

    g0 = lax.ppermute(edge_rows[:, 1, :], "grp", [(i, i + 1) for i in range(n_grp - 2)])
    g1 = lax.ppermute(edge_rows[:, 0, :], "grp", [(i + 1, i) for i in range(n_grp - 2)])
    gl = lax.ppermute(col1, "blk", [(i, (i + 1) % n_blk) for i in range(n_blk)])
    gr = lax.ppermute(col0, "blk", [((i + 1) % n_blk, i) for i in range(n_blk)])
    low_w = 0.5 * (courant + diffusion)
    side_w = 0.5 * diffusion
    row = lax.slice_in_dim(out, 0, 1, axis=1) + low_w * g0[:, None, :]
    out = lax.dynamic_update_slice(out, row, (0, 0, 0))
    row = lax.slice_in_dim(out, rows - 1, rows, axis=1) + side_w * g1[:, None, :]
    out = lax.dynamic_update_slice(out, row, (0, rows - 1, 0))
    col = lax.slice_in_dim(out, 0, 1, axis=2) + side_w * gl
    out = lax.dynamic_update_slice(out, col, (0, 0, 0))
    col = lax.slice_in_dim(out, lanes - 1, lanes, axis=2) + side_w * gr
    return lax.dynamic_update_slice(out, col, (0, 0, lanes - 1))


def solution(mesh):
    in_specs = (
        P(None, "grp", "blk"),
        P("grp", "blk"),
        P(),
        P(),
        P(None, "blk"),
        P(None, "blk"),
        P(None, "blk"),
        P(None, "blk"),
    )
    out_specs = P(None, "grp", "blk")
    return jax.shard_map(shards, mesh=mesh, in_specs=in_specs, out_specs=out_specs, check_vma=False)
```

time: 160 us -> 149 us (0.931)
  matrix products: 30.6 us -> 0 us
  Pallas kernels: 0 us -> 27.1 us
  blocking collectives: 46.5 us -> 25.1 us
  local copies, waits for them, and re-layouts: 42.7 us -> 62 us
  other arithmetic: 7.22 us -> 3.75 us
  waiting for transfers between devices: 1.97 us -> 0.23 us
    dot_general x2 -> x0, matrix products: 30.6 us -> none  [tendency(): jnp.einsum('fg,gxr->fxr', mix_matrix, reaction, precision=lax.Precision.H...]
    pallas_call x0 -> x1, Pallas kernels: none -> 27.1 us  [fused_step(): pl.pallas_call(functools.partial(step_kernel, nf, rows, lanes), out_shape...]
    dynamic_update_slice x0 -> x3, local copies, waits for them, and re-layouts: none -> 22.1 us  [the longest x2 18.2 us: shards(): return lax.dynamic_update_slice(out, col, (0, 0, lanes - 1))]
    all_gather x2 -> x1, blocking collectives: 46.5 us -> 25.1 us  [shards(): planes = lax.all_gather(payload, 'blk', axis=0, tiled=False)]
    pallas_call x0 -> x4, local copies, waits for them, and re-layouts: none -> 7.99 us  [fused_step(): pl.pallas_call(functools.partial(step_kernel, nf, rows, lanes), out_shape...]
    add x2 -> x3, other arithmetic: 4.17 us -> 0.1 us  [the longest x1 0.08 us: shards(): hi1 = halo_hi + bp_term]
    mul x1 -> x0, local copies, waits for them, and re-layouts: 3.96 us -> none  [shards(): 0.5 * (fields + first_section + rate_of(first_section, second_axial, seco...]
    slice x9 -> x10, local copies, waits for them, and re-layouts: 11.6 us -> 8.51 us  [the longest x2 1.95 us: shards(): col = lax.slice_in_dim(out, lanes - 1, lanes, axis=2) + side_w * gr]
  transfers between devices with their start and end apart: 8 -> 9, of which waited for: 2 -> 1; matrix products, arithmetic and copies ran while one was open for 19% -> 28% of each run, Pallas kernels for 0% -> 0%
where the time goes in v1:
time: 149 us
  local copies, waits for them, and re-layouts  62 us (42%)
  starting transfers between devices  30.3 us (20%)
  Pallas kernels  27.1 us (18%)
  blocking collectives  25.1 us (17%)
  other arithmetic  3.75 us (3%)
    pallas_call x1, Pallas kernels, fused_step(): pl.pallas_call(functools.partial(step_kernel, nf, rows, lanes), out_shape...  27.1 us
    all_gather x1, blocking collectives, shards(): planes = lax.all_gather(payload, 'blk', axis=0, tiled=False)  25.1 us
    dynamic_update_slice x2, local copies, waits for them, and re-layouts, shards(): return lax.dynamic_update_slice(out, col, (0, 0, lanes - 1))  18.2 us
    gather x1, local copies, waits for them, and re-layouts, shards(): picked = jnp.take(table, ids, axis=0, mode='clip')  14.2 us
    ppermute x1, starting transfers between devices, shards(): lax.ppermute(edge_rows[:, 1, :], 'grp', [(i, i + 1) for i in range(n_grp...  12.1 us
    pallas_call x4, local copies, waits for them, and re-layouts, fused_step(): pl.pallas_call(functools.partial(step_kernel, nf, rows, lanes), out_shape...  7.99 us
    ppermute x1, starting transfers between devices, shards(): gr = lax.ppermute(col0, 'blk', [((i + 1) % n_blk, i) for i in range(n_blk)])  4.72 us
    ppermute x1, starting transfers between devices, shards(): lax.ppermute(last_row, 'grp', [(i, i + 1) for i in range(n_grp - 2)])  4.54 us
  transfers between devices with their start and end apart: 9, of which 1 were waited for; matrix products, arithmetic and copies ran while one was open for 28% of the time, Pallas kernels for 0%

profile of v1, /device:TPU:1, one launch (start us, length us, event | category | flops | bytes accessed | tf_op | source)
XLA Modules:
  0.0 148.6 jit_solution(2077258989630824177)
XLA Ops:
  0.0 1.1 fusion.5
  1.1 4.5 %collective-permute-start.1 = (f32[14,512]{1,0:T(8,128)S(1)}, f32[14,512]{1,0:T(8,128)S(1)}, u32[]{:S(2)}, u32[]{:S(2)}) collective-permute-start(f32[14,512]{1,0:T(8,128)S(1)} %bitcast.41), channel_id=1, source_target_pairs={{0,8},{8,16},{1,9},{9,17},{2,10},{10,18},{3,11},{11,19},{4,12},{12... | collective-permute-start | bytes 86024 | tf_op jit(solution)/shard_map/ppermute | solution.py:173
  5.7 1.9 %collective-permute-start.2 = (f32[14,512]{1,0:T(8,128)S(1)}, f32[14,512]{1,0:T(8,128)S(1)}, u32[]{:S(2)}, u32[]{:S(2)}) collective-permute-start(f32[14,512]{1,0:T(8,128)S(1)} %bitcast.44), channel_id=1, source_target_pairs={{8,0},{16,8},{9,1},{17,9},{10,2},{18,10},{11,3},{19,11},{12,4},{20... | collective-permute-start | bytes 86024 | tf_op jit(solution)/shard_map/ppermute | solution.py:174
  7.6 0.7 slice_bitcast_fusion.1
  8.3 0.7 add_bitcast_fusion
  9.1 25.1 %all-gather.1 = f32[8,15,512]{2,1,0:T(8,128)S(1)} all-gather(f32[1,15,512]{2,1,0:T(8,128)S(1)} %maximum_bitcast_fusion), channel_id=2, replica_groups=mesh['grp'=4,'blk'=8] {'blk'}, dimensions={0}, use_global_device_ids=true | all-gather | bytes 276480 | tf_op jit(solution)/shard_map/all_gather | solution.py:161
  34.2 0.6 copy.71
  34.8 0.0 copy-start.1
  34.8 14.2 %gather_fusion = f32[4096,15]{1,0:T(8,128)} fusion(f32[4096,15]{1,0:T(8,128)S(1)} %bitcast.36, s32[4096]{0:T(1024)S(1)} %broadcast_clamp_fusion), kind=kCustom, calls=%fused_computation | custom fusion | bytes 507904 | tf_op jit(solution)/shard_map/jit(_take)/gather | solution.py:164
  49.0 0.0 copy-start.2
  49.0 1.6 %slice.68 = f32[4,512,1]{2,1,0:T(8,128)S(1)} slice(f32[8,512,15]{2,1,0:T(8,128)} %bitcast.37), slice={[4:8], [0:512], [14:15]} | slice | bytes 16384 | tf_op jit(solution)/shard_map/slice | solution.py:167
  50.6 0.0 copy-done.1
  50.6 1.6 %fusion = f32[512,14]{1,0:T(8,128)S(1)} fusion(f32[8,512,15]{2,1,0:T(8,128)} %bitcast.38, f32[4,512]{1,0:T(4,128)S(1)} %copy-done.1), kind=kLoop, calls=%fused_computation.2 | loop fusion | flops 50176 | bytes 151552 | tf_op jit(solution)/shard_map/reduce_sum | solution.py:166
  52.2 0.3 copy.75
  52.5 0.1 copy.52
  52.6 0.0 copy-done.2
  52.7 0.7 collective-permute-start
  53.4 1.8 %fusion.4 = (f32[14,128,1]{2,1,0:T(8,128)S(1)}, f32[14,128,1]{2,1,0:T(8,128)S(1)}) fusion(f32[14,128,512]{2,1,0:T(8,128)} %f_hbm.1), kind=kLoop, calls=%fused_computation.27 | loop fusion | bytes 28672 | tf_op jit(solution)/shard_map/slice | solution.py:176
  55.2 0.3 copy.77
  55.5 0.9 collective-permute-start.3
  56.3 0.3 copy.78
  56.6 3.3 %collective-permute-start.4 = (f32[14,128,1]{1,2,0:T(1,128)S(1)}, f32[14,128,1]{1,2,0:T(1,128)S(1)}, u32[]{:S(2)}, u32[]{:S(2)}) collective-permute-start(f32[14,128,1]{1,2,0:T(1,128)S(1)} %copy.78), channel_id=1, source_target_pairs={{1,0},{2,1},{3,2},{4,3},{5,4},{6,5},{7,6},{0,7},{9,8},{10,9},{11,1... | collective-permute-start | bytes 21512 | tf_op jit(solution)/shard_map/ppermute | solution.py:176
  60.0 0.6 broadcast_select_fusion.1.ahi_s
  60.5 0.2 collective-permute-done.4
  60.7 1.3 copy.60.rgt_ref
  62.1 0.0 collective-permute-done.3
  62.1 1.3 copy.59.lft_ref
  63.3 0.0 collective-permute-done
  63.3 0.0 collective-permute-done.2
  63.3 0.1 select_add_fusion
  63.4 0.7 broadcast_select_fusion.hi2_ref
  64.1 0.6 broadcast_in_dim.71.hi1_ref
  64.8 0.0 collective-permute-done.1
  64.8 0.6 copy.58.lo2_ref
  65.4 0.6 copy.57.lo1_ref
  66.0 27.1 %shard_map.82 = (f32[14,128,512]{2,1,0:T(8,128)}, f32[14,2,512]{2,1,0:T(2,128)}, f32[14,128,1]{2,1,0:T(8,128)}, f32[14,128,1]{2,1,0:T(8,128)}) custom-call(f32[14,14]{1,0:T(8,128)} %mix_s.1, f32[14]{0:T(128)} %act_s.1, f32[14]{0:T(128)} %broadcast_select_fusion.1.ahi_s, f32[14,128,512]{2,1,0:T(8,128)} %f_hbm.1, f32[128,512]{1,0:T(8,128)} %rate_ref.1, ...), custom_call_target="tpu_custom_call" | custom-call | flops 95420416 | bytes 7602176 | tf_op jit(solution)/shard_map/pallas_call | solution.py:126
  93.1 0.8 copy.62
  94.0 12.1 %collective-permute-start.5 = (f32[14,512]{1,0:T(8,128)S(1)}, f32[14,512]{1,0:T(8,128)S(1)}, u32[]{:S(2)}, u32[]{:S(2)}) collective-permute-start(f32[14,512]{1,0:T(8,128)S(1)} %slice_bitcast_fusion), channel_id=1, source_target_pairs={{0,8},{8,16},{1,9},{9,17},{2,10},{10,18},{3,11},{11,19},{4,12},{12... | collective-permute-start | bytes 86024 | tf_op jit(solution)/shard_map/ppermute | solution.py:191
  106.1 0.8 slice.62
  106.9 1.5 copy.64
  108.4 1.5 copy.67
  109.9 4.7 %collective-permute-start.8 = (f32[14,128,1]{1,2,0:T(1,128)S(1)}, f32[14,128,1]{1,2,0:T(1,128)S(1)}, u32[]{:S(2)}, u32[]{:S(2)}) collective-permute-start(f32[14,128,1]{1,2,0:T(1,128)S(1)} %copy.67), channel_id=1, source_target_pairs={{1,0},{2,1},{3,2},{4,3},{5,4},{6,5},{7,6},{0,7},{9,8},{10,9},{11,1... | collective-permute-start | bytes 21512 | tf_op jit(solution)/shard_map/ppermute | solution.py:194
  114.6 0.0 collective-permute-start.7
  114.6 2.1 %collective-permute-start.6 = (f32[14,512]{1,0:T(8,128)S(1)}, f32[14,512]{1,0:T(8,128)S(1)}, u32[]{:S(2)}, u32[]{:S(2)}) collective-permute-start(f32[14,512]{1,0:T(8,128)S(1)} %bitcast.45), channel_id=1, source_target_pairs={{8,0},{16,8},{9,1},{17,9},{10,2},{18,10},{11,3},{19,11},{12,4},{20... | collective-permute-start | bytes 86024 | tf_op jit(solution)/shard_map/ppermute | solution.py:192
  116.7 4.2 %copy.63 = f32[14,128,512]{2,0,1:T(8,128)S(1)} copy(f32[14,128,512]{2,1,0:T(8,128)} %get-tuple-element.9) | data formatting | bytes 7340032 | tf_op jit(solution)/shard_map/pallas_call | solution.py:126
  120.9 0.0 collective-permute-done.5
  120.9 0.0 collective-permute-done.6
  121.0 0.0 copy-start
  121.0 1.9 %copy-done = f32[14,128,512]{2,0,1:T(8,128)} copy-done((f32[14,128,512]{2,0,1:T(8,128)}, f32[14,128,512]{2,0,1:T(8,128)S(1)}, u32[]{:S(2)}) %copy-start) | copy-done | bytes 3670040
  122.9 0.1 slice.74
  123.1 0.4 copy.65
  123.5 0.0 collective-permute-done.7
  123.5 0.5 copy.66
  124.0 3.9 %dynamic_update_slice.14 = f32[14,128,512]{2,0,1:T(8,128)} dynamic-update-slice(f32[14,128,512]{2,0,1:T(8,128)} %copy-done, f32[14,128,1]{2,0,1:T(8,128)S(1)} %copy.66, s32[]{:T(128)} %constant.6.clone.1, s32[]{:T(128)} %constant.6.clone.1, s32[]{:T(128)} %constant.6.clone.1) | dynamic-update-slice | bytes 14340 | tf_op jit(solution)/shard_map/dynamic_update_slice | solution.py:202
  128.0 1.6 %slice.75 = f32[14,128,1]{2,0,1:T(8,128)S(1)} slice(f32[14,128,512]{2,0,1:T(8,128)} %dynamic_update_slice.14), slice={[0:14], [0:128], [511:512]} | slice | bytes 14336 | tf_op jit(solution)/shard_map/slice | solution.py:203
  129.5 0.4 copy.68
  129.9 0.0 collective-permute-done.8
  129.9 0.5 copy.69
  130.5 12.0 %dynamic_update_slice.15 = f32[14,128,512]{2,0,1:T(8,128)} dynamic-update-slice(f32[14,128,512]{2,0,1:T(8,128)} %dynamic_update_slice.14, f32[14,128,1]{2,0,1:T(8,128)S(1)} %copy.69, s32[]{:T(128)} %constant.6.clone.1, s32[]{:T(128)} %constant.6.clone.1, s32[]{:T(128)} %constant.9.clone.1) | dynamic-update-slice | bytes 14340 | tf_op jit(solution)/shard_map/dynamic_update_slice | solution.py:204
  142.5 6.1 %copy.70 = f32[14,128,512]{2,1,0:T(8,128)} copy(f32[14,128,512]{2,0,1:T(8,128)} %dynamic_update_slice.15) | data formatting | bytes 7340032 | tf_op jit(solution)/shard_map/dynamic_update_slice | solution.py:204
  (16 shorter events, 0.1 us)
Async XLA Ops:
  1.1 63.6 %collective-permute-start.1 = (f32[14,512]{1,0:T(8,128)S(1)}, f32[14,512]{1,0:T(8,128)S(1)}, u32[]{:S(2)}, u32[]{:S(2)}) collective-permute-start(f32[14,512]{1,0:T(8,128)S(1)} %bitcast.41), channel_id=1, source_target_pairs={{0,8},{8,16},{1,9},{9,17},{2,10},{10,18},{3,11},{11,19},{4,12},{12... | collective-permute-start | bytes 86024 | tf_op jit(solution)/shard_map/ppermute | solution.py:173
  5.7 57.7 %collective-permute-start.2 = (f32[14,512]{1,0:T(8,128)S(1)}, f32[14,512]{1,0:T(8,128)S(1)}, u32[]{:S(2)}, u32[]{:S(2)}) collective-permute-start(f32[14,512]{1,0:T(8,128)S(1)} %bitcast.44), channel_id=1, source_target_pairs={{8,0},{16,8},{9,1},{17,9},{10,2},{18,10},{11,3},{19,11},{12,4},{20... | collective-permute-start | bytes 86024 | tf_op jit(solution)/shard_map/ppermute | solution.py:174
  34.8 15.8 %copy-start.1 = (f32[4,512]{1,0:T(4,128)S(1)}, f32[4,512]{1,0:T(4,128)}, u32[]{:S(2)}) copy-start(f32[4,512]{1,0:T(4,128)} %param.13) | copy-start | bytes 24580
  49.0 3.6 %copy-start.2 = (f32[4,512]{1,0:T(4,128)S(1)}, f32[4,512]{1,0:T(4,128)}, u32[]{:S(2)}) copy-start(f32[4,512]{1,0:T(4,128)} %param.15) | copy-start | bytes 24580
  52.7 10.7 %collective-permute-start = (f32[15,512]{1,0:T(8,128)S(1)}, f32[15,512]{1,0:T(8,128)S(1)}, u32[]{:S(2)}, u32[]{:S(2)}) collective-permute-start(f32[15,512]{1,0:T(8,128)S(1)} %pad_maximum_fusion), channel_id=1, source_target_pairs={{16,24},{24,16},{17,25},{25,17},{18,26},{26,18},{19,27},{27,19},{2... | collective-permute-start | bytes 92168 | tf_op jit(solution)/shard_map/ppermute | solution.py:169
  55.5 6.6 %collective-permute-start.3 = (f32[14,128,1]{1,2,0:T(1,128)S(1)}, f32[14,128,1]{1,2,0:T(1,128)S(1)}, u32[]{:S(2)}, u32[]{:S(2)}) collective-permute-start(f32[14,128,1]{1,2,0:T(1,128)S(1)} %copy.77), channel_id=1, source_target_pairs={{0,1},{1,2},{2,3},{3,4},{4,5},{5,6},{6,7},{7,0},{8,9},{9,10},{10,1... | collective-permute-start | bytes 21512 | tf_op jit(solution)/shard_map/ppermute | solution.py:175
  56.6 4.1 %collective-permute-start.4 = (f32[14,128,1]{1,2,0:T(1,128)S(1)}, f32[14,128,1]{1,2,0:T(1,128)S(1)}, u32[]{:S(2)}, u32[]{:S(2)}) collective-permute-start(f32[14,128,1]{1,2,0:T(1,128)S(1)} %copy.78), channel_id=1, source_target_pairs={{1,0},{2,1},{3,2},{4,3},{5,4},{6,5},{7,6},{0,7},{9,8},{10,9},{11,1... | collective-permute-start | bytes 21512 | tf_op jit(solution)/shard_map/ppermute | solution.py:176
  94.0 27.0 %collective-permute-start.5 = (f32[14,512]{1,0:T(8,128)S(1)}, f32[14,512]{1,0:T(8,128)S(1)}, u32[]{:S(2)}, u32[]{:S(2)}) collective-permute-start(f32[14,512]{1,0:T(8,128)S(1)} %slice_bitcast_fusion), channel_id=1, source_target_pairs={{0,8},{8,16},{1,9},{9,17},{2,10},{10,18},{3,11},{11,19},{4,12},{12... | collective-permute-start | bytes 86024 | tf_op jit(solution)/shard_map/ppermute | solution.py:191
  109.9 20.0 %collective-permute-start.8 = (f32[14,128,1]{1,2,0:T(1,128)S(1)}, f32[14,128,1]{1,2,0:T(1,128)S(1)}, u32[]{:S(2)}, u32[]{:S(2)}) collective-permute-start(f32[14,128,1]{1,2,0:T(1,128)S(1)} %copy.67), channel_id=1, source_target_pairs={{1,0},{2,1},{3,2},{4,3},{5,4},{6,5},{7,6},{0,7},{9,8},{10,9},{11,1... | collective-permute-start | bytes 21512 | tf_op jit(solution)/shard_map/ppermute | solution.py:194
  114.6 8.9 %collective-permute-start.7 = (f32[14,128,1]{1,2,0:T(1,128)S(1)}, f32[14,128,1]{1,2,0:T(1,128)S(1)}, u32[]{:S(2)}, u32[]{:S(2)}) collective-permute-start(f32[14,128,1]{1,2,0:T(1,128)S(1)} %copy.64), channel_id=1, source_target_pairs={{0,1},{1,2},{2,3},{3,4},{4,5},{5,6},{6,7},{7,0},{8,9},{9,10},{10,1... | collective-permute-start | bytes 21512 | tf_op jit(solution)/shard_map/ppermute | solution.py:193
  114.6 6.3 %collective-permute-start.6 = (f32[14,512]{1,0:T(8,128)S(1)}, f32[14,512]{1,0:T(8,128)S(1)}, u32[]{:S(2)}, u32[]{:S(2)}) collective-permute-start(f32[14,512]{1,0:T(8,128)S(1)} %bitcast.45), channel_id=1, source_target_pairs={{8,0},{16,8},{9,1},{17,9},{10,2},{18,10},{11,3},{19,11},{12,4},{20... | collective-permute-start | bytes 86024 | tf_op jit(solution)/shard_map/ppermute | solution.py:192
  121.0 1.9 %copy-start = (f32[14,128,512]{2,0,1:T(8,128)}, f32[14,128,512]{2,0,1:T(8,128)S(1)}, u32[]{:S(2)}) copy-start(f32[14,128,512]{2,0,1:T(8,128)S(1)} %fusion.1) | copy-start | bytes 11010052

commit v2 on v1

--- a/solution.py
+++ b/solution.py
@@ -143,6 +143,85 @@
     )(mix, act, ahi, fields, rate, lo1, lo2, hi1, hi2, lft, rgt)
 
 
+def interp_kernel(ks, ids_s, w_s, table_ref, o_ref):
+    lanes = o_ref.shape[1]
+
+    def body(p, carry):
+        for half in range(2):
+            acc = None
+            for k in range(ks):
+                row = half * ks + k
+                q = ids_s[row, p]
+                term = w_s[row, p] * table_ref[pl.ds(q, 1), :]
+                acc = term if acc is None else acc + term
+            o_ref[half, pl.ds(p, 1), :] = acc
+        return carry
+
+    lax.fori_loop(0, lanes, body, 0)
+
+
+def interpolate(ids, weights, table):
+    ks2, lanes = ids.shape
+    smem = pl.BlockSpec(memory_space=pltpu.SMEM)
+    vspec = pl.BlockSpec(memory_space=pltpu.VMEM)
+    return pl.pallas_call(
+        functools.partial(interp_kernel, ks2 // 2),
+        out_shape=jax.ShapeDtypeStruct((2, lanes, table.shape[1]), jnp.float32),
+        in_specs=[smem, smem, vspec],
+        out_specs=vspec,
+    )(ids, weights, table)
+
+
+def fix_kernel(low_w, side_w, out_in, g0_ref, g1_ref, gl_ref, gr_ref, out_ref, rb, cb, sem):
+    nf, rows, lanes = out_ref.shape
+    row_win = (pl.ds(0, SUB), pl.ds(rows - SUB, SUB))
+    col_win = (pl.ds(0, LANE), pl.ds(lanes - LANE, LANE))
+    loads = [pltpu.make_async_copy(out_ref.at[:, row_win[s], :], rb.at[s], sem.at[s]) for s in range(2)]
+    for c in loads:
+        c.start()
+    for c in loads:
+        c.wait()
+    sub_id = lax.broadcasted_iota(jnp.int32, (nf, SUB, lanes), 1)
+    rb[0] = rb[0] + jnp.where(sub_id == 0, low_w * g0_ref[...], 0.0)
+    rb[1] = rb[1] + jnp.where(sub_id == SUB - 1, side_w * g1_ref[...], 0.0)
+    stores = [pltpu.make_async_copy(rb.at[s], out_ref.at[:, row_win[s], :], sem.at[s]) for s in range(2)]
+    for c in stores:
+        c.start()
+    for c in stores:
+        c.wait()
+    loads = [pltpu.make_async_copy(out_ref.at[:, :, col_win[s]], cb.at[s], sem.at[s]) for s in range(2)]
+    for c in loads:
+        c.start()
+    for c in loads:
+        c.wait()
+    lane_id = lax.broadcasted_iota(jnp.int32, (nf, rows, LANE), 2)
+    cb[0] = cb[0] + jnp.where(lane_id == 0, side_w * gl_ref[...], 0.0)
+    cb[1] = cb[1] + jnp.where(lane_id == LANE - 1, side_w * gr_ref[...], 0.0)
+    stores = [pltpu.make_async_copy(cb.at[s], out_ref.at[:, :, col_win[s]], sem.at[s]) for s in range(2)]
+    for c in stores:
+        c.start()
+    for c in stores:
+        c.wait()
+
+
+def fix_edges(out, g0, g1, gl, gr, low_w, side_w):
+    nf, rows, lanes = out.shape
+    vspec = pl.BlockSpec(memory_space=pltpu.VMEM)
+    anyspec = pl.BlockSpec(memory_space=pl.ANY)
+    return pl.pallas_call(
+        functools.partial(fix_kernel, low_w, side_w),
+        out_shape=jax.ShapeDtypeStruct(out.shape, jnp.float32),
+        in_specs=[anyspec, vspec, vspec, vspec, vspec],
+        out_specs=anyspec,
+        scratch_shapes=[
+            pltpu.VMEM((2, nf, SUB, lanes), jnp.float32),
+            pltpu.VMEM((2, nf, rows, LANE), jnp.float32),
+            pltpu.SemaphoreType.DMA((2,)),
+        ],
+        input_output_aliases={0: 0},
+    )(out, g0, g1, gl, gr)
+
+
 def shards(
     fields, react_rate, mix_matrix, activation, inlet_ids, inlet_weights, outlet_ids, outlet_weights
 ):
@@ -157,14 +236,17 @@
 
     last_row = fields[:, -1, :]
     first_row = fields[:, 0, :]
+    b = lax.axis_index("blk")
     payload = jnp.concatenate([last_row, first_row[4:5]], axis=0)
-    planes = lax.all_gather(payload, "blk", axis=0, tiled=False)
+    slots = jnp.zeros((n_blk, nf + 1, lanes), jnp.float32)
+    slots = lax.dynamic_update_slice(slots, payload[None], (b, 0, 0))
+    planes = lax.psum(slots, "blk")
     table = jnp.transpose(planes, (0, 2, 1)).reshape(n_blk * lanes, nf + 1)
     ids = jnp.concatenate([inlet_ids, outlet_ids], axis=0)
-    picked = jnp.take(table, ids, axis=0, mode="clip")
-    ks = inlet_ids.shape[0]
-    inlet = jnp.sum(picked[:ks, :, :nf] * inlet_weights[:, :, None], axis=0)
-    back = jnp.sum(picked[ks:, :, nf] * outlet_weights, axis=0)
+    wts = jnp.concatenate([inlet_weights, outlet_weights], axis=0)
+    picked = interpolate(ids, wts, table)
+    inlet = picked[0, :, :nf]
+    back = picked[1, :, nf]
     swap = jnp.concatenate([jnp.transpose(inlet), back[None]], axis=0)
     swapped = lax.ppermute(swap, "grp", [(exit_grp, turb_grp), (turb_grp, exit_grp)])
     inlet_values = swapped[:nf]
@@ -194,14 +276,7 @@
     gr = lax.ppermute(col0, "blk", [((i + 1) % n_blk, i) for i in range(n_blk)])
     low_w = 0.5 * (courant + diffusion)
     side_w = 0.5 * diffusion
-    row = lax.slice_in_dim(out, 0, 1, axis=1) + low_w * g0[:, None, :]
-    out = lax.dynamic_update_slice(out, row, (0, 0, 0))
-    row = lax.slice_in_dim(out, rows - 1, rows, axis=1) + side_w * g1[:, None, :]
-    out = lax.dynamic_update_slice(out, row, (0, rows - 1, 0))
-    col = lax.slice_in_dim(out, 0, 1, axis=2) + side_w * gl
-    out = lax.dynamic_update_slice(out, col, (0, 0, 0))
-    col = lax.slice_in_dim(out, lanes - 1, lanes, axis=2) + side_w * gr
-    return lax.dynamic_update_slice(out, col, (0, 0, lanes - 1))
+    return fix_edges(out, g0[:, None, :], g1[:, None, :], gl, gr, low_w, side_w)
 
 
 def solution(mesh):

time: 149 us -> 203 us (1.36)
  waiting for transfers between devices: 0.23 us -> 99.4 us
  local copies, waits for them, and re-layouts: 62 us -> 20.3 us
  blocking collectives: 25.1 us -> 0 us
  Pallas kernels: 27.1 us -> 44.7 us
  between operations: 0.24 us -> 13.6 us
  starting transfers between devices: 30.3 us -> 22.1 us
    psum x0 -> x1, waiting for transfers between devices: none -> 99.4 us  [shards(): planes = lax.psum(slots, 'blk')]
    all_gather x1 -> x0, blocking collectives: 25.1 us -> none  [shards(): planes = lax.all_gather(payload, 'blk', axis=0, tiled=False)]
    dynamic_update_slice x3 -> x1, local copies, waits for them, and re-layouts: 22.1 us -> 0.03 us  [shards(): slots = lax.dynamic_update_slice(slots, payload[None], (b, 0, 0))]
    pallas_call x0 -> x2, Pallas kernels: none -> 17.6 us  [the longest x1 11 us: interpolate(): pl.pallas_call(functools.partial(interp_kernel, ks2 // 2), out_shape=jax....]
    gather x1 -> x0, local copies, waits for them, and re-layouts: 14.2 us -> none  [shards(): picked = jnp.take(table, ids, axis=0, mode='clip')]
    ppermute x1, starting transfers between devices: 12.1 us -> 3.63 us  [shards(): lax.ppermute(edge_rows[:, 1, :], 'grp', [(i, i + 1) for i in range(n_grp...]
    pallas_call x4 -> x3, local copies, waits for them, and re-layouts: 7.99 us -> 3.78 us  [fused_step(): pl.pallas_call(functools.partial(step_kernel, nf, rows, lanes), out_shape...]
    slice x6 -> x2, local copies, waits for them, and re-layouts: 4.89 us -> 2.15 us  [the longest x1 1.18 us: shards(): back = picked[1, :, nf]]
  transfers between devices with their start and end apart: 9 -> 10, of which waited for: 1 -> 1; matrix products, arithmetic and copies ran while one was open for 28% -> 9% of each run, Pallas kernels for 0% -> 5%
where the time goes in v2:
time: 203 us
  waiting for transfers between devices  99.4 us (49%)
  Pallas kernels  44.7 us (22%)
  starting transfers between devices  22.1 us (11%)
  local copies, waits for them, and re-layouts  20.3 us (10%)
  between operations  13.6 us (7%)
  other arithmetic  2.62 us (1%)
    psum x1, waiting for transfers between devices, shards(): planes = lax.psum(slots, 'blk')  99.4 us
    pallas_call x1, Pallas kernels, fused_step(): pl.pallas_call(functools.partial(step_kernel, nf, rows, lanes), out_shape...  27.1 us
    pallas_call x1, Pallas kernels, interpolate(): pl.pallas_call(functools.partial(interp_kernel, ks2 // 2), out_shape=jax....  11 us
    pallas_call x1, Pallas kernels, fix_edges(): pl.pallas_call(functools.partial(fix_kernel, low_w, side_w), out_shape=ja...  6.61 us
    ppermute x1, starting transfers between devices, shards(): lax.ppermute(last_row, 'grp', [(i, i + 1) for i in range(n_grp - 2)])  4.54 us
  transfers between devices with their start and end apart: 10, of which 1 were waited for; matrix products, arithmetic and copies ran while one was open for 9% of the time, Pallas kernels for 5%

profile of v2, /device:TPU:1, one launch (start us, length us, event | category | flops | bytes accessed | tf_op | source)
XLA Modules:
  0.0 202.7 jit_solution(133226585889447819)
XLA Ops:
  6.5 0.0 all-reduce.2.cloned.1.call-start
  6.5 1.1 fusion.1
  7.6 4.5 %collective-permute-start.1 = (f32[14,512]{1,0:T(8,128)S(1)}, f32[14,512]{1,0:T(8,128)S(1)}, u32[]{:S(2)}, u32[]{:S(2)}) collective-permute-start(f32[14,512]{1,0:T(8,128)S(1)} %bitcast.28), channel_id=1, source_target_pairs={{0,8},{8,16},{1,9},{9,17},{2,10},{10,18},{3,11},{11,19},{4,12},{12... | collective-permute-start | bytes 86024 | tf_op jit(solution)/shard_map/ppermute | solution.py:255
  12.2 1.9 collective-permute-start.2
  14.1 1.8 fusion
  15.9 0.0 copy-start.1
  15.9 0.0 copy-start.2
  16.0 0.0 copy-start.3
  16.0 0.0 copy-start.4
  16.0 0.3 copy.45
  16.3 1.2 collective-permute-start.3
  17.5 0.3 copy.46
  17.8 3.1 %collective-permute-start.4 = (f32[14,128,1]{1,2,0:T(1,128)S(1)}, f32[14,128,1]{1,2,0:T(1,128)S(1)}, u32[]{:S(2)}, u32[]{:S(2)}) collective-permute-start(f32[14,128,1]{1,2,0:T(1,128)S(1)} %copy.46), channel_id=1, source_target_pairs={{1,0},{2,1},{3,2},{4,3},{5,4},{6,5},{7,6},{0,7},{9,8},{10,9},{11,1... | collective-permute-start | bytes 21512 | tf_op jit(solution)/shard_map/ppermute | solution.py:258
  20.9 0.7 slice_bitcast_fusion.2
  21.6 0.1 copy.27
  21.8 0.1 broadcast_in_dim.65
  21.9 0.0 copy-start
  21.9 1.3 copy-done
  23.3 0.0 all-reduce.2.cloned.1.call-update
  23.3 0.0 copy-done.1
  23.3 0.0 copy-done.2
  23.3 0.6 pad_add_fusion.ids_s
  23.9 0.0 copy-done.3
  23.9 0.0 copy-done.4
  23.9 0.6 pad_maximum_fusion.1.w_s
  24.5 99.4 %all-reduce.2.cloned.1.call-done.table_ref = f32[4096,15]{1,0:T(8,128)} async-done(((f32[4096,15]{1,0:T(8,128)}), f32[4096,15]{1,0:T(8,128)}) %all-reduce.2.cloned.1.call-update) | async-done | bytes 245776 | tf_op jit(solution)/shard_map/psum | solution.py:243
  123.9 11.0 %shard_map.82 = f32[2,512,15]{2,1,0:T(8,128)} custom-call(s32[8,512]{1,0:T(8,128)} %pad_add_fusion.ids_s, f32[8,512]{1,0:T(8,128)} %pad_maximum_fusion.1.w_s, f32[4096,15]{1,0:T(8,128)} %all-reduce.2.cloned.1.call-done.table_ref), custom_call_target="tpu_custom_call" | custom-call | tf_op jit(solution)/shard_map/pallas_call | solution.py:167
  134.9 1.2 slice_reduce_fusion
  136.1 1.0 slice.49
  137.1 0.1 copy.43
  137.2 0.7 collective-permute-start
  137.9 0.6 broadcast_select_fusion.1.ahi_s
  138.5 0.0 collective-permute-done.4
  138.5 1.3 copy.35.rgt_ref
  139.8 0.0 collective-permute-done.3
  139.8 1.3 copy.34.lft_ref
  141.1 0.0 collective-permute-done
  141.1 0.0 collective-permute-done.2
  141.1 0.1 select_add_fusion
  141.2 0.7 broadcast_select_fusion.hi2_ref
  141.9 0.6 broadcast_in_dim.73.hi1_ref
  142.5 0.0 collective-permute-done.1
  142.5 0.6 copy.33.lo2_ref
  143.2 0.6 copy.32.lo1_ref
  143.8 27.1 %shard_map.83 = (f32[14,128,512]{2,1,0:T(8,128)}, f32[14,2,512]{2,1,0:T(2,128)}, f32[14,128,1]{2,1,0:T(8,128)}, f32[14,128,1]{2,1,0:T(8,128)}) custom-call(f32[14,14]{1,0:T(8,128)} %mix_s.1, f32[14]{0:T(128)} %act_s.1, f32[14]{0:T(128)} %broadcast_select_fusion.1.ahi_s, f32[14,128,512]{2,1,0:T(8,128)} %f_hbm.1, f32[128,512]{1,0:T(8,128)} %rate_ref.1, ...), custom_call_target="tpu_custom_call" | custom-call | flops 95420416 | bytes 7602176 | tf_op jit(solution)/shard_map/pallas_call | solution.py:126
  170.9 0.8 copy.36
  171.7 2.8 %collective-permute-start.6 = (f32[14,512]{1,0:T(8,128)S(1)}, f32[14,512]{1,0:T(8,128)S(1)}, u32[]{:S(2)}, u32[]{:S(2)}) collective-permute-start(f32[14,512]{1,0:T(8,128)S(1)} %get-tuple-element.17), channel_id=1, source_target_pairs={{8,0},{16,8},{9,1},{17,9},{10,2},{18,10},{11,3},{19,11},{12,4},{20... | collective-permute-start | bytes 86024 | tf_op jit(solution)/shard_map/ppermute | solution.py:274
  174.6 3.6 %collective-permute-start.5 = (f32[14,512]{1,0:T(8,128)S(1)}, f32[14,512]{1,0:T(8,128)S(1)}, u32[]{:S(2)}, u32[]{:S(2)}) collective-permute-start(f32[14,512]{1,0:T(8,128)S(1)} %get-tuple-element.18), channel_id=1, source_target_pairs={{0,8},{8,16},{1,9},{9,17},{2,10},{10,18},{3,11},{11,19},{4,12},{12... | collective-permute-start | bytes 86024 | tf_op jit(solution)/shard_map/ppermute | solution.py:273
  178.2 1.5 copy.38
  179.7 1.2 collective-permute-start.7
  180.9 1.5 copy.39
  182.4 3.0 %collective-permute-start.8 = (f32[14,128,1]{1,2,0:T(1,128)S(1)}, f32[14,128,1]{1,2,0:T(1,128)S(1)}, u32[]{:S(2)}, u32[]{:S(2)}) collective-permute-start(f32[14,128,1]{1,2,0:T(1,128)S(1)} %copy.39), channel_id=1, source_target_pairs={{1,0},{2,1},{3,2},{4,3},{5,4},{6,5},{7,6},{0,7},{9,8},{10,9},{11,1... | collective-permute-start | bytes 21512 | tf_op jit(solution)/shard_map/ppermute | solution.py:276
  185.3 0.0 collective-permute-done.7
  185.4 1.3 copy.40.gl_ref
  186.6 0.0 collective-permute-done.8
  186.6 1.3 copy.41.gr_ref
  187.9 0.0 collective-permute-done.6
  188.0 0.6 broadcast_in_dim.78.g1_ref
  188.6 0.0 collective-permute-done.5
  188.6 0.6 broadcast_in_dim.77.g0_ref
  189.2 6.6 %shard_map.84 = f32[14,128,512]{2,1,0:T(8,128)} custom-call(f32[14,128,512]{2,1,0:T(8,128)} %get-tuple-element.9.out_in, f32[14,1,512]{2,1,0:T(1,128)} %broadcast_in_dim.77.g0_ref, f32[14,1,512]{2,1,0:T(1,128)} %broadcast_in_dim.78.g1_ref, f32[14,128,1]{2,1,0:T(8,128)} %copy.40.gl_ref, f32[14,128,1]{2,1,0:T(8,128)} %copy.41.gr_ref), custom_call_target="tpu_custom_call", output_to_operand_aliasing={{}: (0, {})} | custom-call | tf_op jit(solution)/shard_map/pallas_call | solution.py:211
  (9 shorter events, 0.1 us)
Async XLA Ops:
  6.5 117.4 %all-reduce.2.cloned.1.call-start = ((), (), s32[]{:S(2)}) async-start(), calls=%async_computation | async-start | bytes 4194304 | tf_op jit(solution)/shard_map/psum | solution.py:243
  7.6 134.9 %collective-permute-start.1 = (f32[14,512]{1,0:T(8,128)S(1)}, f32[14,512]{1,0:T(8,128)S(1)}, u32[]{:S(2)}, u32[]{:S(2)}) collective-permute-start(f32[14,512]{1,0:T(8,128)S(1)} %bitcast.28), channel_id=1, source_target_pairs={{0,8},{8,16},{1,9},{9,17},{2,10},{10,18},{3,11},{11,19},{4,12},{12... | collective-permute-start | bytes 86024 | tf_op jit(solution)/shard_map/ppermute | solution.py:255
  12.2 128.9 %collective-permute-start.2 = (f32[14,512]{1,0:T(8,128)S(1)}, f32[14,512]{1,0:T(8,128)S(1)}, u32[]{:S(2)}, u32[]{:S(2)}) collective-permute-start(f32[14,512]{1,0:T(8,128)S(1)} %bitcast.30), channel_id=1, source_target_pairs={{8,0},{16,8},{9,1},{17,9},{10,2},{18,10},{11,3},{19,11},{12,4},{20... | collective-permute-start | bytes 86024 | tf_op jit(solution)/shard_map/ppermute | solution.py:256
  15.9 7.4 %copy-start.1 = (s32[4,512]{1,0:T(4,128)S(1)}, s32[4,512]{1,0:T(4,128)}, u32[]{:S(2)}) copy-start(s32[4,512]{1,0:T(4,128)} %param.14) | copy-start | bytes 24580
  15.9 7.4 %copy-start.2 = (s32[4,512]{1,0:T(4,128)S(1)}, s32[4,512]{1,0:T(4,128)}, u32[]{:S(2)}) copy-start(s32[4,512]{1,0:T(4,128)} %param.12) | copy-start | bytes 24580
  16.0 8.0 %copy-start.3 = (f32[4,512]{1,0:T(4,128)S(1)}, f32[4,512]{1,0:T(4,128)}, u32[]{:S(2)}) copy-start(f32[4,512]{1,0:T(4,128)} %param.15) | copy-start | bytes 24580
  16.0 8.0 %copy-start.4 = (f32[4,512]{1,0:T(4,128)S(1)}, f32[4,512]{1,0:T(4,128)}, u32[]{:S(2)}) copy-start(f32[4,512]{1,0:T(4,128)} %param.13) | copy-start | bytes 24580
  16.3 123.6 %collective-permute-start.3 = (f32[14,128,1]{1,2,0:T(1,128)S(1)}, f32[14,128,1]{1,2,0:T(1,128)S(1)}, u32[]{:S(2)}, u32[]{:S(2)}) collective-permute-start(f32[14,128,1]{1,2,0:T(1,128)S(1)} %copy.45), channel_id=1, source_target_pairs={{0,1},{1,2},{2,3},{3,4},{4,5},{5,6},{6,7},{7,0},{8,9},{9,10},{10,1... | collective-permute-start | bytes 21512 | tf_op jit(solution)/shard_map/ppermute | solution.py:257
  17.8 120.7 %collective-permute-start.4 = (f32[14,128,1]{1,2,0:T(1,128)S(1)}, f32[14,128,1]{1,2,0:T(1,128)S(1)}, u32[]{:S(2)}, u32[]{:S(2)}) collective-permute-start(f32[14,128,1]{1,2,0:T(1,128)S(1)} %copy.46), channel_id=1, source_target_pairs={{1,0},{2,1},{3,2},{4,3},{5,4},{6,5},{7,6},{0,7},{9,8},{10,9},{11,1... | collective-permute-start | bytes 21512 | tf_op jit(solution)/shard_map/ppermute | solution.py:258
  21.9 1.3 copy-start
  137.2 3.9 %collective-permute-start = (f32[15,512]{1,0:T(8,128)S(1)}, f32[15,512]{1,0:T(8,128)S(1)}, u32[]{:S(2)}, u32[]{:S(2)}) collective-permute-start(f32[15,512]{1,0:T(8,128)S(1)} %pad_maximum_fusion), channel_id=1, source_target_pairs={{16,24},{24,16},{17,25},{25,17},{18,26},{26,18},{19,27},{27,19},{2... | collective-permute-start | bytes 92168 | tf_op jit(solution)/shard_map/ppermute | solution.py:251
  171.7 16.2 %collective-permute-start.6 = (f32[14,512]{1,0:T(8,128)S(1)}, f32[14,512]{1,0:T(8,128)S(1)}, u32[]{:S(2)}, u32[]{:S(2)}) collective-permute-start(f32[14,512]{1,0:T(8,128)S(1)} %get-tuple-element.17), channel_id=1, source_target_pairs={{8,0},{16,8},{9,1},{17,9},{10,2},{18,10},{11,3},{19,11},{12,4},{20... | collective-permute-start | bytes 86024 | tf_op jit(solution)/shard_map/ppermute | solution.py:274
  174.6 14.0 %collective-permute-start.5 = (f32[14,512]{1,0:T(8,128)S(1)}, f32[14,512]{1,0:T(8,128)S(1)}, u32[]{:S(2)}, u32[]{:S(2)}) collective-permute-start(f32[14,512]{1,0:T(8,128)S(1)} %get-tuple-element.18), channel_id=1, source_target_pairs={{0,8},{8,16},{1,9},{9,17},{2,10},{10,18},{3,11},{11,19},{4,12},{12... | collective-permute-start | bytes 86024 | tf_op jit(solution)/shard_map/ppermute | solution.py:273
  179.7 5.7 %collective-permute-start.7 = (f32[14,128,1]{1,2,0:T(1,128)S(1)}, f32[14,128,1]{1,2,0:T(1,128)S(1)}, u32[]{:S(2)}, u32[]{:S(2)}) collective-permute-start(f32[14,128,1]{1,2,0:T(1,128)S(1)} %copy.38), channel_id=1, source_target_pairs={{0,1},{1,2},{2,3},{3,4},{4,5},{5,6},{6,7},{7,0},{8,9},{9,10},{10,1... | collective-permute-start | bytes 21512 | tf_op jit(solution)/shard_map/ppermute | solution.py:275
  182.4 4.3 %collective-permute-start.8 = (f32[14,128,1]{1,2,0:T(1,128)S(1)}, f32[14,128,1]{1,2,0:T(1,128)S(1)}, u32[]{:S(2)}, u32[]{:S(2)}) collective-permute-start(f32[14,128,1]{1,2,0:T(1,128)S(1)} %copy.39), channel_id=1, source_target_pairs={{1,0},{2,1},{3,2},{4,3},{5,4},{6,5},{7,6},{0,7},{9,8},{10,9},{11,1... | collective-permute-start | bytes 21512 | tf_op jit(solution)/shard_map/ppermute | solution.py:276
Sparse Core Ops, SparseCore 0:
  23.4 100.4 all-reduce.1

commit v3 on v2

--- a/solution.py
+++ b/solution.py
@@ -13,10 +13,6 @@
 
 SUB = 8
 LANE = 128
-
-
-def shift_from(axis, count, step, pairs_of):
-    return [(i, (i + step) % count) for i in pairs_of]
 
 
 def step_kernel(nf, rows, lanes, mix_s, act_s, ahi_s, f_hbm, rate_ref, lo1_ref, lo2_ref, hi1_ref,
@@ -157,7 +153,7 @@
             o_ref[half, pl.ds(p, 1), :] = acc
         return carry
 
-    lax.fori_loop(0, lanes, body, 0)
+    lax.fori_loop(0, lanes, body, 0, unroll=8)
 
 
 def interpolate(ids, weights, table):
@@ -238,11 +234,15 @@
     first_row = fields[:, 0, :]
     b = lax.axis_index("blk")
     payload = jnp.concatenate([last_row, first_row[4:5]], axis=0)
-    slots = jnp.zeros((n_blk, nf + 1, lanes), jnp.float32)
-    slots = lax.dynamic_update_slice(slots, payload[None], (b, 0, 0))
-    planes = lax.psum(slots, "blk")
+    planes = payload[None]
+    span = 1
+    while span < n_blk:
+        partner = [(i, i ^ span) for i in range(n_blk)]
+        planes = jnp.concatenate([planes, lax.ppermute(planes, "blk", partner)], axis=0)
+        span *= 2
     table = jnp.transpose(planes, (0, 2, 1)).reshape(n_blk * lanes, nf + 1)
     ids = jnp.concatenate([inlet_ids, outlet_ids], axis=0)
+    ids = (jnp.bitwise_xor(ids // lanes, b) * lanes) + ids % lanes
     wts = jnp.concatenate([inlet_weights, outlet_weights], axis=0)
     picked = interpolate(ids, wts, table)
     inlet = picked[0, :, :nf]

time: 203 us -> 100 us (0.49)
  waiting for transfers between devices: 99.4 us -> 10.2 us
  between operations: 13.6 us -> 0.17 us
  Pallas kernels: 44.7 us -> 42.2 us
    psum x1 -> x0, waiting for transfers between devices: 99.4 us -> none  [shards(): planes = lax.psum(slots, 'blk')]
    ppermute x0 -> x3, waiting for transfers between devices: none -> 10.1 us  [shards(): lax.ppermute(planes, 'blk', partner)]
    pallas_call x1, Pallas kernels: 11 us -> 8.57 us  [interpolate(): pl.pallas_call(functools.partial(interp_kernel, ks2 // 2), out_shape=jax....]
  transfers between devices with their start and end apart: 10 -> 12, of which waited for: 1 -> 2; matrix products, arithmetic and copies ran while one was open for 9% -> 19% of each run, Pallas kernels for 5% -> 9%
where the time goes in v3:
time: 100 us; the launch traced here: 99.4 us
  Pallas kernels  42.2 us (42%)
  starting transfers between devices  23.6 us (24%)
  local copies, waits for them, and re-layouts  20.7 us (21%)
  waiting for transfers between devices  10.2 us (10%)
  other arithmetic  2.6 us (3%)
    pallas_call x1, Pallas kernels, fused_step(): pl.pallas_call(functools.partial(step_kernel, nf, rows, lanes), out_shape...  27.1 us
    ppermute x3, waiting for transfers between devices, shards(): lax.ppermute(planes, 'blk', partner)  10.1 us
    pallas_call x1, Pallas kernels, interpolate(): pl.pallas_call(functools.partial(interp_kernel, ks2 // 2), out_shape=jax....  8.57 us
    pallas_call x1, Pallas kernels, fix_edges(): pl.pallas_call(functools.partial(fix_kernel, low_w, side_w), out_shape=ja...  6.61 us
    ppermute x1, starting transfers between devices, shards(): lax.ppermute(last_row, 'grp', [(i, i + 1) for i in range(n_grp - 2)])  4.54 us
    ppermute x1, starting transfers between devices, shards(): gr = lax.ppermute(col0, 'blk', [((i + 1) % n_blk, i) for i in range(n_blk)])  4.17 us
    ppermute x1, starting transfers between devices, shards(): lax.ppermute(fields[:, :, :1], 'blk', [((i + 1) % n_blk, i) for i in rang...  3.93 us
    pallas_call x3, local copies, waits for them, and re-layouts, fused_step(): pl.pallas_call(functools.partial(step_kernel, nf, rows, lanes), out_shape...  3.78 us
  transfers between devices with their start and end apart: 12, of which 2 were waited for; matrix products, arithmetic and copies ran while one was open for 19% of the time, Pallas kernels for 9%

profile of v3, /device:TPU:1, one launch (start us, length us, event | category | flops | bytes accessed | tf_op | source)
XLA Modules:
  0.0 99.4 jit_solution(6425567547707690974)
XLA Ops:
  0.0 0.0 copy-start
  0.0 0.0 copy-start.1
  0.0 0.0 copy-start.2
  0.0 0.0 copy-start.3
  0.0 1.1 %fusion.8 = (f32[14,1,512]{2,1,0:T(1,128)S(1)}, f32[14,1,512]{2,1,0:T(1,128)S(1)}) fusion(f32[14,128,512]{2,1,0:T(8,128)} %f_hbm.1), kind=kLoop, calls=%fused_computation.34 | loop fusion | bytes 114688 | tf_op jit(solution)/shard_map/slice | solution.py:234
  1.2 4.5 %collective-permute-start.4 = (f32[14,512]{1,0:T(8,128)S(1)}, f32[14,512]{1,0:T(8,128)S(1)}, u32[]{:S(2)}, u32[]{:S(2)}) collective-permute-start(f32[14,512]{1,0:T(8,128)S(1)} %bitcast.28), channel_id=1, source_target_pairs={{0,8},{8,16},{1,9},{9,17},{2,10},{10,18},{3,11},{11,19},{4,12},{12... | collective-permute-start | bytes 86024 | tf_op jit(solution)/shard_map/ppermute | solution.py:255
  5.7 0.7 slice_bitcast_fusion.2
  6.5 1.3 %collective-permute-start = (f32[1,15,512]{2,1,0:T(8,128)S(1)}, f32[1,15,512]{2,1,0:T(8,128)S(1)}, u32[]{:S(2)}, u32[]{:S(2)}) collective-permute-start(f32[1,15,512]{2,1,0:T(8,128)S(1)} %maximum_bitcast_fusion.1), channel_id=1, source_target_pairs={{0,1},{1,0},{2,3},{3,2},{4,5},{5,4},{6,7},{7,6},{8,9},{9,8},{10,11... | collective-permute-start | bytes 92168 | tf_op jit(solution)/shard_map/ppermute | solution.py:241
  7.7 1.9 %collective-permute-start.5 = (f32[14,512]{1,0:T(8,128)S(1)}, f32[14,512]{1,0:T(8,128)S(1)}, u32[]{:S(2)}, u32[]{:S(2)}) collective-permute-start(f32[14,512]{1,0:T(8,128)S(1)} %bitcast.30), channel_id=1, source_target_pairs={{8,0},{16,8},{9,1},{17,9},{10,2},{18,10},{11,3},{19,11},{12,4},{20... | collective-permute-start | bytes 86024 | tf_op jit(solution)/shard_map/ppermute | solution.py:256
  9.7 1.8 %fusion.7 = (f32[14,128,1]{2,1,0:T(8,128)S(1)}, f32[14,128,1]{2,1,0:T(8,128)S(1)}) fusion(f32[14,128,512]{2,1,0:T(8,128)} %f_hbm.1), kind=kLoop, calls=%fused_computation.33 | loop fusion | bytes 28672 | tf_op jit(solution)/shard_map/slice | solution.py:258
  11.4 0.3 copy.48
  11.7 0.3 collective-permute-start.6
  12.0 0.3 copy.49
  12.3 3.9 %collective-permute-start.7 = (f32[14,128,1]{1,2,0:T(1,128)S(1)}, f32[14,128,1]{1,2,0:T(1,128)S(1)}, u32[]{:S(2)}, u32[]{:S(2)}) collective-permute-start(f32[14,128,1]{1,2,0:T(1,128)S(1)} %copy.49), channel_id=1, source_target_pairs={{1,0},{2,1},{3,2},{4,3},{5,4},{6,5},{7,6},{0,7},{9,8},{10,9},{11,1... | collective-permute-start | bytes 21512 | tf_op jit(solution)/shard_map/ppermute | solution.py:258
  16.2 0.0 collective-permute-done
  16.3 0.1 collective-permute-start.1
  16.3 0.0 copy-done
  16.3 0.0 copy-done.1
  16.4 0.6 pad_maximum_fusion.3.w_s
  17.0 2.6 %collective-permute-done.1 = f32[2,15,512]{2,1,0:T(8,128)S(1)} collective-permute-done((f32[2,15,512]{2,1,0:T(8,128)S(1)}, f32[2,15,512]{2,1,0:T(8,128)S(1)}, u32[]{:S(2)}, u32[]{:S(2)}) %collective-permute-start.1) | collective-permute-done | bytes 61472 | tf_op jit(solution)/shard_map/ppermute | solution.py:241
  19.5 0.7 collective-permute-start.2
  20.2 0.0 copy-done.2
  20.2 0.0 copy-done.3
  20.2 0.6 fusion.2.ids_s
  20.8 7.6 %collective-permute-done.2 = f32[4,15,512]{2,1,0:T(8,128)S(1)} collective-permute-done((f32[4,15,512]{2,1,0:T(8,128)S(1)}, f32[4,15,512]{2,1,0:T(8,128)S(1)}, u32[]{:S(2)}, u32[]{:S(2)}) %collective-permute-start.2) | collective-permute-done | bytes 122912 | tf_op jit(solution)/shard_map/ppermute | solution.py:241
  28.4 2.0 %copy.43 = f32[8,512,15]{2,1,0:T(8,128)} copy(f32[8,512,15]{1,2,0:T(8,128)S(1)} %maximum_bitcast_fusion) | data formatting | bytes 491520 | tf_op jit(solution)/shard_map/reshape | solution.py:243
  30.4 8.6 %shard_map.82 = f32[2,512,15]{2,1,0:T(8,128)} custom-call(s32[8,512]{1,0:T(8,128)} %fusion.2.ids_s, f32[8,512]{1,0:T(8,128)} %pad_maximum_fusion.3.w_s, f32[4096,15]{1,0:T(8,128)} %bitcast.26), custom_call_target="tpu_custom_call" | custom-call | tf_op jit(solution)/shard_map/pallas_call | solution.py:163
  39.0 1.2 %slice_reduce_fusion = f32[512]{0:T(512)S(1)} fusion(f32[2,512,15]{2,1,0:T(8,128)} %shard_map.82), kind=kLoop, calls=%fused_computation | loop fusion | bytes 4096 | tf_op jit(solution)/shard_map/slice | solution.py:249
  40.2 1.0 slice.49
  41.1 0.1 copy.46
  41.3 0.7 collective-permute-start.3
  41.9 0.5 broadcast_select_fusion.1.ahi_s
  42.5 0.0 collective-permute-done.7
  42.5 1.3 %copy.36.rgt_ref = f32[14,128,1]{2,1,0:T(8,128)} copy(f32[14,128,1]{1,2,0:T(1,128)S(1)} %collective-permute-done.7) | data formatting | bytes 14336 | tf_op jit(solution)/shard_map/ppermute | solution.py:258
  43.8 0.0 collective-permute-done.6
  43.8 1.3 %copy.35.lft_ref = f32[14,128,1]{2,1,0:T(8,128)} copy(f32[14,128,1]{1,2,0:T(1,128)S(1)} %collective-permute-done.6) | data formatting | bytes 14336 | tf_op jit(solution)/shard_map/ppermute | solution.py:257
  45.1 0.0 collective-permute-done.3
  45.1 0.0 collective-permute-done.5
  45.1 0.1 select_add_fusion
  45.2 0.7 broadcast_select_fusion.hi2_ref
  45.8 0.6 broadcast_in_dim.69.hi1_ref
  46.5 0.0 collective-permute-done.4
  46.5 0.6 copy.34.lo2_ref
  47.1 0.6 copy.33.lo1_ref
  47.8 27.1 %shard_map.83 = (f32[14,128,512]{2,1,0:T(8,128)}, f32[14,2,512]{2,1,0:T(2,128)}, f32[14,128,1]{2,1,0:T(8,128)}, f32[14,128,1]{2,1,0:T(8,128)}) custom-call(f32[14,14]{1,0:T(8,128)} %mix_s.1, f32[14]{0:T(128)} %act_s.1, f32[14]{0:T(128)} %broadcast_select_fusion.1.ahi_s, f32[14,128,512]{2,1,0:T(8,128)} %f_hbm.1, f32[128,512]{1,0:T(8,128)} %rate_ref.1, ...), custom_call_target="tpu_custom_call" | custom-call | flops 95420416 | bytes 7602176 | tf_op jit(solution)/shard_map/pallas_call | solution.py:122
  74.8 0.8 copy.37
  75.7 2.4 %collective-permute-start.9 = (f32[14,512]{1,0:T(8,128)S(1)}, f32[14,512]{1,0:T(8,128)S(1)}, u32[]{:S(2)}, u32[]{:S(2)}) collective-permute-start(f32[14,512]{1,0:T(8,128)S(1)} %get-tuple-element.17), channel_id=1, source_target_pairs={{8,0},{16,8},{9,1},{17,9},{10,2},{18,10},{11,3},{19,11},{12,4},{20... | collective-permute-start | bytes 86024 | tf_op jit(solution)/shard_map/ppermute | solution.py:274
  78.1 3.7 %collective-permute-start.8 = (f32[14,512]{1,0:T(8,128)S(1)}, f32[14,512]{1,0:T(8,128)S(1)}, u32[]{:S(2)}, u32[]{:S(2)}) collective-permute-start(f32[14,512]{1,0:T(8,128)S(1)} %get-tuple-element.18), channel_id=1, source_target_pairs={{0,8},{8,16},{1,9},{9,17},{2,10},{10,18},{3,11},{11,19},{4,12},{12... | collective-permute-start | bytes 86024 | tf_op jit(solution)/shard_map/ppermute | solution.py:273
  81.8 1.5 %copy.39 = f32[14,128,1]{1,2,0:T(1,128)S(1)} copy(f32[14,128,1]{2,1,0:T(8,128)} %get-tuple-element.11) | data formatting | bytes 14336 | tf_op jit(solution)/shard_map/pallas_call | solution.py:122
  83.3 0.0 collective-permute-start.10
  83.3 1.5 %copy.40 = f32[14,128,1]{1,2,0:T(1,128)S(1)} copy(f32[14,128,1]{2,1,0:T(8,128)} %get-tuple-element.12) | data formatting | bytes 14336 | tf_op jit(solution)/shard_map/pallas_call | solution.py:122
  84.8 4.2 %collective-permute-start.11 = (f32[14,128,1]{1,2,0:T(1,128)S(1)}, f32[14,128,1]{1,2,0:T(1,128)S(1)}, u32[]{:S(2)}, u32[]{:S(2)}) collective-permute-start(f32[14,128,1]{1,2,0:T(1,128)S(1)} %copy.40), channel_id=1, source_target_pairs={{1,0},{2,1},{3,2},{4,3},{5,4},{6,5},{7,6},{0,7},{9,8},{10,9},{11,1... | collective-permute-start | bytes 21512 | tf_op jit(solution)/shard_map/ppermute | solution.py:276
  89.0 0.0 collective-permute-done.10
  89.0 1.3 %copy.41.gl_ref = f32[14,128,1]{2,1,0:T(8,128)} copy(f32[14,128,1]{1,2,0:T(1,128)S(1)} %collective-permute-done.10) | data formatting | bytes 14336 | tf_op jit(solution)/shard_map/ppermute | solution.py:275
  90.2 0.0 collective-permute-done.11
  90.2 1.3 %copy.42.gr_ref = f32[14,128,1]{2,1,0:T(8,128)} copy(f32[14,128,1]{1,2,0:T(1,128)S(1)} %collective-permute-done.11) | data formatting | bytes 14336 | tf_op jit(solution)/shard_map/ppermute | solution.py:276
  91.6 0.0 collective-permute-done.9
  91.6 0.6 broadcast_in_dim.74.g1_ref
  92.2 0.0 collective-permute-done.8
  92.2 0.6 broadcast_in_dim.73.g0_ref
  92.8 6.6 %shard_map.84 = f32[14,128,512]{2,1,0:T(8,128)} custom-call(f32[14,128,512]{2,1,0:T(8,128)} %get-tuple-element.9.out_in, f32[14,1,512]{2,1,0:T(1,128)} %broadcast_in_dim.73.g0_ref, f32[14,1,512]{2,1,0:T(1,128)} %broadcast_in_dim.74.g1_ref, f32[14,128,1]{2,1,0:T(8,128)} %copy.41.gl_ref, f32[14,128,1]{2,1,0:T(8,128)} %copy.42.gr_ref), custom_call_target="tpu_custom_call", output_to_operand_aliasing={{}: (0, {})} | custom-call | tf_op jit(solution)/shard_map/pallas_call | solution.py:207
  (11 shorter events, 0.1 us)
Async XLA Ops:
  0.0 16.3 %copy-start = (f32[4,512]{1,0:T(4,128)S(1)}, f32[4,512]{1,0:T(4,128)}, u32[]{:S(2)}) copy-start(f32[4,512]{1,0:T(4,128)} %param.15) | copy-start | bytes 24580
  0.0 16.3 %copy-start.1 = (f32[4,512]{1,0:T(4,128)S(1)}, f32[4,512]{1,0:T(4,128)}, u32[]{:S(2)}) copy-start(f32[4,512]{1,0:T(4,128)} %param.13) | copy-start | bytes 24580
  0.0 20.2 %copy-start.2 = (s32[4,512]{1,0:T(4,128)S(1)}, s32[4,512]{1,0:T(4,128)}, u32[]{:S(2)}) copy-start(s32[4,512]{1,0:T(4,128)} %param.14) | copy-start | bytes 24580
  0.0 20.2 %copy-start.3 = (s32[4,512]{1,0:T(4,128)S(1)}, s32[4,512]{1,0:T(4,128)}, u32[]{:S(2)}) copy-start(s32[4,512]{1,0:T(4,128)} %param.12) | copy-start | bytes 24580
  1.2 45.3 %collective-permute-start.4 = (f32[14,512]{1,0:T(8,128)S(1)}, f32[14,512]{1,0:T(8,128)S(1)}, u32[]{:S(2)}, u32[]{:S(2)}) collective-permute-start(f32[14,512]{1,0:T(8,128)S(1)} %bitcast.28), channel_id=1, source_target_pairs={{0,8},{8,16},{1,9},{9,17},{2,10},{10,18},{3,11},{11,19},{4,12},{12... | collective-permute-start | bytes 86024 | tf_op jit(solution)/shard_map/ppermute | solution.py:255
  6.5 9.8 %collective-permute-start = (f32[1,15,512]{2,1,0:T(8,128)S(1)}, f32[1,15,512]{2,1,0:T(8,128)S(1)}, u32[]{:S(2)}, u32[]{:S(2)}) collective-permute-start(f32[1,15,512]{2,1,0:T(8,128)S(1)} %maximum_bitcast_fusion.1), channel_id=1, source_target_pairs={{0,1},{1,0},{2,3},{3,2},{4,5},{5,4},{6,7},{7,6},{8,9},{9,8},{10,11... | collective-permute-start | bytes 92168 | tf_op jit(solution)/shard_map/ppermute | solution.py:241
  7.7 37.3 %collective-permute-start.5 = (f32[14,512]{1,0:T(8,128)S(1)}, f32[14,512]{1,0:T(8,128)S(1)}, u32[]{:S(2)}, u32[]{:S(2)}) collective-permute-start(f32[14,512]{1,0:T(8,128)S(1)} %bitcast.30), channel_id=1, source_target_pairs={{8,0},{16,8},{9,1},{17,9},{10,2},{18,10},{11,3},{19,11},{12,4},{20... | collective-permute-start | bytes 86024 | tf_op jit(solution)/shard_map/ppermute | solution.py:256
  11.7 32.0 %collective-permute-start.6 = (f32[14,128,1]{1,2,0:T(1,128)S(1)}, f32[14,128,1]{1,2,0:T(1,128)S(1)}, u32[]{:S(2)}, u32[]{:S(2)}) collective-permute-start(f32[14,128,1]{1,2,0:T(1,128)S(1)} %copy.48), channel_id=1, source_target_pairs={{0,1},{1,2},{2,3},{3,4},{4,5},{5,6},{6,7},{7,0},{8,9},{9,10},{10,1... | collective-permute-start | bytes 21512 | tf_op jit(solution)/shard_map/ppermute | solution.py:257
  12.3 30.1 %collective-permute-start.7 = (f32[14,128,1]{1,2,0:T(1,128)S(1)}, f32[14,128,1]{1,2,0:T(1,128)S(1)}, u32[]{:S(2)}, u32[]{:S(2)}) collective-permute-start(f32[14,128,1]{1,2,0:T(1,128)S(1)} %copy.49), channel_id=1, source_target_pairs={{1,0},{2,1},{3,2},{4,3},{5,4},{6,5},{7,6},{0,7},{9,8},{10,9},{11,1... | collective-permute-start | bytes 21512 | tf_op jit(solution)/shard_map/ppermute | solution.py:258
  16.3 3.3 %collective-permute-start.1 = (f32[2,15,512]{2,1,0:T(8,128)S(1)}, f32[2,15,512]{2,1,0:T(8,128)S(1)}, u32[]{:S(2)}, u32[]{:S(2)}) collective-permute-start(f32[2,15,512]{2,1,0:T(8,128)S(1)} %pad_maximum_fusion.1), channel_id=1, source_target_pairs={{0,2},{1,3},{2,0},{3,1},{4,6},{5,7},{6,4},{7,5},{8,10},{9,11},{10,... | collective-permute-start | bytes 184328 | tf_op jit(solution)/shard_map/ppermute | solution.py:241
  19.5 8.9 %collective-permute-start.2 = (f32[4,15,512]{2,1,0:T(8,128)S(1)}, f32[4,15,512]{2,1,0:T(8,128)S(1)}, u32[]{:S(2)}, u32[]{:S(2)}) collective-permute-start(f32[4,15,512]{2,1,0:T(8,128)S(1)} %pad_maximum_fusion), channel_id=1, source_target_pairs={{0,4},{1,5},{2,6},{3,7},{4,0},{5,1},{6,2},{7,3},{8,12},{9,13},{10,... | collective-permute-start | bytes 368648 | tf_op jit(solution)/shard_map/ppermute | solution.py:241
  41.3 3.8 %collective-permute-start.3 = (f32[15,512]{1,0:T(8,128)S(1)}, f32[15,512]{1,0:T(8,128)S(1)}, u32[]{:S(2)}, u32[]{:S(2)}) collective-permute-start(f32[15,512]{1,0:T(8,128)S(1)} %pad_maximum_fusion.2), channel_id=1, source_target_pairs={{16,24},{24,16},{17,25},{25,17},{18,26},{26,18},{19,27},{27,19},{2... | collective-permute-start | bytes 92168 | tf_op jit(solution)/shard_map/ppermute | solution.py:251
  75.7 15.9 %collective-permute-start.9 = (f32[14,512]{1,0:T(8,128)S(1)}, f32[14,512]{1,0:T(8,128)S(1)}, u32[]{:S(2)}, u32[]{:S(2)}) collective-permute-start(f32[14,512]{1,0:T(8,128)S(1)} %get-tuple-element.17), channel_id=1, source_target_pairs={{8,0},{16,8},{9,1},{17,9},{10,2},{18,10},{11,3},{19,11},{12,4},{20... | collective-permute-start | bytes 86024 | tf_op jit(solution)/shard_map/ppermute | solution.py:274
  78.1 14.1 %collective-permute-start.8 = (f32[14,512]{1,0:T(8,128)S(1)}, f32[14,512]{1,0:T(8,128)S(1)}, u32[]{:S(2)}, u32[]{:S(2)}) collective-permute-start(f32[14,512]{1,0:T(8,128)S(1)} %get-tuple-element.18), channel_id=1, source_target_pairs={{0,8},{8,16},{1,9},{9,17},{2,10},{10,18},{3,11},{11,19},{4,12},{12... | collective-permute-start | bytes 86024 | tf_op jit(solution)/shard_map/ppermute | solution.py:273
  83.3 5.7 %collective-permute-start.10 = (f32[14,128,1]{1,2,0:T(1,128)S(1)}, f32[14,128,1]{1,2,0:T(1,128)S(1)}, u32[]{:S(2)}, u32[]{:S(2)}) collective-permute-start(f32[14,128,1]{1,2,0:T(1,128)S(1)} %copy.39), channel_id=1, source_target_pairs={{0,1},{1,2},{2,3},{3,4},{4,5},{5,6},{6,7},{7,0},{8,9},{9,10},{10,1... | collective-permute-start | bytes 21512 | tf_op jit(solution)/shard_map/ppermute | solution.py:275
  84.8 5.5 %collective-permute-start.11 = (f32[14,128,1]{1,2,0:T(1,128)S(1)}, f32[14,128,1]{1,2,0:T(1,128)S(1)}, u32[]{:S(2)}, u32[]{:S(2)}) collective-permute-start(f32[14,128,1]{1,2,0:T(1,128)S(1)} %copy.40), channel_id=1, source_target_pairs={{1,0},{2,1},{3,2},{4,3},{5,4},{6,5},{7,6},{0,7},{9,8},{10,9},{11,1... | collective-permute-start | bytes 21512 | tf_op jit(solution)/shard_map/ppermute | solution.py:276

commit v4 on v3

v4 whole, which is shorter than its diff:
```python
import functools

import jax
import jax.numpy as jnp
from jax import lax
from jax.experimental import pallas as pl
from jax.experimental.pallas import tpu as pltpu
from jax.sharding import PartitionSpec as P

courant = 0.5
diffusion = 0.1
source_step = 0.5

SUB = 8
LANE = 128


def tile_t(row):
    n = row.shape[1]
    return jnp.transpose(jnp.broadcast_to(row, (n, n)))


def step_kernel(nf, rows, lanes, mix_s, act_s, flag_s, f_hbm, rate_ref, hlo_ref, hhi_ref, sw_ref,
                lft_ref, rgt_ref, out_ref, elo_ref, ehi_ref, clo_ref, chi_ref, ext1, ext2, sem):
    n_i = rows // SUB
    n_j = lanes // LANE
    top = SUB + rows
    right = LANE + lanes
    at_exit = flag_s[0] > 0.5
    at_turb = flag_s[1] > 0.5
    at_end = flag_s[0] + flag_s[1] > 0.5

    copy = pltpu.make_async_copy(f_hbm, ext1.at[:, SUB:top, LANE:right], sem.at[0])
    copy.start()
    zeros = jnp.zeros((rows, LANE), jnp.float32)
    for f in range(nf):
        inlet = sw_ref[f:f + 1, :]
        ext1[f, SUB - 1:SUB, LANE:right] = jnp.where(at_turb, inlet, hlo_ref[f:f + 1, :])
        ext2[f, SUB - 1:SUB, LANE:right] = jnp.where(at_turb, inlet, 0.0)
        ext1[f, SUB:top, 0:LANE] = tile_t(lft_ref[f:f + 1, :])
        ext1[f, SUB:top, right:right + LANE] = tile_t(rgt_ref[f:f + 1, :])
        ext2[f, SUB:top, 0:LANE] = zeros
        ext2[f, SUB:top, right:right + LANE] = zeros
    copy.wait()

    def high_ghost(ext, halo_of):
        for f in range(nf):
            own = ext[f, top - 1:top, LANE:right]
            halo = halo_of(f)
            if f == 4:
                row = jnp.where(at_turb, own, jnp.where(at_exit, sw_ref[nf:nf + 1, :], halo))
            else:
                row = jnp.where(at_end, own, halo)
            ext[f, top:top + 1, LANE:right] = row

    high_ghost(ext1, lambda f: hhi_ref[f:f + 1, :])

    sub_id = lax.broadcasted_iota(jnp.int32, (SUB, LANE), 0)
    lane_id = lax.broadcasted_iota(jnp.int32, (SUB, LANE), 1)
    first_sub = sub_id == 0
    last_sub = sub_id == SUB - 1
    first_lane = lane_id == 0
    last_lane = lane_id == LANE - 1

    def tendency_tile(src, r0, c0, rate_t):
        r = pl.multiple_of(r0 + SUB, SUB)
        c = pl.multiple_of(c0 + LANE, LANE)
        r_up = pl.multiple_of(r0, SUB)
        r_dn = pl.multiple_of(r0 + 2 * SUB, SUB)
        c_w = pl.multiple_of(c0, LANE)
        c_e = pl.multiple_of(c0 + 2 * LANE, LANE)
        v4 = src[4, pl.ds(r, SUB), pl.ds(c, LANE)]
        heat = 1.0 + (jnp.maximum(v4, 0.0) + jnp.log1p(jnp.exp(-jnp.abs(v4))))
        inv_heat = 1.0 / heat
        vals = []
        react = []
        for f in range(nf):
            v = src[f, pl.ds(r, SUB), pl.ds(c, LANE)]
            vals.append(v)
            react.append(rate_t * v * jnp.exp(-act_s[f] * inv_heat))
        tends = []
        for f in range(nf):
            v = vals[f]
            up = src[f, pl.ds(r_up, SUB), pl.ds(c, LANE)]
            down = src[f, pl.ds(r_dn, SUB), pl.ds(c, LANE)]
            west = src[f, pl.ds(r, SUB), pl.ds(c_w, LANE)]
            east = src[f, pl.ds(r, SUB), pl.ds(c_e, LANE)]
            backward = jnp.where(first_sub, pltpu.roll(up, 1, 0), pltpu.roll(v, 1, 0))
            forward = jnp.where(last_sub, pltpu.roll(down, SUB - 1, 0), pltpu.roll(v, SUB - 1, 0))
            left = jnp.where(first_lane, pltpu.roll(west, 1, 1), pltpu.roll(v, 1, 1))
            rgt = jnp.where(last_lane, pltpu.roll(east, LANE - 1, 1), pltpu.roll(v, LANE - 1, 1))
            acc = mix_s[f, 0] * react[0]
            for g in range(1, nf):
                acc = acc + mix_s[f, g] * react[g]
            advect = -courant * (v - backward)
            spread = diffusion * (backward + forward + left + rgt - 4.0 * v)
            tends.append(advect + spread + source_step * acc)
        return vals, tends

    def tile_offsets(t):
        i = t // n_j
        j = t % n_j
        r0 = pl.multiple_of(i * SUB, SUB)
        c0 = pl.multiple_of(j * LANE, LANE)
        return r0, c0

    def stage_one(t, carry):
        r0, c0 = tile_offsets(t)
        rate_t = rate_ref[pl.ds(r0, SUB), pl.ds(c0, LANE)]
        vals, tends = tendency_tile(ext1, r0, c0, rate_t)
        r = pl.multiple_of(r0 + SUB, SUB)
        c = pl.multiple_of(c0 + LANE, LANE)
        for f in range(nf):
            ext2[f, pl.ds(r, SUB), pl.ds(c, LANE)] = vals[f] + tends[f]
        return carry

    lax.fori_loop(0, n_i * n_j, stage_one, 0)

    high_ghost(ext2, lambda f: jnp.zeros((1, lanes), jnp.float32))

    def stage_two(t, carry):
        r0, c0 = tile_offsets(t)
        rate_t = rate_ref[pl.ds(r0, SUB), pl.ds(c0, LANE)]
        vals, tends = tendency_tile(ext2, r0, c0, rate_t)
        r = pl.multiple_of(r0 + SUB, SUB)
        c = pl.multiple_of(c0 + LANE, LANE)
        for f in range(nf):
            base = ext1[f, pl.ds(r, SUB), pl.ds(c, LANE)]
            out_ref[f, pl.ds(r0, SUB), pl.ds(c0, LANE)] = 0.5 * (base + vals[f] + tends[f])
        return carry

    lax.fori_loop(0, n_i * n_j, stage_two, 0)

    for f in range(nf):
        elo_ref[f:f + 1, :] = ext2[f, SUB:SUB + 1, LANE:right]
        ehi_ref[f:f + 1, :] = ext2[f, top - 1:top, LANE:right]
        west = jnp.transpose(ext2[f, SUB:top, LANE:2 * LANE])
        east = jnp.transpose(ext2[f, SUB:top, right - LANE:right])
        clo_ref[f:f + 1, :] = west[0:1, :]
        chi_ref[f:f + 1, :] = east[LANE - 1:LANE, :]


def fused_step(fields, rate, mix, act, flags, halo_lo, halo_hi, swapped, lft, rgt):
    nf, rows, lanes = fields.shape
    vmem = pltpu.VMEM
    smem = pl.BlockSpec(memory_space=pltpu.SMEM)
    vspec = pl.BlockSpec(memory_space=vmem)
    cells = rows * lanes
    cost = pl.CostEstimate(
        flops=2 * cells * nf * (2 * nf + 24),
        transcendentals=2 * cells * (nf + 3),
        bytes_accessed=4 * cells * (2 * nf + 1),
    )
    return pl.pallas_call(
        functools.partial(step_kernel, nf, rows, lanes),
        out_shape=(
            jax.ShapeDtypeStruct((nf, rows, lanes), jnp.float32),
            jax.ShapeDtypeStruct((nf, lanes), jnp.float32),
            jax.ShapeDtypeStruct((nf, lanes), jnp.float32),
            jax.ShapeDtypeStruct((nf, rows), jnp.float32),
            jax.ShapeDtypeStruct((nf, rows), jnp.float32),
        ),
        in_specs=[smem, smem, smem, pl.BlockSpec(memory_space=pl.ANY)] + [vspec] * 6,
        out_specs=(vspec,) * 5,
        scratch_shapes=[
            vmem((nf, rows + 2 * SUB, lanes + 2 * LANE), jnp.float32),
            vmem((nf, rows + 2 * SUB, lanes + 2 * LANE), jnp.float32),
            pltpu.SemaphoreType.DMA((1,)),
        ],
        compiler_params=pltpu.CompilerParams(vmem_limit_bytes=60 * 1024 * 1024),
        cost_estimate=cost,
    )(mix, act, flags, fields, rate, halo_lo, halo_hi, swapped, lft, rgt)


def interp_kernel(ks, flag_s, ids_s, w_s, table_ref, o_ref, acc):
    lanes = o_ref.shape[1]
    half = jnp.where(flag_s[0] > 0.5, 0, ks)
    acc[...] = jnp.zeros(acc.shape, jnp.float32)
    width = table_ref.shape[1]

    @pl.when(flag_s[0] + flag_s[1] > 0.5)
    def _():
        def body(p, carry):
            total = None
            for k in range(ks):
                q = ids_s[half + k, p]
                term = w_s[half + k, p] * table_ref[pl.ds(q, 1), :]
                total = term if total is None else total + term
            acc[pl.ds(p, 1), 0:width] = total
            return carry

        lax.fori_loop(0, lanes, body, 0, unroll=8)

    o_ref[...] = jnp.transpose(acc[...])[0:o_ref.shape[0], :]


def interpolate(flags, ids, weights, table):
    ks2, lanes = ids.shape
    smem = pl.BlockSpec(memory_space=pltpu.SMEM)
    vspec = pl.BlockSpec(memory_space=pltpu.VMEM)
    return pl.pallas_call(
        functools.partial(interp_kernel, ks2 // 2),
        out_shape=jax.ShapeDtypeStruct((table.shape[1], lanes), jnp.float32),
        in_specs=[smem, smem, smem, vspec],
        out_specs=vspec,
        scratch_shapes=[pltpu.VMEM((lanes, LANE), jnp.float32)],
    )(flags, ids, weights, table)


def fix_kernel(low_w, side_w, out_in, g0_ref, g1_ref, gl_ref, gr_ref, out_ref, rb, cb, sem):
    nf, rows, lanes = out_ref.shape
    row_win = (pl.ds(0, SUB), pl.ds(rows - SUB, SUB))
    col_win = (pl.ds(0, LANE), pl.ds(lanes - LANE, LANE))
    loads = [pltpu.make_async_copy(out_ref.at[:, row_win[s], :], rb.at[s], sem.at[s]) for s in range(2)]
    for c in loads:
        c.start()
    for c in loads:
        c.wait()
    for f in range(nf):
        rb[0, f, 0:1, :] = rb[0, f, 0:1, :] + low_w * g0_ref[f:f + 1, :]
        rb[1, f, SUB - 1:SUB, :] = rb[1, f, SUB - 1:SUB, :] + side_w * g1_ref[f:f + 1, :]
    stores = [pltpu.make_async_copy(rb.at[s], out_ref.at[:, row_win[s], :], sem.at[s]) for s in range(2)]
    for c in stores:
        c.start()
    for c in stores:
        c.wait()
    loads = [pltpu.make_async_copy(out_ref.at[:, :, col_win[s]], cb.at[s], sem.at[s]) for s in range(2)]
    for c in loads:
        c.start()
    for c in loads:
        c.wait()
    lane_id = lax.broadcasted_iota(jnp.int32, (rows, LANE), 1)
    for f in range(nf):
        cb[0, f] = cb[0, f] + jnp.where(lane_id == 0, side_w * tile_t(gl_ref[f:f + 1, :]), 0.0)
        cb[1, f] = cb[1, f] + jnp.where(lane_id == LANE - 1, side_w * tile_t(gr_ref[f:f + 1, :]), 0.0)
    stores = [pltpu.make_async_copy(cb.at[s], out_ref.at[:, :, col_win[s]], sem.at[s]) for s in range(2)]
    for c in stores:
        c.start()
    for c in stores:
        c.wait()


def fix_edges(out, g0, g1, gl, gr, low_w, side_w):
    nf, rows, lanes = out.shape
    vspec = pl.BlockSpec(memory_space=pltpu.VMEM)
    anyspec = pl.BlockSpec(memory_space=pl.ANY)
    return pl.pallas_call(
        functools.partial(fix_kernel, low_w, side_w),
        out_shape=jax.ShapeDtypeStruct(out.shape, jnp.float32),
        in_specs=[anyspec, vspec, vspec, vspec, vspec],
        out_specs=anyspec,
        scratch_shapes=[
            pltpu.VMEM((2, nf, SUB, lanes), jnp.float32),
            pltpu.VMEM((2, nf, rows, LANE), jnp.float32),
            pltpu.SemaphoreType.DMA((2,)),
        ],
        input_output_aliases={0: 0},
    )(out, g0, g1, gl, gr)


def shards(
    fields, react_rate, mix_matrix, activation, inlet_ids, inlet_weights, outlet_ids, outlet_weights
):
    nf, rows, lanes = fields.shape
    n_grp = lax.axis_size("grp")
    n_blk = lax.axis_size("blk")
    g = lax.axis_index("grp")
    b = lax.axis_index("blk")
    exit_grp = n_grp - 2
    turb_grp = n_grp - 1
    flags = jnp.stack([g == exit_grp, g == turb_grp]).astype(jnp.float32)

    last_row = fields[:, -1, :]
    first_row = fields[:, 0, :]
    payload = jnp.concatenate([last_row, first_row[4:5]], axis=0)
    planes = payload[None]
    span = 1
    while span < n_blk:
        partner = [(i, i ^ span) for i in range(n_blk)]
        planes = jnp.concatenate([planes, lax.ppermute(planes, "blk", partner)], axis=0)
        span *= 2
    table = jnp.transpose(planes, (0, 2, 1)).reshape(n_blk * lanes, nf + 1)
    ids = jnp.concatenate([inlet_ids, outlet_ids], axis=0)
    ids = (jnp.bitwise_xor(ids // lanes, b) * lanes) + ids % lanes
    wts = jnp.concatenate([inlet_weights, outlet_weights], axis=0)
    swap = interpolate(flags, ids, wts, table)
    swapped = lax.ppermute(swap, "grp", [(exit_grp, turb_grp), (turb_grp, exit_grp)])

    halo_lo = lax.ppermute(last_row, "grp", [(i, i + 1) for i in range(n_grp - 2)])
    halo_hi = lax.ppermute(first_row, "grp", [(i + 1, i) for i in range(n_grp - 2)])
    lft = lax.ppermute(fields[:, :, lanes - 1], "blk", [(i, (i + 1) % n_blk) for i in range(n_blk)])
    rgt = lax.ppermute(fields[:, :, 0], "blk", [((i + 1) % n_blk, i) for i in range(n_blk)])

    out, elo, ehi, clo, chi = fused_step(
        fields, react_rate, mix_matrix, activation, flags, halo_lo, halo_hi, swapped, lft, rgt
    )

    g0 = lax.ppermute(ehi, "grp", [(i, i + 1) for i in range(n_grp - 2)])
    g1 = lax.ppermute(elo, "grp", [(i + 1, i) for i in range(n_grp - 2)])
    gl = lax.ppermute(chi, "blk", [(i, (i + 1) % n_blk) for i in range(n_blk)])
    gr = lax.ppermute(clo, "blk", [((i + 1) % n_blk, i) for i in range(n_blk)])
    low_w = 0.5 * (courant + diffusion)
    side_w = 0.5 * diffusion
    return fix_edges(out, g0, g1, gl, gr, low_w, side_w)


def solution(mesh):
    in_specs = (
        P(None, "grp", "blk"),
        P("grp", "blk"),
        P(),
        P(),
        P(None, "blk"),
        P(None, "blk"),
        P(None, "blk"),
        P(None, "blk"),
    )
    out_specs = P(None, "grp", "blk")
    return jax.shard_map(shards, mesh=mesh, in_specs=in_specs, out_specs=out_specs, check_vma=False)
```

time: 100 us -> 86.3 us (0.86)
  local copies, waits for them, and re-layouts: 20.7 us -> 8.04 us
  starting transfers between devices: 23.6 us -> 33.4 us
  Pallas kernels: 42.2 us -> 34 us
  waiting for transfers between devices: 10.2 us -> 6.53 us
    ppermute x6, starting transfers between devices: 14.5 us -> 21 us  [the longest x1 10 us: shards(): g0 = lax.ppermute(ehi, 'grp', [(i, i + 1) for i in range(n_grp - 2)])]
    pallas_call x1, Pallas kernels: 8.57 us -> 2.32 us  [interpolate(): pl.pallas_call(functools.partial(interp_kernel, ks2 // 2), out_shape=jax....]
    ppermute x3, waiting for transfers between devices: 10.1 us -> 4.54 us  [shards(): lax.ppermute(planes, 'blk', partner)]
    ppermute x4 -> x0, local copies, waits for them, and re-layouts: 5.19 us -> none  [the longest x1 1.32 us: shards(): lax.ppermute(fields[:, :, :1], 'blk', [((i + 1) % n_blk, i) for i in rang...]
    ppermute x3, starting transfers between devices: 2 us -> 5.84 us  [shards(): lax.ppermute(planes, 'blk', partner)]
    pallas_call x3 -> x0, local copies, waits for them, and re-layouts: 3.78 us -> none  [fused_step(): pl.pallas_call(functools.partial(step_kernel, nf, rows, lanes), out_shape...]
    broadcast_in_dim x5 -> x0, local copies, waits for them, and re-layouts: 3.17 us -> none  [the longest x2 1.27 us: shards(): return fix_edges(out, g0[:, None, :], g1[:, None, :], gl, gr, low_w, side_w)]
    slice x4 -> x1, local copies, waits for them, and re-layouts: 3.95 us -> 1.8 us  [shards(): fields[:, :, 0]]
  transfers between devices with their start and end apart: 12 -> 12, of which waited for: 2 -> 5; matrix products, arithmetic and copies ran while one was open for 19% -> 9% of each run, Pallas kernels for 9% -> 3%
where the time goes in v4:
time: 86.3 us; the launch traced here: 85.5 us
  Pallas kernels  34 us (39%)
  starting transfers between devices  33.4 us (39%)
  local copies, waits for them, and re-layouts  8.04 us (9%)
  waiting for transfers between devices  6.53 us (8%)
  other arithmetic  3.36 us (4%)
    pallas_call x1, Pallas kernels, fused_step(): pl.pallas_call(functools.partial(step_kernel, nf, rows, lanes), out_shape...  25.8 us
    ppermute x1, starting transfers between devices, shards(): g0 = lax.ppermute(ehi, 'grp', [(i, i + 1) for i in range(n_grp - 2)])  10 us
    pallas_call x1, Pallas kernels, fix_edges(): pl.pallas_call(functools.partial(fix_kernel, low_w, side_w), out_shape=ja...  5.87 us
    ppermute x3, starting transfers between devices, shards(): lax.ppermute(planes, 'blk', partner)  5.84 us
    ppermute x3, waiting for transfers between devices, shards(): lax.ppermute(planes, 'blk', partner)  4.54 us
    ppermute x1, starting transfers between devices, shards(): lax.ppermute(last_row, 'grp', [(i, i + 1) for i in range(n_grp - 2)])  3.98 us
    ppermute x1, starting transfers between devices, shards(): lax.ppermute(fields[:, :, 0], 'blk', [((i + 1) % n_blk, i) for i in range...  3.07 us
    ppermute x1, starting transfers between devices, shards(): gr = lax.ppermute(clo, 'blk', [((i + 1) % n_blk, i) for i in range(n_blk)])  2.83 us
  transfers between devices with their start and end apart: 12, of which 5 were waited for; matrix products, arithmetic and copies ran while one was open for 9% of the time, Pallas kernels for 3%

profile of v4, /device:TPU:1, one launch (start us, length us, event | category | flops | bytes accessed | tf_op | source)
XLA Modules:
  0.0 85.5 jit_solution(14535124465672043530)
XLA Ops:
  0.0 0.7 slice_bitcast_fusion
  0.7 1.1 %fusion.8 = (f32[14,1,512]{2,1,0:T(1,128)S(1)}, f32[14,1,512]{2,1,0:T(1,128)S(1)}) fusion(f32[14,128,512]{2,1,0:T(8,128)} %f_hbm.1), kind=kLoop, calls=%fused_computation.24 | loop fusion | bytes 114688 | tf_op jit(solution)/shard_map/slice | solution.py:274
  1.8 2.1 %collective-permute-start.2 = (f32[1,15,512]{2,1,0:T(8,128)S(1)}, f32[1,15,512]{2,1,0:T(8,128)S(1)}, u32[]{:S(2)}, u32[]{:S(2)}) collective-permute-start(f32[1,15,512]{2,1,0:T(8,128)S(1)} %maximum_bitcast_fusion.1), channel_id=1, source_target_pairs={{0,1},{1,0},{2,3},{3,2},{4,5},{5,4},{6,7},{7,6},{8,9},{9,8},{10,11... | collective-permute-start | bytes 92168 | tf_op jit(solution)/shard_map/ppermute | solution.py:280
  4.0 4.0 %collective-permute-start = (f32[14,512]{1,0:T(8,128)S(1)}, f32[14,512]{1,0:T(8,128)S(1)}, u32[]{:S(2)}, u32[]{:S(2)}) collective-permute-start(f32[14,512]{1,0:T(8,128)S(1)} %bitcast.19), channel_id=1, source_target_pairs={{0,8},{8,16},{1,9},{9,17},{2,10},{10,18},{3,11},{11,19},{4,12},{12... | collective-permute-start | bytes 86024 | tf_op jit(solution)/shard_map/ppermute | solution.py:289
  8.0 1.9 %collective-permute-start.1 = (f32[14,512]{1,0:T(8,128)S(1)}, f32[14,512]{1,0:T(8,128)S(1)}, u32[]{:S(2)}, u32[]{:S(2)}) collective-permute-start(f32[14,512]{1,0:T(8,128)S(1)} %bitcast.20), channel_id=1, source_target_pairs={{8,0},{16,8},{9,1},{17,9},{10,2},{18,10},{11,3},{19,11},{12,4},{20... | collective-permute-start | bytes 86024 | tf_op jit(solution)/shard_map/ppermute | solution.py:290
  9.9 0.0 collective-permute-done.2
  9.9 1.4 %collective-permute-start.3 = (f32[2,15,512]{2,1,0:T(8,128)S(1)}, f32[2,15,512]{2,1,0:T(8,128)S(1)}, u32[]{:S(2)}, u32[]{:S(2)}) collective-permute-start(f32[2,15,512]{2,1,0:T(8,128)S(1)} %pad_maximum_fusion.1), channel_id=1, source_target_pairs={{0,2},{1,3},{2,0},{3,1},{4,6},{5,7},{6,4},{7,5},{8,10},{9,11},{10,... | collective-permute-start | bytes 184328 | tf_op jit(solution)/shard_map/ppermute | solution.py:280
  11.3 1.3 %pad_maximum_fusion.2.w_s = f32[8,512]{1,0:T(8,128)} fusion(f32[4,512]{1,0:T(4,128)} %param.15, f32[4,512]{1,0:T(4,128)} %param.13), kind=kLoop, calls=%fused_computation.15 | loop fusion | flops 4096 | bytes 32768 | tf_op jit(solution)/shard_map/concatenate | solution.py:285
  12.6 0.5 collective-permute-done.3
  13.1 2.4 %collective-permute-start.4 = (f32[4,15,512]{2,1,0:T(8,128)S(1)}, f32[4,15,512]{2,1,0:T(8,128)S(1)}, u32[]{:S(2)}, u32[]{:S(2)}) collective-permute-start(f32[4,15,512]{2,1,0:T(8,128)S(1)} %pad_maximum_fusion), channel_id=1, source_target_pairs={{0,4},{1,5},{2,6},{3,7},{4,0},{5,1},{6,2},{7,3},{8,12},{9,13},{10,... | collective-permute-start | bytes 368648 | tf_op jit(solution)/shard_map/ppermute | solution.py:280
  15.5 0.7 add_convert_fusion.flag_s
  16.1 1.3 %fusion.2.ids_s = s32[8,512]{1,0:T(8,128)} fusion(s32[4,512]{1,0:T(4,128)} %param.14, s32[4,512]{1,0:T(4,128)} %param.12, s32[]{:T(128)S(6)} %axis_index.25), kind=kLoop, calls=%fused_computation.13 | loop fusion | flops 94208 | bytes 32772 | tf_op jit(solution)/shard_map/add | solution.py:284
  17.5 4.0 %collective-permute-done.4 = f32[4,15,512]{2,1,0:T(8,128)S(1)} collective-permute-done((f32[4,15,512]{2,1,0:T(8,128)S(1)}, f32[4,15,512]{2,1,0:T(8,128)S(1)}, u32[]{:S(2)}, u32[]{:S(2)}) %collective-permute-start.4) | collective-permute-done | bytes 122912 | tf_op jit(solution)/shard_map/ppermute | solution.py:280
  21.5 2.0 %copy.20 = f32[8,512,15]{2,1,0:T(8,128)} copy(f32[8,512,15]{1,2,0:T(8,128)S(1)} %maximum_bitcast_fusion) | data formatting | bytes 491520 | tf_op jit(solution)/shard_map/reshape | solution.py:282
  23.5 2.3 %shard_map.82 = f32[15,512]{1,0:T(8,128)} custom-call(f32[2]{0:T(128)} %add_convert_fusion.flag_s, s32[8,512]{1,0:T(8,128)} %fusion.2.ids_s, f32[8,512]{1,0:T(8,128)} %pad_maximum_fusion.2.w_s, f32[4096,15]{1,0:T(8,128)} %bitcast.17), custom_call_target="tpu_custom_call" | custom-call | tf_op jit(solution)/shard_map/pallas_call | solution.py:201
  25.8 0.7 collective-permute-start.5
  26.5 1.8 %fusion.7 = (f32[14,128,1]{2,1,0:T(8,128)S(1)}, f32[14,128,1]{2,1,0:T(8,128)S(1)}) fusion(f32[14,128,512]{2,1,0:T(8,128)} %f_hbm.1), kind=kLoop, calls=%fused_computation.23 | loop fusion | bytes 28672 | tf_op jit(solution)/shard_map/slice | solution.py:292
  28.3 0.3 copy.24
  28.6 1.1 %collective-permute-start.6 = (f32[14,128]{1,0:T(8,128)S(1)}, f32[14,128]{1,0:T(8,128)S(1)}, u32[]{:S(2)}, u32[]{:S(2)}) collective-permute-start(f32[14,128]{1,0:T(8,128)S(1)} %bitcast.21), channel_id=1, source_target_pairs={{0,1},{1,2},{2,3},{3,4},{4,5},{5,6},{6,7},{7,0},{8,9},{9,10},{10,1... | collective-permute-start | bytes 21512 | tf_op jit(solution)/shard_map/ppermute | solution.py:291
  29.8 0.3 copy.25
  30.1 3.1 %collective-permute-start.7 = (f32[14,128]{1,0:T(8,128)S(1)}, f32[14,128]{1,0:T(8,128)S(1)}, u32[]{:S(2)}, u32[]{:S(2)}) collective-permute-start(f32[14,128]{1,0:T(8,128)S(1)} %bitcast.22), channel_id=1, source_target_pairs={{1,0},{2,1},{3,2},{4,3},{5,4},{6,5},{7,6},{0,7},{9,8},{10,9},{11,1... | collective-permute-start | bytes 21512 | tf_op jit(solution)/shard_map/ppermute | solution.py:292
  33.2 0.7 collective-permute-done.6.lft_ref
  33.8 0.0 copy-start.7
  33.8 0.1 collective-permute-done.7.rgt_ref
  34.0 0.0 copy-start.8
  34.0 0.0 collective-permute-done.hlo_ref
  34.0 0.0 copy-start.4
  34.0 0.0 collective-permute-done.1.hhi_ref
  34.0 0.0 copy-start.5
  34.0 0.0 collective-permute-done.5.sw_ref
  34.0 0.5 copy-done.7
  34.4 0.1 copy-done.8
  34.5 0.0 copy-done.4
  34.6 0.0 copy-done.5
  34.6 0.0 copy-start.6
  34.6 0.6 copy-done.6
  35.2 25.8 %shard_map.83 = (f32[14,128,512]{2,1,0:T(8,128)}, f32[14,512]{1,0:T(8,128)}, f32[14,512]{1,0:T(8,128)}, f32[14,128]{1,0:T(8,128)}, f32[14,128]{1,0:T(8,128)}) custom-call(f32[14,14]{1,0:T(8,128)} %mix_s.1, f32[14]{0:T(128)} %act_s.1, f32[2]{0:T(128)} %add_convert_fusion.flag_s, f32[14,128,512]{2,1,0:T(8,128)} %f_hbm.1, f32[128,512]{1,0:T(8,128)} %rate_ref.1, ...), custom_call_target="tpu_custom_call" | custom-call | flops 95420416 | bytes 7602176 | tf_op jit(solution)/shard_map/pallas_call | solution.py:154
  61.0 10.0 %collective-permute-start.8 = (f32[14,512]{1,0:T(8,128)}, f32[14,512]{1,0:T(8,128)S(1)}, u32[]{:S(2)}, u32[]{:S(2)}) collective-permute-start(f32[14,512]{1,0:T(8,128)} %get-tuple-element.11), channel_id=1, source_target_pairs={{0,8},{8,16},{1,9},{9,17},{2,10},{10,18},{3,11},{11,19},{4,12},{12... | collective-permute-start | bytes 86024 | tf_op jit(solution)/shard_map/ppermute | solution.py:298
  71.1 1.9 %collective-permute-start.9 = (f32[14,512]{1,0:T(8,128)}, f32[14,512]{1,0:T(8,128)S(1)}, u32[]{:S(2)}, u32[]{:S(2)}) collective-permute-start(f32[14,512]{1,0:T(8,128)} %get-tuple-element.12), channel_id=1, source_target_pairs={{8,0},{16,8},{9,1},{17,9},{10,2},{18,10},{11,3},{19,11},{12,4},{20... | collective-permute-start | bytes 86024 | tf_op jit(solution)/shard_map/ppermute | solution.py:299
  73.0 2.0 %collective-permute-start.10 = (f32[14,128]{1,0:T(8,128)}, f32[14,128]{1,0:T(8,128)S(1)}, u32[]{:S(2)}, u32[]{:S(2)}) collective-permute-start(f32[14,128]{1,0:T(8,128)} %get-tuple-element.13), channel_id=1, source_target_pairs={{0,1},{1,2},{2,3},{3,4},{4,5},{5,6},{6,7},{7,0},{8,9},{9,10},{10,1... | collective-permute-start | bytes 21512 | tf_op jit(solution)/shard_map/ppermute | solution.py:300
  75.0 2.8 %collective-permute-start.11 = (f32[14,128]{1,0:T(8,128)}, f32[14,128]{1,0:T(8,128)S(1)}, u32[]{:S(2)}, u32[]{:S(2)}) collective-permute-start(f32[14,128]{1,0:T(8,128)} %get-tuple-element.14), channel_id=1, source_target_pairs={{1,0},{2,1},{3,2},{4,3},{5,4},{6,5},{7,6},{0,7},{9,8},{10,9},{11,1... | collective-permute-start | bytes 21512 | tf_op jit(solution)/shard_map/ppermute | solution.py:301
  77.8 1.2 %collective-permute-done.10.gl_ref = f32[14,128]{1,0:T(8,128)S(1)} collective-permute-done((f32[14,128]{1,0:T(8,128)}, f32[14,128]{1,0:T(8,128)S(1)}, u32[]{:S(2)}, u32[]{:S(2)}) %collective-permute-start.10) | collective-permute-done | bytes 7200 | tf_op jit(solution)/shard_map/ppermute | solution.py:300
  79.0 0.0 copy-start.2
  79.0 0.0 collective-permute-done.11.gr_ref
  79.0 0.0 copy-start.3
  79.0 0.0 collective-permute-done.8.g0_ref
  79.0 0.0 copy-start
  79.0 0.0 collective-permute-done.9.g1_ref
  79.0 0.0 copy-start.1
  79.0 0.5 copy-done.2
  79.6 0.0 copy-done.3
  79.6 0.0 copy-done
  79.6 0.0 copy-done.1
  79.6 5.9 %shard_map.84 = f32[14,128,512]{2,1,0:T(8,128)} custom-call(f32[14,128,512]{2,1,0:T(8,128)} %get-tuple-element.10.out_in, f32[14,512]{1,0:T(8,128)} %copy-done, f32[14,512]{1,0:T(8,128)} %copy-done.1, f32[14,128]{1,0:T(8,128)} %copy-done.2, f32[14,128]{1,0:T(8,128)} %copy-done.3), custom_call_target="tpu_custom_call", output_to_operand_aliasing={{}: (0, {})} | custom-call | tf_op jit(solution)/shard_map/pallas_call | solution.py:247
  (6 shorter events, 0.1 us)
Async XLA Ops:
  1.8 8.0 %collective-permute-start.2 = (f32[1,15,512]{2,1,0:T(8,128)S(1)}, f32[1,15,512]{2,1,0:T(8,128)S(1)}, u32[]{:S(2)}, u32[]{:S(2)}) collective-permute-start(f32[1,15,512]{2,1,0:T(8,128)S(1)} %maximum_bitcast_fusion.1), channel_id=1, source_target_pairs={{0,1},{1,0},{2,3},{3,2},{4,5},{5,4},{6,7},{7,6},{8,9},{9,8},{10,11... | collective-permute-start | bytes 92168 | tf_op jit(solution)/shard_map/ppermute | solution.py:280
  4.0 30.0 %collective-permute-start = (f32[14,512]{1,0:T(8,128)S(1)}, f32[14,512]{1,0:T(8,128)S(1)}, u32[]{:S(2)}, u32[]{:S(2)}) collective-permute-start(f32[14,512]{1,0:T(8,128)S(1)} %bitcast.19), channel_id=1, source_target_pairs={{0,8},{8,16},{1,9},{9,17},{2,10},{10,18},{3,11},{11,19},{4,12},{12... | collective-permute-start | bytes 86024 | tf_op jit(solution)/shard_map/ppermute | solution.py:289
  8.0 26.0 %collective-permute-start.1 = (f32[14,512]{1,0:T(8,128)S(1)}, f32[14,512]{1,0:T(8,128)S(1)}, u32[]{:S(2)}, u32[]{:S(2)}) collective-permute-start(f32[14,512]{1,0:T(8,128)S(1)} %bitcast.20), channel_id=1, source_target_pairs={{8,0},{16,8},{9,1},{17,9},{10,2},{18,10},{11,3},{19,11},{12,4},{20... | collective-permute-start | bytes 86024 | tf_op jit(solution)/shard_map/ppermute | solution.py:290
  9.9 3.2 %collective-permute-start.3 = (f32[2,15,512]{2,1,0:T(8,128)S(1)}, f32[2,15,512]{2,1,0:T(8,128)S(1)}, u32[]{:S(2)}, u32[]{:S(2)}) collective-permute-start(f32[2,15,512]{2,1,0:T(8,128)S(1)} %pad_maximum_fusion.1), channel_id=1, source_target_pairs={{0,2},{1,3},{2,0},{3,1},{4,6},{5,7},{6,4},{7,5},{8,10},{9,11},{10,... | collective-permute-start | bytes 184328 | tf_op jit(solution)/shard_map/ppermute | solution.py:280
  13.1 8.4 %collective-permute-start.4 = (f32[4,15,512]{2,1,0:T(8,128)S(1)}, f32[4,15,512]{2,1,0:T(8,128)S(1)}, u32[]{:S(2)}, u32[]{:S(2)}) collective-permute-start(f32[4,15,512]{2,1,0:T(8,128)S(1)} %pad_maximum_fusion), channel_id=1, source_target_pairs={{0,4},{1,5},{2,6},{3,7},{4,0},{5,1},{6,2},{7,3},{8,12},{9,13},{10,... | collective-permute-start | bytes 368648 | tf_op jit(solution)/shard_map/ppermute | solution.py:280
  25.8 8.1 %collective-permute-start.5 = (f32[15,512]{1,0:T(8,128)}, f32[15,512]{1,0:T(8,128)S(1)}, u32[]{:S(2)}, u32[]{:S(2)}) collective-permute-start(f32[15,512]{1,0:T(8,128)} %shard_map.82), channel_id=1, source_target_pairs={{16,24},{24,16},{17,25},{25,17},{18,26},{26,18},{19,27},{27,19},{2... | collective-permute-start | bytes 92168 | tf_op jit(solution)/shard_map/ppermute | solution.py:287
  28.6 5.2 %collective-permute-start.6 = (f32[14,128]{1,0:T(8,128)S(1)}, f32[14,128]{1,0:T(8,128)S(1)}, u32[]{:S(2)}, u32[]{:S(2)}) collective-permute-start(f32[14,128]{1,0:T(8,128)S(1)} %bitcast.21), channel_id=1, source_target_pairs={{0,1},{1,2},{2,3},{3,4},{4,5},{5,6},{6,7},{7,0},{8,9},{9,10},{10,1... | collective-permute-start | bytes 21512 | tf_op jit(solution)/shard_map/ppermute | solution.py:291
  30.1 3.9 %collective-permute-start.7 = (f32[14,128]{1,0:T(8,128)S(1)}, f32[14,128]{1,0:T(8,128)S(1)}, u32[]{:S(2)}, u32[]{:S(2)}) collective-permute-start(f32[14,128]{1,0:T(8,128)S(1)} %bitcast.22), channel_id=1, source_target_pairs={{1,0},{2,1},{3,2},{4,3},{5,4},{6,5},{7,6},{0,7},{9,8},{10,9},{11,1... | collective-permute-start | bytes 21512 | tf_op jit(solution)/shard_map/ppermute | solution.py:292
  33.8 0.6 copy-start.7
  34.0 0.6 copy-start.8
  34.0 0.6 copy-start.4
  34.0 0.6 copy-start.5
  34.6 0.6 copy-start.6
  61.0 18.0 %collective-permute-start.8 = (f32[14,512]{1,0:T(8,128)}, f32[14,512]{1,0:T(8,128)S(1)}, u32[]{:S(2)}, u32[]{:S(2)}) collective-permute-start(f32[14,512]{1,0:T(8,128)} %get-tuple-element.11), channel_id=1, source_target_pairs={{0,8},{8,16},{1,9},{9,17},{2,10},{10,18},{3,11},{11,19},{4,12},{12... | collective-permute-start | bytes 86024 | tf_op jit(solution)/shard_map/ppermute | solution.py:298
  71.1 7.9 %collective-permute-start.9 = (f32[14,512]{1,0:T(8,128)}, f32[14,512]{1,0:T(8,128)S(1)}, u32[]{:S(2)}, u32[]{:S(2)}) collective-permute-start(f32[14,512]{1,0:T(8,128)} %get-tuple-element.12), channel_id=1, source_target_pairs={{8,0},{16,8},{9,1},{17,9},{10,2},{18,10},{11,3},{19,11},{12,4},{20... | collective-permute-start | bytes 86024 | tf_op jit(solution)/shard_map/ppermute | solution.py:299
  73.0 6.0 %collective-permute-start.10 = (f32[14,128]{1,0:T(8,128)}, f32[14,128]{1,0:T(8,128)S(1)}, u32[]{:S(2)}, u32[]{:S(2)}) collective-permute-start(f32[14,128]{1,0:T(8,128)} %get-tuple-element.13), channel_id=1, source_target_pairs={{0,1},{1,2},{2,3},{3,4},{4,5},{5,6},{6,7},{7,0},{8,9},{9,10},{10,1... | collective-permute-start | bytes 21512 | tf_op jit(solution)/shard_map/ppermute | solution.py:300
  75.0 4.0 %collective-permute-start.11 = (f32[14,128]{1,0:T(8,128)}, f32[14,128]{1,0:T(8,128)S(1)}, u32[]{:S(2)}, u32[]{:S(2)}) collective-permute-start(f32[14,128]{1,0:T(8,128)} %get-tuple-element.14), channel_id=1, source_target_pairs={{1,0},{2,1},{3,2},{4,3},{5,4},{6,5},{7,6},{0,7},{9,8},{10,9},{11,1... | collective-permute-start | bytes 21512 | tf_op jit(solution)/shard_map/ppermute | solution.py:301
  79.0 0.6 copy-start.2
  79.0 0.6 copy-start.3
  79.0 0.6 copy-start
  79.0 0.6 copy-start.1

commit v5 on v4

--- a/solution.py
+++ b/solution.py
@@ -21,7 +21,7 @@
 
 
 def step_kernel(nf, rows, lanes, mix_s, act_s, flag_s, f_hbm, rate_ref, hlo_ref, hhi_ref, sw_ref,
-                lft_ref, rgt_ref, out_ref, elo_ref, ehi_ref, clo_ref, chi_ref, ext1, ext2, sem):
+                lft_ref, rgt_ref, out_ref, elo_ref, ehi_ref, clo_ref, chi_ref, ext1, ext2, coef, sem):
     n_i = rows // SUB
     n_j = lanes // LANE
     top = SUB + rows
@@ -41,6 +41,10 @@
         ext1[f, SUB:top, right:right + LANE] = tile_t(rgt_ref[f:f + 1, :])
         ext2[f, SUB:top, 0:LANE] = zeros
         ext2[f, SUB:top, right:right + LANE] = zeros
+    for f in range(nf):
+        for g in range(nf):
+            coef[f * nf + g] = jnp.full((SUB, LANE), mix_s[f, g], jnp.float32)
+        coef[nf * nf + f] = jnp.full((SUB, LANE), -act_s[f], jnp.float32)
     copy.wait()
 
     def high_ghost(ext, halo_of):
@@ -62,74 +66,85 @@
     first_lane = lane_id == 0
     last_lane = lane_id == LANE - 1
 
-    def tendency_tile(src, r0, c0, rate_t):
+    def tendency_tiles(src, r0, c0s, rate_ts):
         r = pl.multiple_of(r0 + SUB, SUB)
-        c = pl.multiple_of(c0 + LANE, LANE)
         r_up = pl.multiple_of(r0, SUB)
         r_dn = pl.multiple_of(r0 + 2 * SUB, SUB)
-        c_w = pl.multiple_of(c0, LANE)
-        c_e = pl.multiple_of(c0 + 2 * LANE, LANE)
-        v4 = src[4, pl.ds(r, SUB), pl.ds(c, LANE)]
-        heat = 1.0 + (jnp.maximum(v4, 0.0) + jnp.log1p(jnp.exp(-jnp.abs(v4))))
-        inv_heat = 1.0 / heat
-        vals = []
-        react = []
+        cs = [pl.multiple_of(c0 + LANE, LANE) for c0 in c0s]
+        reacts = []
+        for c, rate_t in zip(cs, rate_ts):
+            v4 = src[4, pl.ds(r, SUB), pl.ds(c, LANE)]
+            heat = 1.0 + (jnp.maximum(v4, 0.0) + jnp.log1p(jnp.exp(-jnp.abs(v4))))
+            inv_heat = 1.0 / heat
+            reacts.append([
+                rate_t * src[f, pl.ds(r, SUB), pl.ds(c, LANE)] * jnp.exp(coef[nf * nf + f] * inv_heat)
+                for f in range(nf)
+            ])
+        tends = [[] for _ in cs]
         for f in range(nf):
-            v = src[f, pl.ds(r, SUB), pl.ds(c, LANE)]
-            vals.append(v)
-            react.append(rate_t * v * jnp.exp(-act_s[f] * inv_heat))
-        tends = []
-        for f in range(nf):
-            v = vals[f]
-            up = src[f, pl.ds(r_up, SUB), pl.ds(c, LANE)]
-            down = src[f, pl.ds(r_dn, SUB), pl.ds(c, LANE)]
-            west = src[f, pl.ds(r, SUB), pl.ds(c_w, LANE)]
-            east = src[f, pl.ds(r, SUB), pl.ds(c_e, LANE)]
-            backward = jnp.where(first_sub, pltpu.roll(up, 1, 0), pltpu.roll(v, 1, 0))
-            forward = jnp.where(last_sub, pltpu.roll(down, SUB - 1, 0), pltpu.roll(v, SUB - 1, 0))
-            left = jnp.where(first_lane, pltpu.roll(west, 1, 1), pltpu.roll(v, 1, 1))
-            rgt = jnp.where(last_lane, pltpu.roll(east, LANE - 1, 1), pltpu.roll(v, LANE - 1, 1))
-            acc = mix_s[f, 0] * react[0]
-            for g in range(1, nf):
-                acc = acc + mix_s[f, g] * react[g]
-            advect = -courant * (v - backward)
-            spread = diffusion * (backward + forward + left + rgt - 4.0 * v)
-            tends.append(advect + spread + source_step * acc)
-        return vals, tends
+            accs = [None] * len(cs)
+            for g in range(nf):
+                m = coef[f * nf + g]
+                for h in range(len(cs)):
+                    term = m * reacts[h][g]
+                    accs[h] = term if accs[h] is None else accs[h] + term
+            for h, c in enumerate(cs):
+                c_w = pl.multiple_of(c - LANE, LANE)
+                c_e = pl.multiple_of(c + LANE, LANE)
+                v = src[f, pl.ds(r, SUB), pl.ds(c, LANE)]
+                up = src[f, pl.ds(r_up, SUB), pl.ds(c, LANE)]
+                down = src[f, pl.ds(r_dn, SUB), pl.ds(c, LANE)]
+                west = src[f, pl.ds(r, SUB), pl.ds(c_w, LANE)]
+                east = src[f, pl.ds(r, SUB), pl.ds(c_e, LANE)]
+                backward = jnp.where(first_sub, pltpu.roll(up, 1, 0), pltpu.roll(v, 1, 0))
+                forward = jnp.where(last_sub, pltpu.roll(down, SUB - 1, 0), pltpu.roll(v, SUB - 1, 0))
+                left = jnp.where(first_lane, pltpu.roll(west, 1, 1), pltpu.roll(v, 1, 1))
+                rgt = jnp.where(last_lane, pltpu.roll(east, LANE - 1, 1), pltpu.roll(v, LANE - 1, 1))
+                advect = -courant * (v - backward)
+                spread = diffusion * (backward + forward + left + rgt - 4.0 * v)
+                tends[h].append((v, advect + spread + source_step * accs[h]))
+        return tends
+
+    pair = 2 if n_j % 2 == 0 else 1
+    n_jp = n_j // pair
 
     def tile_offsets(t):
-        i = t // n_j
-        j = t % n_j
+        i = t // n_jp
+        jp = t % n_jp
         r0 = pl.multiple_of(i * SUB, SUB)
-        c0 = pl.multiple_of(j * LANE, LANE)
-        return r0, c0
+        c0s = [pl.multiple_of((jp * pair + h) * LANE, LANE) for h in range(pair)]
+        return r0, c0s
 
     def stage_one(t, carry):
-        r0, c0 = tile_offsets(t)
-        rate_t = rate_ref[pl.ds(r0, SUB), pl.ds(c0, LANE)]
-        vals, tends = tendency_tile(ext1, r0, c0, rate_t)
+        r0, c0s = tile_offsets(t)
+        rate_ts = [rate_ref[pl.ds(r0, SUB), pl.ds(c0, LANE)] for c0 in c0s]
+        tends = tendency_tiles(ext1, r0, c0s, rate_ts)
         r = pl.multiple_of(r0 + SUB, SUB)
-        c = pl.multiple_of(c0 + LANE, LANE)
-        for f in range(nf):
-            ext2[f, pl.ds(r, SUB), pl.ds(c, LANE)] = vals[f] + tends[f]
+        for c0, tend in zip(c0s, tends):
+            c = pl.multiple_of(c0 + LANE, LANE)
+            for f in range(nf):
+                v, tf = tend[f]
+                ext2[f, pl.ds(r, SUB), pl.ds(c, LANE)] = v + tf
         return carry
 
-    lax.fori_loop(0, n_i * n_j, stage_one, 0)
+    lax.fori_loop(0, n_i * n_jp, stage_one, 0)
 
     high_ghost(ext2, lambda f: jnp.zeros((1, lanes), jnp.float32))
 
     def stage_two(t, carry):
-        r0, c0 = tile_offsets(t)
-        rate_t = rate_ref[pl.ds(r0, SUB), pl.ds(c0, LANE)]
-        vals, tends = tendency_tile(ext2, r0, c0, rate_t)
+        r0, c0s = tile_offsets(t)
+        rate_ts = [rate_ref[pl.ds(r0, SUB), pl.ds(c0, LANE)] for c0 in c0s]
+        tends = tendency_tiles(ext2, r0, c0s, rate_ts)
         r = pl.multiple_of(r0 + SUB, SUB)
-        c = pl.multiple_of(c0 + LANE, LANE)
-        for f in range(nf):
-            base = ext1[f, pl.ds(r, SUB), pl.ds(c, LANE)]
-            out_ref[f, pl.ds(r0, SUB), pl.ds(c0, LANE)] = 0.5 * (base + vals[f] + tends[f])
+        for c0, tend in zip(c0s, tends):
+            c = pl.multiple_of(c0 + LANE, LANE)
+            for f in range(nf):
+                v, tf = tend[f]
+                base = ext1[f, pl.ds(r, SUB), pl.ds(c, LANE)]
+                out_ref[f, pl.ds(r0, SUB), pl.ds(c0, LANE)] = 0.5 * (base + v + tf)
         return carry
 
-    lax.fori_loop(0, n_i * n_j, stage_two, 0)
+    lax.fori_loop(0, n_i * n_jp, stage_two, 0)
 
     for f in range(nf):
         elo_ref[f:f + 1, :] = ext2[f, SUB:SUB + 1, LANE:right]
@@ -165,6 +180,7 @@
         scratch_shapes=[
             vmem((nf, rows + 2 * SUB, lanes + 2 * LANE), jnp.float32),
             vmem((nf, rows + 2 * SUB, lanes + 2 * LANE), jnp.float32),
+            vmem((nf * nf + nf, SUB, LANE), jnp.float32),
             pltpu.SemaphoreType.DMA((1,)),
         ],
         compiler_params=pltpu.CompilerParams(vmem_limit_bytes=60 * 1024 * 1024),

time: 86.3 us -> 81.8 us (0.948)
  Pallas kernels: 34 us -> 29.5 us
    pallas_call x1, Pallas kernels: 25.8 us -> 21.3 us  [fused_step(): pl.pallas_call(functools.partial(step_kernel, nf, rows, lanes), out_shape...]
  transfers between devices with their start and end apart: 12 -> 12, of which waited for: 5 -> 5; matrix products, arithmetic and copies ran while one was open for 9% -> 10% of each run, Pallas kernels for 3% -> 3%
where the time goes in v5:
time: 81.8 us; the launch traced here: 81 us
  starting transfers between devices  33.4 us (41%)
  Pallas kernels  29.5 us (36%)
  local copies, waits for them, and re-layouts  8.04 us (10%)
  waiting for transfers between devices  6.53 us (8%)
  other arithmetic  3.36 us (4%)
    pallas_call x1, Pallas kernels, fused_step(): pl.pallas_call(functools.partial(step_kernel, nf, rows, lanes), out_shape...  21.3 us
    ppermute x1, starting transfers between devices, shards(): g0 = lax.ppermute(ehi, 'grp', [(i, i + 1) for i in range(n_grp - 2)])  10 us
    pallas_call x1, Pallas kernels, fix_edges(): pl.pallas_call(functools.partial(fix_kernel, low_w, side_w), out_shape=ja...  5.87 us
    ppermute x3, starting transfers between devices, shards(): lax.ppermute(planes, 'blk', partner)  5.84 us
    ppermute x3, waiting for transfers between devices, shards(): lax.ppermute(planes, 'blk', partner)  4.54 us
    ppermute x1, starting transfers between devices, shards(): lax.ppermute(last_row, 'grp', [(i, i + 1) for i in range(n_grp - 2)])  3.98 us
    ppermute x1, starting transfers between devices, shards(): lax.ppermute(fields[:, :, 0], 'blk', [((i + 1) % n_blk, i) for i in range...  3.07 us
    ppermute x1, starting transfers between devices, shards(): gr = lax.ppermute(clo, 'blk', [((i + 1) % n_blk, i) for i in range(n_blk)])  2.83 us
  transfers between devices with their start and end apart: 12, of which 5 were waited for; matrix products, arithmetic and copies ran while one was open for 10% of the time, Pallas kernels for 3%

profile of v5, /device:TPU:1, one launch (start us, length us, event | category | flops | bytes accessed | tf_op | source)
XLA Modules:
  0.0 81.0 jit_solution(16366169122259685531)
XLA Ops:
  0.0 0.7 slice_bitcast_fusion
  0.7 1.1 %fusion.8 = (f32[14,1,512]{2,1,0:T(1,128)S(1)}, f32[14,1,512]{2,1,0:T(1,128)S(1)}) fusion(f32[14,128,512]{2,1,0:T(8,128)} %f_hbm.1), kind=kLoop, calls=%fused_computation.24 | loop fusion | bytes 114688 | tf_op jit(solution)/shard_map/slice | solution.py:290
  1.8 2.1 %collective-permute-start.2 = (f32[1,15,512]{2,1,0:T(8,128)S(1)}, f32[1,15,512]{2,1,0:T(8,128)S(1)}, u32[]{:S(2)}, u32[]{:S(2)}) collective-permute-start(f32[1,15,512]{2,1,0:T(8,128)S(1)} %maximum_bitcast_fusion.1), channel_id=1, source_target_pairs={{0,1},{1,0},{2,3},{3,2},{4,5},{5,4},{6,7},{7,6},{8,9},{9,8},{10,11... | collective-permute-start | bytes 92168 | tf_op jit(solution)/shard_map/ppermute | solution.py:296
  4.0 4.0 %collective-permute-start = (f32[14,512]{1,0:T(8,128)S(1)}, f32[14,512]{1,0:T(8,128)S(1)}, u32[]{:S(2)}, u32[]{:S(2)}) collective-permute-start(f32[14,512]{1,0:T(8,128)S(1)} %bitcast.19), channel_id=1, source_target_pairs={{0,8},{8,16},{1,9},{9,17},{2,10},{10,18},{3,11},{11,19},{4,12},{12... | collective-permute-start | bytes 86024 | tf_op jit(solution)/shard_map/ppermute | solution.py:305
  8.0 1.9 %collective-permute-start.1 = (f32[14,512]{1,0:T(8,128)S(1)}, f32[14,512]{1,0:T(8,128)S(1)}, u32[]{:S(2)}, u32[]{:S(2)}) collective-permute-start(f32[14,512]{1,0:T(8,128)S(1)} %bitcast.20), channel_id=1, source_target_pairs={{8,0},{16,8},{9,1},{17,9},{10,2},{18,10},{11,3},{19,11},{12,4},{20... | collective-permute-start | bytes 86024 | tf_op jit(solution)/shard_map/ppermute | solution.py:306
  9.9 0.0 collective-permute-done.2
  9.9 1.4 %collective-permute-start.3 = (f32[2,15,512]{2,1,0:T(8,128)S(1)}, f32[2,15,512]{2,1,0:T(8,128)S(1)}, u32[]{:S(2)}, u32[]{:S(2)}) collective-permute-start(f32[2,15,512]{2,1,0:T(8,128)S(1)} %pad_maximum_fusion.1), channel_id=1, source_target_pairs={{0,2},{1,3},{2,0},{3,1},{4,6},{5,7},{6,4},{7,5},{8,10},{9,11},{10,... | collective-permute-start | bytes 184328 | tf_op jit(solution)/shard_map/ppermute | solution.py:296
  11.3 1.3 %pad_maximum_fusion.2.w_s = f32[8,512]{1,0:T(8,128)} fusion(f32[4,512]{1,0:T(4,128)} %param.15, f32[4,512]{1,0:T(4,128)} %param.13), kind=kLoop, calls=%fused_computation.15 | loop fusion | flops 4096 | bytes 32768 | tf_op jit(solution)/shard_map/concatenate | solution.py:301
  12.6 0.5 collective-permute-done.3
  13.1 2.4 %collective-permute-start.4 = (f32[4,15,512]{2,1,0:T(8,128)S(1)}, f32[4,15,512]{2,1,0:T(8,128)S(1)}, u32[]{:S(2)}, u32[]{:S(2)}) collective-permute-start(f32[4,15,512]{2,1,0:T(8,128)S(1)} %pad_maximum_fusion), channel_id=1, source_target_pairs={{0,4},{1,5},{2,6},{3,7},{4,0},{5,1},{6,2},{7,3},{8,12},{9,13},{10,... | collective-permute-start | bytes 368648 | tf_op jit(solution)/shard_map/ppermute | solution.py:296
  15.5 0.7 add_convert_fusion.flag_s
  16.1 1.3 %fusion.2.ids_s = s32[8,512]{1,0:T(8,128)} fusion(s32[4,512]{1,0:T(4,128)} %param.14, s32[4,512]{1,0:T(4,128)} %param.12, s32[]{:T(128)S(6)} %axis_index.25), kind=kLoop, calls=%fused_computation.13 | loop fusion | flops 94208 | bytes 32772 | tf_op jit(solution)/shard_map/add | solution.py:300
  17.5 4.0 %collective-permute-done.4 = f32[4,15,512]{2,1,0:T(8,128)S(1)} collective-permute-done((f32[4,15,512]{2,1,0:T(8,128)S(1)}, f32[4,15,512]{2,1,0:T(8,128)S(1)}, u32[]{:S(2)}, u32[]{:S(2)}) %collective-permute-start.4) | collective-permute-done | bytes 122912 | tf_op jit(solution)/shard_map/ppermute | solution.py:296
  21.5 2.0 %copy.20 = f32[8,512,15]{2,1,0:T(8,128)} copy(f32[8,512,15]{1,2,0:T(8,128)S(1)} %maximum_bitcast_fusion) | data formatting | bytes 491520 | tf_op jit(solution)/shard_map/reshape | solution.py:298
  23.5 2.3 %shard_map.82 = f32[15,512]{1,0:T(8,128)} custom-call(f32[2]{0:T(128)} %add_convert_fusion.flag_s, s32[8,512]{1,0:T(8,128)} %fusion.2.ids_s, f32[8,512]{1,0:T(8,128)} %pad_maximum_fusion.2.w_s, f32[4096,15]{1,0:T(8,128)} %bitcast.17), custom_call_target="tpu_custom_call" | custom-call | tf_op jit(solution)/shard_map/pallas_call | solution.py:217
  25.8 0.7 collective-permute-start.5
  26.5 1.8 %fusion.7 = (f32[14,128,1]{2,1,0:T(8,128)S(1)}, f32[14,128,1]{2,1,0:T(8,128)S(1)}) fusion(f32[14,128,512]{2,1,0:T(8,128)} %f_hbm.1), kind=kLoop, calls=%fused_computation.23 | loop fusion | bytes 28672 | tf_op jit(solution)/shard_map/slice | solution.py:308
  28.3 0.3 copy.24
  28.6 1.1 %collective-permute-start.6 = (f32[14,128]{1,0:T(8,128)S(1)}, f32[14,128]{1,0:T(8,128)S(1)}, u32[]{:S(2)}, u32[]{:S(2)}) collective-permute-start(f32[14,128]{1,0:T(8,128)S(1)} %bitcast.21), channel_id=1, source_target_pairs={{0,1},{1,2},{2,3},{3,4},{4,5},{5,6},{6,7},{7,0},{8,9},{9,10},{10,1... | collective-permute-start | bytes 21512 | tf_op jit(solution)/shard_map/ppermute | solution.py:307
  29.8 0.3 copy.25
  30.1 3.1 %collective-permute-start.7 = (f32[14,128]{1,0:T(8,128)S(1)}, f32[14,128]{1,0:T(8,128)S(1)}, u32[]{:S(2)}, u32[]{:S(2)}) collective-permute-start(f32[14,128]{1,0:T(8,128)S(1)} %bitcast.22), channel_id=1, source_target_pairs={{1,0},{2,1},{3,2},{4,3},{5,4},{6,5},{7,6},{0,7},{9,8},{10,9},{11,1... | collective-permute-start | bytes 21512 | tf_op jit(solution)/shard_map/ppermute | solution.py:308
  33.2 0.7 collective-permute-done.6.lft_ref
  33.8 0.0 copy-start.7
  33.8 0.1 collective-permute-done.7.rgt_ref
  34.0 0.0 copy-start.8
  34.0 0.0 collective-permute-done.hlo_ref
  34.0 0.0 copy-start.4
  34.0 0.0 collective-permute-done.1.hhi_ref
  34.0 0.0 copy-start.5
  34.0 0.0 collective-permute-done.5.sw_ref
  34.0 0.5 copy-done.7
  34.4 0.1 copy-done.8
  34.5 0.0 copy-done.4
  34.6 0.0 copy-done.5
  34.6 0.0 copy-start.6
  34.6 0.6 copy-done.6
  35.2 21.3 %shard_map.83 = (f32[14,128,512]{2,1,0:T(8,128)}, f32[14,512]{1,0:T(8,128)}, f32[14,512]{1,0:T(8,128)}, f32[14,128]{1,0:T(8,128)}, f32[14,128]{1,0:T(8,128)}) custom-call(f32[14,14]{1,0:T(8,128)} %mix_s.1, f32[14]{0:T(128)} %act_s.1, f32[2]{0:T(128)} %add_convert_fusion.flag_s, f32[14,128,512]{2,1,0:T(8,128)} %f_hbm.1, f32[128,512]{1,0:T(8,128)} %rate_ref.1, ...), custom_call_target="tpu_custom_call" | custom-call | flops 95420416 | bytes 7602176 | tf_op jit(solution)/shard_map/pallas_call | solution.py:169
  56.5 10.0 %collective-permute-start.8 = (f32[14,512]{1,0:T(8,128)}, f32[14,512]{1,0:T(8,128)S(1)}, u32[]{:S(2)}, u32[]{:S(2)}) collective-permute-start(f32[14,512]{1,0:T(8,128)} %get-tuple-element.11), channel_id=1, source_target_pairs={{0,8},{8,16},{1,9},{9,17},{2,10},{10,18},{3,11},{11,19},{4,12},{12... | collective-permute-start | bytes 86024 | tf_op jit(solution)/shard_map/ppermute | solution.py:314
  66.6 1.9 %collective-permute-start.9 = (f32[14,512]{1,0:T(8,128)}, f32[14,512]{1,0:T(8,128)S(1)}, u32[]{:S(2)}, u32[]{:S(2)}) collective-permute-start(f32[14,512]{1,0:T(8,128)} %get-tuple-element.12), channel_id=1, source_target_pairs={{8,0},{16,8},{9,1},{17,9},{10,2},{18,10},{11,3},{19,11},{12,4},{20... | collective-permute-start | bytes 86024 | tf_op jit(solution)/shard_map/ppermute | solution.py:315
  68.5 2.0 %collective-permute-start.10 = (f32[14,128]{1,0:T(8,128)}, f32[14,128]{1,0:T(8,128)S(1)}, u32[]{:S(2)}, u32[]{:S(2)}) collective-permute-start(f32[14,128]{1,0:T(8,128)} %get-tuple-element.13), channel_id=1, source_target_pairs={{0,1},{1,2},{2,3},{3,4},{4,5},{5,6},{6,7},{7,0},{8,9},{9,10},{10,1... | collective-permute-start | bytes 21512 | tf_op jit(solution)/shard_map/ppermute | solution.py:316
  70.5 2.8 %collective-permute-start.11 = (f32[14,128]{1,0:T(8,128)}, f32[14,128]{1,0:T(8,128)S(1)}, u32[]{:S(2)}, u32[]{:S(2)}) collective-permute-start(f32[14,128]{1,0:T(8,128)} %get-tuple-element.14), channel_id=1, source_target_pairs={{1,0},{2,1},{3,2},{4,3},{5,4},{6,5},{7,6},{0,7},{9,8},{10,9},{11,1... | collective-permute-start | bytes 21512 | tf_op jit(solution)/shard_map/ppermute | solution.py:317
  73.3 1.2 %collective-permute-done.10.gl_ref = f32[14,128]{1,0:T(8,128)S(1)} collective-permute-done((f32[14,128]{1,0:T(8,128)}, f32[14,128]{1,0:T(8,128)S(1)}, u32[]{:S(2)}, u32[]{:S(2)}) %collective-permute-start.10) | collective-permute-done | bytes 7200 | tf_op jit(solution)/shard_map/ppermute | solution.py:316
  74.5 0.0 copy-start.2
  74.5 0.0 collective-permute-done.11.gr_ref
  74.5 0.0 copy-start.3
  74.5 0.0 collective-permute-done.8.g0_ref
  74.5 0.0 copy-start
  74.5 0.0 collective-permute-done.9.g1_ref
  74.5 0.0 copy-start.1
  74.5 0.5 copy-done.2
  75.1 0.0 copy-done.3
  75.1 0.0 copy-done
  75.1 0.0 copy-done.1
  75.1 5.9 %shard_map.84 = f32[14,128,512]{2,1,0:T(8,128)} custom-call(f32[14,128,512]{2,1,0:T(8,128)} %get-tuple-element.10.out_in, f32[14,512]{1,0:T(8,128)} %copy-done, f32[14,512]{1,0:T(8,128)} %copy-done.1, f32[14,128]{1,0:T(8,128)} %copy-done.2, f32[14,128]{1,0:T(8,128)} %copy-done.3), custom_call_target="tpu_custom_call", output_to_operand_aliasing={{}: (0, {})} | custom-call | tf_op jit(solution)/shard_map/pallas_call | solution.py:263
  (6 shorter events, 0.1 us)
Async XLA Ops:
  1.8 8.0 %collective-permute-start.2 = (f32[1,15,512]{2,1,0:T(8,128)S(1)}, f32[1,15,512]{2,1,0:T(8,128)S(1)}, u32[]{:S(2)}, u32[]{:S(2)}) collective-permute-start(f32[1,15,512]{2,1,0:T(8,128)S(1)} %maximum_bitcast_fusion.1), channel_id=1, source_target_pairs={{0,1},{1,0},{2,3},{3,2},{4,5},{5,4},{6,7},{7,6},{8,9},{9,8},{10,11... | collective-permute-start | bytes 92168 | tf_op jit(solution)/shard_map/ppermute | solution.py:296
  4.0 30.0 %collective-permute-start = (f32[14,512]{1,0:T(8,128)S(1)}, f32[14,512]{1,0:T(8,128)S(1)}, u32[]{:S(2)}, u32[]{:S(2)}) collective-permute-start(f32[14,512]{1,0:T(8,128)S(1)} %bitcast.19), channel_id=1, source_target_pairs={{0,8},{8,16},{1,9},{9,17},{2,10},{10,18},{3,11},{11,19},{4,12},{12... | collective-permute-start | bytes 86024 | tf_op jit(solution)/shard_map/ppermute | solution.py:305
  8.0 26.0 %collective-permute-start.1 = (f32[14,512]{1,0:T(8,128)S(1)}, f32[14,512]{1,0:T(8,128)S(1)}, u32[]{:S(2)}, u32[]{:S(2)}) collective-permute-start(f32[14,512]{1,0:T(8,128)S(1)} %bitcast.20), channel_id=1, source_target_pairs={{8,0},{16,8},{9,1},{17,9},{10,2},{18,10},{11,3},{19,11},{12,4},{20... | collective-permute-start | bytes 86024 | tf_op jit(solution)/shard_map/ppermute | solution.py:306
  9.9 3.2 %collective-permute-start.3 = (f32[2,15,512]{2,1,0:T(8,128)S(1)}, f32[2,15,512]{2,1,0:T(8,128)S(1)}, u32[]{:S(2)}, u32[]{:S(2)}) collective-permute-start(f32[2,15,512]{2,1,0:T(8,128)S(1)} %pad_maximum_fusion.1), channel_id=1, source_target_pairs={{0,2},{1,3},{2,0},{3,1},{4,6},{5,7},{6,4},{7,5},{8,10},{9,11},{10,... | collective-permute-start | bytes 184328 | tf_op jit(solution)/shard_map/ppermute | solution.py:296
  13.1 8.4 %collective-permute-start.4 = (f32[4,15,512]{2,1,0:T(8,128)S(1)}, f32[4,15,512]{2,1,0:T(8,128)S(1)}, u32[]{:S(2)}, u32[]{:S(2)}) collective-permute-start(f32[4,15,512]{2,1,0:T(8,128)S(1)} %pad_maximum_fusion), channel_id=1, source_target_pairs={{0,4},{1,5},{2,6},{3,7},{4,0},{5,1},{6,2},{7,3},{8,12},{9,13},{10,... | collective-permute-start | bytes 368648 | tf_op jit(solution)/shard_map/ppermute | solution.py:296
  25.8 8.1 %collective-permute-start.5 = (f32[15,512]{1,0:T(8,128)}, f32[15,512]{1,0:T(8,128)S(1)}, u32[]{:S(2)}, u32[]{:S(2)}) collective-permute-start(f32[15,512]{1,0:T(8,128)} %shard_map.82), channel_id=1, source_target_pairs={{16,24},{24,16},{17,25},{25,17},{18,26},{26,18},{19,27},{27,19},{2... | collective-permute-start | bytes 92168 | tf_op jit(solution)/shard_map/ppermute | solution.py:303
  28.6 5.2 %collective-permute-start.6 = (f32[14,128]{1,0:T(8,128)S(1)}, f32[14,128]{1,0:T(8,128)S(1)}, u32[]{:S(2)}, u32[]{:S(2)}) collective-permute-start(f32[14,128]{1,0:T(8,128)S(1)} %bitcast.21), channel_id=1, source_target_pairs={{0,1},{1,2},{2,3},{3,4},{4,5},{5,6},{6,7},{7,0},{8,9},{9,10},{10,1... | collective-permute-start | bytes 21512 | tf_op jit(solution)/shard_map/ppermute | solution.py:307
  30.1 3.9 %collective-permute-start.7 = (f32[14,128]{1,0:T(8,128)S(1)}, f32[14,128]{1,0:T(8,128)S(1)}, u32[]{:S(2)}, u32[]{:S(2)}) collective-permute-start(f32[14,128]{1,0:T(8,128)S(1)} %bitcast.22), channel_id=1, source_target_pairs={{1,0},{2,1},{3,2},{4,3},{5,4},{6,5},{7,6},{0,7},{9,8},{10,9},{11,1... | collective-permute-start | bytes 21512 | tf_op jit(solution)/shard_map/ppermute | solution.py:308
  33.8 0.6 copy-start.7
  34.0 0.6 copy-start.8
  34.0 0.6 copy-start.4
  34.0 0.6 copy-start.5
  34.6 0.6 copy-start.6
  56.5 18.0 %collective-permute-start.8 = (f32[14,512]{1,0:T(8,128)}, f32[14,512]{1,0:T(8,128)S(1)}, u32[]{:S(2)}, u32[]{:S(2)}) collective-permute-start(f32[14,512]{1,0:T(8,128)} %get-tuple-element.11), channel_id=1, source_target_pairs={{0,8},{8,16},{1,9},{9,17},{2,10},{10,18},{3,11},{11,19},{4,12},{12... | collective-permute-start | bytes 86024 | tf_op jit(solution)/shard_map/ppermute | solution.py:314
  66.6 7.9 %collective-permute-start.9 = (f32[14,512]{1,0:T(8,128)}, f32[14,512]{1,0:T(8,128)S(1)}, u32[]{:S(2)}, u32[]{:S(2)}) collective-permute-start(f32[14,512]{1,0:T(8,128)} %get-tuple-element.12), channel_id=1, source_target_pairs={{8,0},{16,8},{9,1},{17,9},{10,2},{18,10},{11,3},{19,11},{12,4},{20... | collective-permute-start | bytes 86024 | tf_op jit(solution)/shard_map/ppermute | solution.py:315
  68.5 6.0 %collective-permute-start.10 = (f32[14,128]{1,0:T(8,128)}, f32[14,128]{1,0:T(8,128)S(1)}, u32[]{:S(2)}, u32[]{:S(2)}) collective-permute-start(f32[14,128]{1,0:T(8,128)} %get-tuple-element.13), channel_id=1, source_target_pairs={{0,1},{1,2},{2,3},{3,4},{4,5},{5,6},{6,7},{7,0},{8,9},{9,10},{10,1... | collective-permute-start | bytes 21512 | tf_op jit(solution)/shard_map/ppermute | solution.py:316
  70.5 4.0 %collective-permute-start.11 = (f32[14,128]{1,0:T(8,128)}, f32[14,128]{1,0:T(8,128)S(1)}, u32[]{:S(2)}, u32[]{:S(2)}) collective-permute-start(f32[14,128]{1,0:T(8,128)} %get-tuple-element.14), channel_id=1, source_target_pairs={{1,0},{2,1},{3,2},{4,3},{5,4},{6,5},{7,6},{0,7},{9,8},{10,9},{11,1... | collective-permute-start | bytes 21512 | tf_op jit(solution)/shard_map/ppermute | solution.py:317
  74.5 0.6 copy-start.2
  74.5 0.6 copy-start.3
  74.5 0.6 copy-start
  74.5 0.6 copy-start.1

commit v6 on v5

--- a/solution.py
+++ b/solution.py
@@ -188,7 +188,9 @@
     )(mix, act, flags, fields, rate, halo_lo, halo_hi, swapped, lft, rgt)
 
 
-def interp_kernel(ks, flag_s, ids_s, w_s, table_ref, o_ref, acc):
+def interp_kernel(ks, flag_s, ids_s, w_s, table_ref, *refs):
+    n_pass = (len(refs) - 2) // 2
+    ins, o_ref, outs, acc = refs[:n_pass], refs[n_pass], refs[n_pass + 1:-1], refs[-1]
     lanes = o_ref.shape[1]
     half = jnp.where(flag_s[0] > 0.5, 0, ks)
     acc[...] = jnp.zeros(acc.shape, jnp.float32)
@@ -208,48 +210,51 @@
         lax.fori_loop(0, lanes, body, 0, unroll=8)
 
     o_ref[...] = jnp.transpose(acc[...])[0:o_ref.shape[0], :]
-
-
-def interpolate(flags, ids, weights, table):
+    for src, dst in zip(ins, outs):
+        dst[...] = src[...]
+
+
+def interpolate(flags, ids, weights, table, passed):
     ks2, lanes = ids.shape
     smem = pl.BlockSpec(memory_space=pltpu.SMEM)
     vspec = pl.BlockSpec(memory_space=pltpu.VMEM)
     return pl.pallas_call(
         functools.partial(interp_kernel, ks2 // 2),
-        out_shape=jax.ShapeDtypeStruct((table.shape[1], lanes), jnp.float32),
-        in_specs=[smem, smem, smem, vspec],
-        out_specs=vspec,
+        out_shape=(jax.ShapeDtypeStruct((table.shape[1], lanes), jnp.float32),)
+        + tuple(jax.ShapeDtypeStruct(x.shape, x.dtype) for x in passed),
+        in_specs=[smem, smem, smem] + [vspec] * (1 + len(passed)),
+        out_specs=(vspec,) * (1 + len(passed)),
         scratch_shapes=[pltpu.VMEM((lanes, LANE), jnp.float32)],
-    )(flags, ids, weights, table)
+    )(flags, ids, weights, table, *passed)
 
 
 def fix_kernel(low_w, side_w, out_in, g0_ref, g1_ref, gl_ref, gr_ref, out_ref, rb, cb, sem):
     nf, rows, lanes = out_ref.shape
-    row_win = (pl.ds(0, SUB), pl.ds(rows - SUB, SUB))
-    col_win = (pl.ds(0, LANE), pl.ds(lanes - LANE, LANE))
-    loads = [pltpu.make_async_copy(out_ref.at[:, row_win[s], :], rb.at[s], sem.at[s]) for s in range(2)]
-    for c in loads:
-        c.start()
-    for c in loads:
-        c.wait()
-    for f in range(nf):
-        rb[0, f, 0:1, :] = rb[0, f, 0:1, :] + low_w * g0_ref[f:f + 1, :]
-        rb[1, f, SUB - 1:SUB, :] = rb[1, f, SUB - 1:SUB, :] + side_w * g1_ref[f:f + 1, :]
-    stores = [pltpu.make_async_copy(rb.at[s], out_ref.at[:, row_win[s], :], sem.at[s]) for s in range(2)]
-    for c in stores:
-        c.start()
-    for c in stores:
-        c.wait()
-    loads = [pltpu.make_async_copy(out_ref.at[:, :, col_win[s]], cb.at[s], sem.at[s]) for s in range(2)]
+    mid = rows - 2 * SUB
+    wins = [
+        (out_ref.at[:, pl.ds(0, SUB), :], rb.at[0]),
+        (out_ref.at[:, pl.ds(rows - SUB, SUB), :], rb.at[1]),
+        (out_ref.at[:, pl.ds(SUB, mid), pl.ds(0, LANE)], cb.at[0]),
+        (out_ref.at[:, pl.ds(SUB, mid), pl.ds(lanes - LANE, LANE)], cb.at[1]),
+    ]
+    loads = [pltpu.make_async_copy(hbm, buf, sem.at[s]) for s, (hbm, buf) in enumerate(wins)]
     for c in loads:
         c.start()
     for c in loads:
         c.wait()
     lane_id = lax.broadcasted_iota(jnp.int32, (rows, LANE), 1)
+    row_lane = lax.broadcasted_iota(jnp.int32, (SUB, LANE), 1)
     for f in range(nf):
-        cb[0, f] = cb[0, f] + jnp.where(lane_id == 0, side_w * tile_t(gl_ref[f:f + 1, :]), 0.0)
-        cb[1, f] = cb[1, f] + jnp.where(lane_id == LANE - 1, side_w * tile_t(gr_ref[f:f + 1, :]), 0.0)
-    stores = [pltpu.make_async_copy(cb.at[s], out_ref.at[:, :, col_win[s]], sem.at[s]) for s in range(2)]
+        west = jnp.where(lane_id == 0, side_w * tile_t(gl_ref[f:f + 1, :]), 0.0)
+        east = jnp.where(lane_id == LANE - 1, side_w * tile_t(gr_ref[f:f + 1, :]), 0.0)
+        cb[0, f] = cb[0, f] + west[SUB:rows - SUB]
+        cb[1, f] = cb[1, f] + east[SUB:rows - SUB]
+        for s, lo in ((0, 0), (1, rows - SUB)):
+            rb[s, f, :, 0:LANE] = rb[s, f, :, 0:LANE] + west[lo:lo + SUB]
+            rb[s, f, :, lanes - LANE:lanes] = rb[s, f, :, lanes - LANE:lanes] + east[lo:lo + SUB]
+        rb[0, f, 0:1, :] = rb[0, f, 0:1, :] + low_w * g0_ref[f:f + 1, :]
+        rb[1, f, SUB - 1:SUB, :] = rb[1, f, SUB - 1:SUB, :] + side_w * g1_ref[f:f + 1, :]
+    stores = [pltpu.make_async_copy(buf, hbm, sem.at[s]) for s, (hbm, buf) in enumerate(wins)]
     for c in stores:
         c.start()
     for c in stores:
@@ -267,8 +272,8 @@
         out_specs=anyspec,
         scratch_shapes=[
             pltpu.VMEM((2, nf, SUB, lanes), jnp.float32),
-            pltpu.VMEM((2, nf, rows, LANE), jnp.float32),
-            pltpu.SemaphoreType.DMA((2,)),
+            pltpu.VMEM((2, nf, rows - 2 * SUB, LANE), jnp.float32),
+            pltpu.SemaphoreType.DMA((4,)),
         ],
         input_output_aliases={0: 0},
     )(out, g0, g1, gl, gr)
@@ -299,13 +304,13 @@
     ids = jnp.concatenate([inlet_ids, outlet_ids], axis=0)
     ids = (jnp.bitwise_xor(ids // lanes, b) * lanes) + ids % lanes
     wts = jnp.concatenate([inlet_weights, outlet_weights], axis=0)
-    swap = interpolate(flags, ids, wts, table)
-    swapped = lax.ppermute(swap, "grp", [(exit_grp, turb_grp), (turb_grp, exit_grp)])
-
     halo_lo = lax.ppermute(last_row, "grp", [(i, i + 1) for i in range(n_grp - 2)])
     halo_hi = lax.ppermute(first_row, "grp", [(i + 1, i) for i in range(n_grp - 2)])
     lft = lax.ppermute(fields[:, :, lanes - 1], "blk", [(i, (i + 1) % n_blk) for i in range(n_blk)])
     rgt = lax.ppermute(fields[:, :, 0], "blk", [((i + 1) % n_blk, i) for i in range(n_blk)])
+
+    swap, halo_lo, halo_hi, lft, rgt = interpolate(flags, ids, wts, table, (halo_lo, halo_hi, lft, rgt))
+    swapped = lax.ppermute(swap, "grp", [(exit_grp, turb_grp), (turb_grp, exit_grp)])
 
     out, elo, ehi, clo, chi = fused_step(
         fields, react_rate, mix_matrix, activation, flags, halo_lo, halo_hi, swapped, lft, rgt

time: 81.8 us -> 80.7 us (0.987)
  waiting for transfers between devices: 6.53 us -> 10.8 us
  starting transfers between devices: 33.4 us -> 30.7 us
  other arithmetic: 3.36 us -> 1.87 us
  Pallas kernels: 29.5 us -> 28.1 us
    ppermute x3, waiting for transfers between devices: 4.54 us -> 9.55 us  [shards(): lax.ppermute(planes, 'blk', partner)]
    ppermute x3, starting transfers between devices: 5.84 us -> 2.01 us  [shards(): lax.ppermute(planes, 'blk', partner)]
    ppermute x1, starting transfers between devices: 1.96 us -> 0.06 us  [shards(): gl = lax.ppermute(chi, 'blk', [(i, (i + 1) % n_blk) for i in range(n_blk)])]
    pallas_call x1, Pallas kernels: 5.87 us -> 4.34 us  [fix_edges(): pl.pallas_call(functools.partial(fix_kernel, low_w, side_w), out_shape=ja...]
    ppermute x1, starting transfers between devices: 2.83 us -> 4.15 us  [shards(): gr = lax.ppermute(clo, 'blk', [((i + 1) % n_blk, i) for i in range(n_blk)])]
    ppermute x1, starting transfers between devices: 10 us -> 11.2 us  [shards(): g0 = lax.ppermute(ehi, 'grp', [(i, i + 1) for i in range(n_grp - 2)])]
    ppermute x1, starting transfers between devices: 3.07 us -> 3.93 us  [shards(): lax.ppermute(fields[:, :, 0], 'blk', [((i + 1) % n_blk, i) for i in range...]
    ppermute x1, starting transfers between devices: 1.13 us -> 0.28 us  [shards(): lax.ppermute(fields[:, :, lanes - 1], 'blk', [(i, (i + 1) % n_blk) for i...]
  transfers between devices with their start and end apart: 12 -> 12, of which waited for: 5 -> 3; matrix products, arithmetic and copies ran while one was open for 10% -> 9% of each run, Pallas kernels for 3% -> 0%
where the time goes in v6:
time: 80.7 us; the launch traced here: 79.8 us
  starting transfers between devices  30.7 us (38%)
  Pallas kernels  28.1 us (35%)
  waiting for transfers between devices  10.8 us (13%)
  local copies, waits for them, and re-layouts  8.14 us (10%)
  other arithmetic  1.87 us (2%)
    pallas_call x1, Pallas kernels, fused_step(): pl.pallas_call(functools.partial(step_kernel, nf, rows, lanes), out_shape...  21.3 us
    ppermute x1, starting transfers between devices, shards(): g0 = lax.ppermute(ehi, 'grp', [(i, i + 1) for i in range(n_grp - 2)])  11.2 us
    ppermute x3, waiting for transfers between devices, shards(): lax.ppermute(planes, 'blk', partner)  9.55 us
    ppermute x1, starting transfers between devices, shards(): lax.ppermute(last_row, 'grp', [(i, i + 1) for i in range(n_grp - 2)])  4.54 us
    pallas_call x1, Pallas kernels, fix_edges(): pl.pallas_call(functools.partial(fix_kernel, low_w, side_w), out_shape=ja...  4.34 us
    ppermute x1, starting transfers between devices, shards(): gr = lax.ppermute(clo, 'blk', [((i + 1) % n_blk, i) for i in range(n_blk)])  4.15 us
    ppermute x1, starting transfers between devices, shards(): lax.ppermute(fields[:, :, 0], 'blk', [((i + 1) % n_blk, i) for i in range...  3.93 us
    unnamed x30, local copies, waits for them, and re-layouts  2.51 us
  transfers between devices with their start and end apart: 12, of which 3 were waited for; matrix products, arithmetic and copies ran while one was open for 9% of the time, Pallas kernels for 0%

profile of v6, /device:TPU:1, one launch (start us, length us, event | category | flops | bytes accessed | tf_op | source)
XLA Modules:
  0.0 79.8 jit_solution(4272325238571686618)
XLA Ops:
  0.0 0.0 copy-start.8
  0.0 0.0 copy-start.9
  0.0 0.0 copy-start.10
  0.0 0.0 copy-start.11
  0.0 1.1 %fusion.8 = (f32[14,1,512]{2,1,0:T(1,128)S(1)}, f32[14,1,512]{2,1,0:T(1,128)S(1)}) fusion(f32[14,128,512]{2,1,0:T(8,128)} %f_hbm.1), kind=kLoop, calls=%fused_computation.24 | loop fusion | bytes 114688 | tf_op jit(solution)/shard_map/slice | solution.py:295
  1.2 4.5 %collective-permute-start.3 = (f32[14,512]{1,0:T(8,128)S(1)}, f32[14,512]{1,0:T(8,128)S(1)}, u32[]{:S(2)}, u32[]{:S(2)}) collective-permute-start(f32[14,512]{1,0:T(8,128)S(1)} %bitcast.18), channel_id=1, source_target_pairs={{0,8},{8,16},{1,9},{9,17},{2,10},{10,18},{3,11},{11,19},{4,12},{12... | collective-permute-start | bytes 86024 | tf_op jit(solution)/shard_map/ppermute | solution.py:307
  5.7 0.7 slice_bitcast_fusion
  6.5 1.3 %collective-permute-start = (f32[1,15,512]{2,1,0:T(8,128)S(1)}, f32[1,15,512]{2,1,0:T(8,128)S(1)}, u32[]{:S(2)}, u32[]{:S(2)}) collective-permute-start(f32[1,15,512]{2,1,0:T(8,128)S(1)} %maximum_bitcast_fusion.1), channel_id=1, source_target_pairs={{0,1},{1,0},{2,3},{3,2},{4,5},{5,4},{6,7},{7,6},{8,9},{9,8},{10,11... | collective-permute-start | bytes 92168 | tf_op jit(solution)/shard_map/ppermute | solution.py:301
  7.7 1.9 %collective-permute-start.4 = (f32[14,512]{1,0:T(8,128)S(1)}, f32[14,512]{1,0:T(8,128)S(1)}, u32[]{:S(2)}, u32[]{:S(2)}) collective-permute-start(f32[14,512]{1,0:T(8,128)S(1)} %bitcast.20), channel_id=1, source_target_pairs={{8,0},{16,8},{9,1},{17,9},{10,2},{18,10},{11,3},{19,11},{12,4},{20... | collective-permute-start | bytes 86024 | tf_op jit(solution)/shard_map/ppermute | solution.py:308
  9.7 1.8 %fusion.7 = (f32[14,128,1]{2,1,0:T(8,128)S(1)}, f32[14,128,1]{2,1,0:T(8,128)S(1)}) fusion(f32[14,128,512]{2,1,0:T(8,128)} %f_hbm.1), kind=kLoop, calls=%fused_computation.23 | loop fusion | bytes 28672 | tf_op jit(solution)/shard_map/slice | solution.py:310
  11.4 0.3 copy.24
  11.8 0.3 collective-permute-start.5
  12.1 0.3 copy.25
  12.4 3.9 %collective-permute-start.6 = (f32[14,128]{1,0:T(8,128)S(1)}, f32[14,128]{1,0:T(8,128)S(1)}, u32[]{:S(2)}, u32[]{:S(2)}) collective-permute-start(f32[14,128]{1,0:T(8,128)S(1)} %bitcast.22), channel_id=1, source_target_pairs={{1,0},{2,1},{3,2},{4,3},{5,4},{6,5},{7,6},{0,7},{9,8},{10,9},{11,1... | collective-permute-start | bytes 21512 | tf_op jit(solution)/shard_map/ppermute | solution.py:310
  16.3 0.0 collective-permute-done
  16.3 0.1 collective-permute-start.1
  16.4 0.0 copy-done.8
  16.4 0.0 copy-done.9
  16.4 0.6 pad_maximum_fusion.2.w_s
  17.0 2.6 %collective-permute-done.1 = f32[2,15,512]{2,1,0:T(8,128)S(1)} collective-permute-done((f32[2,15,512]{2,1,0:T(8,128)S(1)}, f32[2,15,512]{2,1,0:T(8,128)S(1)}, u32[]{:S(2)}, u32[]{:S(2)}) %collective-permute-start.1) | collective-permute-done | bytes 61472 | tf_op jit(solution)/shard_map/ppermute | solution.py:301
  19.6 0.7 collective-permute-start.2
  20.3 0.6 add_convert_fusion.flag_s
  20.9 0.0 copy-done.10
  20.9 0.0 copy-done.11
  20.9 0.6 fusion.2.ids_s
  21.5 7.0 %collective-permute-done.2 = f32[4,15,512]{2,1,0:T(8,128)S(1)} collective-permute-done((f32[4,15,512]{2,1,0:T(8,128)S(1)}, f32[4,15,512]{2,1,0:T(8,128)S(1)}, u32[]{:S(2)}, u32[]{:S(2)}) %collective-permute-start.2) | collective-permute-done | bytes 122912 | tf_op jit(solution)/shard_map/ppermute | solution.py:301
  28.5 2.0 %copy.20 = f32[8,512,15]{2,1,0:T(8,128)} copy(f32[8,512,15]{1,2,0:T(8,128)S(1)} %maximum_bitcast_fusion) | data formatting | bytes 491520 | tf_op jit(solution)/shard_map/reshape | solution.py:303
  30.5 0.0 collective-permute-done.5.refs_2_
  30.5 0.0 copy-start.4
  30.5 0.0 collective-permute-done.6.refs_3_
  30.5 0.0 copy-start.5
  30.5 0.0 collective-permute-done.3.refs_0_
  30.5 0.0 copy-start
  30.5 0.0 collective-permute-done.4.refs_1_
  30.5 0.0 copy-start.1
  30.5 0.5 copy-done.4
  31.1 0.0 copy-done.5
  31.1 0.0 copy-done
  31.1 0.0 copy-done.1
  31.1 2.4 %shard_map.82 = (f32[15,512]{1,0:T(8,128)}, f32[14,512]{1,0:T(8,128)}, f32[14,512]{1,0:T(8,128)}, f32[14,128]{1,0:T(8,128)}, f32[14,128]{1,0:T(8,128)}) custom-call(f32[2]{0:T(128)} %add_convert_fusion.flag_s, s32[8,512]{1,0:T(8,128)} %fusion.2.ids_s, f32[8,512]{1,0:T(8,128)} %pad_maximum_fusion.2.w_s, f32[4096,15]{1,0:T(8,128)} %bitcast.17, ...), custom_call_target="tpu_custom_call" | custom-call | tf_op jit(solution)/shard_map/pallas_call | solution.py:221
  33.5 0.7 collective-permute-start.7
  34.2 0.0 collective-permute-done.7.sw_ref
  34.2 0.0 copy-start.12
  34.2 0.6 copy-done.12
  34.8 21.3 %shard_map.83 = (f32[14,128,512]{2,1,0:T(8,128)}, f32[14,512]{1,0:T(8,128)}, f32[14,512]{1,0:T(8,128)}, f32[14,128]{1,0:T(8,128)}, f32[14,128]{1,0:T(8,128)}) custom-call(f32[14,14]{1,0:T(8,128)} %mix_s.1, f32[14]{0:T(128)} %act_s.1, f32[2]{0:T(128)} %add_convert_fusion.flag_s, f32[14,128,512]{2,1,0:T(8,128)} %f_hbm.1, f32[128,512]{1,0:T(8,128)} %rate_ref.1, ...), custom_call_target="tpu_custom_call" | custom-call | flops 95420416 | bytes 7602176 | tf_op jit(solution)/shard_map/pallas_call | solution.py:169
  56.2 11.2 %collective-permute-start.8 = (f32[14,512]{1,0:T(8,128)}, f32[14,512]{1,0:T(8,128)S(1)}, u32[]{:S(2)}, u32[]{:S(2)}) collective-permute-start(f32[14,512]{1,0:T(8,128)} %get-tuple-element.21), channel_id=1, source_target_pairs={{0,8},{8,16},{1,9},{9,17},{2,10},{10,18},{3,11},{11,19},{4,12},{12... | collective-permute-start | bytes 86024 | tf_op jit(solution)/shard_map/ppermute | solution.py:319
  67.4 1.9 %collective-permute-start.9 = (f32[14,512]{1,0:T(8,128)}, f32[14,512]{1,0:T(8,128)S(1)}, u32[]{:S(2)}, u32[]{:S(2)}) collective-permute-start(f32[14,512]{1,0:T(8,128)} %get-tuple-element.22), channel_id=1, source_target_pairs={{8,0},{16,8},{9,1},{17,9},{10,2},{18,10},{11,3},{19,11},{12,4},{20... | collective-permute-start | bytes 86024 | tf_op jit(solution)/shard_map/ppermute | solution.py:320
  69.3 0.1 collective-permute-start.10
  69.4 4.2 %collective-permute-start.11 = (f32[14,128]{1,0:T(8,128)}, f32[14,128]{1,0:T(8,128)S(1)}, u32[]{:S(2)}, u32[]{:S(2)}) collective-permute-start(f32[14,128]{1,0:T(8,128)} %get-tuple-element.24), channel_id=1, source_target_pairs={{1,0},{2,1},{3,2},{4,3},{5,4},{6,5},{7,6},{0,7},{9,8},{10,9},{11,1... | collective-permute-start | bytes 21512 | tf_op jit(solution)/shard_map/ppermute | solution.py:322
  73.5 1.2 %collective-permute-done.10.gl_ref = f32[14,128]{1,0:T(8,128)S(1)} collective-permute-done((f32[14,128]{1,0:T(8,128)}, f32[14,128]{1,0:T(8,128)S(1)}, u32[]{:S(2)}, u32[]{:S(2)}) %collective-permute-start.10) | collective-permute-done | bytes 7200 | tf_op jit(solution)/shard_map/ppermute | solution.py:321
  74.8 0.0 copy-start.6
  74.8 0.0 collective-permute-done.11.gr_ref
  74.8 0.0 copy-start.7
  74.8 0.0 collective-permute-done.8.g0_ref
  74.8 0.0 copy-start.2
  74.8 0.0 collective-permute-done.9.g1_ref
  74.8 0.0 copy-start.3
  74.8 0.6 copy-done.6
  75.4 0.0 copy-done.7
  75.4 0.0 copy-done.2
  75.4 0.0 copy-done.3
  75.4 4.3 %shard_map.84 = f32[14,128,512]{2,1,0:T(8,128)} custom-call(f32[14,128,512]{2,1,0:T(8,128)} %get-tuple-element.20.out_in, f32[14,512]{1,0:T(8,128)} %copy-done.2, f32[14,512]{1,0:T(8,128)} %copy-done.3, f32[14,128]{1,0:T(8,128)} %copy-done.6, f32[14,128]{1,0:T(8,128)} %copy-done.7), custom_call_target="tpu_custom_call", output_to_operand_aliasing={{}: (0, {})} | custom-call | tf_op jit(solution)/shard_map/pallas_call | solution.py:268
  (6 shorter events, 0.1 us)
Async XLA Ops:
  0.0 16.4 %copy-start.8 = (f32[4,512]{1,0:T(4,128)S(1)}, f32[4,512]{1,0:T(4,128)}, u32[]{:S(2)}) copy-start(f32[4,512]{1,0:T(4,128)} %param.15) | copy-start | bytes 24580
  0.0 16.4 %copy-start.9 = (f32[4,512]{1,0:T(4,128)S(1)}, f32[4,512]{1,0:T(4,128)}, u32[]{:S(2)}) copy-start(f32[4,512]{1,0:T(4,128)} %param.13) | copy-start | bytes 24580
  0.0 20.9 %copy-start.10 = (s32[4,512]{1,0:T(4,128)S(1)}, s32[4,512]{1,0:T(4,128)}, u32[]{:S(2)}) copy-start(s32[4,512]{1,0:T(4,128)} %param.14) | copy-start | bytes 24580
  0.0 20.9 %copy-start.11 = (s32[4,512]{1,0:T(4,128)S(1)}, s32[4,512]{1,0:T(4,128)}, u32[]{:S(2)}) copy-start(s32[4,512]{1,0:T(4,128)} %param.12) | copy-start | bytes 24580
  1.2 29.3 %collective-permute-start.3 = (f32[14,512]{1,0:T(8,128)S(1)}, f32[14,512]{1,0:T(8,128)S(1)}, u32[]{:S(2)}, u32[]{:S(2)}) collective-permute-start(f32[14,512]{1,0:T(8,128)S(1)} %bitcast.18), channel_id=1, source_target_pairs={{0,8},{8,16},{1,9},{9,17},{2,10},{10,18},{3,11},{11,19},{4,12},{12... | collective-permute-start | bytes 86024 | tf_op jit(solution)/shard_map/ppermute | solution.py:307
  6.5 9.9 %collective-permute-start = (f32[1,15,512]{2,1,0:T(8,128)S(1)}, f32[1,15,512]{2,1,0:T(8,128)S(1)}, u32[]{:S(2)}, u32[]{:S(2)}) collective-permute-start(f32[1,15,512]{2,1,0:T(8,128)S(1)} %maximum_bitcast_fusion.1), channel_id=1, source_target_pairs={{0,1},{1,0},{2,3},{3,2},{4,5},{5,4},{6,7},{7,6},{8,9},{9,8},{10,11... | collective-permute-start | bytes 92168 | tf_op jit(solution)/shard_map/ppermute | solution.py:301
  7.7 22.8 %collective-permute-start.4 = (f32[14,512]{1,0:T(8,128)S(1)}, f32[14,512]{1,0:T(8,128)S(1)}, u32[]{:S(2)}, u32[]{:S(2)}) collective-permute-start(f32[14,512]{1,0:T(8,128)S(1)} %bitcast.20), channel_id=1, source_target_pairs={{8,0},{16,8},{9,1},{17,9},{10,2},{18,10},{11,3},{19,11},{12,4},{20... | collective-permute-start | bytes 86024 | tf_op jit(solution)/shard_map/ppermute | solution.py:308
  11.8 18.7 %collective-permute-start.5 = (f32[14,128]{1,0:T(8,128)S(1)}, f32[14,128]{1,0:T(8,128)S(1)}, u32[]{:S(2)}, u32[]{:S(2)}) collective-permute-start(f32[14,128]{1,0:T(8,128)S(1)} %bitcast.21), channel_id=1, source_target_pairs={{0,1},{1,2},{2,3},{3,4},{4,5},{5,6},{6,7},{7,0},{8,9},{9,10},{10,1... | collective-permute-start | bytes 21512 | tf_op jit(solution)/shard_map/ppermute | solution.py:309
  12.4 18.1 %collective-permute-start.6 = (f32[14,128]{1,0:T(8,128)S(1)}, f32[14,128]{1,0:T(8,128)S(1)}, u32[]{:S(2)}, u32[]{:S(2)}) collective-permute-start(f32[14,128]{1,0:T(8,128)S(1)} %bitcast.22), channel_id=1, source_target_pairs={{1,0},{2,1},{3,2},{4,3},{5,4},{6,5},{7,6},{0,7},{9,8},{10,9},{11,1... | collective-permute-start | bytes 21512 | tf_op jit(solution)/shard_map/ppermute | solution.py:310
  16.3 3.3 %collective-permute-start.1 = (f32[2,15,512]{2,1,0:T(8,128)S(1)}, f32[2,15,512]{2,1,0:T(8,128)S(1)}, u32[]{:S(2)}, u32[]{:S(2)}) collective-permute-start(f32[2,15,512]{2,1,0:T(8,128)S(1)} %pad_maximum_fusion.1), channel_id=1, source_target_pairs={{0,2},{1,3},{2,0},{3,1},{4,6},{5,7},{6,4},{7,5},{8,10},{9,11},{10,... | collective-permute-start | bytes 184328 | tf_op jit(solution)/shard_map/ppermute | solution.py:301
  19.6 8.9 %collective-permute-start.2 = (f32[4,15,512]{2,1,0:T(8,128)S(1)}, f32[4,15,512]{2,1,0:T(8,128)S(1)}, u32[]{:S(2)}, u32[]{:S(2)}) collective-permute-start(f32[4,15,512]{2,1,0:T(8,128)S(1)} %pad_maximum_fusion), channel_id=1, source_target_pairs={{0,4},{1,5},{2,6},{3,7},{4,0},{5,1},{6,2},{7,3},{8,12},{9,13},{10,... | collective-permute-start | bytes 368648 | tf_op jit(solution)/shard_map/ppermute | solution.py:301
  30.5 0.6 copy-start.4
  30.5 0.6 copy-start.5
  30.5 0.6 copy-start
  30.5 0.6 copy-start.1
  33.5 0.7 collective-permute-start.7
  34.2 0.6 copy-start.12
  56.2 18.6 %collective-permute-start.8 = (f32[14,512]{1,0:T(8,128)}, f32[14,512]{1,0:T(8,128)S(1)}, u32[]{:S(2)}, u32[]{:S(2)}) collective-permute-start(f32[14,512]{1,0:T(8,128)} %get-tuple-element.21), channel_id=1, source_target_pairs={{0,8},{8,16},{1,9},{9,17},{2,10},{10,18},{3,11},{11,19},{4,12},{12... | collective-permute-start | bytes 86024 | tf_op jit(solution)/shard_map/ppermute | solution.py:319
  67.4 7.4 %collective-permute-start.9 = (f32[14,512]{1,0:T(8,128)}, f32[14,512]{1,0:T(8,128)S(1)}, u32[]{:S(2)}, u32[]{:S(2)}) collective-permute-start(f32[14,512]{1,0:T(8,128)} %get-tuple-element.22), channel_id=1, source_target_pairs={{8,0},{16,8},{9,1},{17,9},{10,2},{18,10},{11,3},{19,11},{12,4},{20... | collective-permute-start | bytes 86024 | tf_op jit(solution)/shard_map/ppermute | solution.py:320
  69.3 5.5 %collective-permute-start.10 = (f32[14,128]{1,0:T(8,128)}, f32[14,128]{1,0:T(8,128)S(1)}, u32[]{:S(2)}, u32[]{:S(2)}) collective-permute-start(f32[14,128]{1,0:T(8,128)} %get-tuple-element.23), channel_id=1, source_target_pairs={{0,1},{1,2},{2,3},{3,4},{4,5},{5,6},{6,7},{7,0},{8,9},{9,10},{10,1... | collective-permute-start | bytes 21512 | tf_op jit(solution)/shard_map/ppermute | solution.py:321
  69.4 5.4 %collective-permute-start.11 = (f32[14,128]{1,0:T(8,128)}, f32[14,128]{1,0:T(8,128)S(1)}, u32[]{:S(2)}, u32[]{:S(2)}) collective-permute-start(f32[14,128]{1,0:T(8,128)} %get-tuple-element.24), channel_id=1, source_target_pairs={{1,0},{2,1},{3,2},{4,3},{5,4},{6,5},{7,6},{0,7},{9,8},{10,9},{11,1... | collective-permute-start | bytes 21512 | tf_op jit(solution)/shard_map/ppermute | solution.py:322
  74.8 0.6 copy-start.6
  74.8 0.6 copy-start.7
  74.8 0.6 copy-start.2
  74.8 0.6 copy-start.3

commit v7 on v6

--- a/solution.py
+++ b/solution.py
@@ -100,9 +100,9 @@
                 forward = jnp.where(last_sub, pltpu.roll(down, SUB - 1, 0), pltpu.roll(v, SUB - 1, 0))
                 left = jnp.where(first_lane, pltpu.roll(west, 1, 1), pltpu.roll(v, 1, 1))
                 rgt = jnp.where(last_lane, pltpu.roll(east, LANE - 1, 1), pltpu.roll(v, LANE - 1, 1))
-                advect = -courant * (v - backward)
-                spread = diffusion * (backward + forward + left + rgt - 4.0 * v)
-                tends[h].append((v, advect + spread + source_step * accs[h]))
+                flow = (courant + diffusion) * backward + diffusion * (forward + left + rgt)
+                flow = flow - (courant + 4.0 * diffusion) * v
+                tends[h].append((v, flow + source_step * accs[h]))
         return tends
 
     pair = 2 if n_j % 2 == 0 else 1
@@ -294,15 +294,13 @@
     last_row = fields[:, -1, :]
     first_row = fields[:, 0, :]
     payload = jnp.concatenate([last_row, first_row[4:5]], axis=0)
-    planes = payload[None]
-    span = 1
-    while span < n_blk:
-        partner = [(i, i ^ span) for i in range(n_blk)]
-        planes = jnp.concatenate([planes, lax.ppermute(planes, "blk", partner)], axis=0)
-        span *= 2
-    table = jnp.transpose(planes, (0, 2, 1)).reshape(n_blk * lanes, nf + 1)
+    planes = [payload] + [
+        lax.ppermute(payload, "blk", [(i, (i + d) % n_blk) for i in range(n_blk)])
+        for d in range(1, n_blk)
+    ]
+    table = jnp.transpose(jnp.stack(planes), (0, 2, 1)).reshape(n_blk * lanes, nf + 1)
     ids = jnp.concatenate([inlet_ids, outlet_ids], axis=0)
-    ids = (jnp.bitwise_xor(ids // lanes, b) * lanes) + ids % lanes
+    ids = ((b - ids // lanes) % n_blk) * lanes + ids % lanes
     wts = jnp.concatenate([inlet_weights, outlet_weights], axis=0)
     halo_lo = lax.ppermute(last_row, "grp", [(i, i + 1) for i in range(n_grp - 2)])
     halo_hi = lax.ppermute(first_row, "grp", [(i + 1, i) for i in range(n_grp - 2)])

time: 80.7 us -> 87.7 us (1.087)
  starting transfers between devices: 30.7 us -> 36.7 us
  waiting for transfers between devices: 10.8 us -> 12.1 us
    ppermute x3 -> x7, starting transfers between devices: 2.01 us -> 6.77 us  [shards(): lax.ppermute(payload, 'blk', [(i, (i + d) % n_blk) for i in range(n_blk)])]
    ppermute x1, starting transfers between devices: 1.91 us -> 4.51 us  [shards(): lax.ppermute(first_row, 'grp', [(i + 1, i) for i in range(n_grp - 2)])]
    ppermute x1, starting transfers between devices: 0.28 us -> 1.78 us  [shards(): lax.ppermute(fields[:, :, lanes - 1], 'blk', [(i, (i + 1) % n_blk) for i...]
    ppermute x1, starting transfers between devices: 3.93 us -> 2.43 us  [shards(): lax.ppermute(fields[:, :, 0], 'blk', [((i + 1) % n_blk, i) for i in range...]
    ppermute x1, starting transfers between devices: 11.2 us -> 9.83 us  [shards(): g0 = lax.ppermute(ehi, 'grp', [(i, i + 1) for i in range(n_grp - 2)])]
    ppermute x3 -> x7, waiting for transfers between devices: 9.55 us -> 10.9 us  [shards(): lax.ppermute(payload, 'blk', [(i, (i + d) % n_blk) for i in range(n_blk)])]
    unnamed x30 -> x36, local copies, waits for them, and re-layouts: 2.51 us -> 2.51 us
  transfers between devices with their start and end apart: 12 -> 16, of which waited for: 3 -> 4; matrix products, arithmetic and copies ran while one was open for 9% -> 8% of each run, Pallas kernels for 0% -> 0%
where the time goes in v7:
time: 87.7 us; the launch traced here: 86.7 us
  starting transfers between devices  36.7 us (42%)
  Pallas kernels  27.7 us (32%)
  waiting for transfers between devices  12.1 us (14%)
  local copies, waits for them, and re-layouts  8.14 us (9%)
  other arithmetic  1.86 us (2%)
    pallas_call x1, Pallas kernels, fused_step(): pl.pallas_call(functools.partial(step_kernel, nf, rows, lanes), out_shape...  21 us
    ppermute x7, waiting for transfers between devices, shards(): lax.ppermute(payload, 'blk', [(i, (i + d) % n_blk) for i in range(n_blk)])  10.9 us
    ppermute x1, starting transfers between devices, shards(): g0 = lax.ppermute(ehi, 'grp', [(i, i + 1) for i in range(n_grp - 2)])  9.83 us
    ppermute x7, starting transfers between devices, shards(): lax.ppermute(payload, 'blk', [(i, (i + d) % n_blk) for i in range(n_blk)])  6.77 us
    ppermute x1, starting transfers between devices, shards(): lax.ppermute(last_row, 'grp', [(i, i + 1) for i in range(n_grp - 2)])  4.54 us
    ppermute x1, starting transfers between devices, shards(): lax.ppermute(first_row, 'grp', [(i + 1, i) for i in range(n_grp - 2)])  4.51 us
    pallas_call x1, Pallas kernels, fix_edges(): pl.pallas_call(functools.partial(fix_kernel, low_w, side_w), out_shape=ja...  4.34 us
    ppermute x1, starting transfers between devices, shards(): gr = lax.ppermute(clo, 'blk', [((i + 1) % n_blk, i) for i in range(n_blk)])  3.28 us
  transfers between devices with their start and end apart: 16, of which 4 were waited for; matrix products, arithmetic and copies ran while one was open for 8% of the time, Pallas kernels for 0%

profile of v7, /device:TPU:1, one launch (start us, length us, event | category | flops | bytes accessed | tf_op | source)
XLA Modules:
  0.0 86.7 jit_solution(11529875581853048837)
XLA Ops:
  0.0 0.0 copy-start.11
  0.0 1.1 %fusion.6 = (f32[14,1,512]{2,1,0:T(1,128)S(1)}, f32[14,1,512]{2,1,0:T(1,128)S(1)}) fusion(f32[14,128,512]{2,1,0:T(8,128)} %f_hbm.1), kind=kLoop, calls=%fused_computation.30 | loop fusion | bytes 114688 | tf_op jit(solution)/shard_map/slice | solution.py:295
  1.2 4.5 %collective-permute-start.7 = (f32[14,512]{1,0:T(8,128)S(1)}, f32[14,512]{1,0:T(8,128)S(1)}, u32[]{:S(2)}, u32[]{:S(2)}) collective-permute-start(f32[14,512]{1,0:T(8,128)S(1)} %bitcast.32), channel_id=1, source_target_pairs={{0,8},{8,16},{1,9},{9,17},{2,10},{10,18},{3,11},{11,19},{4,12},{12... | collective-permute-start | bytes 86024 | tf_op jit(solution)/shard_map/ppermute | solution.py:305
  5.7 0.7 slice_bitcast_fusion
  6.5 3.4 %collective-permute-start.5 = (f32[15,512]{1,0:T(8,128)S(1)}, f32[15,512]{1,0:T(8,128)S(1)}, u32[]{:S(2)}, u32[]{:S(2)}) collective-permute-start(f32[15,512]{1,0:T(8,128)S(1)} %get-tuple-element.26), channel_id=1, source_target_pairs={{0,6},{1,7},{2,0},{3,1},{4,2},{5,3},{6,4},{7,5},{8,14},{9,15},{10,... | collective-permute-start | bytes 92168 | tf_op jit(solution)/shard_map/ppermute | solution.py:298
  9.8 0.1 collective-permute-start.4
  9.9 3.2 %collective-permute-start.3 = (f32[15,512]{1,0:T(8,128)S(1)}, f32[15,512]{1,0:T(8,128)S(1)}, u32[]{:S(2)}, u32[]{:S(2)}) collective-permute-start(f32[15,512]{1,0:T(8,128)S(1)} %get-tuple-element.26), channel_id=1, source_target_pairs={{0,4},{1,5},{2,6},{3,7},{4,0},{5,1},{6,2},{7,3},{8,12},{9,13},{10,... | collective-permute-start | bytes 92168 | tf_op jit(solution)/shard_map/ppermute | solution.py:298
  13.1 0.0 collective-permute-start
  13.1 1.8 %fusion.5 = (f32[14,128,1]{2,1,0:T(8,128)S(1)}, f32[14,128,1]{2,1,0:T(8,128)S(1)}) fusion(f32[14,128,512]{2,1,0:T(8,128)} %f_hbm.1), kind=kLoop, calls=%fused_computation.29 | loop fusion | bytes 28672 | tf_op jit(solution)/shard_map/slice | solution.py:308
  14.9 0.0 copy-done.8
  14.9 0.0 copy-done.9
  14.9 0.6 pad_maximum_fusion.1.w_s
  15.6 0.0 copy-done.10
  15.6 0.0 copy-done.11
  15.6 0.6 fusion.3.ids_s
  16.2 0.6 add_convert_fusion.flag_s
  16.8 0.3 copy.25
  17.1 0.3 copy.24
  17.5 1.7 %collective-permute-done = f32[15,512]{1,0:T(8,128)S(1)} collective-permute-done((f32[15,512]{1,0:T(8,128)S(1)}, f32[15,512]{1,0:T(8,128)S(1)}, u32[]{:S(2)}, u32[]{:S(2)}) %collective-permute-start) | collective-permute-done | bytes 30752 | tf_op jit(solution)/shard_map/ppermute | solution.py:298
  19.2 0.0 collective-permute-start.1
  19.2 4.6 %collective-permute-done.1 = f32[15,512]{1,0:T(8,128)S(1)} collective-permute-done((f32[15,512]{1,0:T(8,128)S(1)}, f32[15,512]{1,0:T(8,128)S(1)}, u32[]{:S(2)}, u32[]{:S(2)}) %collective-permute-start.1) | collective-permute-done | bytes 30752 | tf_op jit(solution)/shard_map/ppermute | solution.py:298
  23.8 0.0 collective-permute-start.2
  23.8 4.6 %collective-permute-done.2 = f32[15,512]{1,0:T(8,128)S(1)} collective-permute-done((f32[15,512]{1,0:T(8,128)S(1)}, f32[15,512]{1,0:T(8,128)S(1)}, u32[]{:S(2)}, u32[]{:S(2)}) %collective-permute-start.2) | collective-permute-done | bytes 30752 | tf_op jit(solution)/shard_map/ppermute | solution.py:298
  28.4 0.1 collective-permute-start.6
  28.5 0.0 collective-permute-done.3
  28.5 4.5 %collective-permute-start.8 = (f32[14,512]{1,0:T(8,128)S(1)}, f32[14,512]{1,0:T(8,128)S(1)}, u32[]{:S(2)}, u32[]{:S(2)}) collective-permute-start(f32[14,512]{1,0:T(8,128)S(1)} %bitcast.34), channel_id=1, source_target_pairs={{8,0},{16,8},{9,1},{17,9},{10,2},{18,10},{11,3},{19,11},{12,4},{20... | collective-permute-start | bytes 86024 | tf_op jit(solution)/shard_map/ppermute | solution.py:306
  33.0 0.0 collective-permute-done.4
  33.0 1.8 %collective-permute-start.9 = (f32[14,128]{1,0:T(8,128)S(1)}, f32[14,128]{1,0:T(8,128)S(1)}, u32[]{:S(2)}, u32[]{:S(2)}) collective-permute-start(f32[14,128]{1,0:T(8,128)S(1)} %bitcast.36), channel_id=1, source_target_pairs={{0,1},{1,2},{2,3},{3,4},{4,5},{5,6},{6,7},{7,0},{8,9},{9,10},{10,1... | collective-permute-start | bytes 21512 | tf_op jit(solution)/shard_map/ppermute | solution.py:307
  34.8 0.0 collective-permute-done.5
  34.8 2.4 %collective-permute-start.10 = (f32[14,128]{1,0:T(8,128)S(1)}, f32[14,128]{1,0:T(8,128)S(1)}, u32[]{:S(2)}, u32[]{:S(2)}) collective-permute-start(f32[14,128]{1,0:T(8,128)S(1)} %bitcast.35), channel_id=1, source_target_pairs={{1,0},{2,1},{3,2},{4,3},{5,4},{6,5},{7,6},{0,7},{9,8},{10,9},{11,1... | collective-permute-start | bytes 21512 | tf_op jit(solution)/shard_map/ppermute | solution.py:308
  37.2 0.0 collective-permute-done.6
  37.2 2.0 %copy.20 = f32[8,512,15]{2,1,0:T(8,128)} copy(f32[8,512,15]{1,2,0:T(8,128)S(1)} %bitcast.31) | data formatting | bytes 491520 | tf_op jit(solution)/shard_map/reshape | solution.py:301
  39.2 0.0 collective-permute-done.9.refs_2_
  39.2 0.0 collective-permute-done.10.refs_3_
  39.2 0.0 copy-start.5
  39.2 0.0 collective-permute-done.7.refs_0_
  39.2 0.0 copy-start
  39.3 0.0 collective-permute-done.8.refs_1_
  39.3 0.0 copy-start.1
  39.3 0.5 copy-done.4
  39.8 0.0 copy-done.5
  39.8 0.0 copy-done
  39.9 0.0 copy-done.1
  39.9 2.4 %shard_map.82 = (f32[15,512]{1,0:T(8,128)}, f32[14,512]{1,0:T(8,128)}, f32[14,512]{1,0:T(8,128)}, f32[14,128]{1,0:T(8,128)}, f32[14,128]{1,0:T(8,128)}) custom-call(f32[2]{0:T(128)} %add_convert_fusion.flag_s, s32[8,512]{1,0:T(8,128)} %fusion.3.ids_s, f32[8,512]{1,0:T(8,128)} %pad_maximum_fusion.1.w_s, f32[4096,15]{1,0:T(8,128)} %bitcast.30, ...), custom_call_target="tpu_custom_call" | custom-call | tf_op jit(solution)/shard_map/pallas_call | solution.py:221
  42.2 0.7 collective-permute-start.11
  42.9 0.0 collective-permute-done.11.sw_ref
  42.9 0.0 copy-start.12
  42.9 0.6 copy-done.12
  43.5 21.0 %shard_map.83 = (f32[14,128,512]{2,1,0:T(8,128)}, f32[14,512]{1,0:T(8,128)}, f32[14,512]{1,0:T(8,128)}, f32[14,128]{1,0:T(8,128)}, f32[14,128]{1,0:T(8,128)}) custom-call(f32[14,14]{1,0:T(8,128)} %mix_s.1, f32[14]{0:T(128)} %act_s.1, f32[2]{0:T(128)} %add_convert_fusion.flag_s, f32[14,128,512]{2,1,0:T(8,128)} %f_hbm.1, f32[128,512]{1,0:T(8,128)} %rate_ref.1, ...), custom_call_target="tpu_custom_call" | custom-call | flops 95420416 | bytes 7602176 | tf_op jit(solution)/shard_map/pallas_call | solution.py:169
  64.5 9.8 %collective-permute-start.12 = (f32[14,512]{1,0:T(8,128)}, f32[14,512]{1,0:T(8,128)S(1)}, u32[]{:S(2)}, u32[]{:S(2)}) collective-permute-start(f32[14,512]{1,0:T(8,128)} %get-tuple-element.21), channel_id=1, source_target_pairs={{0,8},{8,16},{1,9},{9,17},{2,10},{10,18},{3,11},{11,19},{4,12},{12... | collective-permute-start | bytes 86024 | tf_op jit(solution)/shard_map/ppermute | solution.py:317
  74.4 1.9 %collective-permute-start.13 = (f32[14,512]{1,0:T(8,128)}, f32[14,512]{1,0:T(8,128)S(1)}, u32[]{:S(2)}, u32[]{:S(2)}) collective-permute-start(f32[14,512]{1,0:T(8,128)} %get-tuple-element.22), channel_id=1, source_target_pairs={{8,0},{16,8},{9,1},{17,9},{10,2},{18,10},{11,3},{19,11},{12,4},{20... | collective-permute-start | bytes 86024 | tf_op jit(solution)/shard_map/ppermute | solution.py:318
  76.3 0.9 %collective-permute-start.14 = (f32[14,128]{1,0:T(8,128)}, f32[14,128]{1,0:T(8,128)S(1)}, u32[]{:S(2)}, u32[]{:S(2)}) collective-permute-start(f32[14,128]{1,0:T(8,128)} %get-tuple-element.23), channel_id=1, source_target_pairs={{0,1},{1,2},{2,3},{3,4},{4,5},{5,6},{6,7},{7,0},{8,9},{9,10},{10,1... | collective-permute-start | bytes 21512 | tf_op jit(solution)/shard_map/ppermute | solution.py:319
  77.2 3.3 %collective-permute-start.15 = (f32[14,128]{1,0:T(8,128)}, f32[14,128]{1,0:T(8,128)S(1)}, u32[]{:S(2)}, u32[]{:S(2)}) collective-permute-start(f32[14,128]{1,0:T(8,128)} %get-tuple-element.24), channel_id=1, source_target_pairs={{1,0},{2,1},{3,2},{4,3},{5,4},{6,5},{7,6},{0,7},{9,8},{10,9},{11,1... | collective-permute-start | bytes 21512 | tf_op jit(solution)/shard_map/ppermute | solution.py:320
  80.5 1.2 %collective-permute-done.14.gl_ref = f32[14,128]{1,0:T(8,128)S(1)} collective-permute-done((f32[14,128]{1,0:T(8,128)}, f32[14,128]{1,0:T(8,128)S(1)}, u32[]{:S(2)}, u32[]{:S(2)}) %collective-permute-start.14) | collective-permute-done | bytes 7200 | tf_op jit(solution)/shard_map/ppermute | solution.py:319
  81.8 0.0 collective-permute-done.15.gr_ref
  81.8 0.0 collective-permute-done.12.g0_ref
  81.8 0.0 copy-start.2
  81.8 0.0 collective-permute-done.13.g1_ref
  81.8 0.0 copy-start.3
  81.8 0.5 copy-done.6
  82.4 0.0 copy-done.7
  82.4 0.0 copy-done.2
  82.4 0.0 copy-done.3
  82.4 4.3 %shard_map.84 = f32[14,128,512]{2,1,0:T(8,128)} custom-call(f32[14,128,512]{2,1,0:T(8,128)} %get-tuple-element.20.out_in, f32[14,512]{1,0:T(8,128)} %copy-done.2, f32[14,512]{1,0:T(8,128)} %copy-done.3, f32[14,128]{1,0:T(8,128)} %copy-done.6, f32[14,128]{1,0:T(8,128)} %copy-done.7), custom_call_target="tpu_custom_call", output_to_operand_aliasing={{}: (0, {})} | custom-call | tf_op jit(solution)/shard_map/pallas_call | solution.py:268
  (16 shorter events, 0.1 us)
Async XLA Ops:
  0.0 14.9 %copy-start.8 = (f32[4,512]{1,0:T(4,128)S(1)}, f32[4,512]{1,0:T(4,128)}, u32[]{:S(2)}) copy-start(f32[4,512]{1,0:T(4,128)} %param.15) | copy-start | bytes 24580
  0.0 14.9 %copy-start.9 = (f32[4,512]{1,0:T(4,128)S(1)}, f32[4,512]{1,0:T(4,128)}, u32[]{:S(2)}) copy-start(f32[4,512]{1,0:T(4,128)} %param.13) | copy-start | bytes 24580
  0.0 15.6 %copy-start.10 = (s32[4,512]{1,0:T(4,128)S(1)}, s32[4,512]{1,0:T(4,128)}, u32[]{:S(2)}) copy-start(s32[4,512]{1,0:T(4,128)} %param.14) | copy-start | bytes 24580
  0.0 15.6 %copy-start.11 = (s32[4,512]{1,0:T(4,128)S(1)}, s32[4,512]{1,0:T(4,128)}, u32[]{:S(2)}) copy-start(s32[4,512]{1,0:T(4,128)} %param.12) | copy-start | bytes 24580
  1.2 38.1 %collective-permute-start.7 = (f32[14,512]{1,0:T(8,128)S(1)}, f32[14,512]{1,0:T(8,128)S(1)}, u32[]{:S(2)}, u32[]{:S(2)}) collective-permute-start(f32[14,512]{1,0:T(8,128)S(1)} %bitcast.32), channel_id=1, source_target_pairs={{0,8},{8,16},{1,9},{9,17},{2,10},{10,18},{3,11},{11,19},{4,12},{12... | collective-permute-start | bytes 86024 | tf_op jit(solution)/shard_map/ppermute | solution.py:305
  6.5 28.3 %collective-permute-start.5 = (f32[15,512]{1,0:T(8,128)S(1)}, f32[15,512]{1,0:T(8,128)S(1)}, u32[]{:S(2)}, u32[]{:S(2)}) collective-permute-start(f32[15,512]{1,0:T(8,128)S(1)} %get-tuple-element.26), channel_id=1, source_target_pairs={{0,6},{1,7},{2,0},{3,1},{4,2},{5,3},{6,4},{7,5},{8,14},{9,15},{10,... | collective-permute-start | bytes 92168 | tf_op jit(solution)/shard_map/ppermute | solution.py:298
  9.8 23.2 %collective-permute-start.4 = (f32[15,512]{1,0:T(8,128)S(1)}, f32[15,512]{1,0:T(8,128)S(1)}, u32[]{:S(2)}, u32[]{:S(2)}) collective-permute-start(f32[15,512]{1,0:T(8,128)S(1)} %get-tuple-element.26), channel_id=1, source_target_pairs={{0,5},{1,6},{2,7},{3,0},{4,1},{5,2},{6,3},{7,4},{8,13},{9,14},{10,... | collective-permute-start | bytes 92168 | tf_op jit(solution)/shard_map/ppermute | solution.py:298
  9.9 18.5 %collective-permute-start.3 = (f32[15,512]{1,0:T(8,128)S(1)}, f32[15,512]{1,0:T(8,128)S(1)}, u32[]{:S(2)}, u32[]{:S(2)}) collective-permute-start(f32[15,512]{1,0:T(8,128)S(1)} %get-tuple-element.26), channel_id=1, source_target_pairs={{0,4},{1,5},{2,6},{3,7},{4,0},{5,1},{6,2},{7,3},{8,12},{9,13},{10,... | collective-permute-start | bytes 92168 | tf_op jit(solution)/shard_map/ppermute | solution.py:298
  13.1 6.1 %collective-permute-start = (f32[15,512]{1,0:T(8,128)S(1)}, f32[15,512]{1,0:T(8,128)S(1)}, u32[]{:S(2)}, u32[]{:S(2)}) collective-permute-start(f32[15,512]{1,0:T(8,128)S(1)} %get-tuple-element.26), channel_id=1, source_target_pairs={{0,1},{1,2},{2,3},{3,4},{4,5},{5,6},{6,7},{7,0},{8,9},{9,10},{10,1... | collective-permute-start | bytes 92168 | tf_op jit(solution)/shard_map/ppermute | solution.py:298
  19.2 4.6 %collective-permute-start.1 = (f32[15,512]{1,0:T(8,128)S(1)}, f32[15,512]{1,0:T(8,128)S(1)}, u32[]{:S(2)}, u32[]{:S(2)}) collective-permute-start(f32[15,512]{1,0:T(8,128)S(1)} %get-tuple-element.26), channel_id=1, source_target_pairs={{0,2},{1,3},{2,4},{3,5},{4,6},{5,7},{6,0},{7,1},{8,10},{9,11},{10,... | collective-permute-start | bytes 92168 | tf_op jit(solution)/shard_map/ppermute | solution.py:298
  23.8 4.6 %collective-permute-start.2 = (f32[15,512]{1,0:T(8,128)S(1)}, f32[15,512]{1,0:T(8,128)S(1)}, u32[]{:S(2)}, u32[]{:S(2)}) collective-permute-start(f32[15,512]{1,0:T(8,128)S(1)} %get-tuple-element.26), channel_id=1, source_target_pairs={{0,3},{1,4},{2,5},{3,6},{4,7},{5,0},{6,1},{7,2},{8,11},{9,12},{10,... | collective-permute-start | bytes 92168 | tf_op jit(solution)/shard_map/ppermute | solution.py:298
  28.4 8.9 %collective-permute-start.6 = (f32[15,512]{1,0:T(8,128)S(1)}, f32[15,512]{1,0:T(8,128)S(1)}, u32[]{:S(2)}, u32[]{:S(2)}) collective-permute-start(f32[15,512]{1,0:T(8,128)S(1)} %get-tuple-element.26), channel_id=1, source_target_pairs={{0,7},{1,0},{2,1},{3,2},{4,3},{5,4},{6,5},{7,6},{8,15},{9,8},{10,9... | collective-permute-start | bytes 92168 | tf_op jit(solution)/shard_map/ppermute | solution.py:298
  28.5 10.8 %collective-permute-start.8 = (f32[14,512]{1,0:T(8,128)S(1)}, f32[14,512]{1,0:T(8,128)S(1)}, u32[]{:S(2)}, u32[]{:S(2)}) collective-permute-start(f32[14,512]{1,0:T(8,128)S(1)} %bitcast.34), channel_id=1, source_target_pairs={{8,0},{16,8},{9,1},{17,9},{10,2},{18,10},{11,3},{19,11},{12,4},{20... | collective-permute-start | bytes 86024 | tf_op jit(solution)/shard_map/ppermute | solution.py:306
  33.0 6.2 %collective-permute-start.9 = (f32[14,128]{1,0:T(8,128)S(1)}, f32[14,128]{1,0:T(8,128)S(1)}, u32[]{:S(2)}, u32[]{:S(2)}) collective-permute-start(f32[14,128]{1,0:T(8,128)S(1)} %bitcast.36), channel_id=1, source_target_pairs={{0,1},{1,2},{2,3},{3,4},{4,5},{5,6},{6,7},{7,0},{8,9},{9,10},{10,1... | collective-permute-start | bytes 21512 | tf_op jit(solution)/shard_map/ppermute | solution.py:307
  34.8 4.4 %collective-permute-start.10 = (f32[14,128]{1,0:T(8,128)S(1)}, f32[14,128]{1,0:T(8,128)S(1)}, u32[]{:S(2)}, u32[]{:S(2)}) collective-permute-start(f32[14,128]{1,0:T(8,128)S(1)} %bitcast.35), channel_id=1, source_target_pairs={{1,0},{2,1},{3,2},{4,3},{5,4},{6,5},{7,6},{0,7},{9,8},{10,9},{11,1... | collective-permute-start | bytes 21512 | tf_op jit(solution)/shard_map/ppermute | solution.py:308
  39.2 0.6 copy-start.4
  39.2 0.6 copy-start.5
  39.2 0.6 copy-start
  39.3 0.6 copy-start.1
  42.2 0.7 collective-permute-start.11
  42.9 0.6 copy-start.12
  64.5 17.2 %collective-permute-start.12 = (f32[14,512]{1,0:T(8,128)}, f32[14,512]{1,0:T(8,128)S(1)}, u32[]{:S(2)}, u32[]{:S(2)}) collective-permute-start(f32[14,512]{1,0:T(8,128)} %get-tuple-element.21), channel_id=1, source_target_pairs={{0,8},{8,16},{1,9},{9,17},{2,10},{10,18},{3,11},{11,19},{4,12},{12... | collective-permute-start | bytes 86024 | tf_op jit(solution)/shard_map/ppermute | solution.py:317
  74.4 7.4 %collective-permute-start.13 = (f32[14,512]{1,0:T(8,128)}, f32[14,512]{1,0:T(8,128)S(1)}, u32[]{:S(2)}, u32[]{:S(2)}) collective-permute-start(f32[14,512]{1,0:T(8,128)} %get-tuple-element.22), channel_id=1, source_target_pairs={{8,0},{16,8},{9,1},{17,9},{10,2},{18,10},{11,3},{19,11},{12,4},{20... | collective-permute-start | bytes 86024 | tf_op jit(solution)/shard_map/ppermute | solution.py:318
  76.3 5.5 %collective-permute-start.14 = (f32[14,128]{1,0:T(8,128)}, f32[14,128]{1,0:T(8,128)S(1)}, u32[]{:S(2)}, u32[]{:S(2)}) collective-permute-start(f32[14,128]{1,0:T(8,128)} %get-tuple-element.23), channel_id=1, source_target_pairs={{0,1},{1,2},{2,3},{3,4},{4,5},{5,6},{6,7},{7,0},{8,9},{9,10},{10,1... | collective-permute-start | bytes 21512 | tf_op jit(solution)/shard_map/ppermute | solution.py:319
  77.2 4.5 %collective-permute-start.15 = (f32[14,128]{1,0:T(8,128)}, f32[14,128]{1,0:T(8,128)S(1)}, u32[]{:S(2)}, u32[]{:S(2)}) collective-permute-start(f32[14,128]{1,0:T(8,128)} %get-tuple-element.24), channel_id=1, source_target_pairs={{1,0},{2,1},{3,2},{4,3},{5,4},{6,5},{7,6},{0,7},{9,8},{10,9},{11,1... | collective-permute-start | bytes 21512 | tf_op jit(solution)/shard_map/ppermute | solution.py:320
  81.8 0.6 copy-start.6
  81.8 0.6 copy-start.7
  81.8 0.6 copy-start.2
  81.8 0.6 copy-start.3

commit v8 on v6

--- a/solution.py
+++ b/solution.py
@@ -20,27 +20,35 @@
     return jnp.transpose(jnp.broadcast_to(row, (n, n)))
 
 
-def step_kernel(nf, rows, lanes, mix_s, act_s, flag_s, f_hbm, rate_ref, hlo_ref, hhi_ref, sw_ref,
-                lft_ref, rgt_ref, out_ref, elo_ref, ehi_ref, clo_ref, chi_ref, ext1, ext2, coef, sem):
+def step_kernel(nf, rows, lanes, phase, *refs):
+    if phase == 0:
+        mix_s, act_s, f_hbm, rate_ref, lft_ref, rgt_ref, first_ref, ext1, coef, sem = refs
+    else:
+        (mix_s, act_s, flag_s, f_hbm, p_hbm, rate_ref, hlo_ref, hhi_ref, sw_ref, lft_ref, rgt_ref,
+         out_ref, elo_ref, ehi_ref, clo_ref, chi_ref, ext1, ext2, coef, sem) = refs
     n_i = rows // SUB
     n_j = lanes // LANE
     top = SUB + rows
     right = LANE + lanes
-    at_exit = flag_s[0] > 0.5
-    at_turb = flag_s[1] > 0.5
-    at_end = flag_s[0] + flag_s[1] > 0.5
 
     copy = pltpu.make_async_copy(f_hbm, ext1.at[:, SUB:top, LANE:right], sem.at[0])
     copy.start()
+    if phase == 1:
+        part = pltpu.make_async_copy(p_hbm, ext2.at[:, SUB:top, LANE:right], sem.at[1])
+        part.start()
+        at_exit = flag_s[0] > 0.5
+        at_turb = flag_s[1] > 0.5
+        at_end = flag_s[0] + flag_s[1] > 0.5
     zeros = jnp.zeros((rows, LANE), jnp.float32)
     for f in range(nf):
-        inlet = sw_ref[f:f + 1, :]
-        ext1[f, SUB - 1:SUB, LANE:right] = jnp.where(at_turb, inlet, hlo_ref[f:f + 1, :])
-        ext2[f, SUB - 1:SUB, LANE:right] = jnp.where(at_turb, inlet, 0.0)
+        if phase == 1:
+            inlet = sw_ref[f:f + 1, :]
+            ext1[f, SUB - 1:SUB, LANE:right] = jnp.where(at_turb, inlet, hlo_ref[f:f + 1, :])
+            ext2[f, SUB - 1:SUB, LANE:right] = jnp.where(at_turb, inlet, 0.0)
+            ext2[f, SUB:top, 0:LANE] = zeros
+            ext2[f, SUB:top, right:right + LANE] = zeros
         ext1[f, SUB:top, 0:LANE] = tile_t(lft_ref[f:f + 1, :])
         ext1[f, SUB:top, right:right + LANE] = tile_t(rgt_ref[f:f + 1, :])
-        ext2[f, SUB:top, 0:LANE] = zeros
-        ext2[f, SUB:top, right:right + LANE] = zeros
     for f in range(nf):
         for g in range(nf):
             coef[f * nf + g] = jnp.full((SUB, LANE), mix_s[f, g], jnp.float32)
@@ -57,7 +65,8 @@
                 row = jnp.where(at_end, own, halo)
             ext[f, top:top + 1, LANE:right] = row
 
-    high_ghost(ext1, lambda f: hhi_ref[f:f + 1, :])
+    if phase == 1:
+        high_ghost(ext1, lambda f: hhi_ref[f:f + 1, :])
 
     sub_id = lax.broadcasted_iota(jnp.int32, (SUB, LANE), 0)
     lane_id = lax.broadcasted_iota(jnp.int32, (SUB, LANE), 1)
@@ -108,31 +117,44 @@
     pair = 2 if n_j % 2 == 0 else 1
     n_jp = n_j // pair
 
-    def tile_offsets(t):
-        i = t // n_jp
-        jp = t % n_jp
+    def offsets(i, jp):
         r0 = pl.multiple_of(i * SUB, SUB)
         c0s = [pl.multiple_of((jp * pair + h) * LANE, LANE) for h in range(pair)]
         return r0, c0s
 
-    def stage_one(t, carry):
-        r0, c0s = tile_offsets(t)
+    def stage_one(i, jp, dst, at):
+        r0, c0s = offsets(i, jp)
         rate_ts = [rate_ref[pl.ds(r0, SUB), pl.ds(c0, LANE)] for c0 in c0s]
         tends = tendency_tiles(ext1, r0, c0s, rate_ts)
-        r = pl.multiple_of(r0 + SUB, SUB)
         for c0, tend in zip(c0s, tends):
-            c = pl.multiple_of(c0 + LANE, LANE)
             for f in range(nf):
                 v, tf = tend[f]
-                ext2[f, pl.ds(r, SUB), pl.ds(c, LANE)] = v + tf
+                dst[f, pl.ds(at + r0, SUB), pl.ds(at // SUB * LANE + c0, LANE)] = v + tf
+
+    if phase == 0:
+        def inner(t, carry):
+            stage_one(1 + t // n_jp, t % n_jp, first_ref, 0)
+            return carry
+
+        lax.fori_loop(0, (n_i - 2) * n_jp, inner, 0)
+        edge = jnp.zeros((nf, SUB, lanes), jnp.float32)
+        first_ref[:, 0:SUB, :] = edge
+        first_ref[:, rows - SUB:rows, :] = edge
+        return
+
+    part.wait()
+
+    def outer(t, carry):
+        i = jnp.where(t < n_jp, 0, n_i - 1)
+        stage_one(i, t % n_jp, ext2, SUB)
         return carry
 
-    lax.fori_loop(0, n_i * n_jp, stage_one, 0)
+    lax.fori_loop(0, 2 * n_jp, outer, 0)
 
     high_ghost(ext2, lambda f: jnp.zeros((1, lanes), jnp.float32))
 
     def stage_two(t, carry):
-        r0, c0s = tile_offsets(t)
+        r0, c0s = offsets(t // n_jp, t % n_jp)
         rate_ts = [rate_ref[pl.ds(r0, SUB), pl.ds(c0, LANE)] for c0 in c0s]
         tends = tendency_tiles(ext2, r0, c0s, rate_ts)
         r = pl.multiple_of(r0 + SUB, SUB)
@@ -155,19 +177,42 @@
         chi_ref[f:f + 1, :] = east[LANE - 1:LANE, :]
 
 
-def fused_step(fields, rate, mix, act, flags, halo_lo, halo_hi, swapped, lft, rgt):
+def step_cost(cells, nf, share):
+    return pl.CostEstimate(
+        flops=int(share * 2 * cells * nf * (2 * nf + 24)),
+        transcendentals=int(share * 2 * cells * (nf + 3)),
+        bytes_accessed=4 * cells * (2 * nf + 1),
+    )
+
+
+def interior_stage(fields, rate, mix, act, lft, rgt):
     nf, rows, lanes = fields.shape
     vmem = pltpu.VMEM
     smem = pl.BlockSpec(memory_space=pltpu.SMEM)
     vspec = pl.BlockSpec(memory_space=vmem)
-    cells = rows * lanes
-    cost = pl.CostEstimate(
-        flops=2 * cells * nf * (2 * nf + 24),
-        transcendentals=2 * cells * (nf + 3),
-        bytes_accessed=4 * cells * (2 * nf + 1),
-    )
     return pl.pallas_call(
-        functools.partial(step_kernel, nf, rows, lanes),
+        functools.partial(step_kernel, nf, rows, lanes, 0),
+        out_shape=jax.ShapeDtypeStruct((nf, rows, lanes), jnp.float32),
+        in_specs=[smem, smem, pl.BlockSpec(memory_space=pl.ANY)] + [vspec] * 3,
+        out_specs=vspec,
+        scratch_shapes=[
+            vmem((nf, rows + 2 * SUB, lanes + 2 * LANE), jnp.float32),
+            vmem((nf * nf + nf, SUB, LANE), jnp.float32),
+            pltpu.SemaphoreType.DMA((1,)),
+        ],
+        compiler_params=pltpu.CompilerParams(vmem_limit_bytes=60 * 1024 * 1024),
+        cost_estimate=step_cost(rows * lanes, nf, 0.45),
+    )(mix, act, fields, rate, lft, rgt)
+
+
+def fused_step(fields, part, rate, mix, act, flags, halo_lo, halo_hi, swapped, lft, rgt):
+    nf, rows, lanes = fields.shape
+    vmem = pltpu.VMEM
+    smem = pl.BlockSpec(memory_space=pltpu.SMEM)
+    vspec = pl.BlockSpec(memory_space=vmem)
+    anyspec = pl.BlockSpec(memory_space=pl.ANY)
+    return pl.pallas_call(
+        functools.partial(step_kernel, nf, rows, lanes, 1),
         out_shape=(
             jax.ShapeDtypeStruct((nf, rows, lanes), jnp.float32),
             jax.ShapeDtypeStruct((nf, lanes), jnp.float32),
@@ -175,17 +220,17 @@
             jax.ShapeDtypeStruct((nf, rows), jnp.float32),
             jax.ShapeDtypeStruct((nf, rows), jnp.float32),
         ),
-        in_specs=[smem, smem, smem, pl.BlockSpec(memory_space=pl.ANY)] + [vspec] * 6,
+        in_specs=[smem, smem, smem, anyspec, anyspec] + [vspec] * 6,
         out_specs=(vspec,) * 5,
         scratch_shapes=[
             vmem((nf, rows + 2 * SUB, lanes + 2 * LANE), jnp.float32),
             vmem((nf, rows + 2 * SUB, lanes + 2 * LANE), jnp.float32),
             vmem((nf * nf + nf, SUB, LANE), jnp.float32),
-            pltpu.SemaphoreType.DMA((1,)),
+            pltpu.SemaphoreType.DMA((2,)),
         ],
         compiler_params=pltpu.CompilerParams(vmem_limit_bytes=60 * 1024 * 1024),
-        cost_estimate=cost,
-    )(mix, act, flags, fields, rate, halo_lo, halo_hi, swapped, lft, rgt)
+        cost_estimate=step_cost(rows * lanes, nf, 0.55),
+    )(mix, act, flags, fields, part, rate, halo_lo, halo_hi, swapped, lft, rgt)
 
 
 def interp_kernel(ks, flag_s, ids_s, w_s, table_ref, *refs):
@@ -309,11 +354,14 @@
     lft = lax.ppermute(fields[:, :, lanes - 1], "blk", [(i, (i + 1) % n_blk) for i in range(n_blk)])
     rgt = lax.ppermute(fields[:, :, 0], "blk", [((i + 1) % n_blk, i) for i in range(n_blk)])
 
-    swap, halo_lo, halo_hi, lft, rgt = interpolate(flags, ids, wts, table, (halo_lo, halo_hi, lft, rgt))
+    part = interior_stage(fields, react_rate, mix_matrix, activation, lft, rgt)
+    swap, halo_lo, halo_hi, _ = interpolate(
+        flags, ids, wts, table, (halo_lo, halo_hi, part[:, 0:SUB, 0:LANE])
+    )
     swapped = lax.ppermute(swap, "grp", [(exit_grp, turb_grp), (turb_grp, exit_grp)])
 
     out, elo, ehi, clo, chi = fused_step(
-        fields, react_rate, mix_matrix, activation, flags, halo_lo, halo_hi, swapped, lft, rgt
+        fields, part, react_rate, mix_matrix, activation, flags, halo_lo, halo_hi, swapped, lft, rgt
     )
 
     g0 = lax.ppermute(ehi, "grp", [(i, i + 1) for i in range(n_grp - 2)])

time: 80.7 us -> 84.7 us (1.050)
  waiting for transfers between devices: 10.8 us -> 3.83 us
  Pallas kernels: 28.1 us -> 34 us
  local copies, waits for them, and re-layouts: 8.14 us -> 10.8 us
  starting transfers between devices: 30.7 us -> 32.6 us
    ppermute x3, waiting for transfers between devices: 9.55 us -> 2.56 us  [shards(): lax.ppermute(planes, 'blk', partner)]
    pallas_call x1 -> x2, Pallas kernels: 21.3 us -> 27.3 us  [the longest x1 15.4 us: fused_step(): pl.pallas_call(functools.partial(step_kernel, nf, rows, lanes, 1), out_sh...]
    ppermute x1, starting transfers between devices: 11.2 us -> 13.2 us  [shards(): g0 = lax.ppermute(ehi, 'grp', [(i, i + 1) for i in range(n_grp - 2)])]
    slice x0 -> x1, local copies, waits for them, and re-layouts: none -> 1.44 us  [shards(): part[:, 0:SUB, 0:LANE]]
    unnamed x30, local copies, waits for them, and re-layouts: 2.51 us -> 3.69 us
  transfers between devices with their start and end apart: 12 -> 12, of which waited for: 3 -> 2; matrix products, arithmetic and copies ran while one was open for 9% -> 10% of each run, Pallas kernels for 0% -> 14%
where the time goes in v8:
time: 84.7 us; the launch traced here: 83.3 us
  Pallas kernels  34 us (40%)
  starting transfers between devices  32.6 us (38%)
  local copies, waits for them, and re-layouts  10.8 us (13%)
  waiting for transfers between devices  3.83 us (5%)
  other arithmetic  1.88 us (2%)
    pallas_call x1, Pallas kernels, fused_step(): pl.pallas_call(functools.partial(step_kernel, nf, rows, lanes, 1), out_sh...  15.4 us
    ppermute x1, starting transfers between devices, shards(): g0 = lax.ppermute(ehi, 'grp', [(i, i + 1) for i in range(n_grp - 2)])  13.2 us
    pallas_call x1, Pallas kernels, interior_stage(): pl.pallas_call(functools.partial(step_kernel, nf, rows, lanes, 0), out_sh...  11.9 us
    ppermute x1, starting transfers between devices, shards(): lax.ppermute(last_row, 'grp', [(i, i + 1) for i in range(n_grp - 2)])  4.54 us
    pallas_call x1, Pallas kernels, fix_edges(): pl.pallas_call(functools.partial(fix_kernel, low_w, side_w), out_shape=ja...  4.34 us
    ppermute x1, starting transfers between devices, shards(): gr = lax.ppermute(clo, 'blk', [((i + 1) % n_blk, i) for i in range(n_blk)])  4.15 us
    ppermute x1, starting transfers between devices, shards(): lax.ppermute(fields[:, :, 0], 'blk', [((i + 1) % n_blk, i) for i in range...  3.93 us
    unnamed x30, local copies, waits for them, and re-layouts  3.69 us
  transfers between devices with their start and end apart: 12, of which 2 were waited for; matrix products, arithmetic and copies ran while one was open for 10% of the time, Pallas kernels for 14%

profile of v8, /device:TPU:1, one launch (start us, length us, event | category | flops | bytes accessed | tf_op | source)
XLA Modules:
  0.0 83.3 jit_solution(15406164775540900690)
XLA Ops:
  0.0 0.0 copy-start.9
  0.0 0.0 copy-start.10
  0.0 0.0 copy-start.11
  0.0 0.0 copy-start.12
  0.0 1.1 %fusion.7 = (f32[14,1,512]{2,1,0:T(1,128)S(1)}, f32[14,1,512]{2,1,0:T(1,128)S(1)}) fusion(f32[14,128,512]{2,1,0:T(8,128)} %refs_3_.3), kind=kLoop, calls=%fused_computation.23 | loop fusion | bytes 114688 | tf_op jit(solution)/shard_map/slice | solution.py:340
  1.2 4.5 %collective-permute-start.5 = (f32[14,512]{1,0:T(8,128)S(1)}, f32[14,512]{1,0:T(8,128)S(1)}, u32[]{:S(2)}, u32[]{:S(2)}) collective-permute-start(f32[14,512]{1,0:T(8,128)S(1)} %bitcast.18), channel_id=1, source_target_pairs={{0,8},{8,16},{1,9},{9,17},{2,10},{10,18},{3,11},{11,19},{4,12},{12... | collective-permute-start | bytes 86024 | tf_op jit(solution)/shard_map/ppermute | solution.py:352
  5.7 0.7 slice_bitcast_fusion
  6.5 1.3 %collective-permute-start.2 = (f32[1,15,512]{2,1,0:T(8,128)S(1)}, f32[1,15,512]{2,1,0:T(8,128)S(1)}, u32[]{:S(2)}, u32[]{:S(2)}) collective-permute-start(f32[1,15,512]{2,1,0:T(8,128)S(1)} %maximum_bitcast_fusion.1), channel_id=1, source_target_pairs={{0,1},{1,0},{2,3},{3,2},{4,5},{5,4},{6,7},{7,6},{8,9},{9,8},{10,11... | collective-permute-start | bytes 92168 | tf_op jit(solution)/shard_map/ppermute | solution.py:346
  7.7 1.9 %collective-permute-start.6 = (f32[14,512]{1,0:T(8,128)S(1)}, f32[14,512]{1,0:T(8,128)S(1)}, u32[]{:S(2)}, u32[]{:S(2)}) collective-permute-start(f32[14,512]{1,0:T(8,128)S(1)} %bitcast.20), channel_id=1, source_target_pairs={{8,0},{16,8},{9,1},{17,9},{10,2},{18,10},{11,3},{19,11},{12,4},{20... | collective-permute-start | bytes 86024 | tf_op jit(solution)/shard_map/ppermute | solution.py:353
  9.7 1.8 %fusion.8 = (f32[14,128,1]{2,1,0:T(8,128)S(1)}, f32[14,128,1]{2,1,0:T(8,128)S(1)}) fusion(f32[14,128,512]{2,1,0:T(8,128)} %refs_3_.3), kind=kLoop, calls=%fused_computation.24 | loop fusion | bytes 28672 | tf_op jit(solution)/shard_map/slice | solution.py:355
  11.4 0.3 copy.22
  11.8 0.3 collective-permute-start
  12.1 0.3 copy.23
  12.4 3.9 %collective-permute-start.1 = (f32[14,128]{1,0:T(8,128)S(1)}, f32[14,128]{1,0:T(8,128)S(1)}, u32[]{:S(2)}, u32[]{:S(2)}) collective-permute-start(f32[14,128]{1,0:T(8,128)S(1)} %bitcast.22), channel_id=1, source_target_pairs={{1,0},{2,1},{3,2},{4,3},{5,4},{6,5},{7,6},{0,7},{9,8},{10,9},{11,1... | collective-permute-start | bytes 21512 | tf_op jit(solution)/shard_map/ppermute | solution.py:355
  16.3 0.0 collective-permute-done.2
  16.3 0.1 collective-permute-start.3
  16.4 0.0 copy-done.9
  16.4 0.0 copy-done.10
  16.4 0.6 pad_maximum_fusion.2.w_s
  17.0 2.6 %collective-permute-done.3 = f32[2,15,512]{2,1,0:T(8,128)S(1)} collective-permute-done((f32[2,15,512]{2,1,0:T(8,128)S(1)}, f32[2,15,512]{2,1,0:T(8,128)S(1)}, u32[]{:S(2)}, u32[]{:S(2)}) %collective-permute-start.3) | collective-permute-done | bytes 61472 | tf_op jit(solution)/shard_map/ppermute | solution.py:346
  19.6 0.7 collective-permute-start.4
  20.3 0.0 copy-done.11
  20.3 0.0 copy-done.12
  20.3 0.6 fusion.2.ids_s
  20.9 0.6 add_convert_fusion.flag_s.refs_2_
  21.5 0.0 collective-permute-done.refs_4_.refs_9_
  21.5 0.0 copy-start.5
  21.5 0.0 collective-permute-done.1.refs_5_.refs_10_
  21.5 0.6 copy-done.5
  22.1 0.0 copy-start.6
  22.1 0.6 copy-done.6
  22.7 11.9 %shard_map.82.refs_4_ = f32[14,128,512]{2,1,0:T(8,128)} custom-call(f32[14,14]{1,0:T(8,128)} %refs_0_.3, f32[14]{0:T(128)} %refs_1_.3, f32[14,128,512]{2,1,0:T(8,128)} %refs_3_.3, f32[128,512]{1,0:T(8,128)} %refs_5_.1, f32[14,128]{1,0:T(8,128)} %copy-done.5, f32[14,128]{1,0:T(8,128)} %copy-done.6), custom_call_target="tpu_custom_call" | custom-call | flops 42939188 | bytes 7602176 | tf_op jit(solution)/shard_map/pallas_call | solution.py:193
  34.6 1.4 %slice.29.refs_2_ = f32[14,8,128]{2,1,0:T(8,128)} slice(f32[14,128,512]{2,1,0:T(8,128)} %shard_map.82.refs_4_), slice={[0:14], [0:8], [0:128]} | slice | bytes 114688 | tf_op jit(solution)/shard_map/slice | solution.py:359
  36.0 0.0 collective-permute-done.4
  36.0 2.0 %copy.20 = f32[8,512,15]{2,1,0:T(8,128)} copy(f32[8,512,15]{1,2,0:T(8,128)S(1)} %maximum_bitcast_fusion) | data formatting | bytes 491520 | tf_op jit(solution)/shard_map/reshape | solution.py:348
  38.0 0.0 collective-permute-done.5.refs_0_
  38.0 0.0 copy-start
  38.0 0.0 collective-permute-done.6.refs_1_
  38.0 0.0 copy-start.1
  38.0 0.6 copy-done
  38.6 0.0 copy-done.1
  38.6 2.4 %shard_map.83 = (f32[15,512]{1,0:T(8,128)}, f32[14,512]{1,0:T(8,128)}, f32[14,512]{1,0:T(8,128)}, f32[14,8,128]{2,1,0:T(8,128)}) custom-call(f32[2]{0:T(128)} %add_convert_fusion.flag_s.refs_2_, s32[8,512]{1,0:T(8,128)} %fusion.2.ids_s, f32[8,512]{1,0:T(8,128)} %pad_maximum_fusion.2.w_s, f32[4096,15]{1,0:T(8,128)} %bitcast.17, f32[14,512]{1,0:T(8,128)} %copy-done, ...), custom_call_target="tpu_custom_call" | custom-call | tf_op jit(solution)/shard_map/pallas_call | solution.py:266
  41.0 0.7 collective-permute-start.7
  41.7 0.0 collective-permute-done.7.refs_8_
  41.7 0.0 copy-start.4
  41.7 0.6 copy-done.4
  42.3 15.4 %shard_map.84 = (f32[14,128,512]{2,1,0:T(8,128)}, f32[14,512]{1,0:T(8,128)}, f32[14,512]{1,0:T(8,128)}, f32[14,128]{1,0:T(8,128)}, f32[14,128]{1,0:T(8,128)}) custom-call(f32[14,14]{1,0:T(8,128)} %refs_0_.3, f32[14]{0:T(128)} %refs_1_.3, f32[2]{0:T(128)} %add_convert_fusion.flag_s.refs_2_, f32[14,128,512]{2,1,0:T(8,128)} %refs_3_.3, ...), custom_call_target="tpu_custom_call" | custom-call | flops 52481228 | bytes 7602176 | tf_op jit(solution)/shard_map/pallas_call | solution.py:214
  57.7 13.2 %collective-permute-start.8 = (f32[14,512]{1,0:T(8,128)}, f32[14,512]{1,0:T(8,128)S(1)}, u32[]{:S(2)}, u32[]{:S(2)}) collective-permute-start(f32[14,512]{1,0:T(8,128)} %get-tuple-element.17), channel_id=1, source_target_pairs={{0,8},{8,16},{1,9},{9,17},{2,10},{10,18},{3,11},{11,19},{4,12},{12... | collective-permute-start | bytes 86024 | tf_op jit(solution)/shard_map/ppermute | solution.py:367
  70.9 1.9 %collective-permute-start.9 = (f32[14,512]{1,0:T(8,128)}, f32[14,512]{1,0:T(8,128)S(1)}, u32[]{:S(2)}, u32[]{:S(2)}) collective-permute-start(f32[14,512]{1,0:T(8,128)} %get-tuple-element.18), channel_id=1, source_target_pairs={{8,0},{16,8},{9,1},{17,9},{10,2},{18,10},{11,3},{19,11},{12,4},{20... | collective-permute-start | bytes 86024 | tf_op jit(solution)/shard_map/ppermute | solution.py:368
  72.8 0.1 collective-permute-start.10
  72.9 4.2 %collective-permute-start.11 = (f32[14,128]{1,0:T(8,128)}, f32[14,128]{1,0:T(8,128)S(1)}, u32[]{:S(2)}, u32[]{:S(2)}) collective-permute-start(f32[14,128]{1,0:T(8,128)} %get-tuple-element.20), channel_id=1, source_target_pairs={{1,0},{2,1},{3,2},{4,3},{5,4},{6,5},{7,6},{0,7},{9,8},{10,9},{11,1... | collective-permute-start | bytes 21512 | tf_op jit(solution)/shard_map/ppermute | solution.py:370
  77.0 1.2 %collective-permute-done.10.gl_ref = f32[14,128]{1,0:T(8,128)S(1)} collective-permute-done((f32[14,128]{1,0:T(8,128)}, f32[14,128]{1,0:T(8,128)S(1)}, u32[]{:S(2)}, u32[]{:S(2)}) %collective-permute-start.10) | collective-permute-done | bytes 7200 | tf_op jit(solution)/shard_map/ppermute | solution.py:369
  78.3 0.0 copy-start.7
  78.3 0.0 collective-permute-done.11.gr_ref
  78.3 0.0 copy-start.8
  78.3 0.0 collective-permute-done.8.g0_ref
  78.3 0.0 copy-start.2
  78.3 0.0 collective-permute-done.9.g1_ref
  78.3 0.0 copy-start.3
  78.3 0.5 copy-done.7
  78.9 0.0 copy-done.8
  78.9 0.0 copy-done.2
  78.9 0.0 copy-done.3
  78.9 4.3 %shard_map.85 = f32[14,128,512]{2,1,0:T(8,128)} custom-call(f32[14,128,512]{2,1,0:T(8,128)} %get-tuple-element.16.out_in, f32[14,512]{1,0:T(8,128)} %copy-done.2, f32[14,512]{1,0:T(8,128)} %copy-done.3, f32[14,128]{1,0:T(8,128)} %copy-done.7, f32[14,128]{1,0:T(8,128)} %copy-done.8), custom_call_target="tpu_custom_call", output_to_operand_aliasing={{}: (0, {})} | custom-call | tf_op jit(solution)/shard_map/pallas_call | solution.py:313
  (6 shorter events, 0.1 us)
Async XLA Ops:
  0.0 16.4 %copy-start.9 = (f32[4,512]{1,0:T(4,128)S(1)}, f32[4,512]{1,0:T(4,128)}, u32[]{:S(2)}) copy-start(f32[4,512]{1,0:T(4,128)} %param.15) | copy-start | bytes 24580
  0.0 16.4 %copy-start.10 = (f32[4,512]{1,0:T(4,128)S(1)}, f32[4,512]{1,0:T(4,128)}, u32[]{:S(2)}) copy-start(f32[4,512]{1,0:T(4,128)} %param.13) | copy-start | bytes 24580
  0.0 20.3 %copy-start.11 = (s32[4,512]{1,0:T(4,128)S(1)}, s32[4,512]{1,0:T(4,128)}, u32[]{:S(2)}) copy-start(s32[4,512]{1,0:T(4,128)} %param.14) | copy-start | bytes 24580
  0.0 20.3 %copy-start.12 = (s32[4,512]{1,0:T(4,128)S(1)}, s32[4,512]{1,0:T(4,128)}, u32[]{:S(2)}) copy-start(s32[4,512]{1,0:T(4,128)} %param.12) | copy-start | bytes 24580
  1.2 36.8 %collective-permute-start.5 = (f32[14,512]{1,0:T(8,128)S(1)}, f32[14,512]{1,0:T(8,128)S(1)}, u32[]{:S(2)}, u32[]{:S(2)}) collective-permute-start(f32[14,512]{1,0:T(8,128)S(1)} %bitcast.18), channel_id=1, source_target_pairs={{0,8},{8,16},{1,9},{9,17},{2,10},{10,18},{3,11},{11,19},{4,12},{12... | collective-permute-start | bytes 86024 | tf_op jit(solution)/shard_map/ppermute | solution.py:352
  6.5 9.9 %collective-permute-start.2 = (f32[1,15,512]{2,1,0:T(8,128)S(1)}, f32[1,15,512]{2,1,0:T(8,128)S(1)}, u32[]{:S(2)}, u32[]{:S(2)}) collective-permute-start(f32[1,15,512]{2,1,0:T(8,128)S(1)} %maximum_bitcast_fusion.1), channel_id=1, source_target_pairs={{0,1},{1,0},{2,3},{3,2},{4,5},{5,4},{6,7},{7,6},{8,9},{9,8},{10,11... | collective-permute-start | bytes 92168 | tf_op jit(solution)/shard_map/ppermute | solution.py:346
  7.7 30.3 %collective-permute-start.6 = (f32[14,512]{1,0:T(8,128)S(1)}, f32[14,512]{1,0:T(8,128)S(1)}, u32[]{:S(2)}, u32[]{:S(2)}) collective-permute-start(f32[14,512]{1,0:T(8,128)S(1)} %bitcast.20), channel_id=1, source_target_pairs={{8,0},{16,8},{9,1},{17,9},{10,2},{18,10},{11,3},{19,11},{12,4},{20... | collective-permute-start | bytes 86024 | tf_op jit(solution)/shard_map/ppermute | solution.py:353
  11.8 9.7 %collective-permute-start = (f32[14,128]{1,0:T(8,128)S(1)}, f32[14,128]{1,0:T(8,128)S(1)}, u32[]{:S(2)}, u32[]{:S(2)}) collective-permute-start(f32[14,128]{1,0:T(8,128)S(1)} %bitcast.21), channel_id=1, source_target_pairs={{0,1},{1,2},{2,3},{3,4},{4,5},{5,6},{6,7},{7,0},{8,9},{9,10},{10,1... | collective-permute-start | bytes 21512 | tf_op jit(solution)/shard_map/ppermute | solution.py:354
  12.4 9.1 %collective-permute-start.1 = (f32[14,128]{1,0:T(8,128)S(1)}, f32[14,128]{1,0:T(8,128)S(1)}, u32[]{:S(2)}, u32[]{:S(2)}) collective-permute-start(f32[14,128]{1,0:T(8,128)S(1)} %bitcast.22), channel_id=1, source_target_pairs={{1,0},{2,1},{3,2},{4,3},{5,4},{6,5},{7,6},{0,7},{9,8},{10,9},{11,1... | collective-permute-start | bytes 21512 | tf_op jit(solution)/shard_map/ppermute | solution.py:355
  16.3 3.3 %collective-permute-start.3 = (f32[2,15,512]{2,1,0:T(8,128)S(1)}, f32[2,15,512]{2,1,0:T(8,128)S(1)}, u32[]{:S(2)}, u32[]{:S(2)}) collective-permute-start(f32[2,15,512]{2,1,0:T(8,128)S(1)} %pad_maximum_fusion.1), channel_id=1, source_target_pairs={{0,2},{1,3},{2,0},{3,1},{4,6},{5,7},{6,4},{7,5},{8,10},{9,11},{10,... | collective-permute-start | bytes 184328 | tf_op jit(solution)/shard_map/ppermute | solution.py:346
  19.6 16.4 %collective-permute-start.4 = (f32[4,15,512]{2,1,0:T(8,128)S(1)}, f32[4,15,512]{2,1,0:T(8,128)S(1)}, u32[]{:S(2)}, u32[]{:S(2)}) collective-permute-start(f32[4,15,512]{2,1,0:T(8,128)S(1)} %pad_maximum_fusion), channel_id=1, source_target_pairs={{0,4},{1,5},{2,6},{3,7},{4,0},{5,1},{6,2},{7,3},{8,12},{9,13},{10,... | collective-permute-start | bytes 368648 | tf_op jit(solution)/shard_map/ppermute | solution.py:346
  21.5 0.6 copy-start.5
  22.1 0.6 copy-start.6
  38.0 0.6 copy-start
  38.0 0.6 copy-start.1
  41.0 0.7 collective-permute-start.7
  41.7 0.6 copy-start.4
  57.7 20.6 %collective-permute-start.8 = (f32[14,512]{1,0:T(8,128)}, f32[14,512]{1,0:T(8,128)S(1)}, u32[]{:S(2)}, u32[]{:S(2)}) collective-permute-start(f32[14,512]{1,0:T(8,128)} %get-tuple-element.17), channel_id=1, source_target_pairs={{0,8},{8,16},{1,9},{9,17},{2,10},{10,18},{3,11},{11,19},{4,12},{12... | collective-permute-start | bytes 86024 | tf_op jit(solution)/shard_map/ppermute | solution.py:367
  70.9 7.4 %collective-permute-start.9 = (f32[14,512]{1,0:T(8,128)}, f32[14,512]{1,0:T(8,128)S(1)}, u32[]{:S(2)}, u32[]{:S(2)}) collective-permute-start(f32[14,512]{1,0:T(8,128)} %get-tuple-element.18), channel_id=1, source_target_pairs={{8,0},{16,8},{9,1},{17,9},{10,2},{18,10},{11,3},{19,11},{12,4},{20... | collective-permute-start | bytes 86024 | tf_op jit(solution)/shard_map/ppermute | solution.py:368
  72.8 5.5 %collective-permute-start.10 = (f32[14,128]{1,0:T(8,128)}, f32[14,128]{1,0:T(8,128)S(1)}, u32[]{:S(2)}, u32[]{:S(2)}) collective-permute-start(f32[14,128]{1,0:T(8,128)} %get-tuple-element.19), channel_id=1, source_target_pairs={{0,1},{1,2},{2,3},{3,4},{4,5},{5,6},{6,7},{7,0},{8,9},{9,10},{10,1... | collective-permute-start | bytes 21512 | tf_op jit(solution)/shard_map/ppermute | solution.py:369
  72.9 5.4 %collective-permute-start.11 = (f32[14,128]{1,0:T(8,128)}, f32[14,128]{1,0:T(8,128)S(1)}, u32[]{:S(2)}, u32[]{:S(2)}) collective-permute-start(f32[14,128]{1,0:T(8,128)} %get-tuple-element.20), channel_id=1, source_target_pairs={{1,0},{2,1},{3,2},{4,3},{5,4},{6,5},{7,6},{0,7},{9,8},{10,9},{11,1... | collective-permute-start | bytes 21512 | tf_op jit(solution)/shard_map/ppermute | solution.py:370
  78.3 0.6 copy-start.7
  78.3 0.6 copy-start.8
  78.3 0.6 copy-start.2
  78.3 0.6 copy-start.3

commit v9 on v6

--- a/solution.py
+++ b/solution.py
@@ -194,20 +194,29 @@
     lanes = o_ref.shape[1]
     half = jnp.where(flag_s[0] > 0.5, 0, ks)
     acc[...] = jnp.zeros(acc.shape, jnp.float32)
-    width = table_ref.shape[1]
+    width = table_ref.shape[2]
+
+    sub = lax.broadcasted_iota(jnp.int32, (SUB, width), 0)
 
     @pl.when(flag_s[0] + flag_s[1] > 0.5)
     def _():
-        def body(p, carry):
-            total = None
-            for k in range(ks):
-                q = ids_s[half + k, p]
-                term = w_s[half + k, p] * table_ref[pl.ds(q, 1), :]
-                total = term if total is None else total + term
-            acc[pl.ds(p, 1), 0:width] = total
+        def group(pg, carry):
+            tile = jnp.zeros((SUB, width), jnp.float32)
+            for s in range(SUB):
+                p = pg * SUB + s
+                total = None
+                for k in range(ks):
+                    q = ids_s[half + k, p]
+                    rows8 = table_ref[q // SUB]
+                    term = jnp.where(sub == q % SUB, rows8, 0.0) * w_s[half + k, p]
+                    total = term if total is None else total + term
+                for shift in (4, 2, 1):
+                    total = total + pltpu.roll(total, shift, 0)
+                tile = jnp.where(sub == s, total, tile)
+            acc[pl.ds(pl.multiple_of(pg * SUB, SUB), SUB), 0:width] = tile
             return carry
 
-        lax.fori_loop(0, lanes, body, 0, unroll=8)
+        lax.fori_loop(0, lanes // SUB, group, 0)
 
     o_ref[...] = jnp.transpose(acc[...])[0:o_ref.shape[0], :]
     for src, dst in zip(ins, outs):
@@ -220,7 +229,7 @@
     vspec = pl.BlockSpec(memory_space=pltpu.VMEM)
     return pl.pallas_call(
         functools.partial(interp_kernel, ks2 // 2),
-        out_shape=(jax.ShapeDtypeStruct((table.shape[1], lanes), jnp.float32),)
+        out_shape=(jax.ShapeDtypeStruct((table.shape[2], lanes), jnp.float32),)
         + tuple(jax.ShapeDtypeStruct(x.shape, x.dtype) for x in passed),
         in_specs=[smem, smem, smem] + [vspec] * (1 + len(passed)),
         out_specs=(vspec,) * (1 + len(passed)),
@@ -300,7 +309,7 @@
         partner = [(i, i ^ span) for i in range(n_blk)]
         planes = jnp.concatenate([planes, lax.ppermute(planes, "blk", partner)], axis=0)
         span *= 2
-    table = jnp.transpose(planes, (0, 2, 1)).reshape(n_blk * lanes, nf + 1)
+    table = jnp.transpose(planes, (0, 2, 1)).reshape(n_blk * lanes // SUB, SUB, nf + 1)
     ids = jnp.concatenate([inlet_ids, outlet_ids], axis=0)
     ids = (jnp.bitwise_xor(ids // lanes, b) * lanes) + ids % lanes
     wts = jnp.concatenate([inlet_weights, outlet_weights], axis=0)

time: 80.7 us -> 94.6 us (1.17)
  starting transfers between devices: 30.7 us -> 44.5 us
    ppermute x1, starting transfers between devices: 11.2 us -> 25.1 us  [shards(): g0 = lax.ppermute(ehi, 'grp', [(i, i + 1) for i in range(n_grp - 2)])]
    reshape x1 -> x0, local copies, waits for them, and re-layouts: 1.97 us -> none  [shards(): table = jnp.transpose(planes, (0, 2, 1)).reshape(n_blk * lanes, nf + 1)]
    transpose x0 -> x1, local copies, waits for them, and re-layouts: none -> 1.97 us  [shards(): jnp.transpose(planes, (0, 2, 1)).reshape(n_blk * lanes // SUB, SUB, nf + 1)]
  transfers between devices with their start and end apart: 12 -> 12, of which waited for: 3 -> 3; matrix products, arithmetic and copies ran while one was open for 9% -> 8% of each run, Pallas kernels for 0% -> 0%
where the time goes in v9:
time: 94.6 us; the launch traced here: 93.6 us
  starting transfers between devices  44.5 us (47%)
  Pallas kernels  28.1 us (30%)
  waiting for transfers between devices  10.8 us (11%)
  local copies, waits for them, and re-layouts  8.14 us (9%)
  other arithmetic  1.87 us (2%)
    ppermute x1, starting transfers between devices, shards(): g0 = lax.ppermute(ehi, 'grp', [(i, i + 1) for i in range(n_grp - 2)])  25.1 us
    pallas_call x1, Pallas kernels, fused_step(): pl.pallas_call(functools.partial(step_kernel, nf, rows, lanes), out_shape...  21.3 us
    ppermute x3, waiting for transfers between devices, shards(): lax.ppermute(planes, 'blk', partner)  9.55 us
    ppermute x1, starting transfers between devices, shards(): lax.ppermute(last_row, 'grp', [(i, i + 1) for i in range(n_grp - 2)])  4.54 us
    pallas_call x1, Pallas kernels, fix_edges(): pl.pallas_call(functools.partial(fix_kernel, low_w, side_w), out_shape=ja...  4.34 us
    ppermute x1, starting transfers between devices, shards(): gr = lax.ppermute(clo, 'blk', [((i + 1) % n_blk, i) for i in range(n_blk)])  4.15 us
    ppermute x1, starting transfers between devices, shards(): lax.ppermute(fields[:, :, 0], 'blk', [((i + 1) % n_blk, i) for i in range...  3.93 us
    unnamed x30, local copies, waits for them, and re-layouts  2.51 us
  transfers between devices with their start and end apart: 12, of which 3 were waited for; matrix products, arithmetic and copies ran while one was open for 8% of the time, Pallas kernels for 0%

profile of v9, /device:TPU:1, one launch (start us, length us, event | category | flops | bytes accessed | tf_op | source)
XLA Modules:
  0.0 93.6 jit_solution(1939288770388005109)
XLA Ops:
  0.0 0.0 copy-start.8
  0.0 0.0 copy-start.9
  0.0 0.0 copy-start.10
  0.0 0.0 copy-start.11
  0.0 1.1 %fusion.8 = (f32[14,1,512]{2,1,0:T(1,128)S(1)}, f32[14,1,512]{2,1,0:T(1,128)S(1)}) fusion(f32[14,128,512]{2,1,0:T(8,128)} %f_hbm.1), kind=kLoop, calls=%fused_computation.24 | loop fusion | bytes 114688 | tf_op jit(solution)/shard_map/slice | solution.py:304
  1.2 4.5 %collective-permute-start.3 = (f32[14,512]{1,0:T(8,128)S(1)}, f32[14,512]{1,0:T(8,128)S(1)}, u32[]{:S(2)}, u32[]{:S(2)}) collective-permute-start(f32[14,512]{1,0:T(8,128)S(1)} %bitcast.18), channel_id=1, source_target_pairs={{0,8},{8,16},{1,9},{9,17},{2,10},{10,18},{3,11},{11,19},{4,12},{12... | collective-permute-start | bytes 86024 | tf_op jit(solution)/shard_map/ppermute | solution.py:316
  5.7 0.7 slice_bitcast_fusion
  6.5 1.3 %collective-permute-start = (f32[1,15,512]{2,1,0:T(8,128)S(1)}, f32[1,15,512]{2,1,0:T(8,128)S(1)}, u32[]{:S(2)}, u32[]{:S(2)}) collective-permute-start(f32[1,15,512]{2,1,0:T(8,128)S(1)} %maximum_bitcast_fusion.1), channel_id=1, source_target_pairs={{0,1},{1,0},{2,3},{3,2},{4,5},{5,4},{6,7},{7,6},{8,9},{9,8},{10,11... | collective-permute-start | bytes 92168 | tf_op jit(solution)/shard_map/ppermute | solution.py:310
  7.7 1.9 %collective-permute-start.4 = (f32[14,512]{1,0:T(8,128)S(1)}, f32[14,512]{1,0:T(8,128)S(1)}, u32[]{:S(2)}, u32[]{:S(2)}) collective-permute-start(f32[14,512]{1,0:T(8,128)S(1)} %bitcast.20), channel_id=1, source_target_pairs={{8,0},{16,8},{9,1},{17,9},{10,2},{18,10},{11,3},{19,11},{12,4},{20... | collective-permute-start | bytes 86024 | tf_op jit(solution)/shard_map/ppermute | solution.py:317
  9.7 1.8 %fusion.7 = (f32[14,128,1]{2,1,0:T(8,128)S(1)}, f32[14,128,1]{2,1,0:T(8,128)S(1)}) fusion(f32[14,128,512]{2,1,0:T(8,128)} %f_hbm.1), kind=kLoop, calls=%fused_computation.23 | loop fusion | bytes 28672 | tf_op jit(solution)/shard_map/slice | solution.py:319
  11.4 0.3 copy.21
  11.8 0.3 collective-permute-start.5
  12.1 0.3 copy.22
  12.4 3.9 %collective-permute-start.6 = (f32[14,128]{1,0:T(8,128)S(1)}, f32[14,128]{1,0:T(8,128)S(1)}, u32[]{:S(2)}, u32[]{:S(2)}) collective-permute-start(f32[14,128]{1,0:T(8,128)S(1)} %bitcast.22), channel_id=1, source_target_pairs={{1,0},{2,1},{3,2},{4,3},{5,4},{6,5},{7,6},{0,7},{9,8},{10,9},{11,1... | collective-permute-start | bytes 21512 | tf_op jit(solution)/shard_map/ppermute | solution.py:319
  16.3 0.0 collective-permute-done
  16.3 0.1 collective-permute-start.1
  16.4 0.0 copy-done.8
  16.4 0.0 copy-done.9
  16.4 0.6 pad_maximum_fusion.2.w_s
  17.0 2.6 %collective-permute-done.1 = f32[2,15,512]{2,1,0:T(8,128)S(1)} collective-permute-done((f32[2,15,512]{2,1,0:T(8,128)S(1)}, f32[2,15,512]{2,1,0:T(8,128)S(1)}, u32[]{:S(2)}, u32[]{:S(2)}) %collective-permute-start.1) | collective-permute-done | bytes 61472 | tf_op jit(solution)/shard_map/ppermute | solution.py:310
  19.6 0.7 collective-permute-start.2
  20.3 0.6 add_convert_fusion.flag_s
  20.9 0.0 copy-done.10
  20.9 0.0 copy-done.11
  20.9 0.6 fusion.2.ids_s
  21.5 7.0 %collective-permute-done.2 = f32[4,15,512]{2,1,0:T(8,128)S(1)} collective-permute-done((f32[4,15,512]{2,1,0:T(8,128)S(1)}, f32[4,15,512]{2,1,0:T(8,128)S(1)}, u32[]{:S(2)}, u32[]{:S(2)}) %collective-permute-start.2) | collective-permute-done | bytes 122912 | tf_op jit(solution)/shard_map/ppermute | solution.py:310
  28.5 2.0 %copy.15 = f32[8,512,15]{2,1,0:T(8,128)} copy(f32[8,512,15]{1,2,0:T(8,128)S(1)} %maximum_bitcast_fusion) | data formatting | bytes 491520 | tf_op jit(solution)/shard_map/transpose | solution.py:312
  30.5 0.0 collective-permute-done.5.refs_2_
  30.5 0.0 copy-start.4
  30.5 0.0 collective-permute-done.6.refs_3_
  30.5 0.0 copy-start.5
  30.5 0.0 collective-permute-done.3.refs_0_
  30.5 0.0 copy-start
  30.5 0.0 collective-permute-done.4.refs_1_
  30.5 0.0 copy-start.1
  30.5 0.5 copy-done.4
  31.1 0.0 copy-done.5
  31.1 0.0 copy-done
  31.1 0.0 copy-done.1
  31.1 2.4 %shard_map.82 = (f32[15,512]{1,0:T(8,128)}, f32[14,512]{1,0:T(8,128)}, f32[14,512]{1,0:T(8,128)}, f32[14,128]{1,0:T(8,128)}, f32[14,128]{1,0:T(8,128)}) custom-call(f32[2]{0:T(128)} %add_convert_fusion.flag_s, s32[8,512]{1,0:T(8,128)} %fusion.2.ids_s, f32[8,512]{1,0:T(8,128)} %pad_maximum_fusion.2.w_s, f32[512,8,15]{2,1,0:T(8,128)} %bitcast.17, ...), custom_call_target="tpu_custom_call" | custom-call | tf_op jit(solution)/shard_map/pallas_call | solution.py:230
  33.5 0.7 collective-permute-start.7
  34.2 0.0 collective-permute-done.7.sw_ref
  34.2 0.0 copy-start.12
  34.2 0.6 copy-done.12
  34.8 21.3 %shard_map.83 = (f32[14,128,512]{2,1,0:T(8,128)}, f32[14,512]{1,0:T(8,128)}, f32[14,512]{1,0:T(8,128)}, f32[14,128]{1,0:T(8,128)}, f32[14,128]{1,0:T(8,128)}) custom-call(f32[14,14]{1,0:T(8,128)} %mix_s.1, f32[14]{0:T(128)} %act_s.1, f32[2]{0:T(128)} %add_convert_fusion.flag_s, f32[14,128,512]{2,1,0:T(8,128)} %f_hbm.1, f32[128,512]{1,0:T(8,128)} %rate_ref.1, ...), custom_call_target="tpu_custom_call" | custom-call | flops 95420416 | bytes 7602176 | tf_op jit(solution)/shard_map/pallas_call | solution.py:169
  56.2 25.1 %collective-permute-start.8 = (f32[14,512]{1,0:T(8,128)}, f32[14,512]{1,0:T(8,128)S(1)}, u32[]{:S(2)}, u32[]{:S(2)}) collective-permute-start(f32[14,512]{1,0:T(8,128)} %get-tuple-element.21), channel_id=1, source_target_pairs={{0,8},{8,16},{1,9},{9,17},{2,10},{10,18},{3,11},{11,19},{4,12},{12... | collective-permute-start | bytes 86024 | tf_op jit(solution)/shard_map/ppermute | solution.py:328
  81.3 1.9 %collective-permute-start.9 = (f32[14,512]{1,0:T(8,128)}, f32[14,512]{1,0:T(8,128)S(1)}, u32[]{:S(2)}, u32[]{:S(2)}) collective-permute-start(f32[14,512]{1,0:T(8,128)} %get-tuple-element.22), channel_id=1, source_target_pairs={{8,0},{16,8},{9,1},{17,9},{10,2},{18,10},{11,3},{19,11},{12,4},{20... | collective-permute-start | bytes 86024 | tf_op jit(solution)/shard_map/ppermute | solution.py:329
  83.2 0.1 collective-permute-start.10
  83.3 4.2 %collective-permute-start.11 = (f32[14,128]{1,0:T(8,128)}, f32[14,128]{1,0:T(8,128)S(1)}, u32[]{:S(2)}, u32[]{:S(2)}) collective-permute-start(f32[14,128]{1,0:T(8,128)} %get-tuple-element.24), channel_id=1, source_target_pairs={{1,0},{2,1},{3,2},{4,3},{5,4},{6,5},{7,6},{0,7},{9,8},{10,9},{11,1... | collective-permute-start | bytes 21512 | tf_op jit(solution)/shard_map/ppermute | solution.py:331
  87.4 1.2 %collective-permute-done.10.gl_ref = f32[14,128]{1,0:T(8,128)S(1)} collective-permute-done((f32[14,128]{1,0:T(8,128)}, f32[14,128]{1,0:T(8,128)S(1)}, u32[]{:S(2)}, u32[]{:S(2)}) %collective-permute-start.10) | collective-permute-done | bytes 7200 | tf_op jit(solution)/shard_map/ppermute | solution.py:330
  88.6 0.0 copy-start.6
  88.7 0.0 collective-permute-done.11.gr_ref
  88.7 0.0 copy-start.7
  88.7 0.0 collective-permute-done.8.g0_ref
  88.7 0.0 copy-start.2
  88.7 0.0 collective-permute-done.9.g1_ref
  88.7 0.0 copy-start.3
  88.7 0.6 copy-done.6
  89.2 0.0 copy-done.7
  89.2 0.0 copy-done.2
  89.3 0.0 copy-done.3
  89.3 4.3 %shard_map.84 = f32[14,128,512]{2,1,0:T(8,128)} custom-call(f32[14,128,512]{2,1,0:T(8,128)} %get-tuple-element.20.out_in, f32[14,512]{1,0:T(8,128)} %copy-done.2, f32[14,512]{1,0:T(8,128)} %copy-done.3, f32[14,128]{1,0:T(8,128)} %copy-done.6, f32[14,128]{1,0:T(8,128)} %copy-done.7), custom_call_target="tpu_custom_call", output_to_operand_aliasing={{}: (0, {})} | custom-call | tf_op jit(solution)/shard_map/pallas_call | solution.py:277
  (6 shorter events, 0.1 us)
Async XLA Ops:
  0.0 16.4 %copy-start.8 = (f32[4,512]{1,0:T(4,128)S(1)}, f32[4,512]{1,0:T(4,128)}, u32[]{:S(2)}) copy-start(f32[4,512]{1,0:T(4,128)} %param.15) | copy-start | bytes 24580
  0.0 16.4 %copy-start.9 = (f32[4,512]{1,0:T(4,128)S(1)}, f32[4,512]{1,0:T(4,128)}, u32[]{:S(2)}) copy-start(f32[4,512]{1,0:T(4,128)} %param.13) | copy-start | bytes 24580
  0.0 20.9 %copy-start.10 = (s32[4,512]{1,0:T(4,128)S(1)}, s32[4,512]{1,0:T(4,128)}, u32[]{:S(2)}) copy-start(s32[4,512]{1,0:T(4,128)} %param.14) | copy-start | bytes 24580
  0.0 20.9 %copy-start.11 = (s32[4,512]{1,0:T(4,128)S(1)}, s32[4,512]{1,0:T(4,128)}, u32[]{:S(2)}) copy-start(s32[4,512]{1,0:T(4,128)} %param.12) | copy-start | bytes 24580
  1.2 29.3 %collective-permute-start.3 = (f32[14,512]{1,0:T(8,128)S(1)}, f32[14,512]{1,0:T(8,128)S(1)}, u32[]{:S(2)}, u32[]{:S(2)}) collective-permute-start(f32[14,512]{1,0:T(8,128)S(1)} %bitcast.18), channel_id=1, source_target_pairs={{0,8},{8,16},{1,9},{9,17},{2,10},{10,18},{3,11},{11,19},{4,12},{12... | collective-permute-start | bytes 86024 | tf_op jit(solution)/shard_map/ppermute | solution.py:316
  6.5 9.9 %collective-permute-start = (f32[1,15,512]{2,1,0:T(8,128)S(1)}, f32[1,15,512]{2,1,0:T(8,128)S(1)}, u32[]{:S(2)}, u32[]{:S(2)}) collective-permute-start(f32[1,15,512]{2,1,0:T(8,128)S(1)} %maximum_bitcast_fusion.1), channel_id=1, source_target_pairs={{0,1},{1,0},{2,3},{3,2},{4,5},{5,4},{6,7},{7,6},{8,9},{9,8},{10,11... | collective-permute-start | bytes 92168 | tf_op jit(solution)/shard_map/ppermute | solution.py:310
  7.7 22.8 %collective-permute-start.4 = (f32[14,512]{1,0:T(8,128)S(1)}, f32[14,512]{1,0:T(8,128)S(1)}, u32[]{:S(2)}, u32[]{:S(2)}) collective-permute-start(f32[14,512]{1,0:T(8,128)S(1)} %bitcast.20), channel_id=1, source_target_pairs={{8,0},{16,8},{9,1},{17,9},{10,2},{18,10},{11,3},{19,11},{12,4},{20... | collective-permute-start | bytes 86024 | tf_op jit(solution)/shard_map/ppermute | solution.py:317
  11.8 18.7 %collective-permute-start.5 = (f32[14,128]{1,0:T(8,128)S(1)}, f32[14,128]{1,0:T(8,128)S(1)}, u32[]{:S(2)}, u32[]{:S(2)}) collective-permute-start(f32[14,128]{1,0:T(8,128)S(1)} %bitcast.21), channel_id=1, source_target_pairs={{0,1},{1,2},{2,3},{3,4},{4,5},{5,6},{6,7},{7,0},{8,9},{9,10},{10,1... | collective-permute-start | bytes 21512 | tf_op jit(solution)/shard_map/ppermute | solution.py:318
  12.4 18.1 %collective-permute-start.6 = (f32[14,128]{1,0:T(8,128)S(1)}, f32[14,128]{1,0:T(8,128)S(1)}, u32[]{:S(2)}, u32[]{:S(2)}) collective-permute-start(f32[14,128]{1,0:T(8,128)S(1)} %bitcast.22), channel_id=1, source_target_pairs={{1,0},{2,1},{3,2},{4,3},{5,4},{6,5},{7,6},{0,7},{9,8},{10,9},{11,1... | collective-permute-start | bytes 21512 | tf_op jit(solution)/shard_map/ppermute | solution.py:319
  16.3 3.3 %collective-permute-start.1 = (f32[2,15,512]{2,1,0:T(8,128)S(1)}, f32[2,15,512]{2,1,0:T(8,128)S(1)}, u32[]{:S(2)}, u32[]{:S(2)}) collective-permute-start(f32[2,15,512]{2,1,0:T(8,128)S(1)} %pad_maximum_fusion.1), channel_id=1, source_target_pairs={{0,2},{1,3},{2,0},{3,1},{4,6},{5,7},{6,4},{7,5},{8,10},{9,11},{10,... | collective-permute-start | bytes 184328 | tf_op jit(solution)/shard_map/ppermute | solution.py:310
  19.6 8.9 %collective-permute-start.2 = (f32[4,15,512]{2,1,0:T(8,128)S(1)}, f32[4,15,512]{2,1,0:T(8,128)S(1)}, u32[]{:S(2)}, u32[]{:S(2)}) collective-permute-start(f32[4,15,512]{2,1,0:T(8,128)S(1)} %pad_maximum_fusion), channel_id=1, source_target_pairs={{0,4},{1,5},{2,6},{3,7},{4,0},{5,1},{6,2},{7,3},{8,12},{9,13},{10,... | collective-permute-start | bytes 368648 | tf_op jit(solution)/shard_map/ppermute | solution.py:310
  30.5 0.6 copy-start.4
  30.5 0.6 copy-start.5
  30.5 0.6 copy-start
  30.5 0.6 copy-start.1
  33.5 0.7 collective-permute-start.7
  34.2 0.6 copy-start.12
  56.2 32.5 %collective-permute-start.8 = (f32[14,512]{1,0:T(8,128)}, f32[14,512]{1,0:T(8,128)S(1)}, u32[]{:S(2)}, u32[]{:S(2)}) collective-permute-start(f32[14,512]{1,0:T(8,128)} %get-tuple-element.21), channel_id=1, source_target_pairs={{0,8},{8,16},{1,9},{9,17},{2,10},{10,18},{3,11},{11,19},{4,12},{12... | collective-permute-start | bytes 86024 | tf_op jit(solution)/shard_map/ppermute | solution.py:328
  81.3 7.4 %collective-permute-start.9 = (f32[14,512]{1,0:T(8,128)}, f32[14,512]{1,0:T(8,128)S(1)}, u32[]{:S(2)}, u32[]{:S(2)}) collective-permute-start(f32[14,512]{1,0:T(8,128)} %get-tuple-element.22), channel_id=1, source_target_pairs={{8,0},{16,8},{9,1},{17,9},{10,2},{18,10},{11,3},{19,11},{12,4},{20... | collective-permute-start | bytes 86024 | tf_op jit(solution)/shard_map/ppermute | solution.py:329
  83.2 5.5 %collective-permute-start.10 = (f32[14,128]{1,0:T(8,128)}, f32[14,128]{1,0:T(8,128)S(1)}, u32[]{:S(2)}, u32[]{:S(2)}) collective-permute-start(f32[14,128]{1,0:T(8,128)} %get-tuple-element.23), channel_id=1, source_target_pairs={{0,1},{1,2},{2,3},{3,4},{4,5},{5,6},{6,7},{7,0},{8,9},{9,10},{10,1... | collective-permute-start | bytes 21512 | tf_op jit(solution)/shard_map/ppermute | solution.py:330
  83.3 5.4 %collective-permute-start.11 = (f32[14,128]{1,0:T(8,128)}, f32[14,128]{1,0:T(8,128)S(1)}, u32[]{:S(2)}, u32[]{:S(2)}) collective-permute-start(f32[14,128]{1,0:T(8,128)} %get-tuple-element.24), channel_id=1, source_target_pairs={{1,0},{2,1},{3,2},{4,3},{5,4},{6,5},{7,6},{0,7},{9,8},{10,9},{11,1... | collective-permute-start | bytes 21512 | tf_op jit(solution)/shard_map/ppermute | solution.py:331
  88.6 0.6 copy-start.6
  88.7 0.6 copy-start.7
  88.7 0.6 copy-start.2
  88.7 0.6 copy-start.3

commit v10 on v6

--- a/solution.py
+++ b/solution.py
@@ -295,14 +295,20 @@
     first_row = fields[:, 0, :]
     payload = jnp.concatenate([last_row, first_row[4:5]], axis=0)
     planes = payload[None]
-    span = 1
-    while span < n_blk:
+    spans = []
+    span = n_blk // 2
+    while span >= 1:
+        spans.append(span)
         partner = [(i, i ^ span) for i in range(n_blk)]
         planes = jnp.concatenate([planes, lax.ppermute(planes, "blk", partner)], axis=0)
-        span *= 2
+        span //= 2
     table = jnp.transpose(planes, (0, 2, 1)).reshape(n_blk * lanes, nf + 1)
     ids = jnp.concatenate([inlet_ids, outlet_ids], axis=0)
-    ids = (jnp.bitwise_xor(ids // lanes, b) * lanes) + ids % lanes
+    m = jnp.bitwise_xor(ids // lanes, b)
+    slot = jnp.zeros_like(m)
+    for r, span in enumerate(spans):
+        slot = slot + ((m // span) % 2) * (1 << r)
+    ids = slot * lanes + ids % lanes
     wts = jnp.concatenate([inlet_weights, outlet_weights], axis=0)
     halo_lo = lax.ppermute(last_row, "grp", [(i, i + 1) for i in range(n_grp - 2)])
     halo_hi = lax.ppermute(first_row, "grp", [(i + 1, i) for i in range(n_grp - 2)])

time: 80.7 us -> 79.6 us (0.986)
  waiting for transfers between devices: 10.8 us -> 7.51 us
  starting transfers between devices: 30.7 us -> 32.9 us
    ppermute x3, waiting for transfers between devices: 9.55 us -> 6.25 us  [shards(): lax.ppermute(planes, 'blk', partner)]
    ppermute x1, starting transfers between devices: 11.2 us -> 12.9 us  [shards(): g0 = lax.ppermute(ehi, 'grp', [(i, i + 1) for i in range(n_grp - 2)])]
    ppermute x1, starting transfers between devices: 3.93 us -> 2.97 us  [shards(): lax.ppermute(fields[:, :, 0], 'blk', [((i + 1) % n_blk, i) for i in range...]
    ppermute x1, starting transfers between devices: 0.28 us -> 1.23 us  [shards(): lax.ppermute(fields[:, :, lanes - 1], 'blk', [(i, (i + 1) % n_blk) for i...]
where the time goes in v10:
time: 79.6 us; the launch traced here: 78.7 us
  starting transfers between devices  32.9 us (41%)
  Pallas kernels  28.1 us (35%)
  local copies, waits for them, and re-layouts  8.14 us (10%)
  waiting for transfers between devices  7.51 us (9%)
  other arithmetic  1.91 us (2%)
    pallas_call x1, Pallas kernels, fused_step(): pl.pallas_call(functools.partial(step_kernel, nf, rows, lanes), out_shape...  21.3 us
    ppermute x1, starting transfers between devices, shards(): g0 = lax.ppermute(ehi, 'grp', [(i, i + 1) for i in range(n_grp - 2)])  12.9 us
    ppermute x3, waiting for transfers between devices, shards(): lax.ppermute(planes, 'blk', partner)  6.25 us
    ppermute x1, starting transfers between devices, shards(): lax.ppermute(last_row, 'grp', [(i, i + 1) for i in range(n_grp - 2)])  4.54 us
    pallas_call x1, Pallas kernels, fix_edges(): pl.pallas_call(functools.partial(fix_kernel, low_w, side_w), out_shape=ja...  4.34 us
    ppermute x1, starting transfers between devices, shards(): gr = lax.ppermute(clo, 'blk', [((i + 1) % n_blk, i) for i in range(n_blk)])  4.15 us
    ppermute x1, starting transfers between devices, shards(): lax.ppermute(fields[:, :, 0], 'blk', [((i + 1) % n_blk, i) for i in range...  2.97 us
    ppermute x3, starting transfers between devices, shards(): lax.ppermute(planes, 'blk', partner)  2.52 us
  transfers between devices with their start and end apart: 12, of which 3 were waited for; matrix products, arithmetic and copies ran while one was open for 9% of the time, Pallas kernels for 0%

profile of v10, /device:TPU:1, one launch (start us, length us, event | category | flops | bytes accessed | tf_op | source)
XLA Modules:
  0.0 78.7 jit_solution(10628748151311765758)
XLA Ops:
  0.0 0.0 copy-start.8
  0.0 0.0 copy-start.9
  0.0 0.0 copy-start.10
  0.0 0.0 copy-start.11
  0.0 1.1 %fusion.13 = (f32[14,1,512]{2,1,0:T(1,128)S(1)}, f32[14,1,512]{2,1,0:T(1,128)S(1)}) fusion(f32[14,128,512]{2,1,0:T(8,128)} %f_hbm.1), kind=kLoop, calls=%fused_computation.44 | loop fusion | bytes 114688 | tf_op jit(solution)/shard_map/slice | solution.py:295
  1.2 4.5 %collective-permute-start.3 = (f32[14,512]{1,0:T(8,128)S(1)}, f32[14,512]{1,0:T(8,128)S(1)}, u32[]{:S(2)}, u32[]{:S(2)}) collective-permute-start(f32[14,512]{1,0:T(8,128)S(1)} %bitcast.18), channel_id=1, source_target_pairs={{0,8},{8,16},{1,9},{9,17},{2,10},{10,18},{3,11},{11,19},{4,12},{12... | collective-permute-start | bytes 86024 | tf_op jit(solution)/shard_map/ppermute | solution.py:313
  5.7 0.7 slice_bitcast_fusion
  6.5 2.4 %collective-permute-start = (f32[1,15,512]{2,1,0:T(8,128)S(1)}, f32[1,15,512]{2,1,0:T(8,128)S(1)}, u32[]{:S(2)}, u32[]{:S(2)}) collective-permute-start(f32[1,15,512]{2,1,0:T(8,128)S(1)} %maximum_bitcast_fusion.1), channel_id=1, source_target_pairs={{0,4},{1,5},{2,6},{3,7},{4,0},{5,1},{6,2},{7,3},{8,12},{9,13},{10,... | collective-permute-start | bytes 92168 | tf_op jit(solution)/shard_map/ppermute | solution.py:303
  8.8 1.9 %collective-permute-start.4 = (f32[14,512]{1,0:T(8,128)S(1)}, f32[14,512]{1,0:T(8,128)S(1)}, u32[]{:S(2)}, u32[]{:S(2)}) collective-permute-start(f32[14,512]{1,0:T(8,128)S(1)} %bitcast.20), channel_id=1, source_target_pairs={{8,0},{16,8},{9,1},{17,9},{10,2},{18,10},{11,3},{19,11},{12,4},{20... | collective-permute-start | bytes 86024 | tf_op jit(solution)/shard_map/ppermute | solution.py:314
  10.7 1.8 %fusion.12 = (f32[14,128,1]{2,1,0:T(8,128)S(1)}, f32[14,128,1]{2,1,0:T(8,128)S(1)}) fusion(f32[14,128,512]{2,1,0:T(8,128)} %f_hbm.1), kind=kLoop, calls=%fused_computation.43 | loop fusion | bytes 28672 | tf_op jit(solution)/shard_map/slice | solution.py:316
  12.5 0.3 copy.24
  12.9 1.2 %collective-permute-start.5 = (f32[14,128]{1,0:T(8,128)S(1)}, f32[14,128]{1,0:T(8,128)S(1)}, u32[]{:S(2)}, u32[]{:S(2)}) collective-permute-start(f32[14,128]{1,0:T(8,128)S(1)} %bitcast.21), channel_id=1, source_target_pairs={{0,1},{1,2},{2,3},{3,4},{4,5},{5,6},{6,7},{7,0},{8,9},{9,10},{10,1... | collective-permute-start | bytes 21512 | tf_op jit(solution)/shard_map/ppermute | solution.py:315
  14.1 0.3 copy.25
  14.4 3.0 %collective-permute-start.6 = (f32[14,128]{1,0:T(8,128)S(1)}, f32[14,128]{1,0:T(8,128)S(1)}, u32[]{:S(2)}, u32[]{:S(2)}) collective-permute-start(f32[14,128]{1,0:T(8,128)S(1)} %bitcast.22), channel_id=1, source_target_pairs={{1,0},{2,1},{3,2},{4,3},{5,4},{6,5},{7,6},{0,7},{9,8},{10,9},{11,1... | collective-permute-start | bytes 21512 | tf_op jit(solution)/shard_map/ppermute | solution.py:316
  17.4 0.0 collective-permute-done
  17.4 0.1 collective-permute-start.1
  17.5 0.0 copy-done.8
  17.5 0.0 copy-done.9
  17.5 0.6 pad_maximum_fusion.2.w_s
  18.1 2.6 %collective-permute-done.1 = f32[2,15,512]{2,1,0:T(8,128)S(1)} collective-permute-done((f32[2,15,512]{2,1,0:T(8,128)S(1)}, f32[2,15,512]{2,1,0:T(8,128)S(1)}, u32[]{:S(2)}, u32[]{:S(2)}) %collective-permute-start.1) | collective-permute-done | bytes 61472 | tf_op jit(solution)/shard_map/ppermute | solution.py:303
  20.7 0.1 collective-permute-start.2
  20.8 0.6 add_convert_fusion.flag_s
  21.4 0.0 copy-done.10
  21.4 0.0 copy-done.11
  21.4 0.7 fusion.6.ids_s
  22.1 3.7 %collective-permute-done.2 = f32[4,15,512]{2,1,0:T(8,128)S(1)} collective-permute-done((f32[4,15,512]{2,1,0:T(8,128)S(1)}, f32[4,15,512]{2,1,0:T(8,128)S(1)}, u32[]{:S(2)}, u32[]{:S(2)}) %collective-permute-start.2) | collective-permute-done | bytes 122912 | tf_op jit(solution)/shard_map/ppermute | solution.py:303
  25.8 2.0 %copy.20 = f32[8,512,15]{2,1,0:T(8,128)} copy(f32[8,512,15]{1,2,0:T(8,128)S(1)} %maximum_bitcast_fusion) | data formatting | bytes 491520 | tf_op jit(solution)/shard_map/reshape | solution.py:305
  27.7 0.0 collective-permute-done.5.refs_2_
  27.7 0.0 copy-start.4
  27.7 0.0 collective-permute-done.6.refs_3_
  27.7 0.0 copy-start.5
  27.7 0.0 collective-permute-done.3.refs_0_
  27.8 0.0 copy-start
  27.8 0.0 collective-permute-done.4.refs_1_
  27.8 0.0 copy-start.1
  27.8 0.5 copy-done.4
  28.3 0.0 copy-done.5
  28.3 0.0 copy-done
  28.4 0.0 copy-done.1
  28.4 2.4 %shard_map.82 = (f32[15,512]{1,0:T(8,128)}, f32[14,512]{1,0:T(8,128)}, f32[14,512]{1,0:T(8,128)}, f32[14,128]{1,0:T(8,128)}, f32[14,128]{1,0:T(8,128)}) custom-call(f32[2]{0:T(128)} %add_convert_fusion.flag_s, s32[8,512]{1,0:T(8,128)} %fusion.6.ids_s, f32[8,512]{1,0:T(8,128)} %pad_maximum_fusion.2.w_s, f32[4096,15]{1,0:T(8,128)} %bitcast.17, ...), custom_call_target="tpu_custom_call" | custom-call | tf_op jit(solution)/shard_map/pallas_call | solution.py:221
  30.8 0.7 collective-permute-start.7
  31.4 0.0 collective-permute-done.7.sw_ref
  31.5 0.0 copy-start.12
  31.5 0.6 copy-done.12
  32.1 21.3 %shard_map.83 = (f32[14,128,512]{2,1,0:T(8,128)}, f32[14,512]{1,0:T(8,128)}, f32[14,512]{1,0:T(8,128)}, f32[14,128]{1,0:T(8,128)}, f32[14,128]{1,0:T(8,128)}) custom-call(f32[14,14]{1,0:T(8,128)} %mix_s.1, f32[14]{0:T(128)} %act_s.1, f32[2]{0:T(128)} %add_convert_fusion.flag_s, f32[14,128,512]{2,1,0:T(8,128)} %f_hbm.1, f32[128,512]{1,0:T(8,128)} %rate_ref.1, ...), custom_call_target="tpu_custom_call" | custom-call | flops 95420416 | bytes 7602176 | tf_op jit(solution)/shard_map/pallas_call | solution.py:169
  53.4 12.9 %collective-permute-start.8 = (f32[14,512]{1,0:T(8,128)}, f32[14,512]{1,0:T(8,128)S(1)}, u32[]{:S(2)}, u32[]{:S(2)}) collective-permute-start(f32[14,512]{1,0:T(8,128)} %get-tuple-element.21), channel_id=1, source_target_pairs={{0,8},{8,16},{1,9},{9,17},{2,10},{10,18},{3,11},{11,19},{4,12},{12... | collective-permute-start | bytes 86024 | tf_op jit(solution)/shard_map/ppermute | solution.py:325
  66.3 1.9 %collective-permute-start.9 = (f32[14,512]{1,0:T(8,128)}, f32[14,512]{1,0:T(8,128)S(1)}, u32[]{:S(2)}, u32[]{:S(2)}) collective-permute-start(f32[14,512]{1,0:T(8,128)} %get-tuple-element.22), channel_id=1, source_target_pairs={{8,0},{16,8},{9,1},{17,9},{10,2},{18,10},{11,3},{19,11},{12,4},{20... | collective-permute-start | bytes 86024 | tf_op jit(solution)/shard_map/ppermute | solution.py:326
  68.3 0.1 collective-permute-start.10
  68.3 4.2 %collective-permute-start.11 = (f32[14,128]{1,0:T(8,128)}, f32[14,128]{1,0:T(8,128)S(1)}, u32[]{:S(2)}, u32[]{:S(2)}) collective-permute-start(f32[14,128]{1,0:T(8,128)} %get-tuple-element.24), channel_id=1, source_target_pairs={{1,0},{2,1},{3,2},{4,3},{5,4},{6,5},{7,6},{0,7},{9,8},{10,9},{11,1... | collective-permute-start | bytes 21512 | tf_op jit(solution)/shard_map/ppermute | solution.py:328
  72.5 1.2 %collective-permute-done.10.gl_ref = f32[14,128]{1,0:T(8,128)S(1)} collective-permute-done((f32[14,128]{1,0:T(8,128)}, f32[14,128]{1,0:T(8,128)S(1)}, u32[]{:S(2)}, u32[]{:S(2)}) %collective-permute-start.10) | collective-permute-done | bytes 7200 | tf_op jit(solution)/shard_map/ppermute | solution.py:327
  73.7 0.0 copy-start.6
  73.7 0.0 collective-permute-done.11.gr_ref
  73.7 0.0 copy-start.7
  73.7 0.0 collective-permute-done.8.g0_ref
  73.7 0.0 copy-start.2
  73.8 0.0 collective-permute-done.9.g1_ref
  73.8 0.0 copy-start.3
  73.8 0.6 copy-done.6
  74.3 0.0 copy-done.7
  74.3 0.0 copy-done.2
  74.3 0.0 copy-done.3
  74.4 4.3 %shard_map.84 = f32[14,128,512]{2,1,0:T(8,128)} custom-call(f32[14,128,512]{2,1,0:T(8,128)} %get-tuple-element.20.out_in, f32[14,512]{1,0:T(8,128)} %copy-done.2, f32[14,512]{1,0:T(8,128)} %copy-done.3, f32[14,128]{1,0:T(8,128)} %copy-done.6, f32[14,128]{1,0:T(8,128)} %copy-done.7), custom_call_target="tpu_custom_call", output_to_operand_aliasing={{}: (0, {})} | custom-call | tf_op jit(solution)/shard_map/pallas_call | solution.py:268
  (6 shorter events, 0.1 us)
Async XLA Ops:
  0.0 17.5 %copy-start.8 = (f32[4,512]{1,0:T(4,128)S(1)}, f32[4,512]{1,0:T(4,128)}, u32[]{:S(2)}) copy-start(f32[4,512]{1,0:T(4,128)} %param.15) | copy-start | bytes 24580
  0.0 17.5 %copy-start.9 = (f32[4,512]{1,0:T(4,128)S(1)}, f32[4,512]{1,0:T(4,128)}, u32[]{:S(2)}) copy-start(f32[4,512]{1,0:T(4,128)} %param.13) | copy-start | bytes 24580
  0.0 21.4 %copy-start.10 = (s32[4,512]{1,0:T(4,128)S(1)}, s32[4,512]{1,0:T(4,128)}, u32[]{:S(2)}) copy-start(s32[4,512]{1,0:T(4,128)} %param.14) | copy-start | bytes 24580
  0.0 21.4 %copy-start.11 = (s32[4,512]{1,0:T(4,128)S(1)}, s32[4,512]{1,0:T(4,128)}, u32[]{:S(2)}) copy-start(s32[4,512]{1,0:T(4,128)} %param.12) | copy-start | bytes 24580
  1.2 26.6 %collective-permute-start.3 = (f32[14,512]{1,0:T(8,128)S(1)}, f32[14,512]{1,0:T(8,128)S(1)}, u32[]{:S(2)}, u32[]{:S(2)}) collective-permute-start(f32[14,512]{1,0:T(8,128)S(1)} %bitcast.18), channel_id=1, source_target_pairs={{0,8},{8,16},{1,9},{9,17},{2,10},{10,18},{3,11},{11,19},{4,12},{12... | collective-permute-start | bytes 86024 | tf_op jit(solution)/shard_map/ppermute | solution.py:313
  6.5 11.0 %collective-permute-start = (f32[1,15,512]{2,1,0:T(8,128)S(1)}, f32[1,15,512]{2,1,0:T(8,128)S(1)}, u32[]{:S(2)}, u32[]{:S(2)}) collective-permute-start(f32[1,15,512]{2,1,0:T(8,128)S(1)} %maximum_bitcast_fusion.1), channel_id=1, source_target_pairs={{0,4},{1,5},{2,6},{3,7},{4,0},{5,1},{6,2},{7,3},{8,12},{9,13},{10,... | collective-permute-start | bytes 92168 | tf_op jit(solution)/shard_map/ppermute | solution.py:303
  8.8 18.9 %collective-permute-start.4 = (f32[14,512]{1,0:T(8,128)S(1)}, f32[14,512]{1,0:T(8,128)S(1)}, u32[]{:S(2)}, u32[]{:S(2)}) collective-permute-start(f32[14,512]{1,0:T(8,128)S(1)} %bitcast.20), channel_id=1, source_target_pairs={{8,0},{16,8},{9,1},{17,9},{10,2},{18,10},{11,3},{19,11},{12,4},{20... | collective-permute-start | bytes 86024 | tf_op jit(solution)/shard_map/ppermute | solution.py:314
  12.9 14.8 %collective-permute-start.5 = (f32[14,128]{1,0:T(8,128)S(1)}, f32[14,128]{1,0:T(8,128)S(1)}, u32[]{:S(2)}, u32[]{:S(2)}) collective-permute-start(f32[14,128]{1,0:T(8,128)S(1)} %bitcast.21), channel_id=1, source_target_pairs={{0,1},{1,2},{2,3},{3,4},{4,5},{5,6},{6,7},{7,0},{8,9},{9,10},{10,1... | collective-permute-start | bytes 21512 | tf_op jit(solution)/shard_map/ppermute | solution.py:315
  14.4 13.3 %collective-permute-start.6 = (f32[14,128]{1,0:T(8,128)S(1)}, f32[14,128]{1,0:T(8,128)S(1)}, u32[]{:S(2)}, u32[]{:S(2)}) collective-permute-start(f32[14,128]{1,0:T(8,128)S(1)} %bitcast.22), channel_id=1, source_target_pairs={{1,0},{2,1},{3,2},{4,3},{5,4},{6,5},{7,6},{0,7},{9,8},{10,9},{11,1... | collective-permute-start | bytes 21512 | tf_op jit(solution)/shard_map/ppermute | solution.py:316
  17.4 3.3 %collective-permute-start.1 = (f32[2,15,512]{2,1,0:T(8,128)S(1)}, f32[2,15,512]{2,1,0:T(8,128)S(1)}, u32[]{:S(2)}, u32[]{:S(2)}) collective-permute-start(f32[2,15,512]{2,1,0:T(8,128)S(1)} %pad_maximum_fusion.1), channel_id=1, source_target_pairs={{0,2},{1,3},{2,0},{3,1},{4,6},{5,7},{6,4},{7,5},{8,10},{9,11},{10,... | collective-permute-start | bytes 184328 | tf_op jit(solution)/shard_map/ppermute | solution.py:303
  20.7 5.0 %collective-permute-start.2 = (f32[4,15,512]{2,1,0:T(8,128)S(1)}, f32[4,15,512]{2,1,0:T(8,128)S(1)}, u32[]{:S(2)}, u32[]{:S(2)}) collective-permute-start(f32[4,15,512]{2,1,0:T(8,128)S(1)} %pad_maximum_fusion), channel_id=1, source_target_pairs={{0,1},{1,0},{2,3},{3,2},{4,5},{5,4},{6,7},{7,6},{8,9},{9,8},{10,11... | collective-permute-start | bytes 368648 | tf_op jit(solution)/shard_map/ppermute | solution.py:303
  27.7 0.6 copy-start.4
  27.7 0.6 copy-start.5
  27.8 0.6 copy-start
  27.8 0.6 copy-start.1
  30.8 0.7 collective-permute-start.7
  31.5 0.6 copy-start.12
  53.4 20.3 %collective-permute-start.8 = (f32[14,512]{1,0:T(8,128)}, f32[14,512]{1,0:T(8,128)S(1)}, u32[]{:S(2)}, u32[]{:S(2)}) collective-permute-start(f32[14,512]{1,0:T(8,128)} %get-tuple-element.21), channel_id=1, source_target_pairs={{0,8},{8,16},{1,9},{9,17},{2,10},{10,18},{3,11},{11,19},{4,12},{12... | collective-permute-start | bytes 86024 | tf_op jit(solution)/shard_map/ppermute | solution.py:325
  66.3 7.4 %collective-permute-start.9 = (f32[14,512]{1,0:T(8,128)}, f32[14,512]{1,0:T(8,128)S(1)}, u32[]{:S(2)}, u32[]{:S(2)}) collective-permute-start(f32[14,512]{1,0:T(8,128)} %get-tuple-element.22), channel_id=1, source_target_pairs={{8,0},{16,8},{9,1},{17,9},{10,2},{18,10},{11,3},{19,11},{12,4},{20... | collective-permute-start | bytes 86024 | tf_op jit(solution)/shard_map/ppermute | solution.py:326
  68.3 5.5 %collective-permute-start.10 = (f32[14,128]{1,0:T(8,128)}, f32[14,128]{1,0:T(8,128)S(1)}, u32[]{:S(2)}, u32[]{:S(2)}) collective-permute-start(f32[14,128]{1,0:T(8,128)} %get-tuple-element.23), channel_id=1, source_target_pairs={{0,1},{1,2},{2,3},{3,4},{4,5},{5,6},{6,7},{7,0},{8,9},{9,10},{10,1... | collective-permute-start | bytes 21512 | tf_op jit(solution)/shard_map/ppermute | solution.py:327
  68.3 5.4 %collective-permute-start.11 = (f32[14,128]{1,0:T(8,128)}, f32[14,128]{1,0:T(8,128)S(1)}, u32[]{:S(2)}, u32[]{:S(2)}) collective-permute-start(f32[14,128]{1,0:T(8,128)} %get-tuple-element.24), channel_id=1, source_target_pairs={{1,0},{2,1},{3,2},{4,3},{5,4},{6,5},{7,6},{0,7},{9,8},{10,9},{11,1... | collective-permute-start | bytes 21512 | tf_op jit(solution)/shard_map/ppermute | solution.py:328
  73.7 0.6 copy-start.6
  73.7 0.6 copy-start.7
  73.7 0.6 copy-start.2
  73.8 0.6 copy-start.3

commit v11 on v10

--- a/solution.py
+++ b/solution.py
@@ -188,44 +188,50 @@
     )(mix, act, flags, fields, rate, halo_lo, halo_hi, swapped, lft, rgt)
 
 
-def interp_kernel(ks, flag_s, ids_s, w_s, table_ref, *refs):
-    n_pass = (len(refs) - 2) // 2
-    ins, o_ref, outs, acc = refs[:n_pass], refs[n_pass], refs[n_pass + 1:-1], refs[-1]
+def interp_kernel(ks, flag_s, ids_s, wt_ref, table_ref, *refs):
+    n_pass = (len(refs) - 3) // 2
+    ins, o_ref, outs, acc, picked = refs[:n_pass], refs[n_pass], refs[n_pass + 1:-2], refs[-2], refs[-1]
     lanes = o_ref.shape[1]
-    half = jnp.where(flag_s[0] > 0.5, 0, ks)
+    width = table_ref.shape[1]
     acc[...] = jnp.zeros(acc.shape, jnp.float32)
-    width = table_ref.shape[1]
 
     @pl.when(flag_s[0] + flag_s[1] > 0.5)
     def _():
-        def body(p, carry):
-            total = None
-            for k in range(ks):
-                q = ids_s[half + k, p]
-                term = w_s[half + k, p] * table_ref[pl.ds(q, 1), :]
-                total = term if total is None else total + term
-            acc[pl.ds(p, 1), 0:width] = total
+        def group(pg, carry):
+            p0 = pl.multiple_of(pg * SUB, SUB)
+            for s in range(SUB):
+                for k in range(ks):
+                    q = ids_s[k, p0 + s]
+                    picked[k, pl.ds(p0 + s, 1), :] = table_ref[pl.ds(q, 1), :]
             return carry
 
-        lax.fori_loop(0, lanes, body, 0, unroll=8)
+        lax.fori_loop(0, lanes // SUB, group, 0)
+        total = wt_ref[:, 0:1] * picked[0]
+        for k in range(1, ks):
+            total = total + wt_ref[:, k:k + 1] * picked[k]
+        acc[:, 0:width] = total
 
     o_ref[...] = jnp.transpose(acc[...])[0:o_ref.shape[0], :]
     for src, dst in zip(ins, outs):
         dst[...] = src[...]
 
 
-def interpolate(flags, ids, weights, table, passed):
-    ks2, lanes = ids.shape
+def interpolate(flags, ids, wt, table, passed):
+    ks, lanes = ids.shape
     smem = pl.BlockSpec(memory_space=pltpu.SMEM)
     vspec = pl.BlockSpec(memory_space=pltpu.VMEM)
+    width = table.shape[1]
     return pl.pallas_call(
-        functools.partial(interp_kernel, ks2 // 2),
-        out_shape=(jax.ShapeDtypeStruct((table.shape[1], lanes), jnp.float32),)
+        functools.partial(interp_kernel, ks),
+        out_shape=(jax.ShapeDtypeStruct((width, lanes), jnp.float32),)
         + tuple(jax.ShapeDtypeStruct(x.shape, x.dtype) for x in passed),
-        in_specs=[smem, smem, smem] + [vspec] * (1 + len(passed)),
+        in_specs=[smem, smem] + [vspec] * (2 + len(passed)),
         out_specs=(vspec,) * (1 + len(passed)),
-        scratch_shapes=[pltpu.VMEM((lanes, LANE), jnp.float32)],
-    )(flags, ids, weights, table, *passed)
+        scratch_shapes=[
+            pltpu.VMEM((lanes, LANE), jnp.float32),
+            pltpu.VMEM((ks, lanes, width), jnp.float32),
+        ],
+    )(flags, ids, wt, table, *passed)
 
 
 def fix_kernel(low_w, side_w, out_in, g0_ref, g1_ref, gl_ref, gr_ref, out_ref, rb, cb, sem):
@@ -303,19 +309,20 @@
         planes = jnp.concatenate([planes, lax.ppermute(planes, "blk", partner)], axis=0)
         span //= 2
     table = jnp.transpose(planes, (0, 2, 1)).reshape(n_blk * lanes, nf + 1)
-    ids = jnp.concatenate([inlet_ids, outlet_ids], axis=0)
+    at_exit = g == exit_grp
+    ids = jnp.where(at_exit, inlet_ids, outlet_ids)
     m = jnp.bitwise_xor(ids // lanes, b)
     slot = jnp.zeros_like(m)
     for r, span in enumerate(spans):
         slot = slot + ((m // span) % 2) * (1 << r)
     ids = slot * lanes + ids % lanes
-    wts = jnp.concatenate([inlet_weights, outlet_weights], axis=0)
+    wt = jnp.transpose(jnp.where(at_exit, inlet_weights, outlet_weights))
     halo_lo = lax.ppermute(last_row, "grp", [(i, i + 1) for i in range(n_grp - 2)])
     halo_hi = lax.ppermute(first_row, "grp", [(i + 1, i) for i in range(n_grp - 2)])
     lft = lax.ppermute(fields[:, :, lanes - 1], "blk", [(i, (i + 1) % n_blk) for i in range(n_blk)])
     rgt = lax.ppermute(fields[:, :, 0], "blk", [((i + 1) % n_blk, i) for i in range(n_blk)])
 
-    swap, halo_lo, halo_hi, lft, rgt = interpolate(flags, ids, wts, table, (halo_lo, halo_hi, lft, rgt))
+    swap, halo_lo, halo_hi, lft, rgt = interpolate(flags, ids, wt, table, (halo_lo, halo_hi, lft, rgt))
     swapped = lax.ppermute(swap, "grp", [(exit_grp, turb_grp), (turb_grp, exit_grp)])
 
     out, elo, ehi, clo, chi = fused_step(

time: 79.6 us -> 78.2 us (0.982)
  starting transfers between devices: 32.9 us -> 31.2 us
  waiting for transfers between devices: 7.51 us -> 6.14 us
  other arithmetic: 1.91 us -> 2.75 us
    ppermute x1, starting transfers between devices: 12.9 us -> 11.1 us  [shards(): g0 = lax.ppermute(ehi, 'grp', [(i, i + 1) for i in range(n_grp - 2)])]
    ppermute x3, waiting for transfers between devices: 6.25 us -> 4.88 us  [shards(): lax.ppermute(planes, 'blk', partner)]
    select_n x0 -> x1, other arithmetic: none -> 0.8 us  [shards(): ids = slot * lanes + ids % lanes]
    unnamed x30 -> x34, local copies, waits for them, and re-layouts: 2.51 us -> 3.06 us
  transfers between devices with their start and end apart: 12 -> 12, of which waited for: 3 -> 3; matrix products, arithmetic and copies ran while one was open for 9% -> 11% of each run, Pallas kernels for 0% -> 0%
where the time goes in v11:
time: 78.2 us; the launch traced here: 77.2 us
  starting transfers between devices  31.2 us (40%)
  Pallas kernels  28 us (36%)
  local copies, waits for them, and re-layouts  8.89 us (11%)
  waiting for transfers between devices  6.14 us (8%)
  other arithmetic  2.75 us (4%)
    pallas_call x1, Pallas kernels, fused_step(): pl.pallas_call(functools.partial(step_kernel, nf, rows, lanes), out_shape...  21.3 us
    ppermute x1, starting transfers between devices, shards(): g0 = lax.ppermute(ehi, 'grp', [(i, i + 1) for i in range(n_grp - 2)])  11.1 us
    ppermute x3, waiting for transfers between devices, shards(): lax.ppermute(planes, 'blk', partner)  4.88 us
    ppermute x1, starting transfers between devices, shards(): lax.ppermute(last_row, 'grp', [(i, i + 1) for i in range(n_grp - 2)])  4.54 us
    pallas_call x1, Pallas kernels, fix_edges(): pl.pallas_call(functools.partial(fix_kernel, low_w, side_w), out_shape=ja...  4.34 us
    ppermute x1, starting transfers between devices, shards(): gr = lax.ppermute(clo, 'blk', [((i + 1) % n_blk, i) for i in range(n_blk)])  4.15 us
    unnamed x34, local copies, waits for them, and re-layouts  3.06 us
    ppermute x1, starting transfers between devices, shards(): lax.ppermute(fields[:, :, 0], 'blk', [((i + 1) % n_blk, i) for i in range...  2.97 us
  transfers between devices with their start and end apart: 12, of which 3 were waited for; matrix products, arithmetic and copies ran while one was open for 11% of the time, Pallas kernels for 0%

profile of v11, /device:TPU:1, one launch (start us, length us, event | category | flops | bytes accessed | tf_op | source)
XLA Modules:
  0.0 77.2 jit_solution(12583830863827471879)
XLA Ops:
  0.0 0.0 copy-start.8
  0.0 1.1 %fusion.13 = (f32[14,1,512]{2,1,0:T(1,128)S(1)}, f32[14,1,512]{2,1,0:T(1,128)S(1)}) fusion(f32[14,128,512]{2,1,0:T(8,128)} %f_hbm.1), kind=kLoop, calls=%fused_computation.44 | loop fusion | bytes 114688 | tf_op jit(solution)/shard_map/slice | solution.py:301
  1.1 4.5 %collective-permute-start.3 = (f32[14,512]{1,0:T(8,128)S(1)}, f32[14,512]{1,0:T(8,128)S(1)}, u32[]{:S(2)}, u32[]{:S(2)}) collective-permute-start(f32[14,512]{1,0:T(8,128)S(1)} %bitcast.20), channel_id=1, source_target_pairs={{0,8},{8,16},{1,9},{9,17},{2,10},{10,18},{3,11},{11,19},{4,12},{12... | collective-permute-start | bytes 86024 | tf_op jit(solution)/shard_map/ppermute | solution.py:320
  5.7 0.7 slice_bitcast_fusion
  6.4 0.0 copy-start.10
  6.4 2.4 %collective-permute-start = (f32[1,15,512]{2,1,0:T(8,128)S(1)}, f32[1,15,512]{2,1,0:T(8,128)S(1)}, u32[]{:S(2)}, u32[]{:S(2)}) collective-permute-start(f32[1,15,512]{2,1,0:T(8,128)S(1)} %maximum_bitcast_fusion.1), channel_id=1, source_target_pairs={{0,4},{1,5},{2,6},{3,7},{4,0},{5,1},{6,2},{7,3},{8,12},{9,13},{10,... | collective-permute-start | bytes 92168 | tf_op jit(solution)/shard_map/ppermute | solution.py:309
  8.8 2.0 %collective-permute-start.4 = (f32[14,512]{1,0:T(8,128)S(1)}, f32[14,512]{1,0:T(8,128)S(1)}, u32[]{:S(2)}, u32[]{:S(2)}) collective-permute-start(f32[14,512]{1,0:T(8,128)S(1)} %bitcast.22), channel_id=1, source_target_pairs={{8,0},{16,8},{9,1},{17,9},{10,2},{18,10},{11,3},{19,11},{12,4},{20... | collective-permute-start | bytes 86024 | tf_op jit(solution)/shard_map/ppermute | solution.py:321
  10.9 1.8 %fusion.12 = (f32[14,128,1]{2,1,0:T(8,128)S(1)}, f32[14,128,1]{2,1,0:T(8,128)S(1)}) fusion(f32[14,128,512]{2,1,0:T(8,128)} %f_hbm.1), kind=kLoop, calls=%fused_computation.43 | loop fusion | bytes 28672 | tf_op jit(solution)/shard_map/slice | solution.py:323
  12.7 0.3 copy.36
  13.0 1.2 %collective-permute-start.5 = (f32[14,128]{1,0:T(8,128)S(1)}, f32[14,128]{1,0:T(8,128)S(1)}, u32[]{:S(2)}, u32[]{:S(2)}) collective-permute-start(f32[14,128]{1,0:T(8,128)S(1)} %bitcast.23), channel_id=1, source_target_pairs={{0,1},{1,2},{2,3},{3,4},{4,5},{5,6},{6,7},{7,0},{8,9},{9,10},{10,1... | collective-permute-start | bytes 21512 | tf_op jit(solution)/shard_map/ppermute | solution.py:322
  14.2 0.3 copy.37
  14.6 3.0 %collective-permute-start.6 = (f32[14,128]{1,0:T(8,128)S(1)}, f32[14,128]{1,0:T(8,128)S(1)}, u32[]{:S(2)}, u32[]{:S(2)}) collective-permute-start(f32[14,128]{1,0:T(8,128)S(1)} %bitcast.24), channel_id=1, source_target_pairs={{1,0},{2,1},{3,2},{4,3},{5,4},{6,5},{7,6},{0,7},{9,8},{10,9},{11,1... | collective-permute-start | bytes 21512 | tf_op jit(solution)/shard_map/ppermute | solution.py:323
  17.5 0.0 copy-done.8
  17.5 0.1 copy.20
  17.7 0.0 copy-done.9
  17.7 0.1 copy.21
  17.9 0.0 collective-permute-done
  17.9 0.1 collective-permute-start.1
  18.0 0.8 %add_select_fusion = (s32[4,512]{0,1:T(8,128)S(1)}, s32[4,512]{0,1:T(8,128)S(1)}) fusion(s32[4,512]{0,1:T(8,128)S(1)} %copy.20, s32[4,512]{0,1:T(8,128)S(1)} %copy.21, pred[]{:T(512)} %eq.12, s32[]{:T(128)S(6)} %axis_index.25), kind=kLoop, calls=%fused_computation | loop fusion | flops 157696 | bytes 32773 | tf_op jit(solution)/shard_map/jit(remainder)/select_n | solution.py:318
  18.8 0.0 copy-done.10
  18.8 0.1 copy.24
  18.9 0.0 copy-done.11
  18.9 0.1 copy.25
  19.1 2.1 %collective-permute-done.1 = f32[2,15,512]{2,1,0:T(8,128)S(1)} collective-permute-done((f32[2,15,512]{2,1,0:T(8,128)S(1)}, f32[2,15,512]{2,1,0:T(8,128)S(1)}, u32[]{:S(2)}, u32[]{:S(2)}) %collective-permute-start.1) | collective-permute-done | bytes 61472 | tf_op jit(solution)/shard_map/ppermute | solution.py:309
  21.2 0.1 collective-permute-start.2
  21.2 0.7 select_bitcast_fusion.wt_ref
  22.0 0.1 copy.23
  22.1 0.1 copy.22
  22.2 0.6 add.37.ids_s
  22.8 0.6 add_convert_fusion.flag_s
  23.4 2.8 %collective-permute-done.2 = f32[4,15,512]{2,1,0:T(8,128)S(1)} collective-permute-done((f32[4,15,512]{2,1,0:T(8,128)S(1)}, f32[4,15,512]{2,1,0:T(8,128)S(1)}, u32[]{:S(2)}, u32[]{:S(2)}) %collective-permute-start.2) | collective-permute-done | bytes 122912 | tf_op jit(solution)/shard_map/ppermute | solution.py:309
  26.2 2.0 %copy.32 = f32[8,512,15]{2,1,0:T(8,128)} copy(f32[8,512,15]{1,2,0:T(8,128)S(1)} %maximum_bitcast_fusion) | data formatting | bytes 491520 | tf_op jit(solution)/shard_map/reshape | solution.py:311
  28.2 0.0 collective-permute-done.5.refs_2_
  28.2 0.0 collective-permute-done.6.refs_3_
  28.2 0.0 copy-start.5
  28.2 0.0 collective-permute-done.3.refs_0_
  28.2 0.0 copy-start
  28.2 0.0 collective-permute-done.4.refs_1_
  28.2 0.0 copy-start.1
  28.2 0.5 copy-done.4
  28.8 0.0 copy-done.5
  28.8 0.0 copy-done
  28.8 0.0 copy-done.1
  28.8 2.3 %shard_map.82 = (f32[15,512]{1,0:T(8,128)}, f32[14,512]{1,0:T(8,128)}, f32[14,512]{1,0:T(8,128)}, f32[14,128]{1,0:T(8,128)}, f32[14,128]{1,0:T(8,128)}) custom-call(f32[2]{0:T(128)} %add_convert_fusion.flag_s, s32[4,512]{1,0:T(4,128)} %add.37.ids_s, f32[512,4]{1,0:T(8,128)} %select_bitcast_fusion.wt_ref, f32[4096,15]{1,0:T(8,128)} %bitcast.19, ...), custom_call_target="tpu_custom_call" | custom-call | tf_op jit(solution)/shard_map/pallas_call | solution.py:224
  31.2 0.7 collective-permute-start.7
  31.8 0.0 collective-permute-done.7.sw_ref
  31.8 0.0 copy-start.12
  31.9 0.6 copy-done.12
  32.5 21.3 %shard_map.83 = (f32[14,128,512]{2,1,0:T(8,128)}, f32[14,512]{1,0:T(8,128)}, f32[14,512]{1,0:T(8,128)}, f32[14,128]{1,0:T(8,128)}, f32[14,128]{1,0:T(8,128)}) custom-call(f32[14,14]{1,0:T(8,128)} %mix_s.1, f32[14]{0:T(128)} %act_s.1, f32[2]{0:T(128)} %add_convert_fusion.flag_s, f32[14,128,512]{2,1,0:T(8,128)} %f_hbm.1, f32[128,512]{1,0:T(8,128)} %rate_ref.1, ...), custom_call_target="tpu_custom_call" | custom-call | flops 95420416 | bytes 7602176 | tf_op jit(solution)/shard_map/pallas_call | solution.py:169
  53.8 11.1 %collective-permute-start.8 = (f32[14,512]{1,0:T(8,128)}, f32[14,512]{1,0:T(8,128)S(1)}, u32[]{:S(2)}, u32[]{:S(2)}) collective-permute-start(f32[14,512]{1,0:T(8,128)} %get-tuple-element.21), channel_id=1, source_target_pairs={{0,8},{8,16},{1,9},{9,17},{2,10},{10,18},{3,11},{11,19},{4,12},{12... | collective-permute-start | bytes 86024 | tf_op jit(solution)/shard_map/ppermute | solution.py:332
  64.9 1.9 %collective-permute-start.9 = (f32[14,512]{1,0:T(8,128)}, f32[14,512]{1,0:T(8,128)S(1)}, u32[]{:S(2)}, u32[]{:S(2)}) collective-permute-start(f32[14,512]{1,0:T(8,128)} %get-tuple-element.22), channel_id=1, source_target_pairs={{8,0},{16,8},{9,1},{17,9},{10,2},{18,10},{11,3},{19,11},{12,4},{20... | collective-permute-start | bytes 86024 | tf_op jit(solution)/shard_map/ppermute | solution.py:333
  66.8 0.1 collective-permute-start.10
  66.9 4.2 %collective-permute-start.11 = (f32[14,128]{1,0:T(8,128)}, f32[14,128]{1,0:T(8,128)S(1)}, u32[]{:S(2)}, u32[]{:S(2)}) collective-permute-start(f32[14,128]{1,0:T(8,128)} %get-tuple-element.24), channel_id=1, source_target_pairs={{1,0},{2,1},{3,2},{4,3},{5,4},{6,5},{7,6},{0,7},{9,8},{10,9},{11,1... | collective-permute-start | bytes 21512 | tf_op jit(solution)/shard_map/ppermute | solution.py:335
  71.0 1.2 %collective-permute-done.10.gl_ref = f32[14,128]{1,0:T(8,128)S(1)} collective-permute-done((f32[14,128]{1,0:T(8,128)}, f32[14,128]{1,0:T(8,128)S(1)}, u32[]{:S(2)}, u32[]{:S(2)}) %collective-permute-start.10) | collective-permute-done | bytes 7200 | tf_op jit(solution)/shard_map/ppermute | solution.py:334
  72.3 0.0 collective-permute-done.11.gr_ref
  72.3 0.0 collective-permute-done.8.g0_ref
  72.3 0.0 copy-start.2
  72.3 0.0 collective-permute-done.9.g1_ref
  72.3 0.0 copy-start.3
  72.3 0.5 copy-done.6
  72.9 0.0 copy-done.7
  72.9 0.0 copy-done.2
  72.9 0.0 copy-done.3
  72.9 4.3 %shard_map.84 = f32[14,128,512]{2,1,0:T(8,128)} custom-call(f32[14,128,512]{2,1,0:T(8,128)} %get-tuple-element.20.out_in, f32[14,512]{1,0:T(8,128)} %copy-done.2, f32[14,512]{1,0:T(8,128)} %copy-done.3, f32[14,128]{1,0:T(8,128)} %copy-done.6, f32[14,128]{1,0:T(8,128)} %copy-done.7), custom_call_target="tpu_custom_call", output_to_operand_aliasing={{}: (0, {})} | custom-call | tf_op jit(solution)/shard_map/pallas_call | solution.py:274
  (11 shorter events, 0.1 us)
Async XLA Ops:
  0.0 17.5 %copy-start.8 = (s32[4,512]{1,0:T(4,128)S(1)}, s32[4,512]{1,0:T(4,128)}, u32[]{:S(2)}) copy-start(s32[4,512]{1,0:T(4,128)} %param.12) | copy-start | bytes 24580
  0.0 17.7 %copy-start.9 = (s32[4,512]{1,0:T(4,128)S(1)}, s32[4,512]{1,0:T(4,128)}, u32[]{:S(2)}) copy-start(s32[4,512]{1,0:T(4,128)} %param.14) | copy-start | bytes 24580
  1.1 27.1 %collective-permute-start.3 = (f32[14,512]{1,0:T(8,128)S(1)}, f32[14,512]{1,0:T(8,128)S(1)}, u32[]{:S(2)}, u32[]{:S(2)}) collective-permute-start(f32[14,512]{1,0:T(8,128)S(1)} %bitcast.20), channel_id=1, source_target_pairs={{0,8},{8,16},{1,9},{9,17},{2,10},{10,18},{3,11},{11,19},{4,12},{12... | collective-permute-start | bytes 86024 | tf_op jit(solution)/shard_map/ppermute | solution.py:320
  6.4 12.3 %copy-start.10 = (f32[4,512]{1,0:T(4,128)S(1)}, f32[4,512]{1,0:T(4,128)}, u32[]{:S(2)}) copy-start(f32[4,512]{1,0:T(4,128)} %param.13) | copy-start | bytes 24580
  6.4 11.4 %collective-permute-start = (f32[1,15,512]{2,1,0:T(8,128)S(1)}, f32[1,15,512]{2,1,0:T(8,128)S(1)}, u32[]{:S(2)}, u32[]{:S(2)}) collective-permute-start(f32[1,15,512]{2,1,0:T(8,128)S(1)} %maximum_bitcast_fusion.1), channel_id=1, source_target_pairs={{0,4},{1,5},{2,6},{3,7},{4,0},{5,1},{6,2},{7,3},{8,12},{9,13},{10,... | collective-permute-start | bytes 92168 | tf_op jit(solution)/shard_map/ppermute | solution.py:309
  8.8 10.1 %copy-start.11 = (f32[4,512]{1,0:T(4,128)S(1)}, f32[4,512]{1,0:T(4,128)}, u32[]{:S(2)}) copy-start(f32[4,512]{1,0:T(4,128)} %param.15) | copy-start | bytes 24580
  8.8 19.4 %collective-permute-start.4 = (f32[14,512]{1,0:T(8,128)S(1)}, f32[14,512]{1,0:T(8,128)S(1)}, u32[]{:S(2)}, u32[]{:S(2)}) collective-permute-start(f32[14,512]{1,0:T(8,128)S(1)} %bitcast.22), channel_id=1, source_target_pairs={{8,0},{16,8},{9,1},{17,9},{10,2},{18,10},{11,3},{19,11},{12,4},{20... | collective-permute-start | bytes 86024 | tf_op jit(solution)/shard_map/ppermute | solution.py:321
  13.0 15.2 %collective-permute-start.5 = (f32[14,128]{1,0:T(8,128)S(1)}, f32[14,128]{1,0:T(8,128)S(1)}, u32[]{:S(2)}, u32[]{:S(2)}) collective-permute-start(f32[14,128]{1,0:T(8,128)S(1)} %bitcast.23), channel_id=1, source_target_pairs={{0,1},{1,2},{2,3},{3,4},{4,5},{5,6},{6,7},{7,0},{8,9},{9,10},{10,1... | collective-permute-start | bytes 21512 | tf_op jit(solution)/shard_map/ppermute | solution.py:322
  14.6 13.6 %collective-permute-start.6 = (f32[14,128]{1,0:T(8,128)S(1)}, f32[14,128]{1,0:T(8,128)S(1)}, u32[]{:S(2)}, u32[]{:S(2)}) collective-permute-start(f32[14,128]{1,0:T(8,128)S(1)} %bitcast.24), channel_id=1, source_target_pairs={{1,0},{2,1},{3,2},{4,3},{5,4},{6,5},{7,6},{0,7},{9,8},{10,9},{11,1... | collective-permute-start | bytes 21512 | tf_op jit(solution)/shard_map/ppermute | solution.py:323
  17.9 3.3 %collective-permute-start.1 = (f32[2,15,512]{2,1,0:T(8,128)S(1)}, f32[2,15,512]{2,1,0:T(8,128)S(1)}, u32[]{:S(2)}, u32[]{:S(2)}) collective-permute-start(f32[2,15,512]{2,1,0:T(8,128)S(1)} %pad_maximum_fusion.1), channel_id=1, source_target_pairs={{0,2},{1,3},{2,0},{3,1},{4,6},{5,7},{6,4},{7,5},{8,10},{9,11},{10,... | collective-permute-start | bytes 184328 | tf_op jit(solution)/shard_map/ppermute | solution.py:309
  21.2 5.0 %collective-permute-start.2 = (f32[4,15,512]{2,1,0:T(8,128)S(1)}, f32[4,15,512]{2,1,0:T(8,128)S(1)}, u32[]{:S(2)}, u32[]{:S(2)}) collective-permute-start(f32[4,15,512]{2,1,0:T(8,128)S(1)} %pad_maximum_fusion), channel_id=1, source_target_pairs={{0,1},{1,0},{2,3},{3,2},{4,5},{5,4},{6,7},{7,6},{8,9},{9,8},{10,11... | collective-permute-start | bytes 368648 | tf_op jit(solution)/shard_map/ppermute | solution.py:309
  28.2 0.6 copy-start.4
  28.2 0.6 copy-start.5
  28.2 0.6 copy-start
  28.2 0.6 copy-start.1
  31.2 0.7 collective-permute-start.7
  31.8 0.6 copy-start.12
  53.8 18.5 %collective-permute-start.8 = (f32[14,512]{1,0:T(8,128)}, f32[14,512]{1,0:T(8,128)S(1)}, u32[]{:S(2)}, u32[]{:S(2)}) collective-permute-start(f32[14,512]{1,0:T(8,128)} %get-tuple-element.21), channel_id=1, source_target_pairs={{0,8},{8,16},{1,9},{9,17},{2,10},{10,18},{3,11},{11,19},{4,12},{12... | collective-permute-start | bytes 86024 | tf_op jit(solution)/shard_map/ppermute | solution.py:332
  64.9 7.4 %collective-permute-start.9 = (f32[14,512]{1,0:T(8,128)}, f32[14,512]{1,0:T(8,128)S(1)}, u32[]{:S(2)}, u32[]{:S(2)}) collective-permute-start(f32[14,512]{1,0:T(8,128)} %get-tuple-element.22), channel_id=1, source_target_pairs={{8,0},{16,8},{9,1},{17,9},{10,2},{18,10},{11,3},{19,11},{12,4},{20... | collective-permute-start | bytes 86024 | tf_op jit(solution)/shard_map/ppermute | solution.py:333
  66.8 5.5 %collective-permute-start.10 = (f32[14,128]{1,0:T(8,128)}, f32[14,128]{1,0:T(8,128)S(1)}, u32[]{:S(2)}, u32[]{:S(2)}) collective-permute-start(f32[14,128]{1,0:T(8,128)} %get-tuple-element.23), channel_id=1, source_target_pairs={{0,1},{1,2},{2,3},{3,4},{4,5},{5,6},{6,7},{7,0},{8,9},{9,10},{10,1... | collective-permute-start | bytes 21512 | tf_op jit(solution)/shard_map/ppermute | solution.py:334
  66.9 5.4 %collective-permute-start.11 = (f32[14,128]{1,0:T(8,128)}, f32[14,128]{1,0:T(8,128)S(1)}, u32[]{:S(2)}, u32[]{:S(2)}) collective-permute-start(f32[14,128]{1,0:T(8,128)} %get-tuple-element.24), channel_id=1, source_target_pairs={{1,0},{2,1},{3,2},{4,3},{5,4},{6,5},{7,6},{0,7},{9,8},{10,9},{11,1... | collective-permute-start | bytes 21512 | tf_op jit(solution)/shard_map/ppermute | solution.py:335
  72.3 0.6 copy-start.6
  72.3 0.6 copy-start.7
  72.3 0.6 copy-start.2
  72.3 0.6 copy-start.3

commit v12 on v11

--- a/solution.py
+++ b/solution.py
@@ -21,7 +21,8 @@
 
 
 def step_kernel(nf, rows, lanes, mix_s, act_s, flag_s, f_hbm, rate_ref, hlo_ref, hhi_ref, sw_ref,
-                lft_ref, rgt_ref, out_ref, elo_ref, ehi_ref, clo_ref, chi_ref, ext1, ext2, coef, sem):
+                lft_ref, rgt_ref, out_hbm, elo_ref, ehi_ref, clo_ref, chi_ref, ext1, ext2, coef, obuf,
+                sem):
     n_i = rows // SUB
     n_j = lanes // LANE
     top = SUB + rows
@@ -43,7 +44,7 @@
         ext2[f, SUB:top, right:right + LANE] = zeros
     for f in range(nf):
         for g in range(nf):
-            coef[f * nf + g] = jnp.full((SUB, LANE), mix_s[f, g], jnp.float32)
+            coef[f * nf + g] = jnp.full((SUB, LANE), source_step * mix_s[f, g], jnp.float32)
         coef[nf * nf + f] = jnp.full((SUB, LANE), -act_s[f], jnp.float32)
     copy.wait()
 
@@ -100,9 +101,9 @@
                 forward = jnp.where(last_sub, pltpu.roll(down, SUB - 1, 0), pltpu.roll(v, SUB - 1, 0))
                 left = jnp.where(first_lane, pltpu.roll(west, 1, 1), pltpu.roll(v, 1, 1))
                 rgt = jnp.where(last_lane, pltpu.roll(east, LANE - 1, 1), pltpu.roll(v, LANE - 1, 1))
-                advect = -courant * (v - backward)
-                spread = diffusion * (backward + forward + left + rgt - 4.0 * v)
-                tends[h].append((v, advect + spread + source_step * accs[h]))
+                flow = (courant + diffusion) * backward + diffusion * (forward + left + rgt)
+                flow = flow - (courant + 4.0 * diffusion) * v
+                tends[h].append((v, flow + accs[h]))
         return tends
 
     pair = 2 if n_j % 2 == 0 else 1
@@ -131,20 +132,25 @@
 
     high_ghost(ext2, lambda f: jnp.zeros((1, lanes), jnp.float32))
 
-    def stage_two(t, carry):
-        r0, c0s = tile_offsets(t)
-        rate_ts = [rate_ref[pl.ds(r0, SUB), pl.ds(c0, LANE)] for c0 in c0s]
-        tends = tendency_tiles(ext2, r0, c0s, rate_ts)
-        r = pl.multiple_of(r0 + SUB, SUB)
-        for c0, tend in zip(c0s, tends):
-            c = pl.multiple_of(c0 + LANE, LANE)
-            for f in range(nf):
-                v, tf = tend[f]
-                base = ext1[f, pl.ds(r, SUB), pl.ds(c, LANE)]
-                out_ref[f, pl.ds(r0, SUB), pl.ds(c0, LANE)] = 0.5 * (base + v + tf)
+    def stage_two(i, carry):
+        for jp in range(n_jp):
+            r0, c0s = tile_offsets(i * n_jp + jp)
+            rate_ts = [rate_ref[pl.ds(r0, SUB), pl.ds(c0, LANE)] for c0 in c0s]
+            tends = tendency_tiles(ext2, r0, c0s, rate_ts)
+            r = pl.multiple_of(r0 + SUB, SUB)
+            for c0, tend in zip(c0s, tends):
+                c = pl.multiple_of(c0 + LANE, LANE)
+                for f in range(nf):
+                    v, tf = tend[f]
+                    base = ext1[f, pl.ds(r, SUB), pl.ds(c, LANE)]
+                    obuf[f, pl.ds(r0, SUB), pl.ds(c0, LANE)] = 0.5 * (base + v + tf)
+        r0 = pl.multiple_of(i * SUB, SUB)
+        pltpu.make_async_copy(
+            obuf.at[:, pl.ds(r0, SUB), :], out_hbm.at[:, pl.ds(r0, SUB), :], sem.at[1]
+        ).start()
         return carry
 
-    lax.fori_loop(0, n_i * n_jp, stage_two, 0)
+    lax.fori_loop(0, n_i, stage_two, 0)
 
     for f in range(nf):
         elo_ref[f:f + 1, :] = ext2[f, SUB:SUB + 1, LANE:right]
@@ -153,6 +159,7 @@
         east = jnp.transpose(ext2[f, SUB:top, right - LANE:right])
         clo_ref[f:f + 1, :] = west[0:1, :]
         chi_ref[f:f + 1, :] = east[LANE - 1:LANE, :]
+    pltpu.make_async_copy(obuf, out_hbm, sem.at[1]).wait()
 
 
 def fused_step(fields, rate, mix, act, flags, halo_lo, halo_hi, swapped, lft, rgt):
@@ -176,12 +183,13 @@
             jax.ShapeDtypeStruct((nf, rows), jnp.float32),
         ),
         in_specs=[smem, smem, smem, pl.BlockSpec(memory_space=pl.ANY)] + [vspec] * 6,
-        out_specs=(vspec,) * 5,
+        out_specs=(pl.BlockSpec(memory_space=pl.ANY),) + (vspec,) * 4,
         scratch_shapes=[
             vmem((nf, rows + 2 * SUB, lanes + 2 * LANE), jnp.float32),
             vmem((nf, rows + 2 * SUB, lanes + 2 * LANE), jnp.float32),
             vmem((nf * nf + nf, SUB, LANE), jnp.float32),
-            pltpu.SemaphoreType.DMA((1,)),
+            vmem((nf, rows, lanes), jnp.float32),
+            pltpu.SemaphoreType.DMA((2,)),
         ],
         compiler_params=pltpu.CompilerParams(vmem_limit_bytes=60 * 1024 * 1024),
         cost_estimate=cost,

time: 78.2 us -> 76.9 us (0.983)
  Pallas kernels: 28 us -> 26.8 us
    pallas_call x1, Pallas kernels: 21.3 us -> 20.1 us  [fused_step(): pl.pallas_call(functools.partial(step_kernel, nf, rows, lanes), out_shape...]
where the time goes in v12:
time: 76.9 us; the launch traced here: 76 us
  starting transfers between devices  31.2 us (41%)
  Pallas kernels  26.8 us (35%)
  local copies, waits for them, and re-layouts  8.89 us (12%)
  waiting for transfers between devices  6.14 us (8%)
  other arithmetic  2.75 us (4%)
    pallas_call x1, Pallas kernels, fused_step(): pl.pallas_call(functools.partial(step_kernel, nf, rows, lanes), out_shape...  20.1 us
    ppermute x1, starting transfers between devices, shards(): g0 = lax.ppermute(ehi, 'grp', [(i, i + 1) for i in range(n_grp - 2)])  11.1 us
    ppermute x3, waiting for transfers between devices, shards(): lax.ppermute(planes, 'blk', partner)  4.88 us
    ppermute x1, starting transfers between devices, shards(): lax.ppermute(last_row, 'grp', [(i, i + 1) for i in range(n_grp - 2)])  4.54 us
    pallas_call x1, Pallas kernels, fix_edges(): pl.pallas_call(functools.partial(fix_kernel, low_w, side_w), out_shape=ja...  4.34 us
    ppermute x1, starting transfers between devices, shards(): gr = lax.ppermute(clo, 'blk', [((i + 1) % n_blk, i) for i in range(n_blk)])  4.15 us
    unnamed x34, local copies, waits for them, and re-layouts  3.06 us
    ppermute x1, starting transfers between devices, shards(): lax.ppermute(fields[:, :, 0], 'blk', [((i + 1) % n_blk, i) for i in range...  2.97 us
  transfers between devices with their start and end apart: 12, of which 3 were waited for; matrix products, arithmetic and copies ran while one was open for 11% of the time, Pallas kernels for 0%

profile of v12, /device:TPU:1, one launch (start us, length us, event | category | flops | bytes accessed | tf_op | source)
XLA Modules:
  0.0 76.0 jit_solution(358552376558689263)
XLA Ops:
  0.0 0.0 copy-start.8
  0.0 1.1 %fusion.13 = (f32[14,1,512]{2,1,0:T(1,128)S(1)}, f32[14,1,512]{2,1,0:T(1,128)S(1)}) fusion(f32[14,128,512]{2,1,0:T(8,128)} %f_hbm.1), kind=kLoop, calls=%fused_computation.44 | loop fusion | bytes 114688 | tf_op jit(solution)/shard_map/slice | solution.py:309
  1.1 4.5 %collective-permute-start.3 = (f32[14,512]{1,0:T(8,128)S(1)}, f32[14,512]{1,0:T(8,128)S(1)}, u32[]{:S(2)}, u32[]{:S(2)}) collective-permute-start(f32[14,512]{1,0:T(8,128)S(1)} %bitcast.20), channel_id=1, source_target_pairs={{0,8},{8,16},{1,9},{9,17},{2,10},{10,18},{3,11},{11,19},{4,12},{12... | collective-permute-start | bytes 86024 | tf_op jit(solution)/shard_map/ppermute | solution.py:328
  5.7 0.7 slice_bitcast_fusion
  6.4 0.0 copy-start.10
  6.4 2.4 %collective-permute-start = (f32[1,15,512]{2,1,0:T(8,128)S(1)}, f32[1,15,512]{2,1,0:T(8,128)S(1)}, u32[]{:S(2)}, u32[]{:S(2)}) collective-permute-start(f32[1,15,512]{2,1,0:T(8,128)S(1)} %maximum_bitcast_fusion.1), channel_id=1, source_target_pairs={{0,4},{1,5},{2,6},{3,7},{4,0},{5,1},{6,2},{7,3},{8,12},{9,13},{10,... | collective-permute-start | bytes 92168 | tf_op jit(solution)/shard_map/ppermute | solution.py:317
  8.8 2.0 %collective-permute-start.4 = (f32[14,512]{1,0:T(8,128)S(1)}, f32[14,512]{1,0:T(8,128)S(1)}, u32[]{:S(2)}, u32[]{:S(2)}) collective-permute-start(f32[14,512]{1,0:T(8,128)S(1)} %bitcast.22), channel_id=1, source_target_pairs={{8,0},{16,8},{9,1},{17,9},{10,2},{18,10},{11,3},{19,11},{12,4},{20... | collective-permute-start | bytes 86024 | tf_op jit(solution)/shard_map/ppermute | solution.py:329
  10.9 1.8 %fusion.12 = (f32[14,128,1]{2,1,0:T(8,128)S(1)}, f32[14,128,1]{2,1,0:T(8,128)S(1)}) fusion(f32[14,128,512]{2,1,0:T(8,128)} %f_hbm.1), kind=kLoop, calls=%fused_computation.43 | loop fusion | bytes 28672 | tf_op jit(solution)/shard_map/slice | solution.py:331
  12.7 0.3 copy.36
  13.0 1.2 %collective-permute-start.5 = (f32[14,128]{1,0:T(8,128)S(1)}, f32[14,128]{1,0:T(8,128)S(1)}, u32[]{:S(2)}, u32[]{:S(2)}) collective-permute-start(f32[14,128]{1,0:T(8,128)S(1)} %bitcast.23), channel_id=1, source_target_pairs={{0,1},{1,2},{2,3},{3,4},{4,5},{5,6},{6,7},{7,0},{8,9},{9,10},{10,1... | collective-permute-start | bytes 21512 | tf_op jit(solution)/shard_map/ppermute | solution.py:330
  14.2 0.3 copy.37
  14.6 3.0 %collective-permute-start.6 = (f32[14,128]{1,0:T(8,128)S(1)}, f32[14,128]{1,0:T(8,128)S(1)}, u32[]{:S(2)}, u32[]{:S(2)}) collective-permute-start(f32[14,128]{1,0:T(8,128)S(1)} %bitcast.24), channel_id=1, source_target_pairs={{1,0},{2,1},{3,2},{4,3},{5,4},{6,5},{7,6},{0,7},{9,8},{10,9},{11,1... | collective-permute-start | bytes 21512 | tf_op jit(solution)/shard_map/ppermute | solution.py:331
  17.5 0.0 copy-done.8
  17.5 0.1 copy.20
  17.7 0.0 copy-done.9
  17.7 0.1 copy.21
  17.9 0.0 collective-permute-done
  17.9 0.1 collective-permute-start.1
  18.0 0.8 %add_select_fusion = (s32[4,512]{0,1:T(8,128)S(1)}, s32[4,512]{0,1:T(8,128)S(1)}) fusion(s32[4,512]{0,1:T(8,128)S(1)} %copy.20, s32[4,512]{0,1:T(8,128)S(1)} %copy.21, pred[]{:T(512)} %eq.12, s32[]{:T(128)S(6)} %axis_index.25), kind=kLoop, calls=%fused_computation | loop fusion | flops 157696 | bytes 32773 | tf_op jit(solution)/shard_map/jit(remainder)/select_n | solution.py:326
  18.8 0.0 copy-done.10
  18.8 0.1 copy.24
  18.9 0.0 copy-done.11
  18.9 0.1 copy.25
  19.1 2.1 %collective-permute-done.1 = f32[2,15,512]{2,1,0:T(8,128)S(1)} collective-permute-done((f32[2,15,512]{2,1,0:T(8,128)S(1)}, f32[2,15,512]{2,1,0:T(8,128)S(1)}, u32[]{:S(2)}, u32[]{:S(2)}) %collective-permute-start.1) | collective-permute-done | bytes 61472 | tf_op jit(solution)/shard_map/ppermute | solution.py:317
  21.2 0.1 collective-permute-start.2
  21.2 0.7 select_bitcast_fusion.wt_ref
  22.0 0.1 copy.23
  22.1 0.1 copy.22
  22.2 0.6 add.37.ids_s
  22.8 0.6 add_convert_fusion.flag_s
  23.4 2.8 %collective-permute-done.2 = f32[4,15,512]{2,1,0:T(8,128)S(1)} collective-permute-done((f32[4,15,512]{2,1,0:T(8,128)S(1)}, f32[4,15,512]{2,1,0:T(8,128)S(1)}, u32[]{:S(2)}, u32[]{:S(2)}) %collective-permute-start.2) | collective-permute-done | bytes 122912 | tf_op jit(solution)/shard_map/ppermute | solution.py:317
  26.2 2.0 %copy.32 = f32[8,512,15]{2,1,0:T(8,128)} copy(f32[8,512,15]{1,2,0:T(8,128)S(1)} %maximum_bitcast_fusion) | data formatting | bytes 491520 | tf_op jit(solution)/shard_map/reshape | solution.py:319
  28.2 0.0 collective-permute-done.5.refs_2_
  28.2 0.0 collective-permute-done.6.refs_3_
  28.2 0.0 copy-start.5
  28.2 0.0 collective-permute-done.3.refs_0_
  28.2 0.0 copy-start
  28.2 0.0 collective-permute-done.4.refs_1_
  28.2 0.0 copy-start.1
  28.2 0.5 copy-done.4
  28.8 0.0 copy-done.5
  28.8 0.0 copy-done
  28.8 0.0 copy-done.1
  28.8 2.3 %shard_map.82 = (f32[15,512]{1,0:T(8,128)}, f32[14,512]{1,0:T(8,128)}, f32[14,512]{1,0:T(8,128)}, f32[14,128]{1,0:T(8,128)}, f32[14,128]{1,0:T(8,128)}) custom-call(f32[2]{0:T(128)} %add_convert_fusion.flag_s, s32[4,512]{1,0:T(4,128)} %add.37.ids_s, f32[512,4]{1,0:T(8,128)} %select_bitcast_fusion.wt_ref, f32[4096,15]{1,0:T(8,128)} %bitcast.19, ...), custom_call_target="tpu_custom_call" | custom-call | tf_op jit(solution)/shard_map/pallas_call | solution.py:232
  31.2 0.7 collective-permute-start.7
  31.8 0.0 collective-permute-done.7.sw_ref
  31.8 0.0 copy-start.12
  31.9 0.6 copy-done.12
  32.5 20.1 %shard_map.83 = (f32[14,128,512]{2,1,0:T(8,128)}, f32[14,512]{1,0:T(8,128)}, f32[14,512]{1,0:T(8,128)}, f32[14,128]{1,0:T(8,128)}, f32[14,128]{1,0:T(8,128)}) custom-call(f32[14,14]{1,0:T(8,128)} %mix_s.1, f32[14]{0:T(128)} %act_s.1, f32[2]{0:T(128)} %add_convert_fusion.flag_s, f32[14,128,512]{2,1,0:T(8,128)} %f_hbm.1, f32[128,512]{1,0:T(8,128)} %rate_ref.1, ...), custom_call_target="tpu_custom_call" | custom-call | flops 95420416 | bytes 7602176 | tf_op jit(solution)/shard_map/pallas_call | solution.py:176
  52.5 11.1 %collective-permute-start.8 = (f32[14,512]{1,0:T(8,128)}, f32[14,512]{1,0:T(8,128)S(1)}, u32[]{:S(2)}, u32[]{:S(2)}) collective-permute-start(f32[14,512]{1,0:T(8,128)} %get-tuple-element.21), channel_id=1, source_target_pairs={{0,8},{8,16},{1,9},{9,17},{2,10},{10,18},{3,11},{11,19},{4,12},{12... | collective-permute-start | bytes 86024 | tf_op jit(solution)/shard_map/ppermute | solution.py:340
  63.6 1.9 %collective-permute-start.9 = (f32[14,512]{1,0:T(8,128)}, f32[14,512]{1,0:T(8,128)S(1)}, u32[]{:S(2)}, u32[]{:S(2)}) collective-permute-start(f32[14,512]{1,0:T(8,128)} %get-tuple-element.22), channel_id=1, source_target_pairs={{8,0},{16,8},{9,1},{17,9},{10,2},{18,10},{11,3},{19,11},{12,4},{20... | collective-permute-start | bytes 86024 | tf_op jit(solution)/shard_map/ppermute | solution.py:341
  65.5 0.1 collective-permute-start.10
  65.6 4.2 %collective-permute-start.11 = (f32[14,128]{1,0:T(8,128)}, f32[14,128]{1,0:T(8,128)S(1)}, u32[]{:S(2)}, u32[]{:S(2)}) collective-permute-start(f32[14,128]{1,0:T(8,128)} %get-tuple-element.24), channel_id=1, source_target_pairs={{1,0},{2,1},{3,2},{4,3},{5,4},{6,5},{7,6},{0,7},{9,8},{10,9},{11,1... | collective-permute-start | bytes 21512 | tf_op jit(solution)/shard_map/ppermute | solution.py:343
  69.8 1.2 %collective-permute-done.10.gl_ref = f32[14,128]{1,0:T(8,128)S(1)} collective-permute-done((f32[14,128]{1,0:T(8,128)}, f32[14,128]{1,0:T(8,128)S(1)}, u32[]{:S(2)}, u32[]{:S(2)}) %collective-permute-start.10) | collective-permute-done | bytes 7200 | tf_op jit(solution)/shard_map/ppermute | solution.py:342
  71.0 0.0 collective-permute-done.11.gr_ref
  71.0 0.0 collective-permute-done.8.g0_ref
  71.0 0.0 copy-start.2
  71.0 0.0 collective-permute-done.9.g1_ref
  71.0 0.0 copy-start.3
  71.1 0.5 copy-done.6
  71.6 0.0 copy-done.7
  71.6 0.0 copy-done.2
  71.6 0.0 copy-done.3
  71.6 4.3 %shard_map.84 = f32[14,128,512]{2,1,0:T(8,128)} custom-call(f32[14,128,512]{2,1,0:T(8,128)} %get-tuple-element.20.out_in, f32[14,512]{1,0:T(8,128)} %copy-done.2, f32[14,512]{1,0:T(8,128)} %copy-done.3, f32[14,128]{1,0:T(8,128)} %copy-done.6, f32[14,128]{1,0:T(8,128)} %copy-done.7), custom_call_target="tpu_custom_call", output_to_operand_aliasing={{}: (0, {})} | custom-call | tf_op jit(solution)/shard_map/pallas_call | solution.py:282
  (11 shorter events, 0.1 us)
Async XLA Ops:
  0.0 17.5 %copy-start.8 = (s32[4,512]{1,0:T(4,128)S(1)}, s32[4,512]{1,0:T(4,128)}, u32[]{:S(2)}) copy-start(s32[4,512]{1,0:T(4,128)} %param.12) | copy-start | bytes 24580
  0.0 17.7 %copy-start.9 = (s32[4,512]{1,0:T(4,128)S(1)}, s32[4,512]{1,0:T(4,128)}, u32[]{:S(2)}) copy-start(s32[4,512]{1,0:T(4,128)} %param.14) | copy-start | bytes 24580
  1.1 27.1 %collective-permute-start.3 = (f32[14,512]{1,0:T(8,128)S(1)}, f32[14,512]{1,0:T(8,128)S(1)}, u32[]{:S(2)}, u32[]{:S(2)}) collective-permute-start(f32[14,512]{1,0:T(8,128)S(1)} %bitcast.20), channel_id=1, source_target_pairs={{0,8},{8,16},{1,9},{9,17},{2,10},{10,18},{3,11},{11,19},{4,12},{12... | collective-permute-start | bytes 86024 | tf_op jit(solution)/shard_map/ppermute | solution.py:328
  6.4 12.3 %copy-start.10 = (f32[4,512]{1,0:T(4,128)S(1)}, f32[4,512]{1,0:T(4,128)}, u32[]{:S(2)}) copy-start(f32[4,512]{1,0:T(4,128)} %param.13) | copy-start | bytes 24580
  6.4 11.4 %collective-permute-start = (f32[1,15,512]{2,1,0:T(8,128)S(1)}, f32[1,15,512]{2,1,0:T(8,128)S(1)}, u32[]{:S(2)}, u32[]{:S(2)}) collective-permute-start(f32[1,15,512]{2,1,0:T(8,128)S(1)} %maximum_bitcast_fusion.1), channel_id=1, source_target_pairs={{0,4},{1,5},{2,6},{3,7},{4,0},{5,1},{6,2},{7,3},{8,12},{9,13},{10,... | collective-permute-start | bytes 92168 | tf_op jit(solution)/shard_map/ppermute | solution.py:317
  8.8 10.1 %copy-start.11 = (f32[4,512]{1,0:T(4,128)S(1)}, f32[4,512]{1,0:T(4,128)}, u32[]{:S(2)}) copy-start(f32[4,512]{1,0:T(4,128)} %param.15) | copy-start | bytes 24580
  8.8 19.4 %collective-permute-start.4 = (f32[14,512]{1,0:T(8,128)S(1)}, f32[14,512]{1,0:T(8,128)S(1)}, u32[]{:S(2)}, u32[]{:S(2)}) collective-permute-start(f32[14,512]{1,0:T(8,128)S(1)} %bitcast.22), channel_id=1, source_target_pairs={{8,0},{16,8},{9,1},{17,9},{10,2},{18,10},{11,3},{19,11},{12,4},{20... | collective-permute-start | bytes 86024 | tf_op jit(solution)/shard_map/ppermute | solution.py:329
  13.0 15.2 %collective-permute-start.5 = (f32[14,128]{1,0:T(8,128)S(1)}, f32[14,128]{1,0:T(8,128)S(1)}, u32[]{:S(2)}, u32[]{:S(2)}) collective-permute-start(f32[14,128]{1,0:T(8,128)S(1)} %bitcast.23), channel_id=1, source_target_pairs={{0,1},{1,2},{2,3},{3,4},{4,5},{5,6},{6,7},{7,0},{8,9},{9,10},{10,1... | collective-permute-start | bytes 21512 | tf_op jit(solution)/shard_map/ppermute | solution.py:330
  14.6 13.6 %collective-permute-start.6 = (f32[14,128]{1,0:T(8,128)S(1)}, f32[14,128]{1,0:T(8,128)S(1)}, u32[]{:S(2)}, u32[]{:S(2)}) collective-permute-start(f32[14,128]{1,0:T(8,128)S(1)} %bitcast.24), channel_id=1, source_target_pairs={{1,0},{2,1},{3,2},{4,3},{5,4},{6,5},{7,6},{0,7},{9,8},{10,9},{11,1... | collective-permute-start | bytes 21512 | tf_op jit(solution)/shard_map/ppermute | solution.py:331
  17.9 3.3 %collective-permute-start.1 = (f32[2,15,512]{2,1,0:T(8,128)S(1)}, f32[2,15,512]{2,1,0:T(8,128)S(1)}, u32[]{:S(2)}, u32[]{:S(2)}) collective-permute-start(f32[2,15,512]{2,1,0:T(8,128)S(1)} %pad_maximum_fusion.1), channel_id=1, source_target_pairs={{0,2},{1,3},{2,0},{3,1},{4,6},{5,7},{6,4},{7,5},{8,10},{9,11},{10,... | collective-permute-start | bytes 184328 | tf_op jit(solution)/shard_map/ppermute | solution.py:317
  21.2 5.0 %collective-permute-start.2 = (f32[4,15,512]{2,1,0:T(8,128)S(1)}, f32[4,15,512]{2,1,0:T(8,128)S(1)}, u32[]{:S(2)}, u32[]{:S(2)}) collective-permute-start(f32[4,15,512]{2,1,0:T(8,128)S(1)} %pad_maximum_fusion), channel_id=1, source_target_pairs={{0,1},{1,0},{2,3},{3,2},{4,5},{5,4},{6,7},{7,6},{8,9},{9,8},{10,11... | collective-permute-start | bytes 368648 | tf_op jit(solution)/shard_map/ppermute | solution.py:317
  28.2 0.6 copy-start.4
  28.2 0.6 copy-start.5
  28.2 0.6 copy-start
  28.2 0.6 copy-start.1
  31.2 0.7 collective-permute-start.7
  31.8 0.6 copy-start.12
  52.5 18.5 %collective-permute-start.8 = (f32[14,512]{1,0:T(8,128)}, f32[14,512]{1,0:T(8,128)S(1)}, u32[]{:S(2)}, u32[]{:S(2)}) collective-permute-start(f32[14,512]{1,0:T(8,128)} %get-tuple-element.21), channel_id=1, source_target_pairs={{0,8},{8,16},{1,9},{9,17},{2,10},{10,18},{3,11},{11,19},{4,12},{12... | collective-permute-start | bytes 86024 | tf_op jit(solution)/shard_map/ppermute | solution.py:340
  63.6 7.4 %collective-permute-start.9 = (f32[14,512]{1,0:T(8,128)}, f32[14,512]{1,0:T(8,128)S(1)}, u32[]{:S(2)}, u32[]{:S(2)}) collective-permute-start(f32[14,512]{1,0:T(8,128)} %get-tuple-element.22), channel_id=1, source_target_pairs={{8,0},{16,8},{9,1},{17,9},{10,2},{18,10},{11,3},{19,11},{12,4},{20... | collective-permute-start | bytes 86024 | tf_op jit(solution)/shard_map/ppermute | solution.py:341
  65.5 5.5 %collective-permute-start.10 = (f32[14,128]{1,0:T(8,128)}, f32[14,128]{1,0:T(8,128)S(1)}, u32[]{:S(2)}, u32[]{:S(2)}) collective-permute-start(f32[14,128]{1,0:T(8,128)} %get-tuple-element.23), channel_id=1, source_target_pairs={{0,1},{1,2},{2,3},{3,4},{4,5},{5,6},{6,7},{7,0},{8,9},{9,10},{10,1... | collective-permute-start | bytes 21512 | tf_op jit(solution)/shard_map/ppermute | solution.py:342
  65.6 5.4 %collective-permute-start.11 = (f32[14,128]{1,0:T(8,128)}, f32[14,128]{1,0:T(8,128)S(1)}, u32[]{:S(2)}, u32[]{:S(2)}) collective-permute-start(f32[14,128]{1,0:T(8,128)} %get-tuple-element.24), channel_id=1, source_target_pairs={{1,0},{2,1},{3,2},{4,3},{5,4},{6,5},{7,6},{0,7},{9,8},{10,9},{11,1... | collective-permute-start | bytes 21512 | tf_op jit(solution)/shard_map/ppermute | solution.py:343
  71.0 0.6 copy-start.6
  71.0 0.6 copy-start.7
  71.0 0.6 copy-start.2
  71.0 0.6 copy-start.3

commit v13 on v12

--- a/solution.py
+++ b/solution.py
@@ -196,11 +196,11 @@
     )(mix, act, flags, fields, rate, halo_lo, halo_hi, swapped, lft, rgt)
 
 
-def interp_kernel(ks, flag_s, ids_s, wt_ref, table_ref, *refs):
+def interp_kernel(ks, width, flag_s, ids_s, wt_ref, table_ref, *refs):
     n_pass = (len(refs) - 3) // 2
     ins, o_ref, outs, acc, picked = refs[:n_pass], refs[n_pass], refs[n_pass + 1:-2], refs[-2], refs[-1]
     lanes = o_ref.shape[1]
-    width = table_ref.shape[1]
+    per_row = LANE // width
     acc[...] = jnp.zeros(acc.shape, jnp.float32)
 
     @pl.when(flag_s[0] + flag_s[1] > 0.5)
@@ -210,34 +210,35 @@
             for s in range(SUB):
                 for k in range(ks):
                     q = ids_s[k, p0 + s]
-                    picked[k, pl.ds(p0 + s, 1), :] = table_ref[pl.ds(q, 1), :]
+                    packed = table_ref[pl.ds(q // per_row, 1), :]
+                    shift = (LANE - (q % per_row) * width) % LANE
+                    picked[k, pl.ds(p0 + s, 1), :] = pltpu.roll(packed, shift, 1)
             return carry
 
         lax.fori_loop(0, lanes // SUB, group, 0)
         total = wt_ref[:, 0:1] * picked[0]
         for k in range(1, ks):
             total = total + wt_ref[:, k:k + 1] * picked[k]
-        acc[:, 0:width] = total
+        acc[...] = total
 
     o_ref[...] = jnp.transpose(acc[...])[0:o_ref.shape[0], :]
     for src, dst in zip(ins, outs):
         dst[...] = src[...]
 
 
-def interpolate(flags, ids, wt, table, passed):
+def interpolate(flags, ids, wt, table, width, passed):
     ks, lanes = ids.shape
     smem = pl.BlockSpec(memory_space=pltpu.SMEM)
     vspec = pl.BlockSpec(memory_space=pltpu.VMEM)
-    width = table.shape[1]
     return pl.pallas_call(
-        functools.partial(interp_kernel, ks),
-        out_shape=(jax.ShapeDtypeStruct((width, lanes), jnp.float32),)
+        functools.partial(interp_kernel, ks, width),
+        out_shape=(jax.ShapeDtypeStruct((width - 1, lanes), jnp.float32),)
         + tuple(jax.ShapeDtypeStruct(x.shape, x.dtype) for x in passed),
         in_specs=[smem, smem] + [vspec] * (2 + len(passed)),
         out_specs=(vspec,) * (1 + len(passed)),
         scratch_shapes=[
             pltpu.VMEM((lanes, LANE), jnp.float32),
-            pltpu.VMEM((ks, lanes, width), jnp.float32),
+            pltpu.VMEM((ks, lanes, LANE), jnp.float32),
         ],
     )(flags, ids, wt, table, *passed)
 
@@ -316,7 +317,9 @@
         partner = [(i, i ^ span) for i in range(n_blk)]
         planes = jnp.concatenate([planes, lax.ppermute(planes, "blk", partner)], axis=0)
         span //= 2
-    table = jnp.transpose(planes, (0, 2, 1)).reshape(n_blk * lanes, nf + 1)
+    width = 16
+    table = jnp.pad(jnp.transpose(planes, (0, 2, 1)), ((0, 0), (0, 0), (0, width - nf - 1)))
+    table = table.reshape(n_blk * lanes * width // LANE, LANE)
     at_exit = g == exit_grp
     ids = jnp.where(at_exit, inlet_ids, outlet_ids)
     m = jnp.bitwise_xor(ids // lanes, b)
@@ -330,7 +333,9 @@
     lft = lax.ppermute(fields[:, :, lanes - 1], "blk", [(i, (i + 1) % n_blk) for i in range(n_blk)])
     rgt = lax.ppermute(fields[:, :, 0], "blk", [((i + 1) % n_blk, i) for i in range(n_blk)])
 
-    swap, halo_lo, halo_hi, lft, rgt = interpolate(flags, ids, wt, table, (halo_lo, halo_hi, lft, rgt))
+    swap, halo_lo, halo_hi, lft, rgt = interpolate(
+        flags, ids, wt, table, width, (halo_lo, halo_hi, lft, rgt)
+    )
     swapped = lax.ppermute(swap, "grp", [(exit_grp, turb_grp), (turb_grp, exit_grp)])
 
     out, elo, ehi, clo, chi = fused_step(

time: 76.9 us -> 98.8 us (1.28)
  starting transfers between devices: 31.2 us -> 50 us
  local copies, waits for them, and re-layouts: 8.89 us -> 12.4 us
    ppermute x1, starting transfers between devices: 11.1 us -> 29.9 us  [shards(): g0 = lax.ppermute(ehi, 'grp', [(i, i + 1) for i in range(n_grp - 2)])]
    pad x0 -> x1, local copies, waits for them, and re-layouts: none -> 1.5 us  [shards(): jnp.pad(jnp.transpose(planes, (0, 2, 1)), ((0, 0), (0, 0), (0, width - nf...]
    unnamed x34 -> x35, local copies, waits for them, and re-layouts: 3.06 us -> 4.31 us
  transfers between devices with their start and end apart: 12 -> 12, of which waited for: 3 -> 3; matrix products, arithmetic and copies ran while one was open for 11% -> 12% of each run, Pallas kernels for 0% -> 0%
where the time goes in v13:
time: 98.8 us; the launch traced here: 97.8 us
  starting transfers between devices  50 us (51%)
  Pallas kernels  26.2 us (27%)
  local copies, waits for them, and re-layouts  12.4 us (13%)
  waiting for transfers between devices  6.09 us (6%)
  other arithmetic  2.8 us (3%)
    ppermute x1, starting transfers between devices, shards(): g0 = lax.ppermute(ehi, 'grp', [(i, i + 1) for i in range(n_grp - 2)])  29.9 us
    pallas_call x1, Pallas kernels, fused_step(): pl.pallas_call(functools.partial(step_kernel, nf, rows, lanes), out_shape...  20.1 us
    ppermute x3, waiting for transfers between devices, shards(): lax.ppermute(planes, 'blk', partner)  4.83 us
    ppermute x1, starting transfers between devices, shards(): lax.ppermute(last_row, 'grp', [(i, i + 1) for i in range(n_grp - 2)])  4.54 us
    pallas_call x1, Pallas kernels, fix_edges(): pl.pallas_call(functools.partial(fix_kernel, low_w, side_w), out_shape=ja...  4.34 us
    unnamed x35, local copies, waits for them, and re-layouts  4.31 us
    ppermute x1, starting transfers between devices, shards(): gr = lax.ppermute(clo, 'blk', [((i + 1) % n_blk, i) for i in range(n_blk)])  4.15 us
    ppermute x1, starting transfers between devices, shards(): lax.ppermute(fields[:, :, 0], 'blk', [((i + 1) % n_blk, i) for i in range...  2.97 us
  transfers between devices with their start and end apart: 12, of which 3 were waited for; matrix products, arithmetic and copies ran while one was open for 12% of the time, Pallas kernels for 0%

profile of v13, /device:TPU:1, one launch (start us, length us, event | category | flops | bytes accessed | tf_op | source)
XLA Modules:
  0.0 97.8 jit_solution(16280534628650641262)
XLA Ops:
  0.0 1.1 %fusion.13 = (f32[14,1,512]{2,1,0:T(1,128)S(1)}, f32[14,1,512]{2,1,0:T(1,128)S(1)}) fusion(f32[14,128,512]{2,1,0:T(8,128)} %f_hbm.1), kind=kLoop, calls=%fused_computation.44 | loop fusion | bytes 114688 | tf_op jit(solution)/shard_map/slice | solution.py:310
  1.1 4.5 %collective-permute-start.3 = (f32[14,512]{1,0:T(8,128)S(1)}, f32[14,512]{1,0:T(8,128)S(1)}, u32[]{:S(2)}, u32[]{:S(2)}) collective-permute-start(f32[14,512]{1,0:T(8,128)S(1)} %bitcast.18), channel_id=1, source_target_pairs={{0,8},{8,16},{1,9},{9,17},{2,10},{10,18},{3,11},{11,19},{4,12},{12... | collective-permute-start | bytes 86024 | tf_op jit(solution)/shard_map/ppermute | solution.py:331
  5.7 0.7 slice_bitcast_fusion
  6.4 0.0 copy-start.10
  6.4 2.4 %collective-permute-start = (f32[1,15,512]{2,1,0:T(8,128)S(1)}, f32[1,15,512]{2,1,0:T(8,128)S(1)}, u32[]{:S(2)}, u32[]{:S(2)}) collective-permute-start(f32[1,15,512]{2,1,0:T(8,128)S(1)} %maximum_bitcast_fusion.1), channel_id=1, source_target_pairs={{0,4},{1,5},{2,6},{3,7},{4,0},{5,1},{6,2},{7,3},{8,12},{9,13},{10,... | collective-permute-start | bytes 92168 | tf_op jit(solution)/shard_map/ppermute | solution.py:318
  8.8 2.0 %collective-permute-start.4 = (f32[14,512]{1,0:T(8,128)S(1)}, f32[14,512]{1,0:T(8,128)S(1)}, u32[]{:S(2)}, u32[]{:S(2)}) collective-permute-start(f32[14,512]{1,0:T(8,128)S(1)} %bitcast.20), channel_id=1, source_target_pairs={{8,0},{16,8},{9,1},{17,9},{10,2},{18,10},{11,3},{19,11},{12,4},{20... | collective-permute-start | bytes 86024 | tf_op jit(solution)/shard_map/ppermute | solution.py:332
  10.9 1.8 %fusion.12 = (f32[14,128,1]{2,1,0:T(8,128)S(1)}, f32[14,128,1]{2,1,0:T(8,128)S(1)}) fusion(f32[14,128,512]{2,1,0:T(8,128)} %f_hbm.1), kind=kLoop, calls=%fused_computation.43 | loop fusion | bytes 28672 | tf_op jit(solution)/shard_map/slice | solution.py:334
  12.7 0.3 copy.33
  13.0 1.2 %collective-permute-start.5 = (f32[14,128]{1,0:T(8,128)S(1)}, f32[14,128]{1,0:T(8,128)S(1)}, u32[]{:S(2)}, u32[]{:S(2)}) collective-permute-start(f32[14,128]{1,0:T(8,128)S(1)} %bitcast.21), channel_id=1, source_target_pairs={{0,1},{1,2},{2,3},{3,4},{4,5},{5,6},{6,7},{7,0},{8,9},{9,10},{10,1... | collective-permute-start | bytes 21512 | tf_op jit(solution)/shard_map/ppermute | solution.py:333
  14.2 0.3 copy.34
  14.6 3.0 %collective-permute-start.6 = (f32[14,128]{1,0:T(8,128)S(1)}, f32[14,128]{1,0:T(8,128)S(1)}, u32[]{:S(2)}, u32[]{:S(2)}) collective-permute-start(f32[14,128]{1,0:T(8,128)S(1)} %bitcast.22), channel_id=1, source_target_pairs={{1,0},{2,1},{3,2},{4,3},{5,4},{6,5},{7,6},{0,7},{9,8},{10,9},{11,1... | collective-permute-start | bytes 21512 | tf_op jit(solution)/shard_map/ppermute | solution.py:334
  17.5 0.0 copy-done.8
  17.5 0.1 copy.20
  17.7 0.0 copy-done.9
  17.7 0.1 copy.21
  17.9 0.0 collective-permute-done
  17.9 0.1 collective-permute-start.1
  18.0 0.8 add_select_fusion
  18.8 0.0 copy-done.10
  18.8 0.1 copy.24
  18.9 0.0 copy-done.11
  18.9 0.1 copy.25
  19.1 2.1 %collective-permute-done.1 = f32[2,15,512]{2,1,0:T(8,128)S(1)} collective-permute-done((f32[2,15,512]{2,1,0:T(8,128)S(1)}, f32[2,15,512]{2,1,0:T(8,128)S(1)}, u32[]{:S(2)}, u32[]{:S(2)}) %collective-permute-start.1) | collective-permute-done | bytes 61472 | tf_op jit(solution)/shard_map/ppermute | solution.py:318
  21.2 0.1 collective-permute-start.2
  21.2 0.7 select_bitcast_fusion.wt_ref
  22.0 0.1 copy.23
  22.1 0.1 copy.22
  22.2 0.6 add.39.ids_s
  22.8 0.6 add_convert_fusion.flag_s
  23.4 2.8 %collective-permute-done.2 = f32[4,15,512]{2,1,0:T(8,128)S(1)} collective-permute-done((f32[4,15,512]{2,1,0:T(8,128)S(1)}, f32[4,15,512]{2,1,0:T(8,128)S(1)}, u32[]{:S(2)}, u32[]{:S(2)}) %collective-permute-start.2) | collective-permute-done | bytes 122912 | tf_op jit(solution)/shard_map/ppermute | solution.py:318
  26.2 0.6 copy.35
  26.9 1.5 %pad.4.clone = f32[8,512,16]{2,1,0:T(8,128)} pad(f32[8,512,15]{2,1,0:T(8,128)S(1)} %copy.35, f32[]{:T(128)} %constant.90.clone.1), padding=0_0x0_0x0_1 | pad | bytes 507908 | tf_op jit(solution)/shard_map/jit(_pad)/pad | solution.py:321
  28.4 2.8 %reshape.4.table_ref = f32[512,128]{1,0:T(8,128)} reshape(f32[8,512,16]{2,1,0:T(8,128)} %pad.4.clone) | data formatting | bytes 524288 | tf_op jit(solution)/shard_map/reshape | solution.py:322
  31.1 0.0 collective-permute-done.5.refs_2_
  31.1 0.0 collective-permute-done.6.refs_3_
  31.1 0.0 copy-start.5
  31.1 0.0 collective-permute-done.3.refs_0_
  31.2 0.0 copy-start.2
  31.2 0.0 collective-permute-done.4.refs_1_
  31.2 0.5 copy-done.4
  31.7 0.0 copy-done.5
  31.7 0.0 copy-done.2
  31.8 0.6 copy-done.3
  32.4 1.8 %shard_map.82 = (f32[15,512]{1,0:T(8,128)}, f32[14,512]{1,0:T(8,128)}, f32[14,512]{1,0:T(8,128)}, f32[14,128]{1,0:T(8,128)}, f32[14,128]{1,0:T(8,128)}) custom-call(f32[2]{0:T(128)} %add_convert_fusion.flag_s, s32[4,512]{1,0:T(4,128)} %add.39.ids_s, f32[512,4]{1,0:T(8,128)} %select_bitcast_fusion.wt_ref, f32[512,128]{1,0:T(8,128)} %reshape.4.table_ref, ...), custom_call_target="tpu_custom_call" | custom-call | tf_op jit(solution)/shard_map/pallas_call | solution.py:233
  34.2 0.7 collective-permute-start.7
  34.8 0.0 collective-permute-done.7.sw_ref
  34.9 0.0 copy-start.12
  34.9 0.6 copy-done.12
  35.5 20.1 %shard_map.83 = (f32[14,128,512]{2,1,0:T(8,128)}, f32[14,512]{1,0:T(8,128)}, f32[14,512]{1,0:T(8,128)}, f32[14,128]{1,0:T(8,128)}, f32[14,128]{1,0:T(8,128)}) custom-call(f32[14,14]{1,0:T(8,128)} %mix_s.1, f32[14]{0:T(128)} %act_s.1, f32[2]{0:T(128)} %add_convert_fusion.flag_s, f32[14,128,512]{2,1,0:T(8,128)} %f_hbm.1, f32[128,512]{1,0:T(8,128)} %rate_ref.1, ...), custom_call_target="tpu_custom_call" | custom-call | flops 95420416 | bytes 7602176 | tf_op jit(solution)/shard_map/pallas_call | solution.py:176
  55.5 29.9 %collective-permute-start.8 = (f32[14,512]{1,0:T(8,128)}, f32[14,512]{1,0:T(8,128)S(1)}, u32[]{:S(2)}, u32[]{:S(2)}) collective-permute-start(f32[14,512]{1,0:T(8,128)} %get-tuple-element.21), channel_id=1, source_target_pairs={{0,8},{8,16},{1,9},{9,17},{2,10},{10,18},{3,11},{11,19},{4,12},{12... | collective-permute-start | bytes 86024 | tf_op jit(solution)/shard_map/ppermute | solution.py:345
  85.4 1.9 %collective-permute-start.9 = (f32[14,512]{1,0:T(8,128)}, f32[14,512]{1,0:T(8,128)S(1)}, u32[]{:S(2)}, u32[]{:S(2)}) collective-permute-start(f32[14,512]{1,0:T(8,128)} %get-tuple-element.22), channel_id=1, source_target_pairs={{8,0},{16,8},{9,1},{17,9},{10,2},{18,10},{11,3},{19,11},{12,4},{20... | collective-permute-start | bytes 86024 | tf_op jit(solution)/shard_map/ppermute | solution.py:346
  87.4 0.1 collective-permute-start.10
  87.4 4.2 %collective-permute-start.11 = (f32[14,128]{1,0:T(8,128)}, f32[14,128]{1,0:T(8,128)S(1)}, u32[]{:S(2)}, u32[]{:S(2)}) collective-permute-start(f32[14,128]{1,0:T(8,128)} %get-tuple-element.24), channel_id=1, source_target_pairs={{1,0},{2,1},{3,2},{4,3},{5,4},{6,5},{7,6},{0,7},{9,8},{10,9},{11,1... | collective-permute-start | bytes 21512 | tf_op jit(solution)/shard_map/ppermute | solution.py:348
  91.6 1.2 %collective-permute-done.10.gl_ref = f32[14,128]{1,0:T(8,128)S(1)} collective-permute-done((f32[14,128]{1,0:T(8,128)}, f32[14,128]{1,0:T(8,128)S(1)}, u32[]{:S(2)}, u32[]{:S(2)}) %collective-permute-start.10) | collective-permute-done | bytes 7200 | tf_op jit(solution)/shard_map/ppermute | solution.py:347
  92.8 0.0 collective-permute-done.11.gr_ref
  92.8 0.0 collective-permute-done.8.g0_ref
  92.8 0.0 copy-start
  92.8 0.0 collective-permute-done.9.g1_ref
  92.8 0.0 copy-start.1
  92.9 0.5 copy-done.6
  93.4 0.0 copy-done.7
  93.4 0.0 copy-done
  93.4 0.0 copy-done.1
  93.5 4.3 %shard_map.84 = f32[14,128,512]{2,1,0:T(8,128)} custom-call(f32[14,128,512]{2,1,0:T(8,128)} %get-tuple-element.20.out_in, f32[14,512]{1,0:T(8,128)} %copy-done, f32[14,512]{1,0:T(8,128)} %copy-done.1, f32[14,128]{1,0:T(8,128)} %copy-done.6, f32[14,128]{1,0:T(8,128)} %copy-done.7), custom_call_target="tpu_custom_call", output_to_operand_aliasing={{}: (0, {})} | custom-call | tf_op jit(solution)/shard_map/pallas_call | solution.py:283
  (13 shorter events, 0.1 us)
Async XLA Ops:
  0.0 17.5 %copy-start.8 = (s32[4,512]{1,0:T(4,128)S(1)}, s32[4,512]{1,0:T(4,128)}, u32[]{:S(2)}) copy-start(s32[4,512]{1,0:T(4,128)} %param.12) | copy-start | bytes 24580
  0.0 17.7 %copy-start.9 = (s32[4,512]{1,0:T(4,128)S(1)}, s32[4,512]{1,0:T(4,128)}, u32[]{:S(2)}) copy-start(s32[4,512]{1,0:T(4,128)} %param.14) | copy-start | bytes 24580
  1.1 30.0 %collective-permute-start.3 = (f32[14,512]{1,0:T(8,128)S(1)}, f32[14,512]{1,0:T(8,128)S(1)}, u32[]{:S(2)}, u32[]{:S(2)}) collective-permute-start(f32[14,512]{1,0:T(8,128)S(1)} %bitcast.18), channel_id=1, source_target_pairs={{0,8},{8,16},{1,9},{9,17},{2,10},{10,18},{3,11},{11,19},{4,12},{12... | collective-permute-start | bytes 86024 | tf_op jit(solution)/shard_map/ppermute | solution.py:331
  6.4 12.3 %copy-start.10 = (f32[4,512]{1,0:T(4,128)S(1)}, f32[4,512]{1,0:T(4,128)}, u32[]{:S(2)}) copy-start(f32[4,512]{1,0:T(4,128)} %param.13) | copy-start | bytes 24580
  6.4 11.4 %collective-permute-start = (f32[1,15,512]{2,1,0:T(8,128)S(1)}, f32[1,15,512]{2,1,0:T(8,128)S(1)}, u32[]{:S(2)}, u32[]{:S(2)}) collective-permute-start(f32[1,15,512]{2,1,0:T(8,128)S(1)} %maximum_bitcast_fusion.1), channel_id=1, source_target_pairs={{0,4},{1,5},{2,6},{3,7},{4,0},{5,1},{6,2},{7,3},{8,12},{9,13},{10,... | collective-permute-start | bytes 92168 | tf_op jit(solution)/shard_map/ppermute | solution.py:318
  8.8 10.1 %copy-start.11 = (f32[4,512]{1,0:T(4,128)S(1)}, f32[4,512]{1,0:T(4,128)}, u32[]{:S(2)}) copy-start(f32[4,512]{1,0:T(4,128)} %param.15) | copy-start | bytes 24580
  8.8 22.4 %collective-permute-start.4 = (f32[14,512]{1,0:T(8,128)S(1)}, f32[14,512]{1,0:T(8,128)S(1)}, u32[]{:S(2)}, u32[]{:S(2)}) collective-permute-start(f32[14,512]{1,0:T(8,128)S(1)} %bitcast.20), channel_id=1, source_target_pairs={{8,0},{16,8},{9,1},{17,9},{10,2},{18,10},{11,3},{19,11},{12,4},{20... | collective-permute-start | bytes 86024 | tf_op jit(solution)/shard_map/ppermute | solution.py:332
  13.0 18.1 %collective-permute-start.5 = (f32[14,128]{1,0:T(8,128)S(1)}, f32[14,128]{1,0:T(8,128)S(1)}, u32[]{:S(2)}, u32[]{:S(2)}) collective-permute-start(f32[14,128]{1,0:T(8,128)S(1)} %bitcast.21), channel_id=1, source_target_pairs={{0,1},{1,2},{2,3},{3,4},{4,5},{5,6},{6,7},{7,0},{8,9},{9,10},{10,1... | collective-permute-start | bytes 21512 | tf_op jit(solution)/shard_map/ppermute | solution.py:333
  14.6 16.6 %collective-permute-start.6 = (f32[14,128]{1,0:T(8,128)S(1)}, f32[14,128]{1,0:T(8,128)S(1)}, u32[]{:S(2)}, u32[]{:S(2)}) collective-permute-start(f32[14,128]{1,0:T(8,128)S(1)} %bitcast.22), channel_id=1, source_target_pairs={{1,0},{2,1},{3,2},{4,3},{5,4},{6,5},{7,6},{0,7},{9,8},{10,9},{11,1... | collective-permute-start | bytes 21512 | tf_op jit(solution)/shard_map/ppermute | solution.py:334
  17.9 3.3 %collective-permute-start.1 = (f32[2,15,512]{2,1,0:T(8,128)S(1)}, f32[2,15,512]{2,1,0:T(8,128)S(1)}, u32[]{:S(2)}, u32[]{:S(2)}) collective-permute-start(f32[2,15,512]{2,1,0:T(8,128)S(1)} %pad_maximum_fusion.1), channel_id=1, source_target_pairs={{0,2},{1,3},{2,0},{3,1},{4,6},{5,7},{6,4},{7,5},{8,10},{9,11},{10,... | collective-permute-start | bytes 184328 | tf_op jit(solution)/shard_map/ppermute | solution.py:318
  21.2 5.0 %collective-permute-start.2 = (f32[4,15,512]{2,1,0:T(8,128)S(1)}, f32[4,15,512]{2,1,0:T(8,128)S(1)}, u32[]{:S(2)}, u32[]{:S(2)}) collective-permute-start(f32[4,15,512]{2,1,0:T(8,128)S(1)} %pad_maximum_fusion), channel_id=1, source_target_pairs={{0,1},{1,0},{2,3},{3,2},{4,5},{5,4},{6,7},{7,6},{8,9},{9,8},{10,11... | collective-permute-start | bytes 368648 | tf_op jit(solution)/shard_map/ppermute | solution.py:318
  31.1 0.6 copy-start.4
  31.1 0.6 copy-start.5
  31.2 0.6 copy-start.2
  31.8 0.6 copy-start.3
  34.2 0.7 collective-permute-start.7
  34.9 0.6 copy-start.12
  55.5 37.3 %collective-permute-start.8 = (f32[14,512]{1,0:T(8,128)}, f32[14,512]{1,0:T(8,128)S(1)}, u32[]{:S(2)}, u32[]{:S(2)}) collective-permute-start(f32[14,512]{1,0:T(8,128)} %get-tuple-element.21), channel_id=1, source_target_pairs={{0,8},{8,16},{1,9},{9,17},{2,10},{10,18},{3,11},{11,19},{4,12},{12... | collective-permute-start | bytes 86024 | tf_op jit(solution)/shard_map/ppermute | solution.py:345
  85.4 7.4 %collective-permute-start.9 = (f32[14,512]{1,0:T(8,128)}, f32[14,512]{1,0:T(8,128)S(1)}, u32[]{:S(2)}, u32[]{:S(2)}) collective-permute-start(f32[14,512]{1,0:T(8,128)} %get-tuple-element.22), channel_id=1, source_target_pairs={{8,0},{16,8},{9,1},{17,9},{10,2},{18,10},{11,3},{19,11},{12,4},{20... | collective-permute-start | bytes 86024 | tf_op jit(solution)/shard_map/ppermute | solution.py:346
  87.4 5.5 %collective-permute-start.10 = (f32[14,128]{1,0:T(8,128)}, f32[14,128]{1,0:T(8,128)S(1)}, u32[]{:S(2)}, u32[]{:S(2)}) collective-permute-start(f32[14,128]{1,0:T(8,128)} %get-tuple-element.23), channel_id=1, source_target_pairs={{0,1},{1,2},{2,3},{3,4},{4,5},{5,6},{6,7},{7,0},{8,9},{9,10},{10,1... | collective-permute-start | bytes 21512 | tf_op jit(solution)/shard_map/ppermute | solution.py:347
  87.4 5.4 %collective-permute-start.11 = (f32[14,128]{1,0:T(8,128)}, f32[14,128]{1,0:T(8,128)S(1)}, u32[]{:S(2)}, u32[]{:S(2)}) collective-permute-start(f32[14,128]{1,0:T(8,128)} %get-tuple-element.24), channel_id=1, source_target_pairs={{1,0},{2,1},{3,2},{4,3},{5,4},{6,5},{7,6},{0,7},{9,8},{10,9},{11,1... | collective-permute-start | bytes 21512 | tf_op jit(solution)/shard_map/ppermute | solution.py:348
  92.8 0.6 copy-start.6
  92.8 0.6 copy-start.7
  92.8 0.6 copy-start
  92.8 0.6 copy-start.1

commit v14 on v12

--- a/solution.py
+++ b/solution.py
@@ -311,8 +311,11 @@
     planes = payload[None]
     spans = []
     span = n_blk // 2
+    edges = (last_row, first_row, fields[:, :, lanes - 1], fields[:, :, 0])
     while span >= 1:
         spans.append(span)
+        if span == 1:
+            edges, planes = lax.optimization_barrier((edges, planes))
         partner = [(i, i ^ span) for i in range(n_blk)]
         planes = jnp.concatenate([planes, lax.ppermute(planes, "blk", partner)], axis=0)
         span //= 2
@@ -325,10 +328,10 @@
         slot = slot + ((m // span) % 2) * (1 << r)
     ids = slot * lanes + ids % lanes
     wt = jnp.transpose(jnp.where(at_exit, inlet_weights, outlet_weights))
-    halo_lo = lax.ppermute(last_row, "grp", [(i, i + 1) for i in range(n_grp - 2)])
-    halo_hi = lax.ppermute(first_row, "grp", [(i + 1, i) for i in range(n_grp - 2)])
-    lft = lax.ppermute(fields[:, :, lanes - 1], "blk", [(i, (i + 1) % n_blk) for i in range(n_blk)])
-    rgt = lax.ppermute(fields[:, :, 0], "blk", [((i + 1) % n_blk, i) for i in range(n_blk)])
+    halo_lo = lax.ppermute(edges[0], "grp", [(i, i + 1) for i in range(n_grp - 2)])
+    halo_hi = lax.ppermute(edges[1], "grp", [(i + 1, i) for i in range(n_grp - 2)])
+    lft = lax.ppermute(edges[2], "blk", [(i, (i + 1) % n_blk) for i in range(n_blk)])
+    rgt = lax.ppermute(edges[3], "blk", [((i + 1) % n_blk, i) for i in range(n_blk)])
 
     swap, halo_lo, halo_hi, lft, rgt = interpolate(flags, ids, wt, table, (halo_lo, halo_hi, lft, rgt))
     swapped = lax.ppermute(swap, "grp", [(exit_grp, turb_grp), (turb_grp, exit_grp)])

time: 76.9 us -> 75.3 us (0.979)
  waiting for transfers between devices: 6.14 us -> 2.53 us
  starting transfers between devices: 31.2 us -> 33.2 us
    ppermute x3, waiting for transfers between devices: 4.88 us -> 0.01 us  [shards(): lax.ppermute(planes, 'blk', partner)]
    ppermute x3, starting transfers between devices: 2.52 us -> 5.84 us  [shards(): lax.ppermute(planes, 'blk', partner)]
    ppermute x1, starting transfers between devices: 11.1 us -> 8.2 us  [shards(): g0 = lax.ppermute(ehi, 'grp', [(i, i + 1) for i in range(n_grp - 2)])]
    ppermute x4, starting transfers between devices: 10.8 us -> 12.3 us  [the longest x1 6.26 us: shards(): lax.ppermute(edges[0], 'grp', [(i, i + 1) for i in range(n_grp - 2)])]
    ppermute x4, waiting for transfers between devices: 0.01 us -> 1.26 us  [the longest x1 1.25 us: shards(): lax.ppermute(edges[1], 'grp', [(i + 1, i) for i in range(n_grp - 2)])]
  transfers between devices with their start and end apart: 12 -> 12, of which waited for: 3 -> 2; matrix products, arithmetic and copies ran while one was open for 11% -> 11% of each run, Pallas kernels for 0% -> 0%
where the time goes in v14:
time: 75.3 us; the launch traced here: 74.4 us
  starting transfers between devices  33.2 us (44%)
  Pallas kernels  26.8 us (36%)
  local copies, waits for them, and re-layouts  8.92 us (12%)
  other arithmetic  2.76 us (4%)
  waiting for transfers between devices  2.53 us (3%)
    pallas_call x1, Pallas kernels, fused_step(): pl.pallas_call(functools.partial(step_kernel, nf, rows, lanes), out_shape...  20.1 us
    ppermute x1, starting transfers between devices, shards(): g0 = lax.ppermute(ehi, 'grp', [(i, i + 1) for i in range(n_grp - 2)])  8.2 us
    ppermute x1, starting transfers between devices, shards(): lax.ppermute(edges[0], 'grp', [(i, i + 1) for i in range(n_grp - 2)])  6.26 us
    ppermute x3, starting transfers between devices, shards(): lax.ppermute(planes, 'blk', partner)  5.84 us
    pallas_call x1, Pallas kernels, fix_edges(): pl.pallas_call(functools.partial(fix_kernel, low_w, side_w), out_shape=ja...  4.34 us
    ppermute x1, starting transfers between devices, shards(): gr = lax.ppermute(clo, 'blk', [((i + 1) % n_blk, i) for i in range(n_blk)])  4.15 us
    ppermute x1, starting transfers between devices, shards(): lax.ppermute(edges[3], 'blk', [((i + 1) % n_blk, i) for i in range(n_blk)])  3.91 us
    unnamed x34, local copies, waits for them, and re-layouts  3.07 us
  transfers between devices with their start and end apart: 12, of which 2 were waited for; matrix products, arithmetic and copies ran while one was open for 11% of the time, Pallas kernels for 0%

profile of v14, /device:TPU:1, one launch (start us, length us, event | category | flops | bytes accessed | tf_op | source)
XLA Modules:
  0.0 74.4 jit_solution(232605661091867619)
XLA Ops:
  0.0 0.0 copy-start.8
  0.0 0.0 copy-start.9
  0.0 0.0 copy-start.11
  0.0 0.8 %slice_bitcast_fusion = f32[1,512]{1,0:T(1,128)S(1)} fusion(f32[14,128,512]{2,1,0:T(8,128)} %f_hbm.1), kind=kLoop, calls=%fused_computation.41 | loop fusion | bytes 4096 | tf_op jit(solution)/shard_map/slice | solution.py:310
  0.8 1.1 %fusion.13 = (f32[14,1,512]{2,1,0:T(1,128)S(1)}, f32[14,1,512]{2,1,0:T(1,128)S(1)}) fusion(f32[14,128,512]{2,1,0:T(8,128)} %f_hbm.1), kind=kLoop, calls=%fused_computation.44 | loop fusion | bytes 114688 | tf_op jit(solution)/shard_map/slice | solution.py:309
  1.9 3.2 %collective-permute-start = (f32[1,15,512]{2,1,0:T(8,128)S(1)}, f32[1,15,512]{2,1,0:T(8,128)S(1)}, u32[]{:S(2)}, u32[]{:S(2)}) collective-permute-start(f32[1,15,512]{2,1,0:T(8,128)S(1)} %maximum_bitcast_fusion.1), channel_id=1, source_target_pairs={{0,4},{1,5},{2,6},{3,7},{4,0},{5,1},{6,2},{7,3},{8,12},{9,13},{10,... | collective-permute-start | bytes 92168 | tf_op jit(solution)/shard_map/ppermute | solution.py:320
  5.1 1.8 %fusion.12 = (f32[14,128,1]{2,1,0:T(8,128)S(1)}, f32[14,128,1]{2,1,0:T(8,128)S(1)}) fusion(f32[14,128,512]{2,1,0:T(8,128)} %f_hbm.1), kind=kLoop, calls=%fused_computation.43 | loop fusion | bytes 28672 | tf_op jit(solution)/shard_map/slice | solution.py:314
  6.9 0.0 copy-done.8
  6.9 0.1 copy.20
  7.1 0.0 copy-done.9
  7.1 0.1 copy.21
  7.2 0.0 collective-permute-done
  7.3 1.4 %collective-permute-start.1 = (f32[2,15,512]{2,1,0:T(8,128)S(1)}, f32[2,15,512]{2,1,0:T(8,128)S(1)}, u32[]{:S(2)}, u32[]{:S(2)}) collective-permute-start(f32[2,15,512]{2,1,0:T(8,128)S(1)} %pad_maximum_fusion.1), channel_id=1, source_target_pairs={{0,2},{1,3},{2,0},{3,1},{4,6},{5,7},{6,4},{7,5},{8,10},{9,11},{10,... | collective-permute-start | bytes 184328 | tf_op jit(solution)/shard_map/ppermute | solution.py:320
  8.6 0.8 %add_select_fusion = (s32[4,512]{0,1:T(8,128)S(1)}, s32[4,512]{0,1:T(8,128)S(1)}) fusion(s32[4,512]{0,1:T(8,128)S(1)} %copy.20, s32[4,512]{0,1:T(8,128)S(1)} %copy.21, pred[]{:T(512)} %eq.12, s32[]{:T(128)S(6)} %axis_index.25), kind=kLoop, calls=%fused_computation | loop fusion | flops 157696 | bytes 32773 | tf_op jit(solution)/shard_map/jit(remainder)/select_n | solution.py:329
  9.4 0.0 copy-done.10
  9.5 0.1 copy.24
  9.6 0.0 copy-done.11
  9.6 0.1 copy.25
  9.8 0.3 copy.37
  10.1 0.3 copy.36
  10.4 0.0 collective-permute-done.1
  10.5 1.3 %collective-permute-start.2 = (f32[4,15,512]{2,1,0:T(8,128)S(1)}, f32[4,15,512]{2,1,0:T(8,128)S(1)}, u32[]{:S(2)}, u32[]{:S(2)}) collective-permute-start(f32[4,15,512]{2,1,0:T(8,128)S(1)} %pad_maximum_fusion), channel_id=1, source_target_pairs={{0,1},{1,0},{2,3},{3,2},{4,5},{5,4},{6,7},{7,6},{8,9},{9,8},{10,11... | collective-permute-start | bytes 368648 | tf_op jit(solution)/shard_map/ppermute | solution.py:320
  11.8 0.7 select_bitcast_fusion.wt_ref
  12.5 0.1 copy.23
  12.6 0.1 copy.22
  12.7 0.6 add.37.ids_s
  13.3 0.6 add_convert_fusion.flag_s
  13.9 0.3 collective-permute-start.5
  14.1 3.9 %collective-permute-start.6 = (f32[14,128]{1,0:T(8,128)S(1)}, f32[14,128]{1,0:T(8,128)S(1)}, u32[]{:S(2)}, u32[]{:S(2)}) collective-permute-start(f32[14,128]{1,0:T(8,128)S(1)} %bitcast.23), channel_id=1, source_target_pairs={{1,0},{2,1},{3,2},{4,3},{5,4},{6,5},{7,6},{0,7},{9,8},{10,9},{11,1... | collective-permute-start | bytes 21512 | tf_op jit(solution)/shard_map/ppermute | solution.py:334
  18.0 6.3 %collective-permute-start.3 = (f32[14,512]{1,0:T(8,128)S(1)}, f32[14,512]{1,0:T(8,128)S(1)}, u32[]{:S(2)}, u32[]{:S(2)}) collective-permute-start(f32[14,512]{1,0:T(8,128)S(1)} %bitcast.21), channel_id=1, source_target_pairs={{0,8},{8,16},{1,9},{9,17},{2,10},{10,18},{3,11},{11,19},{4,12},{12... | collective-permute-start | bytes 86024 | tf_op jit(solution)/shard_map/ppermute | solution.py:331
  24.3 1.9 %collective-permute-start.4 = (f32[14,512]{1,0:T(8,128)S(1)}, f32[14,512]{1,0:T(8,128)S(1)}, u32[]{:S(2)}, u32[]{:S(2)}) collective-permute-start(f32[14,512]{1,0:T(8,128)S(1)} %bitcast.22), channel_id=1, source_target_pairs={{8,0},{16,8},{9,1},{17,9},{10,2},{18,10},{11,3},{19,11},{12,4},{20... | collective-permute-start | bytes 86024 | tf_op jit(solution)/shard_map/ppermute | solution.py:332
  26.2 0.0 collective-permute-done.2
  26.3 2.0 %copy.32 = f32[8,512,15]{2,1,0:T(8,128)} copy(f32[8,512,15]{1,2,0:T(8,128)S(1)} %maximum_bitcast_fusion) | data formatting | bytes 491520 | tf_op jit(solution)/shard_map/reshape | solution.py:322
  28.2 0.0 collective-permute-done.5.refs_2_
  28.3 0.0 collective-permute-done.6.refs_3_
  28.3 0.0 copy-start.5
  28.3 0.0 collective-permute-done.3.refs_0_
  28.3 0.0 copy-start
  28.3 1.3 %collective-permute-done.4.refs_1_ = f32[14,512]{1,0:T(8,128)S(1)} collective-permute-done((f32[14,512]{1,0:T(8,128)S(1)}, f32[14,512]{1,0:T(8,128)S(1)}, u32[]{:S(2)}, u32[]{:S(2)}) %collective-permute-start.4) | collective-permute-done | bytes 28704 | tf_op jit(solution)/shard_map/ppermute | solution.py:332
  29.5 0.0 copy-done.4
  29.6 0.0 copy-done.5
  29.6 0.0 copy-done
  29.6 0.6 copy-done.1
  30.1 2.3 %shard_map.82 = (f32[15,512]{1,0:T(8,128)}, f32[14,512]{1,0:T(8,128)}, f32[14,512]{1,0:T(8,128)}, f32[14,128]{1,0:T(8,128)}, f32[14,128]{1,0:T(8,128)}) custom-call(f32[2]{0:T(128)} %add_convert_fusion.flag_s, s32[4,512]{1,0:T(4,128)} %add.37.ids_s, f32[512,4]{1,0:T(8,128)} %select_bitcast_fusion.wt_ref, f32[4096,15]{1,0:T(8,128)} %bitcast.19, ...), custom_call_target="tpu_custom_call" | custom-call | tf_op jit(solution)/shard_map/pallas_call | solution.py:232
  32.5 0.7 collective-permute-start.7
  33.1 0.0 collective-permute-done.7.sw_ref
  33.2 0.0 copy-start.12
  33.2 0.6 copy-done.12
  33.8 20.1 %shard_map.83 = (f32[14,128,512]{2,1,0:T(8,128)}, f32[14,512]{1,0:T(8,128)}, f32[14,512]{1,0:T(8,128)}, f32[14,128]{1,0:T(8,128)}, f32[14,128]{1,0:T(8,128)}) custom-call(f32[14,14]{1,0:T(8,128)} %mix_s.1, f32[14]{0:T(128)} %act_s.1, f32[2]{0:T(128)} %add_convert_fusion.flag_s, f32[14,128,512]{2,1,0:T(8,128)} %f_hbm.1, f32[128,512]{1,0:T(8,128)} %rate_ref.1, ...), custom_call_target="tpu_custom_call" | custom-call | flops 95420416 | bytes 7602176 | tf_op jit(solution)/shard_map/pallas_call | solution.py:176
  53.9 8.2 %collective-permute-start.8 = (f32[14,512]{1,0:T(8,128)}, f32[14,512]{1,0:T(8,128)S(1)}, u32[]{:S(2)}, u32[]{:S(2)}) collective-permute-start(f32[14,512]{1,0:T(8,128)} %get-tuple-element.31), channel_id=1, source_target_pairs={{0,8},{8,16},{1,9},{9,17},{2,10},{10,18},{3,11},{11,19},{4,12},{12... | collective-permute-start | bytes 86024 | tf_op jit(solution)/shard_map/ppermute | solution.py:343
  62.1 1.9 %collective-permute-start.9 = (f32[14,512]{1,0:T(8,128)}, f32[14,512]{1,0:T(8,128)S(1)}, u32[]{:S(2)}, u32[]{:S(2)}) collective-permute-start(f32[14,512]{1,0:T(8,128)} %get-tuple-element.32), channel_id=1, source_target_pairs={{8,0},{16,8},{9,1},{17,9},{10,2},{18,10},{11,3},{19,11},{12,4},{20... | collective-permute-start | bytes 86024 | tf_op jit(solution)/shard_map/ppermute | solution.py:344
  64.0 0.1 collective-permute-start.10
  64.1 4.2 %collective-permute-start.11 = (f32[14,128]{1,0:T(8,128)}, f32[14,128]{1,0:T(8,128)S(1)}, u32[]{:S(2)}, u32[]{:S(2)}) collective-permute-start(f32[14,128]{1,0:T(8,128)} %get-tuple-element.34), channel_id=1, source_target_pairs={{1,0},{2,1},{3,2},{4,3},{5,4},{6,5},{7,6},{0,7},{9,8},{10,9},{11,1... | collective-permute-start | bytes 21512 | tf_op jit(solution)/shard_map/ppermute | solution.py:346
  68.2 1.2 %collective-permute-done.10.gl_ref = f32[14,128]{1,0:T(8,128)S(1)} collective-permute-done((f32[14,128]{1,0:T(8,128)}, f32[14,128]{1,0:T(8,128)S(1)}, u32[]{:S(2)}, u32[]{:S(2)}) %collective-permute-start.10) | collective-permute-done | bytes 7200 | tf_op jit(solution)/shard_map/ppermute | solution.py:345
  69.4 0.0 collective-permute-done.11.gr_ref
  69.5 0.0 collective-permute-done.8.g0_ref
  69.5 0.0 copy-start.2
  69.5 0.0 collective-permute-done.9.g1_ref
  69.5 0.0 copy-start.3
  69.5 0.5 copy-done.6
  70.0 0.0 copy-done.7
  70.0 0.0 copy-done.2
  70.1 0.0 copy-done.3
  70.1 4.3 %shard_map.84 = f32[14,128,512]{2,1,0:T(8,128)} custom-call(f32[14,128,512]{2,1,0:T(8,128)} %get-tuple-element.30.out_in, f32[14,512]{1,0:T(8,128)} %copy-done.2, f32[14,512]{1,0:T(8,128)} %copy-done.3, f32[14,128]{1,0:T(8,128)} %copy-done.6, f32[14,128]{1,0:T(8,128)} %copy-done.7), custom_call_target="tpu_custom_call", output_to_operand_aliasing={{}: (0, {})} | custom-call | tf_op jit(solution)/shard_map/pallas_call | solution.py:282
  (11 shorter events, 0.1 us)
Async XLA Ops:
  0.0 6.9 %copy-start.8 = (s32[4,512]{1,0:T(4,128)S(1)}, s32[4,512]{1,0:T(4,128)}, u32[]{:S(2)}) copy-start(s32[4,512]{1,0:T(4,128)} %param.12) | copy-start | bytes 24580
  0.0 7.1 %copy-start.9 = (s32[4,512]{1,0:T(4,128)S(1)}, s32[4,512]{1,0:T(4,128)}, u32[]{:S(2)}) copy-start(s32[4,512]{1,0:T(4,128)} %param.14) | copy-start | bytes 24580
  0.0 9.4 %copy-start.10 = (f32[4,512]{1,0:T(4,128)S(1)}, f32[4,512]{1,0:T(4,128)}, u32[]{:S(2)}) copy-start(f32[4,512]{1,0:T(4,128)} %param.13) | copy-start | bytes 24580
  0.0 9.6 %copy-start.11 = (f32[4,512]{1,0:T(4,128)S(1)}, f32[4,512]{1,0:T(4,128)}, u32[]{:S(2)}) copy-start(f32[4,512]{1,0:T(4,128)} %param.15) | copy-start | bytes 24580
  1.9 5.3 %collective-permute-start = (f32[1,15,512]{2,1,0:T(8,128)S(1)}, f32[1,15,512]{2,1,0:T(8,128)S(1)}, u32[]{:S(2)}, u32[]{:S(2)}) collective-permute-start(f32[1,15,512]{2,1,0:T(8,128)S(1)} %maximum_bitcast_fusion.1), channel_id=1, source_target_pairs={{0,4},{1,5},{2,6},{3,7},{4,0},{5,1},{6,2},{7,3},{8,12},{9,13},{10,... | collective-permute-start | bytes 92168 | tf_op jit(solution)/shard_map/ppermute | solution.py:320
  7.3 3.2 %collective-permute-start.1 = (f32[2,15,512]{2,1,0:T(8,128)S(1)}, f32[2,15,512]{2,1,0:T(8,128)S(1)}, u32[]{:S(2)}, u32[]{:S(2)}) collective-permute-start(f32[2,15,512]{2,1,0:T(8,128)S(1)} %pad_maximum_fusion.1), channel_id=1, source_target_pairs={{0,2},{1,3},{2,0},{3,1},{4,6},{5,7},{6,4},{7,5},{8,10},{9,11},{10,... | collective-permute-start | bytes 184328 | tf_op jit(solution)/shard_map/ppermute | solution.py:320
  10.5 15.8 %collective-permute-start.2 = (f32[4,15,512]{2,1,0:T(8,128)S(1)}, f32[4,15,512]{2,1,0:T(8,128)S(1)}, u32[]{:S(2)}, u32[]{:S(2)}) collective-permute-start(f32[4,15,512]{2,1,0:T(8,128)S(1)} %pad_maximum_fusion), channel_id=1, source_target_pairs={{0,1},{1,0},{2,3},{3,2},{4,5},{5,4},{6,7},{7,6},{8,9},{9,8},{10,11... | collective-permute-start | bytes 368648 | tf_op jit(solution)/shard_map/ppermute | solution.py:320
  13.9 14.4 %collective-permute-start.5 = (f32[14,128]{1,0:T(8,128)S(1)}, f32[14,128]{1,0:T(8,128)S(1)}, u32[]{:S(2)}, u32[]{:S(2)}) collective-permute-start(f32[14,128]{1,0:T(8,128)S(1)} %bitcast.24), channel_id=1, source_target_pairs={{0,1},{1,2},{2,3},{3,4},{4,5},{5,6},{6,7},{7,0},{8,9},{9,10},{10,1... | collective-permute-start | bytes 21512 | tf_op jit(solution)/shard_map/ppermute | solution.py:333
  14.1 14.1 %collective-permute-start.6 = (f32[14,128]{1,0:T(8,128)S(1)}, f32[14,128]{1,0:T(8,128)S(1)}, u32[]{:S(2)}, u32[]{:S(2)}) collective-permute-start(f32[14,128]{1,0:T(8,128)S(1)} %bitcast.23), channel_id=1, source_target_pairs={{1,0},{2,1},{3,2},{4,3},{5,4},{6,5},{7,6},{0,7},{9,8},{10,9},{11,1... | collective-permute-start | bytes 21512 | tf_op jit(solution)/shard_map/ppermute | solution.py:334
  18.0 10.2 %collective-permute-start.3 = (f32[14,512]{1,0:T(8,128)S(1)}, f32[14,512]{1,0:T(8,128)S(1)}, u32[]{:S(2)}, u32[]{:S(2)}) collective-permute-start(f32[14,512]{1,0:T(8,128)S(1)} %bitcast.21), channel_id=1, source_target_pairs={{0,8},{8,16},{1,9},{9,17},{2,10},{10,18},{3,11},{11,19},{4,12},{12... | collective-permute-start | bytes 86024 | tf_op jit(solution)/shard_map/ppermute | solution.py:331
  24.3 5.2 %collective-permute-start.4 = (f32[14,512]{1,0:T(8,128)S(1)}, f32[14,512]{1,0:T(8,128)S(1)}, u32[]{:S(2)}, u32[]{:S(2)}) collective-permute-start(f32[14,512]{1,0:T(8,128)S(1)} %bitcast.22), channel_id=1, source_target_pairs={{8,0},{16,8},{9,1},{17,9},{10,2},{18,10},{11,3},{19,11},{12,4},{20... | collective-permute-start | bytes 86024 | tf_op jit(solution)/shard_map/ppermute | solution.py:332
  28.3 1.3 %copy-start.4 = (f32[14,128]{1,0:T(8,128)}, f32[14,128]{1,0:T(8,128)S(1)}, u32[]{:S(2)}) copy-start(f32[14,128]{1,0:T(8,128)S(1)} %collective-permute-done.5.refs_2_) | copy-start | bytes 21508
  28.3 1.3 %copy-start.5 = (f32[14,128]{1,0:T(8,128)}, f32[14,128]{1,0:T(8,128)S(1)}, u32[]{:S(2)}) copy-start(f32[14,128]{1,0:T(8,128)S(1)} %collective-permute-done.6.refs_3_) | copy-start | bytes 21508
  28.3 1.3 %copy-start = (f32[14,512]{1,0:T(8,128)}, f32[14,512]{1,0:T(8,128)S(1)}, u32[]{:S(2)}) copy-start(f32[14,512]{1,0:T(8,128)S(1)} %collective-permute-done.3.refs_0_) | copy-start | bytes 86020
  29.5 0.6 copy-start.1
  32.5 0.7 collective-permute-start.7
  33.2 0.6 copy-start.12
  53.9 15.6 %collective-permute-start.8 = (f32[14,512]{1,0:T(8,128)}, f32[14,512]{1,0:T(8,128)S(1)}, u32[]{:S(2)}, u32[]{:S(2)}) collective-permute-start(f32[14,512]{1,0:T(8,128)} %get-tuple-element.31), channel_id=1, source_target_pairs={{0,8},{8,16},{1,9},{9,17},{2,10},{10,18},{3,11},{11,19},{4,12},{12... | collective-permute-start | bytes 86024 | tf_op jit(solution)/shard_map/ppermute | solution.py:343
  62.1 7.4 %collective-permute-start.9 = (f32[14,512]{1,0:T(8,128)}, f32[14,512]{1,0:T(8,128)S(1)}, u32[]{:S(2)}, u32[]{:S(2)}) collective-permute-start(f32[14,512]{1,0:T(8,128)} %get-tuple-element.32), channel_id=1, source_target_pairs={{8,0},{16,8},{9,1},{17,9},{10,2},{18,10},{11,3},{19,11},{12,4},{20... | collective-permute-start | bytes 86024 | tf_op jit(solution)/shard_map/ppermute | solution.py:344
  64.0 5.5 %collective-permute-start.10 = (f32[14,128]{1,0:T(8,128)}, f32[14,128]{1,0:T(8,128)S(1)}, u32[]{:S(2)}, u32[]{:S(2)}) collective-permute-start(f32[14,128]{1,0:T(8,128)} %get-tuple-element.33), channel_id=1, source_target_pairs={{0,1},{1,2},{2,3},{3,4},{4,5},{5,6},{6,7},{7,0},{8,9},{9,10},{10,1... | collective-permute-start | bytes 21512 | tf_op jit(solution)/shard_map/ppermute | solution.py:345
  64.1 5.4 %collective-permute-start.11 = (f32[14,128]{1,0:T(8,128)}, f32[14,128]{1,0:T(8,128)S(1)}, u32[]{:S(2)}, u32[]{:S(2)}) collective-permute-start(f32[14,128]{1,0:T(8,128)} %get-tuple-element.34), channel_id=1, source_target_pairs={{1,0},{2,1},{3,2},{4,3},{5,4},{6,5},{7,6},{0,7},{9,8},{10,9},{11,1... | collective-permute-start | bytes 21512 | tf_op jit(solution)/shard_map/ppermute | solution.py:346
  69.4 0.6 copy-start.6
  69.5 0.6 copy-start.7
  69.5 0.6 copy-start.2
  69.5 0.6 copy-start.3

commit v15 on v14

--- a/solution.py
+++ b/solution.py
@@ -20,7 +20,7 @@
     return jnp.transpose(jnp.broadcast_to(row, (n, n)))
 
 
-def step_kernel(nf, rows, lanes, mix_s, act_s, flag_s, f_hbm, rate_ref, hlo_ref, hhi_ref, sw_ref,
+def step_kernel(nf, rows, lanes, mix_s, act_s, flag_s, f_hbm, rate_ref, hlo_ref, hhi_ref,
                 lft_ref, rgt_ref, out_hbm, elo_ref, ehi_ref, clo_ref, chi_ref, ext1, ext2, coef, obuf,
                 sem):
     n_i = rows // SUB
@@ -35,9 +35,9 @@
     copy.start()
     zeros = jnp.zeros((rows, LANE), jnp.float32)
     for f in range(nf):
-        inlet = sw_ref[f:f + 1, :]
-        ext1[f, SUB - 1:SUB, LANE:right] = jnp.where(at_turb, inlet, hlo_ref[f:f + 1, :])
-        ext2[f, SUB - 1:SUB, LANE:right] = jnp.where(at_turb, inlet, 0.0)
+        low = hlo_ref[f:f + 1, :]
+        ext1[f, SUB - 1:SUB, LANE:right] = low
+        ext2[f, SUB - 1:SUB, LANE:right] = jnp.where(at_turb, low, 0.0)
         ext1[f, SUB:top, 0:LANE] = tile_t(lft_ref[f:f + 1, :])
         ext1[f, SUB:top, right:right + LANE] = tile_t(rgt_ref[f:f + 1, :])
         ext2[f, SUB:top, 0:LANE] = zeros
@@ -48,17 +48,17 @@
         coef[nf * nf + f] = jnp.full((SUB, LANE), -act_s[f], jnp.float32)
     copy.wait()
 
-    def high_ghost(ext, halo_of):
+    def high_ghost(ext, outside):
         for f in range(nf):
             own = ext[f, top - 1:top, LANE:right]
-            halo = halo_of(f)
+            halo = hhi_ref[f:f + 1, :]
             if f == 4:
-                row = jnp.where(at_turb, own, jnp.where(at_exit, sw_ref[nf:nf + 1, :], halo))
+                row = jnp.where(at_turb, own, jnp.where(at_exit | outside, halo, 0.0))
             else:
-                row = jnp.where(at_end, own, halo)
+                row = jnp.where(at_end, own, jnp.where(outside, halo, 0.0))
             ext[f, top:top + 1, LANE:right] = row
 
-    high_ghost(ext1, lambda f: hhi_ref[f:f + 1, :])
+    high_ghost(ext1, True)
 
     sub_id = lax.broadcasted_iota(jnp.int32, (SUB, LANE), 0)
     lane_id = lax.broadcasted_iota(jnp.int32, (SUB, LANE), 1)
@@ -130,7 +130,7 @@
 
     lax.fori_loop(0, n_i * n_jp, stage_one, 0)
 
-    high_ghost(ext2, lambda f: jnp.zeros((1, lanes), jnp.float32))
+    high_ghost(ext2, False)
 
     def stage_two(i, carry):
         for jp in range(n_jp):
@@ -162,7 +162,7 @@
     pltpu.make_async_copy(obuf, out_hbm, sem.at[1]).wait()
 
 
-def fused_step(fields, rate, mix, act, flags, halo_lo, halo_hi, swapped, lft, rgt):
+def fused_step(fields, rate, mix, act, flags, halo_lo, halo_hi, lft, rgt):
     nf, rows, lanes = fields.shape
     vmem = pltpu.VMEM
     smem = pl.BlockSpec(memory_space=pltpu.SMEM)
@@ -182,7 +182,7 @@
             jax.ShapeDtypeStruct((nf, rows), jnp.float32),
             jax.ShapeDtypeStruct((nf, rows), jnp.float32),
         ),
-        in_specs=[smem, smem, smem, pl.BlockSpec(memory_space=pl.ANY)] + [vspec] * 6,
+        in_specs=[smem, smem, smem, pl.BlockSpec(memory_space=pl.ANY)] + [vspec] * 5,
         out_specs=(pl.BlockSpec(memory_space=pl.ANY),) + (vspec,) * 4,
         scratch_shapes=[
             vmem((nf, rows + 2 * SUB, lanes + 2 * LANE), jnp.float32),
@@ -193,12 +193,12 @@
         ],
         compiler_params=pltpu.CompilerParams(vmem_limit_bytes=60 * 1024 * 1024),
         cost_estimate=cost,
-    )(mix, act, flags, fields, rate, halo_lo, halo_hi, swapped, lft, rgt)
+    )(mix, act, flags, fields, rate, halo_lo, halo_hi, lft, rgt)
 
 
 def interp_kernel(ks, flag_s, ids_s, wt_ref, table_ref, *refs):
-    n_pass = (len(refs) - 3) // 2
-    ins, o_ref, outs, acc, picked = refs[:n_pass], refs[n_pass], refs[n_pass + 1:-2], refs[-2], refs[-1]
+    n_in = (len(refs) - 1) // 2
+    ins, o_ref, outs, acc, picked = refs[:n_in], refs[n_in], refs[n_in + 1:-2], refs[-2], refs[-1]
     lanes = o_ref.shape[1]
     width = table_ref.shape[1]
     acc[...] = jnp.zeros(acc.shape, jnp.float32)
@@ -219,8 +219,14 @@
             total = total + wt_ref[:, k:k + 1] * picked[k]
         acc[:, 0:width] = total
 
-    o_ref[...] = jnp.transpose(acc[...])[0:o_ref.shape[0], :]
-    for src, dst in zip(ins, outs):
+    picked_t = jnp.transpose(acc[...])
+    nf = o_ref.shape[0] // 2
+    last_ref, first_ref = ins[0], ins[1]
+    o_ref[0:nf, :] = jnp.where(flag_s[0] > 0.5, picked_t[0:nf, :], last_ref[...])
+    o_ref[nf:2 * nf, :] = jnp.where(
+        flag_s[1] > 0.5, jnp.broadcast_to(picked_t[nf:nf + 1, :], (nf, lanes)), first_ref[...]
+    )
+    for src, dst in zip(ins[2:], outs):
         dst[...] = src[...]
 
 
@@ -231,10 +237,10 @@
     width = table.shape[1]
     return pl.pallas_call(
         functools.partial(interp_kernel, ks),
-        out_shape=(jax.ShapeDtypeStruct((width, lanes), jnp.float32),)
-        + tuple(jax.ShapeDtypeStruct(x.shape, x.dtype) for x in passed),
+        out_shape=(jax.ShapeDtypeStruct((2 * (width - 1), lanes), jnp.float32),)
+        + tuple(jax.ShapeDtypeStruct(x.shape, x.dtype) for x in passed[2:]),
         in_specs=[smem, smem] + [vspec] * (2 + len(passed)),
-        out_specs=(vspec,) * (1 + len(passed)),
+        out_specs=(vspec,) * (len(passed) - 1),
         scratch_shapes=[
             pltpu.VMEM((lanes, LANE), jnp.float32),
             pltpu.VMEM((ks, lanes, width), jnp.float32),
@@ -328,16 +334,15 @@
         slot = slot + ((m // span) % 2) * (1 << r)
     ids = slot * lanes + ids % lanes
     wt = jnp.transpose(jnp.where(at_exit, inlet_weights, outlet_weights))
-    halo_lo = lax.ppermute(edges[0], "grp", [(i, i + 1) for i in range(n_grp - 2)])
-    halo_hi = lax.ppermute(edges[1], "grp", [(i + 1, i) for i in range(n_grp - 2)])
     lft = lax.ppermute(edges[2], "blk", [(i, (i + 1) % n_blk) for i in range(n_blk)])
     rgt = lax.ppermute(edges[3], "blk", [((i + 1) % n_blk, i) for i in range(n_blk)])
 
-    swap, halo_lo, halo_hi, lft, rgt = interpolate(flags, ids, wt, table, (halo_lo, halo_hi, lft, rgt))
-    swapped = lax.ppermute(swap, "grp", [(exit_grp, turb_grp), (turb_grp, exit_grp)])
+    sends, lft, rgt = interpolate(flags, ids, wt, table, (edges[0], edges[1], lft, rgt))
+    halo_lo = lax.ppermute(sends[:nf], "grp", [(i, i + 1) for i in range(n_grp - 1)])
+    halo_hi = lax.ppermute(sends[nf:], "grp", [(i + 1, i) for i in range(n_grp - 1)])
 
     out, elo, ehi, clo, chi = fused_step(
-        fields, react_rate, mix_matrix, activation, flags, halo_lo, halo_hi, swapped, lft, rgt
+        fields, react_rate, mix_matrix, activation, flags, halo_lo, halo_hi, lft, rgt
     )
 
     g0 = lax.ppermute(ehi, "grp", [(i, i + 1) for i in range(n_grp - 2)])

time: 75.3 us -> 74.5 us (0.989)
  starting transfers between devices: 33.2 us -> 31.1 us
  local copies, waits for them, and re-layouts: 8.92 us -> 10.4 us
    ppermute x1, starting transfers between devices: 8.2 us -> 4.22 us  [shards(): g0 = lax.ppermute(ehi, 'grp', [(i, i + 1) for i in range(n_grp - 2)])]
    ppermute x3 -> x2, starting transfers between devices: 8.83 us -> 10.8 us  [the longest x1 6.22 us: shards(): lax.ppermute(sends[:nf], 'grp', [(i, i + 1) for i in range(n_grp - 1)])]
    slice x0 -> x1, local copies, waits for them, and re-layouts: none -> 0.84 us  [shards(): sends[nf:]]
  transfers between devices with their start and end apart: 12 -> 11, of which waited for: 2 -> 2; matrix products, arithmetic and copies ran while one was open for 11% -> 12% of each run, Pallas kernels for 0% -> 0%
where the time goes in v15:
time: 74.5 us; the launch traced here: 73.5 us
  starting transfers between devices  31.1 us (42%)
  Pallas kernels  26.7 us (36%)
  local copies, waits for them, and re-layouts  10.4 us (14%)
  other arithmetic  2.8 us (4%)
  waiting for transfers between devices  2.25 us (3%)
    pallas_call x1, Pallas kernels, fused_step(): pl.pallas_call(functools.partial(step_kernel, nf, rows, lanes), out_shape...  20 us
    ppermute x1, starting transfers between devices, shards(): lax.ppermute(sends[:nf], 'grp', [(i, i + 1) for i in range(n_grp - 1)])  6.22 us
    ppermute x3, starting transfers between devices, shards(): lax.ppermute(planes, 'blk', partner)  5.84 us
    ppermute x1, starting transfers between devices, shards(): lax.ppermute(sends[nf:], 'grp', [(i + 1, i) for i in range(n_grp - 1)])  4.55 us
    pallas_call x1, Pallas kernels, fix_edges(): pl.pallas_call(functools.partial(fix_kernel, low_w, side_w), out_shape=ja...  4.34 us
    ppermute x1, starting transfers between devices, shards(): g0 = lax.ppermute(ehi, 'grp', [(i, i + 1) for i in range(n_grp - 2)])  4.22 us
    ppermute x1, starting transfers between devices, shards(): lax.ppermute(edges[3], 'blk', [((i + 1) % n_blk, i) for i in range(n_blk)])  3.91 us
    ppermute x1, starting transfers between devices, shards(): gr = lax.ppermute(clo, 'blk', [((i + 1) % n_blk, i) for i in range(n_blk)])  3.82 us
  transfers between devices with their start and end apart: 11, of which 2 were waited for; matrix products, arithmetic and copies ran while one was open for 12% of the time, Pallas kernels for 0%

profile of v15, /device:TPU:1, one launch (start us, length us, event | category | flops | bytes accessed | tf_op | source)
XLA Modules:
  0.0 73.5 jit_solution(5357354791132834212)
XLA Ops:
  0.0 0.0 copy-start.7
  0.0 0.0 copy-start.8
  0.0 0.0 copy-start.10
  0.0 0.8 %slice_bitcast_fusion = f32[1,512]{1,0:T(1,128)S(1)} fusion(f32[14,128,512]{2,1,0:T(8,128)} %f_hbm.1), kind=kLoop, calls=%fused_computation.41 | loop fusion | bytes 4096 | tf_op jit(solution)/shard_map/slice | solution.py:316
  0.8 1.1 %fusion.13 = (f32[14,1,512]{2,1,0:T(1,128)S(1)}, f32[14,1,512]{2,1,0:T(1,128)S(1)}) fusion(f32[14,128,512]{2,1,0:T(8,128)} %f_hbm.1), kind=kLoop, calls=%fused_computation.44 | loop fusion | bytes 114688 | tf_op jit(solution)/shard_map/slice | solution.py:315
  1.9 0.0 copy-start
  1.9 3.2 %collective-permute-start = (f32[1,15,512]{2,1,0:T(8,128)S(1)}, f32[1,15,512]{2,1,0:T(8,128)S(1)}, u32[]{:S(2)}, u32[]{:S(2)}) collective-permute-start(f32[1,15,512]{2,1,0:T(8,128)S(1)} %maximum_bitcast_fusion.1), channel_id=1, source_target_pairs={{0,4},{1,5},{2,6},{3,7},{4,0},{5,1},{6,2},{7,3},{8,12},{9,13},{10,... | collective-permute-start | bytes 92168 | tf_op jit(solution)/shard_map/ppermute | solution.py:326
  5.1 1.8 %fusion.12 = (f32[14,128,1]{2,1,0:T(8,128)S(1)}, f32[14,128,1]{2,1,0:T(8,128)S(1)}) fusion(f32[14,128,512]{2,1,0:T(8,128)} %f_hbm.1), kind=kLoop, calls=%fused_computation.43 | loop fusion | bytes 28672 | tf_op jit(solution)/shard_map/slice | solution.py:320
  6.9 0.0 copy-done.7
  6.9 0.1 copy.20
  7.1 0.0 copy-done.8
  7.1 0.1 copy.21
  7.3 0.0 collective-permute-done
  7.3 1.4 %collective-permute-start.1 = (f32[2,15,512]{2,1,0:T(8,128)S(1)}, f32[2,15,512]{2,1,0:T(8,128)S(1)}, u32[]{:S(2)}, u32[]{:S(2)}) collective-permute-start(f32[2,15,512]{2,1,0:T(8,128)S(1)} %pad_maximum_fusion.1), channel_id=1, source_target_pairs={{0,2},{1,3},{2,0},{3,1},{4,6},{5,7},{6,4},{7,5},{8,10},{9,11},{10,... | collective-permute-start | bytes 184328 | tf_op jit(solution)/shard_map/ppermute | solution.py:326
  8.6 0.8 %add_select_fusion = (s32[4,512]{0,1:T(8,128)S(1)}, s32[4,512]{0,1:T(8,128)S(1)}) fusion(s32[4,512]{0,1:T(8,128)S(1)} %copy.20, s32[4,512]{0,1:T(8,128)S(1)} %copy.21, pred[]{:T(512)} %eq.12, s32[]{:T(128)S(6)} %axis_index.25), kind=kLoop, calls=%fused_computation | loop fusion | flops 157696 | bytes 32773 | tf_op jit(solution)/shard_map/jit(remainder)/select_n | solution.py:335
  9.4 0.6 copy.40
  10.0 0.0 copy-done.9
  10.0 0.1 copy.24
  10.2 0.0 copy-done.10
  10.2 0.1 copy.25
  10.4 0.3 copy.37
  10.7 0.3 copy.36
  11.0 0.0 copy-done
  11.0 0.0 collective-permute-done.1
  11.1 1.3 %collective-permute-start.2 = (f32[4,15,512]{2,1,0:T(8,128)S(1)}, f32[4,15,512]{2,1,0:T(8,128)S(1)}, u32[]{:S(2)}, u32[]{:S(2)}) collective-permute-start(f32[4,15,512]{2,1,0:T(8,128)S(1)} %pad_maximum_fusion), channel_id=1, source_target_pairs={{0,1},{1,0},{2,3},{3,2},{4,5},{5,4},{6,7},{7,6},{8,9},{9,8},{10,11... | collective-permute-start | bytes 368648 | tf_op jit(solution)/shard_map/ppermute | solution.py:326
  12.3 0.7 select_bitcast_fusion.wt_ref
  13.1 0.1 copy.23
  13.2 0.1 copy.22
  13.3 0.6 add.37.ids_s
  13.9 0.6 add_convert_fusion.flag_s
  14.5 0.3 collective-permute-start.3
  14.8 3.9 %collective-permute-start.4 = (f32[14,128]{1,0:T(8,128)S(1)}, f32[14,128]{1,0:T(8,128)S(1)}, u32[]{:S(2)}, u32[]{:S(2)}) collective-permute-start(f32[14,128]{1,0:T(8,128)S(1)} %bitcast.23), channel_id=1, source_target_pairs={{1,0},{2,1},{3,2},{4,3},{5,4},{6,5},{7,6},{0,7},{9,8},{10,9},{11,1... | collective-permute-start | bytes 21512 | tf_op jit(solution)/shard_map/ppermute | solution.py:338
  18.7 0.0 collective-permute-done.2
  18.7 2.0 %copy.32 = f32[8,512,15]{2,1,0:T(8,128)} copy(f32[8,512,15]{1,2,0:T(8,128)S(1)} %maximum_bitcast_fusion) | data formatting | bytes 491520 | tf_op jit(solution)/shard_map/reshape | solution.py:328
  20.7 0.0 collective-permute-done.3.refs_2_
  20.7 0.0 collective-permute-done.4.refs_3_
  20.7 0.0 copy-start.4
  20.7 0.6 copy-done.3
  21.3 0.0 copy-done.4
  21.3 2.4 %shard_map.82 = (f32[28,512]{1,0:T(8,128)}, f32[14,128]{1,0:T(8,128)}, f32[14,128]{1,0:T(8,128)}) custom-call(f32[2]{0:T(128)} %add_convert_fusion.flag_s, s32[4,512]{1,0:T(4,128)} %add.37.ids_s, f32[512,4]{1,0:T(8,128)} %select_bitcast_fusion.wt_ref, f32[4096,15]{1,0:T(8,128)} %bitcast.19, f32[14,512]{1,0:T(8,128)} %bitcast.21, f32[14,512]{1,0:T(8,128)} %bitcast.22, ...), custom_call_target="tpu_custom_call" | custom-call | tf_op jit(solution)/shard_map/pallas_call | solution.py:238
  23.7 0.8 %fusion.14 = (f32[14,512]{1,0:T(8,128)S(1)}, f32[14,512]{1,0:T(8,128)S(1)}) fusion(f32[28,512]{1,0:T(8,128)} %get-tuple-element.23), kind=kLoop, calls=%fused_computation.45 | loop fusion | bytes 114688 | tf_op jit(solution)/shard_map/slice | solution.py:342
  24.5 4.5 %collective-permute-start.6 = (f32[14,512]{1,0:T(8,128)S(1)}, f32[14,512]{1,0:T(8,128)S(1)}, u32[]{:S(2)}, u32[]{:S(2)}) collective-permute-start(f32[14,512]{1,0:T(8,128)S(1)} %get-tuple-element.37), channel_id=1, source_target_pairs={{8,0},{16,8},{24,16},{9,1},{17,9},{25,17},{10,2},{18,10},{26,18},{... | collective-permute-start | bytes 86024 | tf_op jit(solution)/shard_map/ppermute | solution.py:342
  29.1 6.2 %collective-permute-start.5 = (f32[14,512]{1,0:T(8,128)S(1)}, f32[14,512]{1,0:T(8,128)S(1)}, u32[]{:S(2)}, u32[]{:S(2)}) collective-permute-start(f32[14,512]{1,0:T(8,128)S(1)} %get-tuple-element.38), channel_id=1, source_target_pairs={{0,8},{8,16},{16,24},{1,9},{9,17},{17,25},{2,10},{10,18},{18,26},{... | collective-permute-start | bytes 86024 | tf_op jit(solution)/shard_map/ppermute | solution.py:341
  35.3 0.0 collective-permute-done.6.hhi_ref
  35.3 0.0 copy-start.11
  35.3 1.0 %collective-permute-done.5.hlo_ref = f32[14,512]{1,0:T(8,128)S(1)} collective-permute-done((f32[14,512]{1,0:T(8,128)S(1)}, f32[14,512]{1,0:T(8,128)S(1)}, u32[]{:S(2)}, u32[]{:S(2)}) %collective-permute-start.5) | collective-permute-done | bytes 28704 | tf_op jit(solution)/shard_map/ppermute | solution.py:341
  36.3 0.0 copy-done.11
  36.3 0.6 copy-done.12
  36.9 20.0 %shard_map.83 = (f32[14,128,512]{2,1,0:T(8,128)}, f32[14,512]{1,0:T(8,128)}, f32[14,512]{1,0:T(8,128)}, f32[14,128]{1,0:T(8,128)}, f32[14,128]{1,0:T(8,128)}) custom-call(f32[14,14]{1,0:T(8,128)} %mix_s.1, f32[14]{0:T(128)} %act_s.1, f32[2]{0:T(128)} %add_convert_fusion.flag_s, f32[14,128,512]{2,1,0:T(8,128)} %f_hbm.1, f32[128,512]{1,0:T(8,128)} %rate_ref.1, ...), custom_call_target="tpu_custom_call" | custom-call | flops 95420416 | bytes 7602176 | tf_op jit(solution)/shard_map/pallas_call | solution.py:176
  56.9 4.2 %collective-permute-start.7 = (f32[14,512]{1,0:T(8,128)}, f32[14,512]{1,0:T(8,128)S(1)}, u32[]{:S(2)}, u32[]{:S(2)}) collective-permute-start(f32[14,512]{1,0:T(8,128)} %get-tuple-element.27), channel_id=1, source_target_pairs={{0,8},{8,16},{1,9},{9,17},{2,10},{10,18},{3,11},{11,19},{4,12},{12... | collective-permute-start | bytes 86024 | tf_op jit(solution)/shard_map/ppermute | solution.py:348
  61.2 1.9 %collective-permute-start.8 = (f32[14,512]{1,0:T(8,128)}, f32[14,512]{1,0:T(8,128)S(1)}, u32[]{:S(2)}, u32[]{:S(2)}) collective-permute-start(f32[14,512]{1,0:T(8,128)} %get-tuple-element.28), channel_id=1, source_target_pairs={{8,0},{16,8},{9,1},{17,9},{10,2},{18,10},{11,3},{19,11},{12,4},{20... | collective-permute-start | bytes 86024 | tf_op jit(solution)/shard_map/ppermute | solution.py:349
  63.1 0.4 collective-permute-start.9
  63.5 3.8 %collective-permute-start.10 = (f32[14,128]{1,0:T(8,128)}, f32[14,128]{1,0:T(8,128)S(1)}, u32[]{:S(2)}, u32[]{:S(2)}) collective-permute-start(f32[14,128]{1,0:T(8,128)} %get-tuple-element.30), channel_id=1, source_target_pairs={{1,0},{2,1},{3,2},{4,3},{5,4},{6,5},{7,6},{0,7},{9,8},{10,9},{11,1... | collective-permute-start | bytes 21512 | tf_op jit(solution)/shard_map/ppermute | solution.py:351
  67.3 1.2 %collective-permute-done.9.gl_ref = f32[14,128]{1,0:T(8,128)S(1)} collective-permute-done((f32[14,128]{1,0:T(8,128)}, f32[14,128]{1,0:T(8,128)S(1)}, u32[]{:S(2)}, u32[]{:S(2)}) %collective-permute-start.9) | collective-permute-done | bytes 7200 | tf_op jit(solution)/shard_map/ppermute | solution.py:350
  68.6 0.0 collective-permute-done.10.gr_ref
  68.6 0.0 collective-permute-done.7.g0_ref
  68.6 0.0 copy-start.1
  68.6 0.0 collective-permute-done.8.g1_ref
  68.6 0.0 copy-start.2
  68.6 0.5 copy-done.5
  69.2 0.0 copy-done.6
  69.2 0.0 copy-done.1
  69.2 0.0 copy-done.2
  69.2 4.3 %shard_map.84 = f32[14,128,512]{2,1,0:T(8,128)} custom-call(f32[14,128,512]{2,1,0:T(8,128)} %get-tuple-element.26.out_in, f32[14,512]{1,0:T(8,128)} %copy-done.1, f32[14,512]{1,0:T(8,128)} %copy-done.2, f32[14,128]{1,0:T(8,128)} %copy-done.5, f32[14,128]{1,0:T(8,128)} %copy-done.6), custom_call_target="tpu_custom_call", output_to_operand_aliasing={{}: (0, {})} | custom-call | tf_op jit(solution)/shard_map/pallas_call | solution.py:288
  (10 shorter events, 0.1 us)
Async XLA Ops:
  0.0 6.9 %copy-start.7 = (s32[4,512]{1,0:T(4,128)S(1)}, s32[4,512]{1,0:T(4,128)}, u32[]{:S(2)}) copy-start(s32[4,512]{1,0:T(4,128)} %param.12) | copy-start | bytes 24580
  0.0 7.1 %copy-start.8 = (s32[4,512]{1,0:T(4,128)S(1)}, s32[4,512]{1,0:T(4,128)}, u32[]{:S(2)}) copy-start(s32[4,512]{1,0:T(4,128)} %param.14) | copy-start | bytes 24580
  0.0 10.0 %copy-start.9 = (f32[4,512]{1,0:T(4,128)S(1)}, f32[4,512]{1,0:T(4,128)}, u32[]{:S(2)}) copy-start(f32[4,512]{1,0:T(4,128)} %param.13) | copy-start | bytes 24580
  0.0 10.2 %copy-start.10 = (f32[4,512]{1,0:T(4,128)S(1)}, f32[4,512]{1,0:T(4,128)}, u32[]{:S(2)}) copy-start(f32[4,512]{1,0:T(4,128)} %param.15) | copy-start | bytes 24580
  1.9 9.1 %copy-start = (f32[14,1,512]{2,0,1:T(8,128)}, f32[14,1,512]{2,0,1:T(8,128)S(1)}, u32[]{:S(2)}) copy-start(f32[14,1,512]{2,0,1:T(8,128)S(1)} %copy.41) | copy-start | bytes 86020
  1.9 5.3 %collective-permute-start = (f32[1,15,512]{2,1,0:T(8,128)S(1)}, f32[1,15,512]{2,1,0:T(8,128)S(1)}, u32[]{:S(2)}, u32[]{:S(2)}) collective-permute-start(f32[1,15,512]{2,1,0:T(8,128)S(1)} %maximum_bitcast_fusion.1), channel_id=1, source_target_pairs={{0,4},{1,5},{2,6},{3,7},{4,0},{5,1},{6,2},{7,3},{8,12},{9,13},{10,... | collective-permute-start | bytes 92168 | tf_op jit(solution)/shard_map/ppermute | solution.py:326
  7.3 3.8 %collective-permute-start.1 = (f32[2,15,512]{2,1,0:T(8,128)S(1)}, f32[2,15,512]{2,1,0:T(8,128)S(1)}, u32[]{:S(2)}, u32[]{:S(2)}) collective-permute-start(f32[2,15,512]{2,1,0:T(8,128)S(1)} %pad_maximum_fusion.1), channel_id=1, source_target_pairs={{0,2},{1,3},{2,0},{3,1},{4,6},{5,7},{6,4},{7,5},{8,10},{9,11},{10,... | collective-permute-start | bytes 184328 | tf_op jit(solution)/shard_map/ppermute | solution.py:326
  11.1 7.6 %collective-permute-start.2 = (f32[4,15,512]{2,1,0:T(8,128)S(1)}, f32[4,15,512]{2,1,0:T(8,128)S(1)}, u32[]{:S(2)}, u32[]{:S(2)}) collective-permute-start(f32[4,15,512]{2,1,0:T(8,128)S(1)} %pad_maximum_fusion), channel_id=1, source_target_pairs={{0,1},{1,0},{2,3},{3,2},{4,5},{5,4},{6,7},{7,6},{8,9},{9,8},{10,11... | collective-permute-start | bytes 368648 | tf_op jit(solution)/shard_map/ppermute | solution.py:326
  14.5 6.2 %collective-permute-start.3 = (f32[14,128]{1,0:T(8,128)S(1)}, f32[14,128]{1,0:T(8,128)S(1)}, u32[]{:S(2)}, u32[]{:S(2)}) collective-permute-start(f32[14,128]{1,0:T(8,128)S(1)} %bitcast.24), channel_id=1, source_target_pairs={{0,1},{1,2},{2,3},{3,4},{4,5},{5,6},{6,7},{7,0},{8,9},{9,10},{10,1... | collective-permute-start | bytes 21512 | tf_op jit(solution)/shard_map/ppermute | solution.py:337
  14.8 5.9 %collective-permute-start.4 = (f32[14,128]{1,0:T(8,128)S(1)}, f32[14,128]{1,0:T(8,128)S(1)}, u32[]{:S(2)}, u32[]{:S(2)}) collective-permute-start(f32[14,128]{1,0:T(8,128)S(1)} %bitcast.23), channel_id=1, source_target_pairs={{1,0},{2,1},{3,2},{4,3},{5,4},{6,5},{7,6},{0,7},{9,8},{10,9},{11,1... | collective-permute-start | bytes 21512 | tf_op jit(solution)/shard_map/ppermute | solution.py:338
  20.7 0.6 copy-start.3
  20.7 0.6 copy-start.4
  24.5 10.8 %collective-permute-start.6 = (f32[14,512]{1,0:T(8,128)S(1)}, f32[14,512]{1,0:T(8,128)S(1)}, u32[]{:S(2)}, u32[]{:S(2)}) collective-permute-start(f32[14,512]{1,0:T(8,128)S(1)} %get-tuple-element.37), channel_id=1, source_target_pairs={{8,0},{16,8},{24,16},{9,1},{17,9},{25,17},{10,2},{18,10},{26,18},{... | collective-permute-start | bytes 86024 | tf_op jit(solution)/shard_map/ppermute | solution.py:342
  29.1 7.2 %collective-permute-start.5 = (f32[14,512]{1,0:T(8,128)S(1)}, f32[14,512]{1,0:T(8,128)S(1)}, u32[]{:S(2)}, u32[]{:S(2)}) collective-permute-start(f32[14,512]{1,0:T(8,128)S(1)} %get-tuple-element.38), channel_id=1, source_target_pairs={{0,8},{8,16},{16,24},{1,9},{9,17},{17,25},{2,10},{10,18},{18,26},{... | collective-permute-start | bytes 86024 | tf_op jit(solution)/shard_map/ppermute | solution.py:341
  35.3 1.0 %copy-start.11 = (f32[14,512]{1,0:T(8,128)}, f32[14,512]{1,0:T(8,128)S(1)}, u32[]{:S(2)}) copy-start(f32[14,512]{1,0:T(8,128)S(1)} %collective-permute-done.6.hhi_ref) | copy-start | bytes 86020
  36.3 0.6 copy-start.12
  56.9 11.6 %collective-permute-start.7 = (f32[14,512]{1,0:T(8,128)}, f32[14,512]{1,0:T(8,128)S(1)}, u32[]{:S(2)}, u32[]{:S(2)}) collective-permute-start(f32[14,512]{1,0:T(8,128)} %get-tuple-element.27), channel_id=1, source_target_pairs={{0,8},{8,16},{1,9},{9,17},{2,10},{10,18},{3,11},{11,19},{4,12},{12... | collective-permute-start | bytes 86024 | tf_op jit(solution)/shard_map/ppermute | solution.py:348
  61.2 7.4 %collective-permute-start.8 = (f32[14,512]{1,0:T(8,128)}, f32[14,512]{1,0:T(8,128)S(1)}, u32[]{:S(2)}, u32[]{:S(2)}) collective-permute-start(f32[14,512]{1,0:T(8,128)} %get-tuple-element.28), channel_id=1, source_target_pairs={{8,0},{16,8},{9,1},{17,9},{10,2},{18,10},{11,3},{19,11},{12,4},{20... | collective-permute-start | bytes 86024 | tf_op jit(solution)/shard_map/ppermute | solution.py:349
  63.1 5.5 %collective-permute-start.9 = (f32[14,128]{1,0:T(8,128)}, f32[14,128]{1,0:T(8,128)S(1)}, u32[]{:S(2)}, u32[]{:S(2)}) collective-permute-start(f32[14,128]{1,0:T(8,128)} %get-tuple-element.29), channel_id=1, source_target_pairs={{0,1},{1,2},{2,3},{3,4},{4,5},{5,6},{6,7},{7,0},{8,9},{9,10},{10,1... | collective-permute-start | bytes 21512 | tf_op jit(solution)/shard_map/ppermute | solution.py:350
  63.5 5.1 %collective-permute-start.10 = (f32[14,128]{1,0:T(8,128)}, f32[14,128]{1,0:T(8,128)S(1)}, u32[]{:S(2)}, u32[]{:S(2)}) collective-permute-start(f32[14,128]{1,0:T(8,128)} %get-tuple-element.30), channel_id=1, source_target_pairs={{1,0},{2,1},{3,2},{4,3},{5,4},{6,5},{7,6},{0,7},{9,8},{10,9},{11,1... | collective-permute-start | bytes 21512 | tf_op jit(solution)/shard_map/ppermute | solution.py:351
  68.6 0.6 copy-start.5
  68.6 0.6 copy-start.6
  68.6 0.6 copy-start.1
  68.6 0.6 copy-start.2

commit v16 on v15

--- a/solution.py
+++ b/solution.py
@@ -197,9 +197,10 @@
 
 
 def interp_kernel(ks, flag_s, ids_s, wt_ref, table_ref, *refs):
-    n_in = (len(refs) - 1) // 2
-    ins, o_ref, outs, acc, picked = refs[:n_in], refs[n_in], refs[n_in + 1:-2], refs[-2], refs[-1]
-    lanes = o_ref.shape[1]
+    n_in = (len(refs) - 2) // 2
+    ins, outs, acc, picked = refs[:n_in], refs[n_in:2 * n_in], refs[-2], refs[-1]
+    up_ref, down_ref = outs[0], outs[1]
+    lanes = outs[0].shape[1]
     width = table_ref.shape[1]
     acc[...] = jnp.zeros(acc.shape, jnp.float32)
 
@@ -220,13 +221,13 @@
         acc[:, 0:width] = total
 
     picked_t = jnp.transpose(acc[...])
-    nf = o_ref.shape[0] // 2
+    nf = up_ref.shape[0]
     last_ref, first_ref = ins[0], ins[1]
-    o_ref[0:nf, :] = jnp.where(flag_s[0] > 0.5, picked_t[0:nf, :], last_ref[...])
-    o_ref[nf:2 * nf, :] = jnp.where(
+    up_ref[...] = jnp.where(flag_s[0] > 0.5, picked_t[0:nf, :], last_ref[...])
+    down_ref[...] = jnp.where(
         flag_s[1] > 0.5, jnp.broadcast_to(picked_t[nf:nf + 1, :], (nf, lanes)), first_ref[...]
     )
-    for src, dst in zip(ins[2:], outs):
+    for src, dst in zip(ins[2:], outs[2:]):
         dst[...] = src[...]
 
 
@@ -237,10 +238,9 @@
     width = table.shape[1]
     return pl.pallas_call(
         functools.partial(interp_kernel, ks),
-        out_shape=(jax.ShapeDtypeStruct((2 * (width - 1), lanes), jnp.float32),)
-        + tuple(jax.ShapeDtypeStruct(x.shape, x.dtype) for x in passed[2:]),
+        out_shape=tuple(jax.ShapeDtypeStruct(x.shape, x.dtype) for x in passed),
         in_specs=[smem, smem] + [vspec] * (2 + len(passed)),
-        out_specs=(vspec,) * (len(passed) - 1),
+        out_specs=(vspec,) * len(passed),
         scratch_shapes=[
             pltpu.VMEM((lanes, LANE), jnp.float32),
             pltpu.VMEM((ks, lanes, width), jnp.float32),
@@ -337,9 +337,9 @@
     lft = lax.ppermute(edges[2], "blk", [(i, (i + 1) % n_blk) for i in range(n_blk)])
     rgt = lax.ppermute(edges[3], "blk", [((i + 1) % n_blk, i) for i in range(n_blk)])
 
-    sends, lft, rgt = interpolate(flags, ids, wt, table, (edges[0], edges[1], lft, rgt))
-    halo_lo = lax.ppermute(sends[:nf], "grp", [(i, i + 1) for i in range(n_grp - 1)])
-    halo_hi = lax.ppermute(sends[nf:], "grp", [(i + 1, i) for i in range(n_grp - 1)])
+    up, down, lft, rgt = interpolate(flags, ids, wt, table, (edges[0], edges[1], lft, rgt))
+    halo_lo = lax.ppermute(up, "grp", [(i, i + 1) for i in range(n_grp - 1)])
+    halo_hi = lax.ppermute(down, "grp", [(i + 1, i) for i in range(n_grp - 1)])
 
     out, elo, ehi, clo, chi = fused_step(
         fields, react_rate, mix_matrix, activation, flags, halo_lo, halo_hi, lft, rgt

time: 74.5 us -> 74.4 us (level)
  waiting for transfers between devices: 2.25 us -> 4.9 us
  starting transfers between devices: 31.1 us -> 29.3 us
  local copies, waits for them, and re-layouts: 10.4 us -> 9.54 us
    ppermute x2, waiting for transfers between devices: 0.98 us -> 3.5 us  [the longest x1 3.5 us: shards(): halo_hi = lax.ppermute(down, 'grp', [(i + 1, i) for i in range(n_grp - 1)])]
    ppermute x1, starting transfers between devices: 4.22 us -> 2.02 us  [shards(): g0 = lax.ppermute(ehi, 'grp', [(i, i + 1) for i in range(n_grp - 2)])]
    slice x1 -> x0, local copies, waits for them, and re-layouts: 0.84 us -> none  [shards(): sends[nf:]]
where the time goes in v16:
time: 74.4 us; the launch traced here: 73.6 us
  starting transfers between devices  29.3 us (39%)
  Pallas kernels  26.8 us (36%)
  local copies, waits for them, and re-layouts  9.54 us (13%)
  waiting for transfers between devices  4.9 us (7%)
  other arithmetic  2.85 us (4%)
    pallas_call x1, Pallas kernels, fused_step(): pl.pallas_call(functools.partial(step_kernel, nf, rows, lanes), out_shape...  20.1 us
    ppermute x1, starting transfers between devices, shards(): halo_lo = lax.ppermute(up, 'grp', [(i, i + 1) for i in range(n_grp - 1)])  8.84 us
    ppermute x3, starting transfers between devices, shards(): lax.ppermute(planes, 'blk', partner)  5.84 us
    pallas_call x1, Pallas kernels, fix_edges(): pl.pallas_call(functools.partial(fix_kernel, low_w, side_w), out_shape=ja...  4.34 us
    ppermute x1, starting transfers between devices, shards(): lax.ppermute(edges[3], 'blk', [((i + 1) % n_blk, i) for i in range(n_blk)])  3.91 us
    ppermute x1, starting transfers between devices, shards(): gr = lax.ppermute(clo, 'blk', [((i + 1) % n_blk, i) for i in range(n_blk)])  3.81 us
    unnamed x34, local copies, waits for them, and re-layouts  3.69 us
    ppermute x1, waiting for transfers between devices, shards(): halo_hi = lax.ppermute(down, 'grp', [(i + 1, i) for i in range(n_grp - 1)])  3.5 us
  transfers between devices with their start and end apart: 11, of which 2 were waited for; matrix products, arithmetic and copies ran while one was open for 12% of the time, Pallas kernels for 0%

profile of v16, /device:TPU:1, one launch (start us, length us, event | category | flops | bytes accessed | tf_op | source)
XLA Modules:
  0.0 73.6 jit_solution(13702179514736210679)
XLA Ops:
  0.0 0.0 copy-start.7
  0.0 0.0 copy-start.8
  0.0 0.0 copy-start.9
  0.0 0.0 copy-start.10
  0.0 0.8 %slice_bitcast_fusion = f32[1,512]{1,0:T(1,128)S(1)} fusion(f32[14,128,512]{2,1,0:T(8,128)} %f_hbm.1), kind=kLoop, calls=%fused_computation.41 | loop fusion | bytes 4096 | tf_op jit(solution)/shard_map/slice | solution.py:316
  0.8 1.1 %fusion.13 = (f32[14,1,512]{2,1,0:T(1,128)S(1)}, f32[14,1,512]{2,1,0:T(1,128)S(1)}) fusion(f32[14,128,512]{2,1,0:T(8,128)} %f_hbm.1), kind=kLoop, calls=%fused_computation.44 | loop fusion | bytes 114688 | tf_op jit(solution)/shard_map/slice | solution.py:315
  1.9 0.0 copy-start
  1.9 3.2 %collective-permute-start = (f32[1,15,512]{2,1,0:T(8,128)S(1)}, f32[1,15,512]{2,1,0:T(8,128)S(1)}, u32[]{:S(2)}, u32[]{:S(2)}) collective-permute-start(f32[1,15,512]{2,1,0:T(8,128)S(1)} %maximum_bitcast_fusion.1), channel_id=1, source_target_pairs={{0,4},{1,5},{2,6},{3,7},{4,0},{5,1},{6,2},{7,3},{8,12},{9,13},{10,... | collective-permute-start | bytes 92168 | tf_op jit(solution)/shard_map/ppermute | solution.py:326
  5.1 1.8 %fusion.12 = (f32[14,128,1]{2,1,0:T(8,128)S(1)}, f32[14,128,1]{2,1,0:T(8,128)S(1)}) fusion(f32[14,128,512]{2,1,0:T(8,128)} %f_hbm.1), kind=kLoop, calls=%fused_computation.43 | loop fusion | bytes 28672 | tf_op jit(solution)/shard_map/slice | solution.py:320
  6.9 0.0 copy-done.7
  6.9 0.1 copy.20
  7.1 0.0 copy-done.8
  7.1 0.1 copy.21
  7.3 0.0 collective-permute-done
  7.3 1.4 %collective-permute-start.1 = (f32[2,15,512]{2,1,0:T(8,128)S(1)}, f32[2,15,512]{2,1,0:T(8,128)S(1)}, u32[]{:S(2)}, u32[]{:S(2)}) collective-permute-start(f32[2,15,512]{2,1,0:T(8,128)S(1)} %pad_maximum_fusion.1), channel_id=1, source_target_pairs={{0,2},{1,3},{2,0},{3,1},{4,6},{5,7},{6,4},{7,5},{8,10},{9,11},{10,... | collective-permute-start | bytes 184328 | tf_op jit(solution)/shard_map/ppermute | solution.py:326
  8.6 0.8 %add_select_fusion = (s32[4,512]{0,1:T(8,128)S(1)}, s32[4,512]{0,1:T(8,128)S(1)}) fusion(s32[4,512]{0,1:T(8,128)S(1)} %copy.20, s32[4,512]{0,1:T(8,128)S(1)} %copy.21, pred[]{:T(512)} %eq.12, s32[]{:T(128)S(6)} %axis_index.25), kind=kLoop, calls=%fused_computation | loop fusion | flops 157696 | bytes 32773 | tf_op jit(solution)/shard_map/jit(remainder)/select_n | solution.py:335
  9.4 0.6 copy.40
  10.1 0.0 copy-done.9
  10.1 0.1 copy.24
  10.2 0.0 copy-done.10
  10.2 0.1 copy.25
  10.4 0.3 copy.37
  10.7 0.3 copy.36
  11.0 0.0 copy-done
  11.0 0.0 collective-permute-done.1
  11.1 1.3 %collective-permute-start.2 = (f32[4,15,512]{2,1,0:T(8,128)S(1)}, f32[4,15,512]{2,1,0:T(8,128)S(1)}, u32[]{:S(2)}, u32[]{:S(2)}) collective-permute-start(f32[4,15,512]{2,1,0:T(8,128)S(1)} %pad_maximum_fusion), channel_id=1, source_target_pairs={{0,1},{1,0},{2,3},{3,2},{4,5},{5,4},{6,7},{7,6},{8,9},{9,8},{10,11... | collective-permute-start | bytes 368648 | tf_op jit(solution)/shard_map/ppermute | solution.py:326
  12.4 0.7 %select_bitcast_fusion.wt_ref = f32[512,4]{1,0:T(8,128)} fusion(f32[4,512]{0,1:T(8,128)S(1)} %copy.24, f32[4,512]{0,1:T(8,128)S(1)} %copy.25, pred[]{:T(512)} %eq.12), kind=kLoop, calls=%fused_computation.29 | loop fusion | flops 2048 | bytes 24577 | tf_op jit(solution)/shard_map/transpose | solution.py:336
  13.1 0.1 copy.23
  13.2 0.1 copy.22
  13.3 0.6 add.37.ids_s
  13.9 0.6 add_convert_fusion.flag_s
  14.6 0.3 collective-permute-start.3
  14.8 3.9 %collective-permute-start.4 = (f32[14,128]{1,0:T(8,128)S(1)}, f32[14,128]{1,0:T(8,128)S(1)}, u32[]{:S(2)}, u32[]{:S(2)}) collective-permute-start(f32[14,128]{1,0:T(8,128)S(1)} %bitcast.23), channel_id=1, source_target_pairs={{1,0},{2,1},{3,2},{4,3},{5,4},{6,5},{7,6},{0,7},{9,8},{10,9},{11,1... | collective-permute-start | bytes 21512 | tf_op jit(solution)/shard_map/ppermute | solution.py:338
  18.7 0.0 collective-permute-done.2
  18.8 2.0 %copy.32 = f32[8,512,15]{2,1,0:T(8,128)} copy(f32[8,512,15]{1,2,0:T(8,128)S(1)} %maximum_bitcast_fusion) | data formatting | bytes 491520 | tf_op jit(solution)/shard_map/reshape | solution.py:328
  20.7 0.0 collective-permute-done.3.refs_2_
  20.8 0.0 collective-permute-done.4.refs_3_
  20.8 0.0 copy-start.4
  20.8 0.6 copy-done.3
  21.3 0.0 copy-done.4
  21.4 2.4 %shard_map.82 = (f32[14,512]{1,0:T(8,128)}, f32[14,512]{1,0:T(8,128)}, f32[14,128]{1,0:T(8,128)}, f32[14,128]{1,0:T(8,128)}) custom-call(f32[2]{0:T(128)} %add_convert_fusion.flag_s, s32[4,512]{1,0:T(4,128)} %add.37.ids_s, f32[512,4]{1,0:T(8,128)} %select_bitcast_fusion.wt_ref, f32[4096,15]{1,0:T(8,128)} %bitcast.19, f32[14,512]{1,0:T(8,128)} %bitcast.21, ...), custom_call_target="tpu_custom_call" | custom-call | tf_op jit(solution)/shard_map/pallas_call | solution.py:239
  23.7 8.8 %collective-permute-start.5 = (f32[14,512]{1,0:T(8,128)}, f32[14,512]{1,0:T(8,128)S(1)}, u32[]{:S(2)}, u32[]{:S(2)}) collective-permute-start(f32[14,512]{1,0:T(8,128)} %get-tuple-element.24), channel_id=1, source_target_pairs={{0,8},{8,16},{16,24},{1,9},{9,17},{17,25},{2,10},{10,18},{18,26},{... | collective-permute-start | bytes 86024 | tf_op jit(solution)/shard_map/ppermute | solution.py:341
  32.6 1.9 %collective-permute-start.6 = (f32[14,512]{1,0:T(8,128)}, f32[14,512]{1,0:T(8,128)S(1)}, u32[]{:S(2)}, u32[]{:S(2)}) collective-permute-start(f32[14,512]{1,0:T(8,128)} %get-tuple-element.25), channel_id=1, source_target_pairs={{8,0},{16,8},{24,16},{9,1},{17,9},{25,17},{10,2},{18,10},{26,18},{... | collective-permute-start | bytes 86024 | tf_op jit(solution)/shard_map/ppermute | solution.py:342
  34.5 0.0 collective-permute-done.5.hlo_ref
  34.5 0.0 copy-start.11
  34.5 3.5 %collective-permute-done.6.hhi_ref = f32[14,512]{1,0:T(8,128)S(1)} collective-permute-done((f32[14,512]{1,0:T(8,128)}, f32[14,512]{1,0:T(8,128)S(1)}, u32[]{:S(2)}, u32[]{:S(2)}) %collective-permute-start.6) | collective-permute-done | bytes 28704 | tf_op jit(solution)/shard_map/ppermute | solution.py:342
  38.0 0.0 copy-done.11
  38.0 0.6 copy-done.12
  38.6 20.1 %shard_map.83 = (f32[14,128,512]{2,1,0:T(8,128)}, f32[14,512]{1,0:T(8,128)}, f32[14,512]{1,0:T(8,128)}, f32[14,128]{1,0:T(8,128)}, f32[14,128]{1,0:T(8,128)}) custom-call(f32[14,14]{1,0:T(8,128)} %mix_s.1, f32[14]{0:T(128)} %act_s.1, f32[2]{0:T(128)} %add_convert_fusion.flag_s, f32[14,128,512]{2,1,0:T(8,128)} %f_hbm.1, f32[128,512]{1,0:T(8,128)} %rate_ref.1, ...), custom_call_target="tpu_custom_call" | custom-call | flops 95420416 | bytes 7602176 | tf_op jit(solution)/shard_map/pallas_call | solution.py:176
  58.7 2.0 %collective-permute-start.7 = (f32[14,512]{1,0:T(8,128)}, f32[14,512]{1,0:T(8,128)S(1)}, u32[]{:S(2)}, u32[]{:S(2)}) collective-permute-start(f32[14,512]{1,0:T(8,128)} %get-tuple-element.29), channel_id=1, source_target_pairs={{0,8},{8,16},{1,9},{9,17},{2,10},{10,18},{3,11},{11,19},{4,12},{12... | collective-permute-start | bytes 86024 | tf_op jit(solution)/shard_map/ppermute | solution.py:348
  60.7 2.3 %collective-permute-start.8 = (f32[14,512]{1,0:T(8,128)}, f32[14,512]{1,0:T(8,128)S(1)}, u32[]{:S(2)}, u32[]{:S(2)}) collective-permute-start(f32[14,512]{1,0:T(8,128)} %get-tuple-element.30), channel_id=1, source_target_pairs={{8,0},{16,8},{9,1},{17,9},{10,2},{18,10},{11,3},{19,11},{12,4},{20... | collective-permute-start | bytes 86024 | tf_op jit(solution)/shard_map/ppermute | solution.py:349
  63.0 0.4 collective-permute-start.9
  63.4 3.8 %collective-permute-start.10 = (f32[14,128]{1,0:T(8,128)}, f32[14,128]{1,0:T(8,128)S(1)}, u32[]{:S(2)}, u32[]{:S(2)}) collective-permute-start(f32[14,128]{1,0:T(8,128)} %get-tuple-element.32), channel_id=1, source_target_pairs={{1,0},{2,1},{3,2},{4,3},{5,4},{6,5},{7,6},{0,7},{9,8},{10,9},{11,1... | collective-permute-start | bytes 21512 | tf_op jit(solution)/shard_map/ppermute | solution.py:351
  67.3 1.4 %collective-permute-done.9.gl_ref = f32[14,128]{1,0:T(8,128)S(1)} collective-permute-done((f32[14,128]{1,0:T(8,128)}, f32[14,128]{1,0:T(8,128)S(1)}, u32[]{:S(2)}, u32[]{:S(2)}) %collective-permute-start.9) | collective-permute-done | bytes 7200 | tf_op jit(solution)/shard_map/ppermute | solution.py:350
  68.6 0.0 collective-permute-done.10.gr_ref
  68.6 0.0 collective-permute-done.7.g0_ref
  68.6 0.0 copy-start.1
  68.7 0.0 collective-permute-done.8.g1_ref
  68.7 0.0 copy-start.2
  68.7 0.5 copy-done.5
  69.2 0.0 copy-done.6
  69.2 0.0 copy-done.1
  69.3 0.0 copy-done.2
  69.3 4.3 %shard_map.84 = f32[14,128,512]{2,1,0:T(8,128)} custom-call(f32[14,128,512]{2,1,0:T(8,128)} %get-tuple-element.28.out_in, f32[14,512]{1,0:T(8,128)} %copy-done.1, f32[14,512]{1,0:T(8,128)} %copy-done.2, f32[14,128]{1,0:T(8,128)} %copy-done.5, f32[14,128]{1,0:T(8,128)} %copy-done.6), custom_call_target="tpu_custom_call", output_to_operand_aliasing={{}: (0, {})} | custom-call | tf_op jit(solution)/shard_map/pallas_call | solution.py:288
  (9 shorter events, 0.1 us)
Async XLA Ops:
  0.0 6.9 %copy-start.7 = (s32[4,512]{1,0:T(4,128)S(1)}, s32[4,512]{1,0:T(4,128)}, u32[]{:S(2)}) copy-start(s32[4,512]{1,0:T(4,128)} %param.12) | copy-start | bytes 24580
  0.0 7.1 %copy-start.8 = (s32[4,512]{1,0:T(4,128)S(1)}, s32[4,512]{1,0:T(4,128)}, u32[]{:S(2)}) copy-start(s32[4,512]{1,0:T(4,128)} %param.14) | copy-start | bytes 24580
  0.0 10.0 %copy-start.9 = (f32[4,512]{1,0:T(4,128)S(1)}, f32[4,512]{1,0:T(4,128)}, u32[]{:S(2)}) copy-start(f32[4,512]{1,0:T(4,128)} %param.13) | copy-start | bytes 24580
  0.0 10.2 %copy-start.10 = (f32[4,512]{1,0:T(4,128)S(1)}, f32[4,512]{1,0:T(4,128)}, u32[]{:S(2)}) copy-start(f32[4,512]{1,0:T(4,128)} %param.15) | copy-start | bytes 24580
  1.9 9.2 %copy-start = (f32[14,1,512]{2,0,1:T(8,128)}, f32[14,1,512]{2,0,1:T(8,128)S(1)}, u32[]{:S(2)}) copy-start(f32[14,1,512]{2,0,1:T(8,128)S(1)} %copy.41) | copy-start | bytes 86020
  1.9 5.3 %collective-permute-start = (f32[1,15,512]{2,1,0:T(8,128)S(1)}, f32[1,15,512]{2,1,0:T(8,128)S(1)}, u32[]{:S(2)}, u32[]{:S(2)}) collective-permute-start(f32[1,15,512]{2,1,0:T(8,128)S(1)} %maximum_bitcast_fusion.1), channel_id=1, source_target_pairs={{0,4},{1,5},{2,6},{3,7},{4,0},{5,1},{6,2},{7,3},{8,12},{9,13},{10,... | collective-permute-start | bytes 92168 | tf_op jit(solution)/shard_map/ppermute | solution.py:326
  7.3 3.8 %collective-permute-start.1 = (f32[2,15,512]{2,1,0:T(8,128)S(1)}, f32[2,15,512]{2,1,0:T(8,128)S(1)}, u32[]{:S(2)}, u32[]{:S(2)}) collective-permute-start(f32[2,15,512]{2,1,0:T(8,128)S(1)} %pad_maximum_fusion.1), channel_id=1, source_target_pairs={{0,2},{1,3},{2,0},{3,1},{4,6},{5,7},{6,4},{7,5},{8,10},{9,11},{10,... | collective-permute-start | bytes 184328 | tf_op jit(solution)/shard_map/ppermute | solution.py:326
  11.1 7.7 %collective-permute-start.2 = (f32[4,15,512]{2,1,0:T(8,128)S(1)}, f32[4,15,512]{2,1,0:T(8,128)S(1)}, u32[]{:S(2)}, u32[]{:S(2)}) collective-permute-start(f32[4,15,512]{2,1,0:T(8,128)S(1)} %pad_maximum_fusion), channel_id=1, source_target_pairs={{0,1},{1,0},{2,3},{3,2},{4,5},{5,4},{6,7},{7,6},{8,9},{9,8},{10,11... | collective-permute-start | bytes 368648 | tf_op jit(solution)/shard_map/ppermute | solution.py:326
  14.6 6.2 %collective-permute-start.3 = (f32[14,128]{1,0:T(8,128)S(1)}, f32[14,128]{1,0:T(8,128)S(1)}, u32[]{:S(2)}, u32[]{:S(2)}) collective-permute-start(f32[14,128]{1,0:T(8,128)S(1)} %bitcast.24), channel_id=1, source_target_pairs={{0,1},{1,2},{2,3},{3,4},{4,5},{5,6},{6,7},{7,0},{8,9},{9,10},{10,1... | collective-permute-start | bytes 21512 | tf_op jit(solution)/shard_map/ppermute | solution.py:337
  14.8 5.9 %collective-permute-start.4 = (f32[14,128]{1,0:T(8,128)S(1)}, f32[14,128]{1,0:T(8,128)S(1)}, u32[]{:S(2)}, u32[]{:S(2)}) collective-permute-start(f32[14,128]{1,0:T(8,128)S(1)} %bitcast.23), channel_id=1, source_target_pairs={{1,0},{2,1},{3,2},{4,3},{5,4},{6,5},{7,6},{0,7},{9,8},{10,9},{11,1... | collective-permute-start | bytes 21512 | tf_op jit(solution)/shard_map/ppermute | solution.py:338
  20.7 0.6 copy-start.3
  20.8 0.6 copy-start.4
  23.7 10.8 %collective-permute-start.5 = (f32[14,512]{1,0:T(8,128)}, f32[14,512]{1,0:T(8,128)S(1)}, u32[]{:S(2)}, u32[]{:S(2)}) collective-permute-start(f32[14,512]{1,0:T(8,128)} %get-tuple-element.24), channel_id=1, source_target_pairs={{0,8},{8,16},{16,24},{1,9},{9,17},{17,25},{2,10},{10,18},{18,26},{... | collective-permute-start | bytes 86024 | tf_op jit(solution)/shard_map/ppermute | solution.py:341
  32.6 5.4 %collective-permute-start.6 = (f32[14,512]{1,0:T(8,128)}, f32[14,512]{1,0:T(8,128)S(1)}, u32[]{:S(2)}, u32[]{:S(2)}) collective-permute-start(f32[14,512]{1,0:T(8,128)} %get-tuple-element.25), channel_id=1, source_target_pairs={{8,0},{16,8},{24,16},{9,1},{17,9},{25,17},{10,2},{18,10},{26,18},{... | collective-permute-start | bytes 86024 | tf_op jit(solution)/shard_map/ppermute | solution.py:342
  34.5 3.5 %copy-start.11 = (f32[14,512]{1,0:T(8,128)}, f32[14,512]{1,0:T(8,128)S(1)}, u32[]{:S(2)}) copy-start(f32[14,512]{1,0:T(8,128)S(1)} %collective-permute-done.5.hlo_ref) | copy-start | bytes 86020
  38.0 0.6 copy-start.12
  58.7 9.9 %collective-permute-start.7 = (f32[14,512]{1,0:T(8,128)}, f32[14,512]{1,0:T(8,128)S(1)}, u32[]{:S(2)}, u32[]{:S(2)}) collective-permute-start(f32[14,512]{1,0:T(8,128)} %get-tuple-element.29), channel_id=1, source_target_pairs={{0,8},{8,16},{1,9},{9,17},{2,10},{10,18},{3,11},{11,19},{4,12},{12... | collective-permute-start | bytes 86024 | tf_op jit(solution)/shard_map/ppermute | solution.py:348
  60.7 7.9 %collective-permute-start.8 = (f32[14,512]{1,0:T(8,128)}, f32[14,512]{1,0:T(8,128)S(1)}, u32[]{:S(2)}, u32[]{:S(2)}) collective-permute-start(f32[14,512]{1,0:T(8,128)} %get-tuple-element.30), channel_id=1, source_target_pairs={{8,0},{16,8},{9,1},{17,9},{10,2},{18,10},{11,3},{19,11},{12,4},{20... | collective-permute-start | bytes 86024 | tf_op jit(solution)/shard_map/ppermute | solution.py:349
  63.0 5.6 %collective-permute-start.9 = (f32[14,128]{1,0:T(8,128)}, f32[14,128]{1,0:T(8,128)S(1)}, u32[]{:S(2)}, u32[]{:S(2)}) collective-permute-start(f32[14,128]{1,0:T(8,128)} %get-tuple-element.31), channel_id=1, source_target_pairs={{0,1},{1,2},{2,3},{3,4},{4,5},{5,6},{6,7},{7,0},{8,9},{9,10},{10,1... | collective-permute-start | bytes 21512 | tf_op jit(solution)/shard_map/ppermute | solution.py:350
  63.4 5.2 %collective-permute-start.10 = (f32[14,128]{1,0:T(8,128)}, f32[14,128]{1,0:T(8,128)S(1)}, u32[]{:S(2)}, u32[]{:S(2)}) collective-permute-start(f32[14,128]{1,0:T(8,128)} %get-tuple-element.32), channel_id=1, source_target_pairs={{1,0},{2,1},{3,2},{4,3},{5,4},{6,5},{7,6},{0,7},{9,8},{10,9},{11,1... | collective-permute-start | bytes 21512 | tf_op jit(solution)/shard_map/ppermute | solution.py:351
  68.6 0.6 copy-start.5
  68.6 0.6 copy-start.6
  68.6 0.6 copy-start.1
  68.7 0.6 copy-start.2

commit v17 on v16

--- a/solution.py
+++ b/solution.py
@@ -196,9 +196,9 @@
     )(mix, act, flags, fields, rate, halo_lo, halo_hi, lft, rgt)
 
 
-def interp_kernel(ks, flag_s, ids_s, wt_ref, table_ref, *refs):
-    n_in = (len(refs) - 2) // 2
-    ins, outs, acc, picked = refs[:n_in], refs[n_in:2 * n_in], refs[-2], refs[-1]
+def interp_kernel(ks, flag_s, ids_s, wt_ref, planes_ref, *refs):
+    n_in = (len(refs) - 3) // 2
+    ins, outs, acc, picked, table_ref = refs[:n_in], refs[n_in:2 * n_in], refs[-3], refs[-2], refs[-1]
     up_ref, down_ref = outs[0], outs[1]
     lanes = outs[0].shape[1]
     width = table_ref.shape[1]
@@ -206,6 +206,9 @@
 
     @pl.when(flag_s[0] + flag_s[1] > 0.5)
     def _():
+        for m in range(planes_ref.shape[0]):
+            table_ref[m * lanes:(m + 1) * lanes, :] = jnp.transpose(planes_ref[m])
+
         def group(pg, carry):
             p0 = pl.multiple_of(pg * SUB, SUB)
             for s in range(SUB):
@@ -231,11 +234,11 @@
         dst[...] = src[...]
 
 
-def interpolate(flags, ids, wt, table, passed):
+def interpolate(flags, ids, wt, planes, passed):
     ks, lanes = ids.shape
     smem = pl.BlockSpec(memory_space=pltpu.SMEM)
     vspec = pl.BlockSpec(memory_space=pltpu.VMEM)
-    width = table.shape[1]
+    n_planes, width, _ = planes.shape
     return pl.pallas_call(
         functools.partial(interp_kernel, ks),
         out_shape=tuple(jax.ShapeDtypeStruct(x.shape, x.dtype) for x in passed),
@@ -244,8 +247,9 @@
         scratch_shapes=[
             pltpu.VMEM((lanes, LANE), jnp.float32),
             pltpu.VMEM((ks, lanes, width), jnp.float32),
+            pltpu.VMEM((n_planes * lanes, width), jnp.float32),
         ],
-    )(flags, ids, wt, table, *passed)
+    )(flags, ids, wt, planes, *passed)
 
 
 def fix_kernel(low_w, side_w, out_in, g0_ref, g1_ref, gl_ref, gr_ref, out_ref, rb, cb, sem):
@@ -325,7 +329,6 @@
         partner = [(i, i ^ span) for i in range(n_blk)]
         planes = jnp.concatenate([planes, lax.ppermute(planes, "blk", partner)], axis=0)
         span //= 2
-    table = jnp.transpose(planes, (0, 2, 1)).reshape(n_blk * lanes, nf + 1)
     at_exit = g == exit_grp
     ids = jnp.where(at_exit, inlet_ids, outlet_ids)
     m = jnp.bitwise_xor(ids // lanes, b)
@@ -337,7 +340,7 @@
     lft = lax.ppermute(edges[2], "blk", [(i, (i + 1) % n_blk) for i in range(n_blk)])
     rgt = lax.ppermute(edges[3], "blk", [((i + 1) % n_blk, i) for i in range(n_blk)])
 
-    up, down, lft, rgt = interpolate(flags, ids, wt, table, (edges[0], edges[1], lft, rgt))
+    up, down, lft, rgt = interpolate(flags, ids, wt, planes, (edges[0], edges[1], lft, rgt))
     halo_lo = lax.ppermute(up, "grp", [(i, i + 1) for i in range(n_grp - 1)])
     halo_hi = lax.ppermute(down, "grp", [(i + 1, i) for i in range(n_grp - 1)])
 

time: 74.4 us -> 74.7 us (level)
  local copies, waits for them, and re-layouts: 9.54 us -> 8.16 us
  starting transfers between devices: 29.3 us -> 30.5 us
    reshape x1 -> x0, local copies, waits for them, and re-layouts: 1.97 us -> none  [shards(): table = jnp.transpose(planes, (0, 2, 1)).reshape(n_blk * lanes, nf + 1)]
    ppermute x1, starting transfers between devices: 8.84 us -> 10 us  [shards(): halo_lo = lax.ppermute(up, 'grp', [(i, i + 1) for i in range(n_grp - 1)])]
  transfers between devices with their start and end apart: 11 -> 11, of which waited for: 2 -> 3; matrix products, arithmetic and copies ran while one was open for 12% -> 10% of each run, Pallas kernels for 0% -> 0%
where the time goes in v17:
time: 74.7 us; the launch traced here: 73.9 us
  starting transfers between devices  30.5 us (41%)
  Pallas kernels  26.2 us (35%)
  local copies, waits for them, and re-layouts  8.16 us (11%)
  waiting for transfers between devices  5.19 us (7%)
  other arithmetic  3.56 us (5%)
    pallas_call x1, Pallas kernels, fused_step(): pl.pallas_call(functools.partial(step_kernel, nf, rows, lanes), out_shape...  20.1 us
    ppermute x1, starting transfers between devices, shards(): halo_lo = lax.ppermute(up, 'grp', [(i, i + 1) for i in range(n_grp - 1)])  10 us
    ppermute x3, starting transfers between devices, shards(): lax.ppermute(planes, 'blk', partner)  5.84 us
    pallas_call x1, Pallas kernels, fix_edges(): pl.pallas_call(functools.partial(fix_kernel, low_w, side_w), out_shape=ja...  4.34 us
    unnamed x34, local copies, waits for them, and re-layouts  4.28 us
    ppermute x1, starting transfers between devices, shards(): gr = lax.ppermute(clo, 'blk', [((i + 1) % n_blk, i) for i in range(n_blk)])  4.02 us
    ppermute x1, starting transfers between devices, shards(): lax.ppermute(edges[3], 'blk', [((i + 1) % n_blk, i) for i in range(n_blk)])  3.91 us
    ppermute x1, waiting for transfers between devices, shards(): halo_hi = lax.ppermute(down, 'grp', [(i + 1, i) for i in range(n_grp - 1)])  3.5 us
  transfers between devices with their start and end apart: 11, of which 3 were waited for; matrix products, arithmetic and copies ran while one was open for 10% of the time, Pallas kernels for 0%

profile of v17, /device:TPU:1, one launch (start us, length us, event | category | flops | bytes accessed | tf_op | source)
XLA Modules:
  0.0 73.9 jit_solution(17184040096198856689)
XLA Ops:
  0.0 0.0 copy-start.7
  0.0 0.0 copy-start.8
  0.0 0.0 copy-start.9
  0.0 0.0 copy-start.10
  0.0 0.8 %slice_bitcast_fusion = f32[1,512]{1,0:T(1,128)S(1)} fusion(f32[14,128,512]{2,1,0:T(8,128)} %f_hbm.1), kind=kLoop, calls=%fused_computation.41 | loop fusion | bytes 4096 | tf_op jit(solution)/shard_map/slice | solution.py:320
  0.8 1.1 %fusion.13 = (f32[14,1,512]{2,1,0:T(1,128)S(1)}, f32[14,1,512]{2,1,0:T(1,128)S(1)}) fusion(f32[14,128,512]{2,1,0:T(8,128)} %f_hbm.1), kind=kLoop, calls=%fused_computation.44 | loop fusion | bytes 114688 | tf_op jit(solution)/shard_map/slice | solution.py:319
  1.9 0.0 copy-start
  1.9 3.2 %collective-permute-start = (f32[1,15,512]{2,1,0:T(8,128)S(1)}, f32[1,15,512]{2,1,0:T(8,128)S(1)}, u32[]{:S(2)}, u32[]{:S(2)}) collective-permute-start(f32[1,15,512]{2,1,0:T(8,128)S(1)} %maximum_bitcast_fusion), channel_id=1, source_target_pairs={{0,4},{1,5},{2,6},{3,7},{4,0},{5,1},{6,2},{7,3},{8,12},{9,13},{10,... | collective-permute-start | bytes 92168 | tf_op jit(solution)/shard_map/ppermute | solution.py:330
  5.1 1.8 %fusion.12 = (f32[14,128,1]{2,1,0:T(8,128)S(1)}, f32[14,128,1]{2,1,0:T(8,128)S(1)}) fusion(f32[14,128,512]{2,1,0:T(8,128)} %f_hbm.1), kind=kLoop, calls=%fused_computation.43 | loop fusion | bytes 28672 | tf_op jit(solution)/shard_map/slice | solution.py:324
  6.9 0.0 copy-done.7
  6.9 0.1 copy.10
  7.1 0.0 copy-done.8
  7.1 0.1 copy.11
  7.3 0.0 collective-permute-done
  7.3 1.4 %collective-permute-start.1 = (f32[2,15,512]{2,1,0:T(8,128)S(1)}, f32[2,15,512]{2,1,0:T(8,128)S(1)}, u32[]{:S(2)}, u32[]{:S(2)}) collective-permute-start(f32[2,15,512]{2,1,0:T(8,128)S(1)} %pad_maximum_fusion.2), channel_id=1, source_target_pairs={{0,2},{1,3},{2,0},{3,1},{4,6},{5,7},{6,4},{7,5},{8,10},{9,11},{10,... | collective-permute-start | bytes 184328 | tf_op jit(solution)/shard_map/ppermute | solution.py:330
  8.6 0.8 %add_select_fusion = (s32[4,512]{0,1:T(8,128)S(1)}, s32[4,512]{0,1:T(8,128)S(1)}) fusion(s32[4,512]{0,1:T(8,128)S(1)} %copy.10, s32[4,512]{0,1:T(8,128)S(1)} %copy.11, pred[]{:T(512)} %eq.12, s32[]{:T(128)S(6)} %axis_index.25), kind=kLoop, calls=%fused_computation | loop fusion | flops 157696 | bytes 32773 | tf_op jit(solution)/shard_map/jit(remainder)/select_n | solution.py:338
  9.4 0.6 copy.26
  10.1 0.0 copy-done.9
  10.1 0.1 copy.14
  10.2 0.0 copy-done.10
  10.2 0.1 copy.15
  10.4 0.3 copy.23
  10.7 0.3 copy.22
  11.0 0.0 copy-done
  11.0 0.0 collective-permute-done.1
  11.1 1.3 %collective-permute-start.2 = (f32[4,15,512]{2,1,0:T(8,128)S(1)}, f32[4,15,512]{2,1,0:T(8,128)S(1)}, u32[]{:S(2)}, u32[]{:S(2)}) collective-permute-start(f32[4,15,512]{2,1,0:T(8,128)S(1)} %pad_maximum_fusion.1), channel_id=1, source_target_pairs={{0,1},{1,0},{2,3},{3,2},{4,5},{5,4},{6,7},{7,6},{8,9},{9,8},{10,11... | collective-permute-start | bytes 368648 | tf_op jit(solution)/shard_map/ppermute | solution.py:330
  12.4 0.7 select_bitcast_fusion.wt_ref
  13.1 0.1 copy.13
  13.2 0.1 copy.12
  13.3 0.6 add.37.ids_s
  13.9 0.6 add_convert_fusion.flag_s
  14.6 0.3 collective-permute-start.3
  14.8 3.9 %collective-permute-start.4 = (f32[14,128]{1,0:T(8,128)S(1)}, f32[14,128]{1,0:T(8,128)S(1)}, u32[]{:S(2)}, u32[]{:S(2)}) collective-permute-start(f32[14,128]{1,0:T(8,128)S(1)} %bitcast.19), channel_id=1, source_target_pairs={{1,0},{2,1},{3,2},{4,3},{5,4},{6,5},{7,6},{0,7},{9,8},{10,9},{11,1... | collective-permute-start | bytes 21512 | tf_op jit(solution)/shard_map/ppermute | solution.py:341
  18.7 0.0 collective-permute-done.2
  18.7 0.7 pad_maximum_fusion.planes_ref
  19.5 0.3 collective-permute-done.3.refs_2_
  19.8 0.0 copy-start.3
  19.8 0.0 collective-permute-done.4.refs_3_
  19.8 0.6 copy-done.3
  20.4 0.6 copy-done.5
  21.0 1.8 %shard_map.82 = (f32[14,512]{1,0:T(8,128)}, f32[14,512]{1,0:T(8,128)}, f32[14,128]{1,0:T(8,128)}, f32[14,128]{1,0:T(8,128)}) custom-call(f32[2]{0:T(128)} %add_convert_fusion.flag_s, s32[4,512]{1,0:T(4,128)} %add.37.ids_s, f32[512,4]{1,0:T(8,128)} %select_bitcast_fusion.wt_ref, f32[8,15,512]{2,1,0:T(8,128)} %pad_maximum_fusion.planes_ref, ...), custom_call_target="tpu_custom_call" | custom-call | tf_op jit(solution)/shard_map/pallas_call | solution.py:242
  22.8 10.0 %collective-permute-start.5 = (f32[14,512]{1,0:T(8,128)}, f32[14,512]{1,0:T(8,128)S(1)}, u32[]{:S(2)}, u32[]{:S(2)}) collective-permute-start(f32[14,512]{1,0:T(8,128)} %get-tuple-element.24), channel_id=1, source_target_pairs={{0,8},{8,16},{16,24},{1,9},{9,17},{17,25},{2,10},{10,18},{18,26},{... | collective-permute-start | bytes 86024 | tf_op jit(solution)/shard_map/ppermute | solution.py:344
  32.8 1.9 %collective-permute-start.6 = (f32[14,512]{1,0:T(8,128)}, f32[14,512]{1,0:T(8,128)S(1)}, u32[]{:S(2)}, u32[]{:S(2)}) collective-permute-start(f32[14,512]{1,0:T(8,128)} %get-tuple-element.25), channel_id=1, source_target_pairs={{8,0},{16,8},{24,16},{9,1},{17,9},{25,17},{10,2},{18,10},{26,18},{... | collective-permute-start | bytes 86024 | tf_op jit(solution)/shard_map/ppermute | solution.py:345
  34.7 0.0 collective-permute-done.5.hlo_ref
  34.8 0.0 copy-start.11
  34.8 3.5 %collective-permute-done.6.hhi_ref = f32[14,512]{1,0:T(8,128)S(1)} collective-permute-done((f32[14,512]{1,0:T(8,128)}, f32[14,512]{1,0:T(8,128)S(1)}, u32[]{:S(2)}, u32[]{:S(2)}) %collective-permute-start.6) | collective-permute-done | bytes 28704 | tf_op jit(solution)/shard_map/ppermute | solution.py:345
  38.3 0.0 copy-done.11
  38.3 0.6 copy-done.12
  38.9 20.1 %shard_map.83 = (f32[14,128,512]{2,1,0:T(8,128)}, f32[14,512]{1,0:T(8,128)}, f32[14,512]{1,0:T(8,128)}, f32[14,128]{1,0:T(8,128)}, f32[14,128]{1,0:T(8,128)}) custom-call(f32[14,14]{1,0:T(8,128)} %mix_s.1, f32[14]{0:T(128)} %act_s.1, f32[2]{0:T(128)} %add_convert_fusion.flag_s, f32[14,128,512]{2,1,0:T(8,128)} %f_hbm.1, f32[128,512]{1,0:T(8,128)} %rate_ref.1, ...), custom_call_target="tpu_custom_call" | custom-call | flops 95420416 | bytes 7602176 | tf_op jit(solution)/shard_map/pallas_call | solution.py:176
  58.9 2.0 %collective-permute-start.7 = (f32[14,512]{1,0:T(8,128)}, f32[14,512]{1,0:T(8,128)S(1)}, u32[]{:S(2)}, u32[]{:S(2)}) collective-permute-start(f32[14,512]{1,0:T(8,128)} %get-tuple-element.29), channel_id=1, source_target_pairs={{0,8},{8,16},{1,9},{9,17},{2,10},{10,18},{3,11},{11,19},{4,12},{12... | collective-permute-start | bytes 86024 | tf_op jit(solution)/shard_map/ppermute | solution.py:351
  61.0 2.3 %collective-permute-start.8 = (f32[14,512]{1,0:T(8,128)}, f32[14,512]{1,0:T(8,128)S(1)}, u32[]{:S(2)}, u32[]{:S(2)}) collective-permute-start(f32[14,512]{1,0:T(8,128)} %get-tuple-element.30), channel_id=1, source_target_pairs={{8,0},{16,8},{9,1},{17,9},{10,2},{18,10},{11,3},{19,11},{12,4},{20... | collective-permute-start | bytes 86024 | tf_op jit(solution)/shard_map/ppermute | solution.py:352
  63.3 0.2 collective-permute-start.9
  63.5 4.0 %collective-permute-start.10 = (f32[14,128]{1,0:T(8,128)}, f32[14,128]{1,0:T(8,128)S(1)}, u32[]{:S(2)}, u32[]{:S(2)}) collective-permute-start(f32[14,128]{1,0:T(8,128)} %get-tuple-element.32), channel_id=1, source_target_pairs={{1,0},{2,1},{3,2},{4,3},{5,4},{6,5},{7,6},{0,7},{9,8},{10,9},{11,1... | collective-permute-start | bytes 21512 | tf_op jit(solution)/shard_map/ppermute | solution.py:354
  67.5 1.4 %collective-permute-done.9.gl_ref = f32[14,128]{1,0:T(8,128)S(1)} collective-permute-done((f32[14,128]{1,0:T(8,128)}, f32[14,128]{1,0:T(8,128)S(1)}, u32[]{:S(2)}, u32[]{:S(2)}) %collective-permute-start.9) | collective-permute-done | bytes 7200 | tf_op jit(solution)/shard_map/ppermute | solution.py:353
  68.9 0.0 collective-permute-done.10.gr_ref
  68.9 0.0 collective-permute-done.7.g0_ref
  68.9 0.0 copy-start.1
  68.9 0.0 collective-permute-done.8.g1_ref
  68.9 0.0 copy-start.2
  68.9 0.5 copy-done.4
  69.5 0.0 copy-done.6
  69.5 0.0 copy-done.1
  69.5 0.0 copy-done.2
  69.5 4.3 %shard_map.84 = f32[14,128,512]{2,1,0:T(8,128)} custom-call(f32[14,128,512]{2,1,0:T(8,128)} %get-tuple-element.28.out_in, f32[14,512]{1,0:T(8,128)} %copy-done.1, f32[14,512]{1,0:T(8,128)} %copy-done.2, f32[14,128]{1,0:T(8,128)} %copy-done.4, f32[14,128]{1,0:T(8,128)} %copy-done.6), custom_call_target="tpu_custom_call", output_to_operand_aliasing={{}: (0, {})} | custom-call | tf_op jit(solution)/shard_map/pallas_call | solution.py:292
  (8 shorter events, 0.0 us)
Async XLA Ops:
  0.0 6.9 %copy-start.7 = (s32[4,512]{1,0:T(4,128)S(1)}, s32[4,512]{1,0:T(4,128)}, u32[]{:S(2)}) copy-start(s32[4,512]{1,0:T(4,128)} %param.12) | copy-start | bytes 24580
  0.0 7.1 %copy-start.8 = (s32[4,512]{1,0:T(4,128)S(1)}, s32[4,512]{1,0:T(4,128)}, u32[]{:S(2)}) copy-start(s32[4,512]{1,0:T(4,128)} %param.14) | copy-start | bytes 24580
  0.0 10.0 %copy-start.9 = (f32[4,512]{1,0:T(4,128)S(1)}, f32[4,512]{1,0:T(4,128)}, u32[]{:S(2)}) copy-start(f32[4,512]{1,0:T(4,128)} %param.13) | copy-start | bytes 24580
  0.0 10.2 %copy-start.10 = (f32[4,512]{1,0:T(4,128)S(1)}, f32[4,512]{1,0:T(4,128)}, u32[]{:S(2)}) copy-start(f32[4,512]{1,0:T(4,128)} %param.15) | copy-start | bytes 24580
  1.9 9.2 %copy-start = (f32[14,1,512]{2,0,1:T(8,128)}, f32[14,1,512]{2,0,1:T(8,128)S(1)}, u32[]{:S(2)}) copy-start(f32[14,1,512]{2,0,1:T(8,128)S(1)} %copy.27) | copy-start | bytes 86020
  1.9 5.3 %collective-permute-start = (f32[1,15,512]{2,1,0:T(8,128)S(1)}, f32[1,15,512]{2,1,0:T(8,128)S(1)}, u32[]{:S(2)}, u32[]{:S(2)}) collective-permute-start(f32[1,15,512]{2,1,0:T(8,128)S(1)} %maximum_bitcast_fusion), channel_id=1, source_target_pairs={{0,4},{1,5},{2,6},{3,7},{4,0},{5,1},{6,2},{7,3},{8,12},{9,13},{10,... | collective-permute-start | bytes 92168 | tf_op jit(solution)/shard_map/ppermute | solution.py:330
  7.3 3.8 %collective-permute-start.1 = (f32[2,15,512]{2,1,0:T(8,128)S(1)}, f32[2,15,512]{2,1,0:T(8,128)S(1)}, u32[]{:S(2)}, u32[]{:S(2)}) collective-permute-start(f32[2,15,512]{2,1,0:T(8,128)S(1)} %pad_maximum_fusion.2), channel_id=1, source_target_pairs={{0,2},{1,3},{2,0},{3,1},{4,6},{5,7},{6,4},{7,5},{8,10},{9,11},{10,... | collective-permute-start | bytes 184328 | tf_op jit(solution)/shard_map/ppermute | solution.py:330
  11.1 7.7 %collective-permute-start.2 = (f32[4,15,512]{2,1,0:T(8,128)S(1)}, f32[4,15,512]{2,1,0:T(8,128)S(1)}, u32[]{:S(2)}, u32[]{:S(2)}) collective-permute-start(f32[4,15,512]{2,1,0:T(8,128)S(1)} %pad_maximum_fusion.1), channel_id=1, source_target_pairs={{0,1},{1,0},{2,3},{3,2},{4,5},{5,4},{6,7},{7,6},{8,9},{9,8},{10,11... | collective-permute-start | bytes 368648 | tf_op jit(solution)/shard_map/ppermute | solution.py:330
  14.6 5.2 %collective-permute-start.3 = (f32[14,128]{1,0:T(8,128)S(1)}, f32[14,128]{1,0:T(8,128)S(1)}, u32[]{:S(2)}, u32[]{:S(2)}) collective-permute-start(f32[14,128]{1,0:T(8,128)S(1)} %bitcast.20), channel_id=1, source_target_pairs={{0,1},{1,2},{2,3},{3,4},{4,5},{5,6},{6,7},{7,0},{8,9},{9,10},{10,1... | collective-permute-start | bytes 21512 | tf_op jit(solution)/shard_map/ppermute | solution.py:340
  14.8 4.9 %collective-permute-start.4 = (f32[14,128]{1,0:T(8,128)S(1)}, f32[14,128]{1,0:T(8,128)S(1)}, u32[]{:S(2)}, u32[]{:S(2)}) collective-permute-start(f32[14,128]{1,0:T(8,128)S(1)} %bitcast.19), channel_id=1, source_target_pairs={{1,0},{2,1},{3,2},{4,3},{5,4},{6,5},{7,6},{0,7},{9,8},{10,9},{11,1... | collective-permute-start | bytes 21512 | tf_op jit(solution)/shard_map/ppermute | solution.py:341
  19.8 0.6 copy-start.3
  20.4 0.6 copy-start.5
  22.8 12.0 %collective-permute-start.5 = (f32[14,512]{1,0:T(8,128)}, f32[14,512]{1,0:T(8,128)S(1)}, u32[]{:S(2)}, u32[]{:S(2)}) collective-permute-start(f32[14,512]{1,0:T(8,128)} %get-tuple-element.24), channel_id=1, source_target_pairs={{0,8},{8,16},{16,24},{1,9},{9,17},{17,25},{2,10},{10,18},{18,26},{... | collective-permute-start | bytes 86024 | tf_op jit(solution)/shard_map/ppermute | solution.py:344
  32.8 5.4 %collective-permute-start.6 = (f32[14,512]{1,0:T(8,128)}, f32[14,512]{1,0:T(8,128)S(1)}, u32[]{:S(2)}, u32[]{:S(2)}) collective-permute-start(f32[14,512]{1,0:T(8,128)} %get-tuple-element.25), channel_id=1, source_target_pairs={{8,0},{16,8},{24,16},{9,1},{17,9},{25,17},{10,2},{18,10},{26,18},{... | collective-permute-start | bytes 86024 | tf_op jit(solution)/shard_map/ppermute | solution.py:345
  34.8 3.5 %copy-start.11 = (f32[14,512]{1,0:T(8,128)}, f32[14,512]{1,0:T(8,128)S(1)}, u32[]{:S(2)}) copy-start(f32[14,512]{1,0:T(8,128)S(1)} %collective-permute-done.5.hlo_ref) | copy-start | bytes 86020
  38.3 0.6 copy-start.12
  58.9 9.9 %collective-permute-start.7 = (f32[14,512]{1,0:T(8,128)}, f32[14,512]{1,0:T(8,128)S(1)}, u32[]{:S(2)}, u32[]{:S(2)}) collective-permute-start(f32[14,512]{1,0:T(8,128)} %get-tuple-element.29), channel_id=1, source_target_pairs={{0,8},{8,16},{1,9},{9,17},{2,10},{10,18},{3,11},{11,19},{4,12},{12... | collective-permute-start | bytes 86024 | tf_op jit(solution)/shard_map/ppermute | solution.py:351
  61.0 7.9 %collective-permute-start.8 = (f32[14,512]{1,0:T(8,128)}, f32[14,512]{1,0:T(8,128)S(1)}, u32[]{:S(2)}, u32[]{:S(2)}) collective-permute-start(f32[14,512]{1,0:T(8,128)} %get-tuple-element.30), channel_id=1, source_target_pairs={{8,0},{16,8},{9,1},{17,9},{10,2},{18,10},{11,3},{19,11},{12,4},{20... | collective-permute-start | bytes 86024 | tf_op jit(solution)/shard_map/ppermute | solution.py:352
  63.3 5.6 %collective-permute-start.9 = (f32[14,128]{1,0:T(8,128)}, f32[14,128]{1,0:T(8,128)S(1)}, u32[]{:S(2)}, u32[]{:S(2)}) collective-permute-start(f32[14,128]{1,0:T(8,128)} %get-tuple-element.31), channel_id=1, source_target_pairs={{0,1},{1,2},{2,3},{3,4},{4,5},{5,6},{6,7},{7,0},{8,9},{9,10},{10,1... | collective-permute-start | bytes 21512 | tf_op jit(solution)/shard_map/ppermute | solution.py:353
  63.5 5.4 %collective-permute-start.10 = (f32[14,128]{1,0:T(8,128)}, f32[14,128]{1,0:T(8,128)S(1)}, u32[]{:S(2)}, u32[]{:S(2)}) collective-permute-start(f32[14,128]{1,0:T(8,128)} %get-tuple-element.32), channel_id=1, source_target_pairs={{1,0},{2,1},{3,2},{4,3},{5,4},{6,5},{7,6},{0,7},{9,8},{10,9},{11,1... | collective-permute-start | bytes 21512 | tf_op jit(solution)/shard_map/ppermute | solution.py:354
  68.9 0.6 copy-start.4
  68.9 0.6 copy-start.6
  68.9 0.6 copy-start.1
  68.9 0.6 copy-start.2

commit v18 on v16

--- a/solution.py
+++ b/solution.py
@@ -106,7 +106,7 @@
                 tends[h].append((v, flow + accs[h]))
         return tends
 
-    pair = 2 if n_j % 2 == 0 else 1
+    pair = 4 if n_j % 4 == 0 else (2 if n_j % 2 == 0 else 1)
     n_jp = n_j // pair
 
     def tile_offsets(t):

time: 74.4 us -> 73 us (0.981)
  Pallas kernels: 26.8 us -> 25.3 us
    pallas_call x1, Pallas kernels: 20.1 us -> 18.6 us  [fused_step(): pl.pallas_call(functools.partial(step_kernel, nf, rows, lanes), out_shape...]
where the time goes in v18:
time: 73 us; the launch traced here: 72.1 us
  starting transfers between devices  29.3 us (40%)
  Pallas kernels  25.3 us (35%)
  local copies, waits for them, and re-layouts  9.54 us (13%)
  waiting for transfers between devices  4.9 us (7%)
  other arithmetic  2.85 us (4%)
    pallas_call x1, Pallas kernels, fused_step(): pl.pallas_call(functools.partial(step_kernel, nf, rows, lanes), out_shape...  18.6 us
    ppermute x1, starting transfers between devices, shards(): halo_lo = lax.ppermute(up, 'grp', [(i, i + 1) for i in range(n_grp - 1)])  8.84 us
    ppermute x3, starting transfers between devices, shards(): lax.ppermute(planes, 'blk', partner)  5.84 us
    pallas_call x1, Pallas kernels, fix_edges(): pl.pallas_call(functools.partial(fix_kernel, low_w, side_w), out_shape=ja...  4.34 us
    ppermute x1, starting transfers between devices, shards(): lax.ppermute(edges[3], 'blk', [((i + 1) % n_blk, i) for i in range(n_blk)])  3.91 us
    ppermute x1, starting transfers between devices, shards(): gr = lax.ppermute(clo, 'blk', [((i + 1) % n_blk, i) for i in range(n_blk)])  3.81 us
    unnamed x34, local copies, waits for them, and re-layouts  3.69 us
    ppermute x1, waiting for transfers between devices, shards(): halo_hi = lax.ppermute(down, 'grp', [(i + 1, i) for i in range(n_grp - 1)])  3.5 us
  transfers between devices with their start and end apart: 11, of which 2 were waited for; matrix products, arithmetic and copies ran while one was open for 12% of the time, Pallas kernels for 0%

profile of v18, /device:TPU:1, one launch (start us, length us, event | category | flops | bytes accessed | tf_op | source)
XLA Modules:
  0.0 72.1 jit_solution(1760603385165590490)
XLA Ops:
  0.0 0.0 copy-start.7
  0.0 0.0 copy-start.8
  0.0 0.0 copy-start.9
  0.0 0.0 copy-start.10
  0.0 0.8 %slice_bitcast_fusion = f32[1,512]{1,0:T(1,128)S(1)} fusion(f32[14,128,512]{2,1,0:T(8,128)} %f_hbm.1), kind=kLoop, calls=%fused_computation.41 | loop fusion | bytes 4096 | tf_op jit(solution)/shard_map/slice | solution.py:316
  0.8 1.1 %fusion.13 = (f32[14,1,512]{2,1,0:T(1,128)S(1)}, f32[14,1,512]{2,1,0:T(1,128)S(1)}) fusion(f32[14,128,512]{2,1,0:T(8,128)} %f_hbm.1), kind=kLoop, calls=%fused_computation.44 | loop fusion | bytes 114688 | tf_op jit(solution)/shard_map/slice | solution.py:315
  1.9 0.0 copy-start
  1.9 3.2 %collective-permute-start = (f32[1,15,512]{2,1,0:T(8,128)S(1)}, f32[1,15,512]{2,1,0:T(8,128)S(1)}, u32[]{:S(2)}, u32[]{:S(2)}) collective-permute-start(f32[1,15,512]{2,1,0:T(8,128)S(1)} %maximum_bitcast_fusion.1), channel_id=1, source_target_pairs={{0,4},{1,5},{2,6},{3,7},{4,0},{5,1},{6,2},{7,3},{8,12},{9,13},{10,... | collective-permute-start | bytes 92168 | tf_op jit(solution)/shard_map/ppermute | solution.py:326
  5.1 1.8 %fusion.12 = (f32[14,128,1]{2,1,0:T(8,128)S(1)}, f32[14,128,1]{2,1,0:T(8,128)S(1)}) fusion(f32[14,128,512]{2,1,0:T(8,128)} %f_hbm.1), kind=kLoop, calls=%fused_computation.43 | loop fusion | bytes 28672 | tf_op jit(solution)/shard_map/slice | solution.py:320
  6.9 0.0 copy-done.7
  6.9 0.1 copy.20
  7.1 0.0 copy-done.8
  7.1 0.1 copy.21
  7.3 0.0 collective-permute-done
  7.3 1.4 %collective-permute-start.1 = (f32[2,15,512]{2,1,0:T(8,128)S(1)}, f32[2,15,512]{2,1,0:T(8,128)S(1)}, u32[]{:S(2)}, u32[]{:S(2)}) collective-permute-start(f32[2,15,512]{2,1,0:T(8,128)S(1)} %pad_maximum_fusion.1), channel_id=1, source_target_pairs={{0,2},{1,3},{2,0},{3,1},{4,6},{5,7},{6,4},{7,5},{8,10},{9,11},{10,... | collective-permute-start | bytes 184328 | tf_op jit(solution)/shard_map/ppermute | solution.py:326
  8.6 0.8 %add_select_fusion = (s32[4,512]{0,1:T(8,128)S(1)}, s32[4,512]{0,1:T(8,128)S(1)}) fusion(s32[4,512]{0,1:T(8,128)S(1)} %copy.20, s32[4,512]{0,1:T(8,128)S(1)} %copy.21, pred[]{:T(512)} %eq.12, s32[]{:T(128)S(6)} %axis_index.25), kind=kLoop, calls=%fused_computation | loop fusion | flops 157696 | bytes 32773 | tf_op jit(solution)/shard_map/jit(remainder)/select_n | solution.py:335
  9.4 0.6 copy.40
  10.1 0.0 copy-done.9
  10.1 0.1 copy.24
  10.2 0.0 copy-done.10
  10.2 0.1 copy.25
  10.4 0.3 copy.37
  10.7 0.3 copy.36
  11.0 0.0 copy-done
  11.0 0.0 collective-permute-done.1
  11.1 1.3 %collective-permute-start.2 = (f32[4,15,512]{2,1,0:T(8,128)S(1)}, f32[4,15,512]{2,1,0:T(8,128)S(1)}, u32[]{:S(2)}, u32[]{:S(2)}) collective-permute-start(f32[4,15,512]{2,1,0:T(8,128)S(1)} %pad_maximum_fusion), channel_id=1, source_target_pairs={{0,1},{1,0},{2,3},{3,2},{4,5},{5,4},{6,7},{7,6},{8,9},{9,8},{10,11... | collective-permute-start | bytes 368648 | tf_op jit(solution)/shard_map/ppermute | solution.py:326
  12.4 0.7 %select_bitcast_fusion.wt_ref = f32[512,4]{1,0:T(8,128)} fusion(f32[4,512]{0,1:T(8,128)S(1)} %copy.24, f32[4,512]{0,1:T(8,128)S(1)} %copy.25, pred[]{:T(512)} %eq.12), kind=kLoop, calls=%fused_computation.29 | loop fusion | flops 2048 | bytes 24577 | tf_op jit(solution)/shard_map/transpose | solution.py:336
  13.1 0.1 copy.23
  13.2 0.1 copy.22
  13.3 0.6 add.37.ids_s
  13.9 0.6 add_convert_fusion.flag_s
  14.6 0.3 collective-permute-start.3
  14.8 3.9 %collective-permute-start.4 = (f32[14,128]{1,0:T(8,128)S(1)}, f32[14,128]{1,0:T(8,128)S(1)}, u32[]{:S(2)}, u32[]{:S(2)}) collective-permute-start(f32[14,128]{1,0:T(8,128)S(1)} %bitcast.23), channel_id=1, source_target_pairs={{1,0},{2,1},{3,2},{4,3},{5,4},{6,5},{7,6},{0,7},{9,8},{10,9},{11,1... | collective-permute-start | bytes 21512 | tf_op jit(solution)/shard_map/ppermute | solution.py:338
  18.7 0.0 collective-permute-done.2
  18.8 2.0 %copy.32 = f32[8,512,15]{2,1,0:T(8,128)} copy(f32[8,512,15]{1,2,0:T(8,128)S(1)} %maximum_bitcast_fusion) | data formatting | bytes 491520 | tf_op jit(solution)/shard_map/reshape | solution.py:328
  20.7 0.0 collective-permute-done.3.refs_2_
  20.8 0.0 collective-permute-done.4.refs_3_
  20.8 0.0 copy-start.4
  20.8 0.6 copy-done.3
  21.3 0.0 copy-done.4
  21.4 2.4 %shard_map.82 = (f32[14,512]{1,0:T(8,128)}, f32[14,512]{1,0:T(8,128)}, f32[14,128]{1,0:T(8,128)}, f32[14,128]{1,0:T(8,128)}) custom-call(f32[2]{0:T(128)} %add_convert_fusion.flag_s, s32[4,512]{1,0:T(4,128)} %add.37.ids_s, f32[512,4]{1,0:T(8,128)} %select_bitcast_fusion.wt_ref, f32[4096,15]{1,0:T(8,128)} %bitcast.19, f32[14,512]{1,0:T(8,128)} %bitcast.21, ...), custom_call_target="tpu_custom_call" | custom-call | tf_op jit(solution)/shard_map/pallas_call | solution.py:239
  23.7 8.8 %collective-permute-start.5 = (f32[14,512]{1,0:T(8,128)}, f32[14,512]{1,0:T(8,128)S(1)}, u32[]{:S(2)}, u32[]{:S(2)}) collective-permute-start(f32[14,512]{1,0:T(8,128)} %get-tuple-element.24), channel_id=1, source_target_pairs={{0,8},{8,16},{16,24},{1,9},{9,17},{17,25},{2,10},{10,18},{18,26},{... | collective-permute-start | bytes 86024 | tf_op jit(solution)/shard_map/ppermute | solution.py:341
  32.6 1.9 %collective-permute-start.6 = (f32[14,512]{1,0:T(8,128)}, f32[14,512]{1,0:T(8,128)S(1)}, u32[]{:S(2)}, u32[]{:S(2)}) collective-permute-start(f32[14,512]{1,0:T(8,128)} %get-tuple-element.25), channel_id=1, source_target_pairs={{8,0},{16,8},{24,16},{9,1},{17,9},{25,17},{10,2},{18,10},{26,18},{... | collective-permute-start | bytes 86024 | tf_op jit(solution)/shard_map/ppermute | solution.py:342
  34.5 0.0 collective-permute-done.5.hlo_ref
  34.5 0.0 copy-start.11
  34.5 3.5 %collective-permute-done.6.hhi_ref = f32[14,512]{1,0:T(8,128)S(1)} collective-permute-done((f32[14,512]{1,0:T(8,128)}, f32[14,512]{1,0:T(8,128)S(1)}, u32[]{:S(2)}, u32[]{:S(2)}) %collective-permute-start.6) | collective-permute-done | bytes 28704 | tf_op jit(solution)/shard_map/ppermute | solution.py:342
  38.0 0.0 copy-done.11
  38.0 0.6 copy-done.12
  38.6 18.6 %shard_map.83 = (f32[14,128,512]{2,1,0:T(8,128)}, f32[14,512]{1,0:T(8,128)}, f32[14,512]{1,0:T(8,128)}, f32[14,128]{1,0:T(8,128)}, f32[14,128]{1,0:T(8,128)}) custom-call(f32[14,14]{1,0:T(8,128)} %mix_s.1, f32[14]{0:T(128)} %act_s.1, f32[2]{0:T(128)} %add_convert_fusion.flag_s, f32[14,128,512]{2,1,0:T(8,128)} %f_hbm.1, f32[128,512]{1,0:T(8,128)} %rate_ref.1, ...), custom_call_target="tpu_custom_call" | custom-call | flops 95420416 | bytes 7602176 | tf_op jit(solution)/shard_map/pallas_call | solution.py:176
  57.2 2.0 %collective-permute-start.7 = (f32[14,512]{1,0:T(8,128)}, f32[14,512]{1,0:T(8,128)S(1)}, u32[]{:S(2)}, u32[]{:S(2)}) collective-permute-start(f32[14,512]{1,0:T(8,128)} %get-tuple-element.29), channel_id=1, source_target_pairs={{0,8},{8,16},{1,9},{9,17},{2,10},{10,18},{3,11},{11,19},{4,12},{12... | collective-permute-start | bytes 86024 | tf_op jit(solution)/shard_map/ppermute | solution.py:348
  59.2 2.3 %collective-permute-start.8 = (f32[14,512]{1,0:T(8,128)}, f32[14,512]{1,0:T(8,128)S(1)}, u32[]{:S(2)}, u32[]{:S(2)}) collective-permute-start(f32[14,512]{1,0:T(8,128)} %get-tuple-element.30), channel_id=1, source_target_pairs={{8,0},{16,8},{9,1},{17,9},{10,2},{18,10},{11,3},{19,11},{12,4},{20... | collective-permute-start | bytes 86024 | tf_op jit(solution)/shard_map/ppermute | solution.py:349
  61.6 0.4 collective-permute-start.9
  62.0 3.8 %collective-permute-start.10 = (f32[14,128]{1,0:T(8,128)}, f32[14,128]{1,0:T(8,128)S(1)}, u32[]{:S(2)}, u32[]{:S(2)}) collective-permute-start(f32[14,128]{1,0:T(8,128)} %get-tuple-element.32), channel_id=1, source_target_pairs={{1,0},{2,1},{3,2},{4,3},{5,4},{6,5},{7,6},{0,7},{9,8},{10,9},{11,1... | collective-permute-start | bytes 21512 | tf_op jit(solution)/shard_map/ppermute | solution.py:351
  65.8 1.4 %collective-permute-done.9.gl_ref = f32[14,128]{1,0:T(8,128)S(1)} collective-permute-done((f32[14,128]{1,0:T(8,128)}, f32[14,128]{1,0:T(8,128)S(1)}, u32[]{:S(2)}, u32[]{:S(2)}) %collective-permute-start.9) | collective-permute-done | bytes 7200 | tf_op jit(solution)/shard_map/ppermute | solution.py:350
  67.2 0.0 collective-permute-done.10.gr_ref
  67.2 0.0 collective-permute-done.7.g0_ref
  67.2 0.0 copy-start.1
  67.2 0.0 collective-permute-done.8.g1_ref
  67.2 0.0 copy-start.2
  67.2 0.5 copy-done.5
  67.8 0.0 copy-done.6
  67.8 0.0 copy-done.1
  67.8 0.0 copy-done.2
  67.8 4.3 %shard_map.84 = f32[14,128,512]{2,1,0:T(8,128)} custom-call(f32[14,128,512]{2,1,0:T(8,128)} %get-tuple-element.28.out_in, f32[14,512]{1,0:T(8,128)} %copy-done.1, f32[14,512]{1,0:T(8,128)} %copy-done.2, f32[14,128]{1,0:T(8,128)} %copy-done.5, f32[14,128]{1,0:T(8,128)} %copy-done.6), custom_call_target="tpu_custom_call", output_to_operand_aliasing={{}: (0, {})} | custom-call | tf_op jit(solution)/shard_map/pallas_call | solution.py:288
  (9 shorter events, 0.1 us)
Async XLA Ops:
  0.0 6.9 %copy-start.7 = (s32[4,512]{1,0:T(4,128)S(1)}, s32[4,512]{1,0:T(4,128)}, u32[]{:S(2)}) copy-start(s32[4,512]{1,0:T(4,128)} %param.12) | copy-start | bytes 24580
  0.0 7.1 %copy-start.8 = (s32[4,512]{1,0:T(4,128)S(1)}, s32[4,512]{1,0:T(4,128)}, u32[]{:S(2)}) copy-start(s32[4,512]{1,0:T(4,128)} %param.14) | copy-start | bytes 24580
  0.0 10.0 %copy-start.9 = (f32[4,512]{1,0:T(4,128)S(1)}, f32[4,512]{1,0:T(4,128)}, u32[]{:S(2)}) copy-start(f32[4,512]{1,0:T(4,128)} %param.13) | copy-start | bytes 24580
  0.0 10.2 %copy-start.10 = (f32[4,512]{1,0:T(4,128)S(1)}, f32[4,512]{1,0:T(4,128)}, u32[]{:S(2)}) copy-start(f32[4,512]{1,0:T(4,128)} %param.15) | copy-start | bytes 24580
  1.9 9.2 %copy-start = (f32[14,1,512]{2,0,1:T(8,128)}, f32[14,1,512]{2,0,1:T(8,128)S(1)}, u32[]{:S(2)}) copy-start(f32[14,1,512]{2,0,1:T(8,128)S(1)} %copy.41) | copy-start | bytes 86020
  1.9 5.3 %collective-permute-start = (f32[1,15,512]{2,1,0:T(8,128)S(1)}, f32[1,15,512]{2,1,0:T(8,128)S(1)}, u32[]{:S(2)}, u32[]{:S(2)}) collective-permute-start(f32[1,15,512]{2,1,0:T(8,128)S(1)} %maximum_bitcast_fusion.1), channel_id=1, source_target_pairs={{0,4},{1,5},{2,6},{3,7},{4,0},{5,1},{6,2},{7,3},{8,12},{9,13},{10,... | collective-permute-start | bytes 92168 | tf_op jit(solution)/shard_map/ppermute | solution.py:326
  7.3 3.8 %collective-permute-start.1 = (f32[2,15,512]{2,1,0:T(8,128)S(1)}, f32[2,15,512]{2,1,0:T(8,128)S(1)}, u32[]{:S(2)}, u32[]{:S(2)}) collective-permute-start(f32[2,15,512]{2,1,0:T(8,128)S(1)} %pad_maximum_fusion.1), channel_id=1, source_target_pairs={{0,2},{1,3},{2,0},{3,1},{4,6},{5,7},{6,4},{7,5},{8,10},{9,11},{10,... | collective-permute-start | bytes 184328 | tf_op jit(solution)/shard_map/ppermute | solution.py:326
  11.1 7.7 %collective-permute-start.2 = (f32[4,15,512]{2,1,0:T(8,128)S(1)}, f32[4,15,512]{2,1,0:T(8,128)S(1)}, u32[]{:S(2)}, u32[]{:S(2)}) collective-permute-start(f32[4,15,512]{2,1,0:T(8,128)S(1)} %pad_maximum_fusion), channel_id=1, source_target_pairs={{0,1},{1,0},{2,3},{3,2},{4,5},{5,4},{6,7},{7,6},{8,9},{9,8},{10,11... | collective-permute-start | bytes 368648 | tf_op jit(solution)/shard_map/ppermute | solution.py:326
  14.6 6.2 %collective-permute-start.3 = (f32[14,128]{1,0:T(8,128)S(1)}, f32[14,128]{1,0:T(8,128)S(1)}, u32[]{:S(2)}, u32[]{:S(2)}) collective-permute-start(f32[14,128]{1,0:T(8,128)S(1)} %bitcast.24), channel_id=1, source_target_pairs={{0,1},{1,2},{2,3},{3,4},{4,5},{5,6},{6,7},{7,0},{8,9},{9,10},{10,1... | collective-permute-start | bytes 21512 | tf_op jit(solution)/shard_map/ppermute | solution.py:337
  14.8 5.9 %collective-permute-start.4 = (f32[14,128]{1,0:T(8,128)S(1)}, f32[14,128]{1,0:T(8,128)S(1)}, u32[]{:S(2)}, u32[]{:S(2)}) collective-permute-start(f32[14,128]{1,0:T(8,128)S(1)} %bitcast.23), channel_id=1, source_target_pairs={{1,0},{2,1},{3,2},{4,3},{5,4},{6,5},{7,6},{0,7},{9,8},{10,9},{11,1... | collective-permute-start | bytes 21512 | tf_op jit(solution)/shard_map/ppermute | solution.py:338
  20.7 0.6 copy-start.3
  20.8 0.6 copy-start.4
  23.7 10.8 %collective-permute-start.5 = (f32[14,512]{1,0:T(8,128)}, f32[14,512]{1,0:T(8,128)S(1)}, u32[]{:S(2)}, u32[]{:S(2)}) collective-permute-start(f32[14,512]{1,0:T(8,128)} %get-tuple-element.24), channel_id=1, source_target_pairs={{0,8},{8,16},{16,24},{1,9},{9,17},{17,25},{2,10},{10,18},{18,26},{... | collective-permute-start | bytes 86024 | tf_op jit(solution)/shard_map/ppermute | solution.py:341
  32.6 5.4 %collective-permute-start.6 = (f32[14,512]{1,0:T(8,128)}, f32[14,512]{1,0:T(8,128)S(1)}, u32[]{:S(2)}, u32[]{:S(2)}) collective-permute-start(f32[14,512]{1,0:T(8,128)} %get-tuple-element.25), channel_id=1, source_target_pairs={{8,0},{16,8},{24,16},{9,1},{17,9},{25,17},{10,2},{18,10},{26,18},{... | collective-permute-start | bytes 86024 | tf_op jit(solution)/shard_map/ppermute | solution.py:342
  34.5 3.5 %copy-start.11 = (f32[14,512]{1,0:T(8,128)}, f32[14,512]{1,0:T(8,128)S(1)}, u32[]{:S(2)}) copy-start(f32[14,512]{1,0:T(8,128)S(1)} %collective-permute-done.5.hlo_ref) | copy-start | bytes 86020
  38.0 0.6 copy-start.12
  57.2 9.9 %collective-permute-start.7 = (f32[14,512]{1,0:T(8,128)}, f32[14,512]{1,0:T(8,128)S(1)}, u32[]{:S(2)}, u32[]{:S(2)}) collective-permute-start(f32[14,512]{1,0:T(8,128)} %get-tuple-element.29), channel_id=1, source_target_pairs={{0,8},{8,16},{1,9},{9,17},{2,10},{10,18},{3,11},{11,19},{4,12},{12... | collective-permute-start | bytes 86024 | tf_op jit(solution)/shard_map/ppermute | solution.py:348
  59.2 7.9 %collective-permute-start.8 = (f32[14,512]{1,0:T(8,128)}, f32[14,512]{1,0:T(8,128)S(1)}, u32[]{:S(2)}, u32[]{:S(2)}) collective-permute-start(f32[14,512]{1,0:T(8,128)} %get-tuple-element.30), channel_id=1, source_target_pairs={{8,0},{16,8},{9,1},{17,9},{10,2},{18,10},{11,3},{19,11},{12,4},{20... | collective-permute-start | bytes 86024 | tf_op jit(solution)/shard_map/ppermute | solution.py:349
  61.6 5.6 %collective-permute-start.9 = (f32[14,128]{1,0:T(8,128)}, f32[14,128]{1,0:T(8,128)S(1)}, u32[]{:S(2)}, u32[]{:S(2)}) collective-permute-start(f32[14,128]{1,0:T(8,128)} %get-tuple-element.31), channel_id=1, source_target_pairs={{0,1},{1,2},{2,3},{3,4},{4,5},{5,6},{6,7},{7,0},{8,9},{9,10},{10,1... | collective-permute-start | bytes 21512 | tf_op jit(solution)/shard_map/ppermute | solution.py:350
  62.0 5.2 %collective-permute-start.10 = (f32[14,128]{1,0:T(8,128)}, f32[14,128]{1,0:T(8,128)S(1)}, u32[]{:S(2)}, u32[]{:S(2)}) collective-permute-start(f32[14,128]{1,0:T(8,128)} %get-tuple-element.32), channel_id=1, source_target_pairs={{1,0},{2,1},{3,2},{4,3},{5,4},{6,5},{7,6},{0,7},{9,8},{10,9},{11,1... | collective-permute-start | bytes 21512 | tf_op jit(solution)/shard_map/ppermute | solution.py:351
  67.2 0.6 copy-start.5
  67.2 0.6 copy-start.6
  67.2 0.6 copy-start.1
  67.2 0.6 copy-start.2

commit v19 on v18

--- a/solution.py
+++ b/solution.py
@@ -317,13 +317,20 @@
     planes = payload[None]
     spans = []
     span = n_blk // 2
+    even = b % 2 == 0
     edges = (last_row, first_row, fields[:, :, lanes - 1], fields[:, :, 0])
     while span >= 1:
         spans.append(span)
+        partner = [(i, i ^ span) for i in range(n_blk)]
         if span == 1:
             edges, planes = lax.optimization_barrier((edges, planes))
-        partner = [(i, i ^ span) for i in range(n_blk)]
-        planes = jnp.concatenate([planes, lax.ppermute(planes, "blk", partner)], axis=0)
+            side = jnp.where(even, edges[2], edges[3])
+            side = jnp.pad(side, ((0, 1), (0, lanes - side.shape[1])))[None]
+            got = lax.ppermute(jnp.concatenate([planes, side], axis=0), "blk", partner)
+            side_got = got[-1, :nf, :edges[2].shape[1]]
+            planes = jnp.concatenate([planes, got[:-1]], axis=0)
+        else:
+            planes = jnp.concatenate([planes, lax.ppermute(planes, "blk", partner)], axis=0)
         span //= 2
     table = jnp.transpose(planes, (0, 2, 1)).reshape(n_blk * lanes, nf + 1)
     at_exit = g == exit_grp
@@ -334,8 +341,13 @@
         slot = slot + ((m // span) % 2) * (1 << r)
     ids = slot * lanes + ids % lanes
     wt = jnp.transpose(jnp.where(at_exit, inlet_weights, outlet_weights))
-    lft = lax.ppermute(edges[2], "blk", [(i, (i + 1) % n_blk) for i in range(n_blk)])
-    rgt = lax.ppermute(edges[3], "blk", [((i + 1) % n_blk, i) for i in range(n_blk)])
+    other = lax.ppermute(
+        jnp.where(even, edges[3], edges[2]),
+        "blk",
+        [(i, (i + 1) % n_blk if i % 2 else (i - 1) % n_blk) for i in range(n_blk)],
+    )
+    lft = jnp.where(even, other, side_got)
+    rgt = jnp.where(even, side_got, other)
 
     up, down, lft, rgt = interpolate(flags, ids, wt, table, (edges[0], edges[1], lft, rgt))
     halo_lo = lax.ppermute(up, "grp", [(i, i + 1) for i in range(n_grp - 1)])

time: 73 us -> 72.6 us (level)
  starting transfers between devices: 29.3 us -> 27.8 us
  waiting for transfers between devices: 4.9 us -> 5.95 us
    ppermute x3 -> x2, starting transfers between devices: 5.84 us -> 4.57 us  [shards(): lax.ppermute(planes, 'blk', partner)]
    ppermute x2, waiting for transfers between devices: 0.01 us -> 1.06 us  [the longest x1 1.06 us: shards(): lax.ppermute(jnp.where(even, edges[3], edges[2]), 'blk', [(i, (i + 1) % n...]
    ppermute x2, starting transfers between devices: 4.16 us -> 3.4 us  [the longest x1 2.13 us: shards(): lax.ppermute(jnp.where(even, edges[3], edges[2]), 'blk', [(i, (i + 1) % n...]
    unnamed x34 -> x30, local copies, waits for them, and re-layouts: 3.69 us -> 3.08 us
  transfers between devices with their start and end apart: 11 -> 10, of which waited for: 2 -> 3; matrix products, arithmetic and copies ran while one was open for 12% -> 12% of each run, Pallas kernels for 0% -> 0%
where the time goes in v19:
time: 72.6 us; the launch traced here: 71.8 us
  starting transfers between devices  27.8 us (38%)
  Pallas kernels  25.3 us (35%)
  local copies, waits for them, and re-layouts  8.95 us (12%)
  waiting for transfers between devices  5.95 us (8%)
  other arithmetic  3.46 us (5%)
    pallas_call x1, Pallas kernels, fused_step(): pl.pallas_call(functools.partial(step_kernel, nf, rows, lanes), out_shape...  18.6 us
    ppermute x1, starting transfers between devices, shards(): halo_lo = lax.ppermute(up, 'grp', [(i, i + 1) for i in range(n_grp - 1)])  9.42 us
    ppermute x2, starting transfers between devices, shards(): lax.ppermute(planes, 'blk', partner)  4.57 us
    pallas_call x1, Pallas kernels, fix_edges(): pl.pallas_call(functools.partial(fix_kernel, low_w, side_w), out_shape=ja...  4.34 us
    ppermute x1, starting transfers between devices, shards(): gr = lax.ppermute(clo, 'blk', [((i + 1) % n_blk, i) for i in range(n_blk)])  4.15 us
    ppermute x1, waiting for transfers between devices, shards(): halo_hi = lax.ppermute(down, 'grp', [(i + 1, i) for i in range(n_grp - 1)])  3.5 us
    unnamed x30, local copies, waits for them, and re-layouts  3.08 us
    pallas_call x1, Pallas kernels, interpolate(): pl.pallas_call(functools.partial(interp_kernel, ks), out_shape=tuple((jax...  2.37 us
  transfers between devices with their start and end apart: 10, of which 3 were waited for; matrix products, arithmetic and copies ran while one was open for 12% of the time, Pallas kernels for 0%

profile of v19, /device:TPU:1, one launch (start us, length us, event | category | flops | bytes accessed | tf_op | source)
XLA Modules:
  0.0 71.8 jit_solution(16614908338379936839)
XLA Ops:
  0.0 0.0 copy-start.5
  0.0 0.0 copy-start.6
  0.0 0.0 copy-start.7
  0.0 0.0 copy-start.8
  0.0 0.8 %slice_bitcast_fusion.1 = f32[1,512]{1,0:T(1,128)S(1)} fusion(f32[14,128,512]{2,1,0:T(8,128)} %f_hbm.1), kind=kLoop, calls=%fused_computation.48 | loop fusion | bytes 4096 | tf_op jit(solution)/shard_map/slice | solution.py:316
  0.8 1.1 %fusion.15 = (f32[14,1,512]{2,1,0:T(1,128)S(1)}, f32[14,1,512]{2,1,0:T(1,128)S(1)}) fusion(f32[14,128,512]{2,1,0:T(8,128)} %f_hbm.1), kind=kLoop, calls=%fused_computation.51 | loop fusion | bytes 114688 | tf_op jit(solution)/shard_map/slice | solution.py:315
  1.9 0.0 copy-start
  1.9 3.2 %collective-permute-start = (f32[1,15,512]{2,1,0:T(8,128)S(1)}, f32[1,15,512]{2,1,0:T(8,128)S(1)}, u32[]{:S(2)}, u32[]{:S(2)}) collective-permute-start(f32[1,15,512]{2,1,0:T(8,128)S(1)} %maximum_bitcast_fusion.1), channel_id=1, source_target_pairs={{0,4},{1,5},{2,6},{3,7},{4,0},{5,1},{6,2},{7,3},{8,12},{9,13},{10,... | collective-permute-start | bytes 92168 | tf_op jit(solution)/shard_map/ppermute | solution.py:333
  5.1 1.8 %fusion.14 = (f32[14,128,1]{2,1,0:T(8,128)S(1)}, f32[14,128,1]{2,1,0:T(8,128)S(1)}) fusion(f32[14,128,512]{2,1,0:T(8,128)} %f_hbm.1), kind=kLoop, calls=%fused_computation.50 | loop fusion | bytes 28672 | tf_op jit(solution)/shard_map/slice | solution.py:321
  6.9 0.0 copy-done.5
  6.9 0.1 copy.20
  7.1 0.0 copy-done.6
  7.1 0.1 copy.21
  7.3 0.0 collective-permute-done
  7.3 1.4 %collective-permute-start.1 = (f32[2,15,512]{2,1,0:T(8,128)S(1)}, f32[2,15,512]{2,1,0:T(8,128)S(1)}, u32[]{:S(2)}, u32[]{:S(2)}) collective-permute-start(f32[2,15,512]{2,1,0:T(8,128)S(1)} %pad_maximum_fusion.2), channel_id=1, source_target_pairs={{0,2},{1,3},{2,0},{3,1},{4,6},{5,7},{6,4},{7,5},{8,10},{9,11},{10,... | collective-permute-start | bytes 184328 | tf_op jit(solution)/shard_map/ppermute | solution.py:333
  8.6 0.8 %add_select_fusion = (s32[4,512]{0,1:T(8,128)S(1)}, s32[4,512]{0,1:T(8,128)S(1)}) fusion(s32[4,512]{0,1:T(8,128)S(1)} %copy.20, s32[4,512]{0,1:T(8,128)S(1)} %copy.21, pred[]{:T(512)} %eq.17, s32[]{:T(128)S(6)} %axis_index.25), kind=kLoop, calls=%fused_computation | loop fusion | flops 157696 | bytes 32773 | tf_op jit(solution)/shard_map/jit(remainder)/select_n | solution.py:342
  9.5 0.6 copy.40
  10.1 0.0 copy-done.7
  10.1 0.1 copy.24
  10.2 0.0 copy-done.8
  10.2 0.1 copy.25
  10.4 0.3 copy.37
  10.7 0.3 copy.36
  11.0 0.0 copy-done
  11.1 0.0 collective-permute-done.1
  11.1 1.3 %collective-permute-start.2 = (f32[5,15,512]{2,1,0:T(8,128)S(1)}, f32[5,15,512]{2,1,0:T(8,128)S(1)}, u32[]{:S(2)}, u32[]{:S(2)}) collective-permute-start(f32[5,15,512]{2,1,0:T(8,128)S(1)} %pad_maximum_fusion), channel_id=1, source_target_pairs={{0,1},{1,0},{2,3},{3,2},{4,5},{5,4},{6,7},{7,6},{8,9},{9,8},{10,11... | collective-permute-start | bytes 460808 | tf_op jit(solution)/shard_map/ppermute | solution.py:329
  12.4 0.7 %select_bitcast_fusion.wt_ref = f32[512,4]{1,0:T(8,128)} fusion(f32[4,512]{0,1:T(8,128)S(1)} %copy.24, f32[4,512]{0,1:T(8,128)S(1)} %copy.25, pred[]{:T(512)} %eq.17), kind=kLoop, calls=%fused_computation.29 | loop fusion | flops 2048 | bytes 24577 | tf_op jit(solution)/shard_map/transpose | solution.py:343
  13.1 0.1 copy.23
  13.2 0.1 copy.22
  13.4 0.6 add.43.ids_s
  14.0 0.6 add_convert_fusion.flag_s
  14.6 2.1 %collective-permute-start.3 = (f32[14,128]{1,0:T(8,128)S(1)}, f32[14,128]{1,0:T(8,128)S(1)}, u32[]{:S(2)}, u32[]{:S(2)}) collective-permute-start(f32[14,128]{1,0:T(8,128)S(1)} %get-tuple-element.41), channel_id=1, source_target_pairs={{0,7},{1,2},{2,1},{3,4},{4,3},{5,6},{6,5},{7,0},{8,15},{9,10},{10,... | collective-permute-start | bytes 21512 | tf_op jit(solution)/shard_map/ppermute | solution.py:344
  16.8 0.0 collective-permute-done.2
  16.8 2.0 %copy.32 = f32[8,512,15]{2,1,0:T(8,128)} copy(f32[8,512,15]{1,2,0:T(8,128)S(1)} %maximum_bitcast_fusion) | data formatting | bytes 491520 | tf_op jit(solution)/shard_map/reshape | solution.py:335
  18.8 1.1 %collective-permute-done.3 = f32[14,128]{1,0:T(8,128)S(1)} collective-permute-done((f32[14,128]{1,0:T(8,128)S(1)}, f32[14,128]{1,0:T(8,128)S(1)}, u32[]{:S(2)}, u32[]{:S(2)}) %collective-permute-start.3) | collective-permute-done | bytes 7200 | tf_op jit(solution)/shard_map/ppermute | solution.py:344
  19.8 0.6 fusion.12
  20.4 2.4 %shard_map.82 = (f32[14,512]{1,0:T(8,128)}, f32[14,512]{1,0:T(8,128)}, f32[14,128]{1,0:T(8,128)}, f32[14,128]{1,0:T(8,128)}) custom-call(f32[2]{0:T(128)} %add_convert_fusion.flag_s, s32[4,512]{1,0:T(4,128)} %add.43.ids_s, f32[512,4]{1,0:T(8,128)} %select_bitcast_fusion.wt_ref, f32[4096,15]{1,0:T(8,128)} %bitcast.27, f32[14,512]{1,0:T(8,128)} %bitcast.29, ...), custom_call_target="tpu_custom_call" | custom-call | tf_op jit(solution)/shard_map/pallas_call | solution.py:239
  22.8 9.4 %collective-permute-start.4 = (f32[14,512]{1,0:T(8,128)}, f32[14,512]{1,0:T(8,128)S(1)}, u32[]{:S(2)}, u32[]{:S(2)}) collective-permute-start(f32[14,512]{1,0:T(8,128)} %get-tuple-element.24), channel_id=1, source_target_pairs={{0,8},{8,16},{16,24},{1,9},{9,17},{17,25},{2,10},{10,18},{18,26},{... | collective-permute-start | bytes 86024 | tf_op jit(solution)/shard_map/ppermute | solution.py:353
  32.2 1.9 %collective-permute-start.5 = (f32[14,512]{1,0:T(8,128)}, f32[14,512]{1,0:T(8,128)S(1)}, u32[]{:S(2)}, u32[]{:S(2)}) collective-permute-start(f32[14,512]{1,0:T(8,128)} %get-tuple-element.25), channel_id=1, source_target_pairs={{8,0},{16,8},{24,16},{9,1},{17,9},{25,17},{10,2},{18,10},{26,18},{... | collective-permute-start | bytes 86024 | tf_op jit(solution)/shard_map/ppermute | solution.py:354
  34.1 0.0 collective-permute-done.4.hlo_ref
  34.2 0.0 copy-start.9
  34.2 3.5 %collective-permute-done.5.hhi_ref = f32[14,512]{1,0:T(8,128)S(1)} collective-permute-done((f32[14,512]{1,0:T(8,128)}, f32[14,512]{1,0:T(8,128)S(1)}, u32[]{:S(2)}, u32[]{:S(2)}) %collective-permute-start.5) | collective-permute-done | bytes 28704 | tf_op jit(solution)/shard_map/ppermute | solution.py:354
  37.7 0.0 copy-start.10
  37.7 0.0 copy-done.9
  37.7 0.6 copy-done.10
  38.3 18.6 %shard_map.83 = (f32[14,128,512]{2,1,0:T(8,128)}, f32[14,512]{1,0:T(8,128)}, f32[14,512]{1,0:T(8,128)}, f32[14,128]{1,0:T(8,128)}, f32[14,128]{1,0:T(8,128)}) custom-call(f32[14,14]{1,0:T(8,128)} %mix_s.1, f32[14]{0:T(128)} %act_s.1, f32[2]{0:T(128)} %add_convert_fusion.flag_s, f32[14,128,512]{2,1,0:T(8,128)} %f_hbm.1, f32[128,512]{1,0:T(8,128)} %rate_ref.1, ...), custom_call_target="tpu_custom_call" | custom-call | flops 95420416 | bytes 7602176 | tf_op jit(solution)/shard_map/pallas_call | solution.py:176
  56.9 2.0 %collective-permute-start.6 = (f32[14,512]{1,0:T(8,128)}, f32[14,512]{1,0:T(8,128)S(1)}, u32[]{:S(2)}, u32[]{:S(2)}) collective-permute-start(f32[14,512]{1,0:T(8,128)} %get-tuple-element.29), channel_id=1, source_target_pairs={{0,8},{8,16},{1,9},{9,17},{2,10},{10,18},{3,11},{11,19},{4,12},{12... | collective-permute-start | bytes 86024 | tf_op jit(solution)/shard_map/ppermute | solution.py:360
  58.9 2.3 %collective-permute-start.7 = (f32[14,512]{1,0:T(8,128)}, f32[14,512]{1,0:T(8,128)S(1)}, u32[]{:S(2)}, u32[]{:S(2)}) collective-permute-start(f32[14,512]{1,0:T(8,128)} %get-tuple-element.30), channel_id=1, source_target_pairs={{8,0},{16,8},{9,1},{17,9},{10,2},{18,10},{11,3},{19,11},{12,4},{20... | collective-permute-start | bytes 86024 | tf_op jit(solution)/shard_map/ppermute | solution.py:361
  61.2 0.1 collective-permute-start.8
  61.3 4.2 %collective-permute-start.9 = (f32[14,128]{1,0:T(8,128)}, f32[14,128]{1,0:T(8,128)S(1)}, u32[]{:S(2)}, u32[]{:S(2)}) collective-permute-start(f32[14,128]{1,0:T(8,128)} %get-tuple-element.32), channel_id=1, source_target_pairs={{1,0},{2,1},{3,2},{4,3},{5,4},{6,5},{7,6},{0,7},{9,8},{10,9},{11,1... | collective-permute-start | bytes 21512 | tf_op jit(solution)/shard_map/ppermute | solution.py:363
  65.4 1.4 %collective-permute-done.8.gl_ref = f32[14,128]{1,0:T(8,128)S(1)} collective-permute-done((f32[14,128]{1,0:T(8,128)}, f32[14,128]{1,0:T(8,128)S(1)}, u32[]{:S(2)}, u32[]{:S(2)}) %collective-permute-start.8) | collective-permute-done | bytes 7200 | tf_op jit(solution)/shard_map/ppermute | solution.py:362
  66.8 0.0 copy-start.3
  66.8 0.0 collective-permute-done.9.gr_ref
  66.8 0.0 copy-start.4
  66.8 0.0 collective-permute-done.6.g0_ref
  66.8 0.0 copy-start.1
  66.8 0.0 collective-permute-done.7.g1_ref
  66.8 0.0 copy-start.2
  66.8 0.5 copy-done.3
  67.4 0.0 copy-done.4
  67.4 0.0 copy-done.1
  67.4 0.0 copy-done.2
  67.4 4.3 %shard_map.84 = f32[14,128,512]{2,1,0:T(8,128)} custom-call(f32[14,128,512]{2,1,0:T(8,128)} %get-tuple-element.28.out_in, f32[14,512]{1,0:T(8,128)} %copy-done.1, f32[14,512]{1,0:T(8,128)} %copy-done.2, f32[14,128]{1,0:T(8,128)} %copy-done.3, f32[14,128]{1,0:T(8,128)} %copy-done.4), custom_call_target="tpu_custom_call", output_to_operand_aliasing={{}: (0, {})} | custom-call | tf_op jit(solution)/shard_map/pallas_call | solution.py:288
  (9 shorter events, 0.1 us)
Async XLA Ops:
  0.0 6.9 %copy-start.5 = (s32[4,512]{1,0:T(4,128)S(1)}, s32[4,512]{1,0:T(4,128)}, u32[]{:S(2)}) copy-start(s32[4,512]{1,0:T(4,128)} %param.12) | copy-start | bytes 24580
  0.0 7.1 %copy-start.6 = (s32[4,512]{1,0:T(4,128)S(1)}, s32[4,512]{1,0:T(4,128)}, u32[]{:S(2)}) copy-start(s32[4,512]{1,0:T(4,128)} %param.14) | copy-start | bytes 24580
  0.0 10.1 %copy-start.7 = (f32[4,512]{1,0:T(4,128)S(1)}, f32[4,512]{1,0:T(4,128)}, u32[]{:S(2)}) copy-start(f32[4,512]{1,0:T(4,128)} %param.13) | copy-start | bytes 24580
  0.0 10.2 %copy-start.8 = (f32[4,512]{1,0:T(4,128)S(1)}, f32[4,512]{1,0:T(4,128)}, u32[]{:S(2)}) copy-start(f32[4,512]{1,0:T(4,128)} %param.15) | copy-start | bytes 24580
  1.9 9.2 %copy-start = (f32[14,1,512]{2,0,1:T(8,128)}, f32[14,1,512]{2,0,1:T(8,128)S(1)}, u32[]{:S(2)}) copy-start(f32[14,1,512]{2,0,1:T(8,128)S(1)} %copy.41) | copy-start | bytes 86020
  1.9 5.3 %collective-permute-start = (f32[1,15,512]{2,1,0:T(8,128)S(1)}, f32[1,15,512]{2,1,0:T(8,128)S(1)}, u32[]{:S(2)}, u32[]{:S(2)}) collective-permute-start(f32[1,15,512]{2,1,0:T(8,128)S(1)} %maximum_bitcast_fusion.1), channel_id=1, source_target_pairs={{0,4},{1,5},{2,6},{3,7},{4,0},{5,1},{6,2},{7,3},{8,12},{9,13},{10,... | collective-permute-start | bytes 92168 | tf_op jit(solution)/shard_map/ppermute | solution.py:333
  7.3 3.8 %collective-permute-start.1 = (f32[2,15,512]{2,1,0:T(8,128)S(1)}, f32[2,15,512]{2,1,0:T(8,128)S(1)}, u32[]{:S(2)}, u32[]{:S(2)}) collective-permute-start(f32[2,15,512]{2,1,0:T(8,128)S(1)} %pad_maximum_fusion.2), channel_id=1, source_target_pairs={{0,2},{1,3},{2,0},{3,1},{4,6},{5,7},{6,4},{7,5},{8,10},{9,11},{10,... | collective-permute-start | bytes 184328 | tf_op jit(solution)/shard_map/ppermute | solution.py:333
  11.1 5.6 %collective-permute-start.2 = (f32[5,15,512]{2,1,0:T(8,128)S(1)}, f32[5,15,512]{2,1,0:T(8,128)S(1)}, u32[]{:S(2)}, u32[]{:S(2)}) collective-permute-start(f32[5,15,512]{2,1,0:T(8,128)S(1)} %pad_maximum_fusion), channel_id=1, source_target_pairs={{0,1},{1,0},{2,3},{3,2},{4,5},{5,4},{6,7},{7,6},{8,9},{9,8},{10,11... | collective-permute-start | bytes 460808 | tf_op jit(solution)/shard_map/ppermute | solution.py:329
  14.6 5.2 %collective-permute-start.3 = (f32[14,128]{1,0:T(8,128)S(1)}, f32[14,128]{1,0:T(8,128)S(1)}, u32[]{:S(2)}, u32[]{:S(2)}) collective-permute-start(f32[14,128]{1,0:T(8,128)S(1)} %get-tuple-element.41), channel_id=1, source_target_pairs={{0,7},{1,2},{2,1},{3,4},{4,3},{5,6},{6,5},{7,0},{8,15},{9,10},{10,... | collective-permute-start | bytes 21512 | tf_op jit(solution)/shard_map/ppermute | solution.py:344
  22.8 11.4 %collective-permute-start.4 = (f32[14,512]{1,0:T(8,128)}, f32[14,512]{1,0:T(8,128)S(1)}, u32[]{:S(2)}, u32[]{:S(2)}) collective-permute-start(f32[14,512]{1,0:T(8,128)} %get-tuple-element.24), channel_id=1, source_target_pairs={{0,8},{8,16},{16,24},{1,9},{9,17},{17,25},{2,10},{10,18},{18,26},{... | collective-permute-start | bytes 86024 | tf_op jit(solution)/shard_map/ppermute | solution.py:353
  32.2 5.4 %collective-permute-start.5 = (f32[14,512]{1,0:T(8,128)}, f32[14,512]{1,0:T(8,128)S(1)}, u32[]{:S(2)}, u32[]{:S(2)}) collective-permute-start(f32[14,512]{1,0:T(8,128)} %get-tuple-element.25), channel_id=1, source_target_pairs={{8,0},{16,8},{24,16},{9,1},{17,9},{25,17},{10,2},{18,10},{26,18},{... | collective-permute-start | bytes 86024 | tf_op jit(solution)/shard_map/ppermute | solution.py:354
  34.2 3.5 %copy-start.9 = (f32[14,512]{1,0:T(8,128)}, f32[14,512]{1,0:T(8,128)S(1)}, u32[]{:S(2)}) copy-start(f32[14,512]{1,0:T(8,128)S(1)} %collective-permute-done.4.hlo_ref) | copy-start | bytes 86020
  37.7 0.6 copy-start.10
  56.9 9.9 %collective-permute-start.6 = (f32[14,512]{1,0:T(8,128)}, f32[14,512]{1,0:T(8,128)S(1)}, u32[]{:S(2)}, u32[]{:S(2)}) collective-permute-start(f32[14,512]{1,0:T(8,128)} %get-tuple-element.29), channel_id=1, source_target_pairs={{0,8},{8,16},{1,9},{9,17},{2,10},{10,18},{3,11},{11,19},{4,12},{12... | collective-permute-start | bytes 86024 | tf_op jit(solution)/shard_map/ppermute | solution.py:360
  58.9 7.9 %collective-permute-start.7 = (f32[14,512]{1,0:T(8,128)}, f32[14,512]{1,0:T(8,128)S(1)}, u32[]{:S(2)}, u32[]{:S(2)}) collective-permute-start(f32[14,512]{1,0:T(8,128)} %get-tuple-element.30), channel_id=1, source_target_pairs={{8,0},{16,8},{9,1},{17,9},{10,2},{18,10},{11,3},{19,11},{12,4},{20... | collective-permute-start | bytes 86024 | tf_op jit(solution)/shard_map/ppermute | solution.py:361
  61.2 5.6 %collective-permute-start.8 = (f32[14,128]{1,0:T(8,128)}, f32[14,128]{1,0:T(8,128)S(1)}, u32[]{:S(2)}, u32[]{:S(2)}) collective-permute-start(f32[14,128]{1,0:T(8,128)} %get-tuple-element.31), channel_id=1, source_target_pairs={{0,1},{1,2},{2,3},{3,4},{4,5},{5,6},{6,7},{7,0},{8,9},{9,10},{10,1... | collective-permute-start | bytes 21512 | tf_op jit(solution)/shard_map/ppermute | solution.py:362
  61.3 5.5 %collective-permute-start.9 = (f32[14,128]{1,0:T(8,128)}, f32[14,128]{1,0:T(8,128)S(1)}, u32[]{:S(2)}, u32[]{:S(2)}) collective-permute-start(f32[14,128]{1,0:T(8,128)} %get-tuple-element.32), channel_id=1, source_target_pairs={{1,0},{2,1},{3,2},{4,3},{5,4},{6,5},{7,6},{0,7},{9,8},{10,9},{11,1... | collective-permute-start | bytes 21512 | tf_op jit(solution)/shard_map/ppermute | solution.py:363
  66.8 0.6 copy-start.3
  66.8 0.6 copy-start.4
  66.8 0.6 copy-start.1
  66.8 0.6 copy-start.2

commit v20 on v19

--- a/solution.py
+++ b/solution.py
@@ -359,8 +359,14 @@
 
     g0 = lax.ppermute(ehi, "grp", [(i, i + 1) for i in range(n_grp - 2)])
     g1 = lax.ppermute(elo, "grp", [(i + 1, i) for i in range(n_grp - 2)])
-    gl = lax.ppermute(chi, "blk", [(i, (i + 1) % n_blk) for i in range(n_blk)])
-    gr = lax.ppermute(clo, "blk", [((i + 1) % n_blk, i) for i in range(n_blk)])
+    near = lax.ppermute(jnp.where(even, chi, clo), "blk", [(i, i ^ 1) for i in range(n_blk)])
+    far = lax.ppermute(
+        jnp.where(even, clo, chi),
+        "blk",
+        [(i, (i + 1) % n_blk if i % 2 else (i - 1) % n_blk) for i in range(n_blk)],
+    )
+    gl = jnp.where(even, far, near)
+    gr = jnp.where(even, near, far)
     low_w = 0.5 * (courant + diffusion)
     side_w = 0.5 * diffusion
     return fix_edges(out, g0, g1, gl, gr, low_w, side_w)

time: 72.6 us -> 74.1 us (1.021)
  waiting for transfers between devices: 5.95 us -> 7.35 us
  other arithmetic: 3.46 us -> 4.78 us
  starting transfers between devices: 27.8 us -> 26.9 us
    ppermute x1, waiting for transfers between devices: 0.01 us -> 2.78 us  [shards(): g1 = lax.ppermute(elo, 'grp', [(i + 1, i) for i in range(n_grp - 2)])]
    ppermute x2, waiting for transfers between devices: 1.39 us -> 0.01 us  [the longest x1 0.01 us: shards(): lax.ppermute(jnp.where(even, chi, clo), 'blk', [(i, i ^ 1) for i in range...]
    select_n x0 -> x2, other arithmetic: none -> 1.32 us  [the longest x1 0.72 us: shards(): jnp.where(even, chi, clo)]
    ppermute x2, starting transfers between devices: 4.21 us -> 3.3 us  [the longest x1 3.3 us: shards(): lax.ppermute(jnp.where(even, clo, chi), 'blk', [(i, (i + 1) % n_blk if i...]
    unnamed x30 -> x26, local copies, waits for them, and re-layouts: 3.08 us -> 3.09 us
  transfers between devices with their start and end apart: 10 -> 10, of which waited for: 3 -> 3; matrix products, arithmetic and copies ran while one was open for 12% -> 13% of each run, Pallas kernels for 0% -> 0%
where the time goes in v20:
time: 74.1 us; the launch traced here: 73.6 us
  starting transfers between devices  26.9 us (36%)
  Pallas kernels  25.3 us (34%)
  local copies, waits for them, and re-layouts  8.95 us (12%)
  waiting for transfers between devices  7.35 us (10%)
  other arithmetic  4.78 us (6%)
    pallas_call x1, Pallas kernels, fused_step(): pl.pallas_call(functools.partial(step_kernel, nf, rows, lanes), out_shape...  18.6 us
    ppermute x1, starting transfers between devices, shards(): halo_lo = lax.ppermute(up, 'grp', [(i, i + 1) for i in range(n_grp - 1)])  9.42 us
    ppermute x2, starting transfers between devices, shards(): lax.ppermute(planes, 'blk', partner)  4.57 us
    pallas_call x1, Pallas kernels, fix_edges(): pl.pallas_call(functools.partial(fix_kernel, low_w, side_w), out_shape=ja...  4.34 us
    ppermute x1, waiting for transfers between devices, shards(): halo_hi = lax.ppermute(down, 'grp', [(i + 1, i) for i in range(n_grp - 1)])  3.5 us
    ppermute x1, starting transfers between devices, shards(): lax.ppermute(jnp.where(even, clo, chi), 'blk', [(i, (i + 1) % n_blk if i...  3.3 us
    unnamed x26, local copies, waits for them, and re-layouts  3.09 us
    ppermute x1, waiting for transfers between devices, shards(): g1 = lax.ppermute(elo, 'grp', [(i + 1, i) for i in range(n_grp - 2)])  2.78 us
  transfers between devices with their start and end apart: 10, of which 3 were waited for; matrix products, arithmetic and copies ran while one was open for 13% of the time, Pallas kernels for 0%

profile of v20, /device:TPU:1, one launch (start us, length us, event | category | flops | bytes accessed | tf_op | source)
XLA Modules:
  0.0 73.6 jit_solution(696222859047766314)
XLA Ops:
  0.0 0.0 copy-start.3
  0.0 0.0 copy-start.4
  0.0 0.0 copy-start.5
  0.0 0.0 copy-start.6
  0.0 0.8 %slice_bitcast_fusion.1 = f32[1,512]{1,0:T(1,128)S(1)} fusion(f32[14,128,512]{2,1,0:T(8,128)} %f_hbm.1), kind=kLoop, calls=%fused_computation.52 | loop fusion | bytes 4096 | tf_op jit(solution)/shard_map/slice | solution.py:316
  0.8 1.1 %fusion.15 = (f32[14,1,512]{2,1,0:T(1,128)S(1)}, f32[14,1,512]{2,1,0:T(1,128)S(1)}) fusion(f32[14,128,512]{2,1,0:T(8,128)} %f_hbm.1), kind=kLoop, calls=%fused_computation.55 | loop fusion | bytes 114688 | tf_op jit(solution)/shard_map/slice | solution.py:315
  1.9 0.0 copy-start
  1.9 3.2 %collective-permute-start = (f32[1,15,512]{2,1,0:T(8,128)S(1)}, f32[1,15,512]{2,1,0:T(8,128)S(1)}, u32[]{:S(2)}, u32[]{:S(2)}) collective-permute-start(f32[1,15,512]{2,1,0:T(8,128)S(1)} %maximum_bitcast_fusion.1), channel_id=1, source_target_pairs={{0,4},{1,5},{2,6},{3,7},{4,0},{5,1},{6,2},{7,3},{8,12},{9,13},{10,... | collective-permute-start | bytes 92168 | tf_op jit(solution)/shard_map/ppermute | solution.py:333
  5.1 1.8 %fusion.14 = (f32[14,128,1]{2,1,0:T(8,128)S(1)}, f32[14,128,1]{2,1,0:T(8,128)S(1)}) fusion(f32[14,128,512]{2,1,0:T(8,128)} %f_hbm.1), kind=kLoop, calls=%fused_computation.54 | loop fusion | bytes 28672 | tf_op jit(solution)/shard_map/slice | solution.py:321
  6.9 0.0 copy-done.3
  6.9 0.1 copy.20
  7.1 0.0 copy-done.4
  7.1 0.1 copy.21
  7.3 0.0 collective-permute-done
  7.3 1.4 %collective-permute-start.1 = (f32[2,15,512]{2,1,0:T(8,128)S(1)}, f32[2,15,512]{2,1,0:T(8,128)S(1)}, u32[]{:S(2)}, u32[]{:S(2)}) collective-permute-start(f32[2,15,512]{2,1,0:T(8,128)S(1)} %pad_maximum_fusion.2), channel_id=1, source_target_pairs={{0,2},{1,3},{2,0},{3,1},{4,6},{5,7},{6,4},{7,5},{8,10},{9,11},{10,... | collective-permute-start | bytes 184328 | tf_op jit(solution)/shard_map/ppermute | solution.py:333
  8.6 0.8 %add_select_fusion = (s32[4,512]{0,1:T(8,128)S(1)}, s32[4,512]{0,1:T(8,128)S(1)}) fusion(s32[4,512]{0,1:T(8,128)S(1)} %copy.20, s32[4,512]{0,1:T(8,128)S(1)} %copy.21, pred[]{:T(512)} %eq.17, s32[]{:T(128)S(6)} %axis_index.25), kind=kLoop, calls=%fused_computation | loop fusion | flops 157696 | bytes 32773 | tf_op jit(solution)/shard_map/jit(remainder)/select_n | solution.py:342
  9.5 0.6 copy.40
  10.1 0.0 copy-done.5
  10.1 0.1 copy.24
  10.2 0.0 copy-done.6
  10.2 0.1 copy.25
  10.4 0.3 copy.37
  10.7 0.3 copy.36
  11.0 0.0 copy-done
  11.1 0.0 collective-permute-done.1
  11.1 1.3 %collective-permute-start.2 = (f32[5,15,512]{2,1,0:T(8,128)S(1)}, f32[5,15,512]{2,1,0:T(8,128)S(1)}, u32[]{:S(2)}, u32[]{:S(2)}) collective-permute-start(f32[5,15,512]{2,1,0:T(8,128)S(1)} %pad_maximum_fusion), channel_id=1, source_target_pairs={{0,1},{1,0},{2,3},{3,2},{4,5},{5,4},{6,7},{7,6},{8,9},{9,8},{10,11... | collective-permute-start | bytes 460808 | tf_op jit(solution)/shard_map/ppermute | solution.py:329
  12.4 0.7 select_bitcast_fusion.wt_ref
  13.1 0.1 copy.23
  13.2 0.1 copy.22
  13.4 0.6 add.43.ids_s
  14.0 0.6 add_convert_fusion.flag_s
  14.6 2.1 %collective-permute-start.3 = (f32[14,128]{1,0:T(8,128)S(1)}, f32[14,128]{1,0:T(8,128)S(1)}, u32[]{:S(2)}, u32[]{:S(2)}) collective-permute-start(f32[14,128]{1,0:T(8,128)S(1)} %get-tuple-element.45), channel_id=1, source_target_pairs={{0,7},{1,2},{2,1},{3,4},{4,3},{5,6},{6,5},{7,0},{8,15},{9,10},{10,... | collective-permute-start | bytes 21512 | tf_op jit(solution)/shard_map/ppermute | solution.py:344
  16.8 0.0 collective-permute-done.2
  16.8 2.0 %copy.32 = f32[8,512,15]{2,1,0:T(8,128)} copy(f32[8,512,15]{1,2,0:T(8,128)S(1)} %maximum_bitcast_fusion) | data formatting | bytes 491520 | tf_op jit(solution)/shard_map/reshape | solution.py:335
  18.8 1.1 %collective-permute-done.3 = f32[14,128]{1,0:T(8,128)S(1)} collective-permute-done((f32[14,128]{1,0:T(8,128)S(1)}, f32[14,128]{1,0:T(8,128)S(1)}, u32[]{:S(2)}, u32[]{:S(2)}) %collective-permute-start.3) | collective-permute-done | bytes 7200 | tf_op jit(solution)/shard_map/ppermute | solution.py:344
  19.8 0.6 fusion.12
  20.4 2.4 %shard_map.82 = (f32[14,512]{1,0:T(8,128)}, f32[14,512]{1,0:T(8,128)}, f32[14,128]{1,0:T(8,128)}, f32[14,128]{1,0:T(8,128)}) custom-call(f32[2]{0:T(128)} %add_convert_fusion.flag_s, s32[4,512]{1,0:T(4,128)} %add.43.ids_s, f32[512,4]{1,0:T(8,128)} %select_bitcast_fusion.wt_ref, f32[4096,15]{1,0:T(8,128)} %bitcast.27, f32[14,512]{1,0:T(8,128)} %bitcast.29, ...), custom_call_target="tpu_custom_call" | custom-call | tf_op jit(solution)/shard_map/pallas_call | solution.py:239
  22.8 9.4 %collective-permute-start.4 = (f32[14,512]{1,0:T(8,128)}, f32[14,512]{1,0:T(8,128)S(1)}, u32[]{:S(2)}, u32[]{:S(2)}) collective-permute-start(f32[14,512]{1,0:T(8,128)} %get-tuple-element.24), channel_id=1, source_target_pairs={{0,8},{8,16},{16,24},{1,9},{9,17},{17,25},{2,10},{10,18},{18,26},{... | collective-permute-start | bytes 86024 | tf_op jit(solution)/shard_map/ppermute | solution.py:353
  32.2 1.9 %collective-permute-start.5 = (f32[14,512]{1,0:T(8,128)}, f32[14,512]{1,0:T(8,128)S(1)}, u32[]{:S(2)}, u32[]{:S(2)}) collective-permute-start(f32[14,512]{1,0:T(8,128)} %get-tuple-element.25), channel_id=1, source_target_pairs={{8,0},{16,8},{24,16},{9,1},{17,9},{25,17},{10,2},{18,10},{26,18},{... | collective-permute-start | bytes 86024 | tf_op jit(solution)/shard_map/ppermute | solution.py:354
  34.1 0.0 collective-permute-done.4.hlo_ref
  34.2 0.0 copy-start.7
  34.2 3.5 %collective-permute-done.5.hhi_ref = f32[14,512]{1,0:T(8,128)S(1)} collective-permute-done((f32[14,512]{1,0:T(8,128)}, f32[14,512]{1,0:T(8,128)S(1)}, u32[]{:S(2)}, u32[]{:S(2)}) %collective-permute-start.5) | collective-permute-done | bytes 28704 | tf_op jit(solution)/shard_map/ppermute | solution.py:354
  37.7 0.0 copy-start.8
  37.7 0.0 copy-done.7
  37.7 0.6 copy-done.8
  38.3 18.6 %shard_map.83 = (f32[14,128,512]{2,1,0:T(8,128)}, f32[14,512]{1,0:T(8,128)}, f32[14,512]{1,0:T(8,128)}, f32[14,128]{1,0:T(8,128)}, f32[14,128]{1,0:T(8,128)}) custom-call(f32[14,14]{1,0:T(8,128)} %mix_s.1, f32[14]{0:T(128)} %act_s.1, f32[2]{0:T(128)} %add_convert_fusion.flag_s, f32[14,128,512]{2,1,0:T(8,128)} %f_hbm.1, f32[128,512]{1,0:T(8,128)} %rate_ref.1, ...), custom_call_target="tpu_custom_call" | custom-call | flops 95420416 | bytes 7602176 | tf_op jit(solution)/shard_map/pallas_call | solution.py:176
  56.9 0.7 broadcast_select_fusion.3
  57.6 0.0 collective-permute-start.9
  57.6 3.3 %collective-permute-start.8 = (f32[14,128]{1,0:T(8,128)S(1)}, f32[14,128]{1,0:T(8,128)S(1)}, u32[]{:S(2)}, u32[]{:S(2)}) collective-permute-start(f32[14,128]{1,0:T(8,128)S(1)} %get-tuple-element.44), channel_id=1, source_target_pairs={{0,7},{1,2},{2,1},{3,4},{4,3},{5,6},{6,5},{7,0},{8,15},{9,10},{10,... | collective-permute-start | bytes 21512 | tf_op jit(solution)/shard_map/ppermute | solution.py:363
  60.9 2.3 %collective-permute-start.6 = (f32[14,512]{1,0:T(8,128)}, f32[14,512]{1,0:T(8,128)S(1)}, u32[]{:S(2)}, u32[]{:S(2)}) collective-permute-start(f32[14,512]{1,0:T(8,128)} %get-tuple-element.29), channel_id=1, source_target_pairs={{0,8},{8,16},{1,9},{9,17},{2,10},{10,18},{3,11},{11,19},{4,12},{12... | collective-permute-start | bytes 86024 | tf_op jit(solution)/shard_map/ppermute | solution.py:360
  63.2 2.0 %collective-permute-start.7 = (f32[14,512]{1,0:T(8,128)}, f32[14,512]{1,0:T(8,128)S(1)}, u32[]{:S(2)}, u32[]{:S(2)}) collective-permute-start(f32[14,512]{1,0:T(8,128)} %get-tuple-element.30), channel_id=1, source_target_pairs={{8,0},{16,8},{9,1},{17,9},{10,2},{18,10},{11,3},{19,11},{12,4},{20... | collective-permute-start | bytes 86024 | tf_op jit(solution)/shard_map/ppermute | solution.py:361
  65.2 0.0 collective-permute-done.9
  65.2 0.0 collective-permute-done.8
  65.2 0.6 broadcast_select_fusion.1
  65.8 0.0 collective-permute-done.6.g0_ref
  65.8 0.0 copy-start.1
  65.8 2.8 %collective-permute-done.7.g1_ref = f32[14,512]{1,0:T(8,128)S(1)} collective-permute-done((f32[14,512]{1,0:T(8,128)}, f32[14,512]{1,0:T(8,128)S(1)}, u32[]{:S(2)}, u32[]{:S(2)}) %collective-permute-start.7) | collective-permute-done | bytes 28704 | tf_op jit(solution)/shard_map/ppermute | solution.py:361
  68.6 0.0 copy-start.2
  68.6 0.0 copy-done.1
  68.6 0.6 copy-done.2
  69.2 4.3 %shard_map.84 = f32[14,128,512]{2,1,0:T(8,128)} custom-call(f32[14,128,512]{2,1,0:T(8,128)} %get-tuple-element.28.out_in, f32[14,512]{1,0:T(8,128)} %copy-done.1, f32[14,512]{1,0:T(8,128)} %copy-done.2, f32[14,128]{1,0:T(8,128)} %get-tuple-element.42.gl_ref, f32[14,128]{1,0:T(8,128)} %get-tuple-element.41.gr_ref), custom_call_target="tpu_custom_call", output_to_operand_aliasing={{}: (0, {})} | custom-call | tf_op jit(solution)/shard_map/pallas_call | solution.py:288
  (9 shorter events, 0.1 us)
Async XLA Ops:
  0.0 6.9 %copy-start.3 = (s32[4,512]{1,0:T(4,128)S(1)}, s32[4,512]{1,0:T(4,128)}, u32[]{:S(2)}) copy-start(s32[4,512]{1,0:T(4,128)} %param.12) | copy-start | bytes 24580
  0.0 7.1 %copy-start.4 = (s32[4,512]{1,0:T(4,128)S(1)}, s32[4,512]{1,0:T(4,128)}, u32[]{:S(2)}) copy-start(s32[4,512]{1,0:T(4,128)} %param.14) | copy-start | bytes 24580
  0.0 10.1 %copy-start.5 = (f32[4,512]{1,0:T(4,128)S(1)}, f32[4,512]{1,0:T(4,128)}, u32[]{:S(2)}) copy-start(f32[4,512]{1,0:T(4,128)} %param.13) | copy-start | bytes 24580
  0.0 10.2 %copy-start.6 = (f32[4,512]{1,0:T(4,128)S(1)}, f32[4,512]{1,0:T(4,128)}, u32[]{:S(2)}) copy-start(f32[4,512]{1,0:T(4,128)} %param.15) | copy-start | bytes 24580
  1.9 9.2 %copy-start = (f32[14,1,512]{2,0,1:T(8,128)}, f32[14,1,512]{2,0,1:T(8,128)S(1)}, u32[]{:S(2)}) copy-start(f32[14,1,512]{2,0,1:T(8,128)S(1)} %copy.41) | copy-start | bytes 86020
  1.9 5.3 %collective-permute-start = (f32[1,15,512]{2,1,0:T(8,128)S(1)}, f32[1,15,512]{2,1,0:T(8,128)S(1)}, u32[]{:S(2)}, u32[]{:S(2)}) collective-permute-start(f32[1,15,512]{2,1,0:T(8,128)S(1)} %maximum_bitcast_fusion.1), channel_id=1, source_target_pairs={{0,4},{1,5},{2,6},{3,7},{4,0},{5,1},{6,2},{7,3},{8,12},{9,13},{10,... | collective-permute-start | bytes 92168 | tf_op jit(solution)/shard_map/ppermute | solution.py:333
  7.3 3.8 %collective-permute-start.1 = (f32[2,15,512]{2,1,0:T(8,128)S(1)}, f32[2,15,512]{2,1,0:T(8,128)S(1)}, u32[]{:S(2)}, u32[]{:S(2)}) collective-permute-start(f32[2,15,512]{2,1,0:T(8,128)S(1)} %pad_maximum_fusion.2), channel_id=1, source_target_pairs={{0,2},{1,3},{2,0},{3,1},{4,6},{5,7},{6,4},{7,5},{8,10},{9,11},{10,... | collective-permute-start | bytes 184328 | tf_op jit(solution)/shard_map/ppermute | solution.py:333
  11.1 5.6 %collective-permute-start.2 = (f32[5,15,512]{2,1,0:T(8,128)S(1)}, f32[5,15,512]{2,1,0:T(8,128)S(1)}, u32[]{:S(2)}, u32[]{:S(2)}) collective-permute-start(f32[5,15,512]{2,1,0:T(8,128)S(1)} %pad_maximum_fusion), channel_id=1, source_target_pairs={{0,1},{1,0},{2,3},{3,2},{4,5},{5,4},{6,7},{7,6},{8,9},{9,8},{10,11... | collective-permute-start | bytes 460808 | tf_op jit(solution)/shard_map/ppermute | solution.py:329
  14.6 5.2 %collective-permute-start.3 = (f32[14,128]{1,0:T(8,128)S(1)}, f32[14,128]{1,0:T(8,128)S(1)}, u32[]{:S(2)}, u32[]{:S(2)}) collective-permute-start(f32[14,128]{1,0:T(8,128)S(1)} %get-tuple-element.45), channel_id=1, source_target_pairs={{0,7},{1,2},{2,1},{3,4},{4,3},{5,6},{6,5},{7,0},{8,15},{9,10},{10,... | collective-permute-start | bytes 21512 | tf_op jit(solution)/shard_map/ppermute | solution.py:344
  22.8 11.4 %collective-permute-start.4 = (f32[14,512]{1,0:T(8,128)}, f32[14,512]{1,0:T(8,128)S(1)}, u32[]{:S(2)}, u32[]{:S(2)}) collective-permute-start(f32[14,512]{1,0:T(8,128)} %get-tuple-element.24), channel_id=1, source_target_pairs={{0,8},{8,16},{16,24},{1,9},{9,17},{17,25},{2,10},{10,18},{18,26},{... | collective-permute-start | bytes 86024 | tf_op jit(solution)/shard_map/ppermute | solution.py:353
  32.2 5.4 %collective-permute-start.5 = (f32[14,512]{1,0:T(8,128)}, f32[14,512]{1,0:T(8,128)S(1)}, u32[]{:S(2)}, u32[]{:S(2)}) collective-permute-start(f32[14,512]{1,0:T(8,128)} %get-tuple-element.25), channel_id=1, source_target_pairs={{8,0},{16,8},{24,16},{9,1},{17,9},{25,17},{10,2},{18,10},{26,18},{... | collective-permute-start | bytes 86024 | tf_op jit(solution)/shard_map/ppermute | solution.py:354
  34.2 3.5 %copy-start.7 = (f32[14,512]{1,0:T(8,128)}, f32[14,512]{1,0:T(8,128)S(1)}, u32[]{:S(2)}) copy-start(f32[14,512]{1,0:T(8,128)S(1)} %collective-permute-done.4.hlo_ref) | copy-start | bytes 86020
  37.7 0.6 copy-start.8
  57.6 7.6 %collective-permute-start.9 = (f32[14,128]{1,0:T(8,128)S(1)}, f32[14,128]{1,0:T(8,128)S(1)}, u32[]{:S(2)}, u32[]{:S(2)}) collective-permute-start(f32[14,128]{1,0:T(8,128)S(1)} %get-tuple-element.43), channel_id=1, source_target_pairs={{0,1},{1,0},{2,3},{3,2},{4,5},{5,4},{6,7},{7,6},{8,9},{9,8},{10,11... | collective-permute-start | bytes 21512 | tf_op jit(solution)/shard_map/ppermute | solution.py:362
  57.6 7.6 %collective-permute-start.8 = (f32[14,128]{1,0:T(8,128)S(1)}, f32[14,128]{1,0:T(8,128)S(1)}, u32[]{:S(2)}, u32[]{:S(2)}) collective-permute-start(f32[14,128]{1,0:T(8,128)S(1)} %get-tuple-element.44), channel_id=1, source_target_pairs={{0,7},{1,2},{2,1},{3,4},{4,3},{5,6},{6,5},{7,0},{8,15},{9,10},{10,... | collective-permute-start | bytes 21512 | tf_op jit(solution)/shard_map/ppermute | solution.py:363
  60.9 5.0 %collective-permute-start.6 = (f32[14,512]{1,0:T(8,128)}, f32[14,512]{1,0:T(8,128)S(1)}, u32[]{:S(2)}, u32[]{:S(2)}) collective-permute-start(f32[14,512]{1,0:T(8,128)} %get-tuple-element.29), channel_id=1, source_target_pairs={{0,8},{8,16},{1,9},{9,17},{2,10},{10,18},{3,11},{11,19},{4,12},{12... | collective-permute-start | bytes 86024 | tf_op jit(solution)/shard_map/ppermute | solution.py:360
  63.2 5.4 %collective-permute-start.7 = (f32[14,512]{1,0:T(8,128)}, f32[14,512]{1,0:T(8,128)S(1)}, u32[]{:S(2)}, u32[]{:S(2)}) collective-permute-start(f32[14,512]{1,0:T(8,128)} %get-tuple-element.30), channel_id=1, source_target_pairs={{8,0},{16,8},{9,1},{17,9},{10,2},{18,10},{11,3},{19,11},{12,4},{20... | collective-permute-start | bytes 86024 | tf_op jit(solution)/shard_map/ppermute | solution.py:361
  65.8 2.8 %copy-start.1 = (f32[14,512]{1,0:T(8,128)}, f32[14,512]{1,0:T(8,128)S(1)}, u32[]{:S(2)}) copy-start(f32[14,512]{1,0:T(8,128)S(1)} %collective-permute-done.6.g0_ref) | copy-start | bytes 86020
  68.6 0.6 copy-start.2

commit v21 on v19

--- a/solution.py
+++ b/solution.py
@@ -349,7 +349,7 @@
     lft = jnp.where(even, other, side_got)
     rgt = jnp.where(even, side_got, other)
 
-    up, down, lft, rgt = interpolate(flags, ids, wt, table, (edges[0], edges[1], lft, rgt))
+    up, down = interpolate(flags, ids, wt, table, (edges[0], edges[1]))
     halo_lo = lax.ppermute(up, "grp", [(i, i + 1) for i in range(n_grp - 1)])
     halo_hi = lax.ppermute(down, "grp", [(i + 1, i) for i in range(n_grp - 1)])
 

time: 72.6 us -> 71.2 us (0.981)
  waiting for transfers between devices: 5.95 us -> 4.3 us
    ppermute x1, waiting for transfers between devices: 1.06 us -> 0.01 us  [shards(): lax.ppermute(jnp.where(even, edges[3], edges[2]), 'blk', [(i, (i + 1) % n...]
  transfers between devices with their start and end apart: 10 -> 10, of which waited for: 3 -> 2; matrix products, arithmetic and copies ran while one was open for 12% -> 13% of each run, Pallas kernels for 0% -> 3%
where the time goes in v21:
time: 71.2 us; the launch traced here: 70.4 us
  starting transfers between devices  28.1 us (39%)
  Pallas kernels  25.3 us (36%)
  local copies, waits for them, and re-layouts  8.95 us (13%)
  waiting for transfers between devices  4.3 us (6%)
  other arithmetic  3.46 us (5%)
    pallas_call x1, Pallas kernels, fused_step(): pl.pallas_call(functools.partial(step_kernel, nf, rows, lanes), out_shape...  18.6 us
    ppermute x1, starting transfers between devices, shards(): halo_lo = lax.ppermute(up, 'grp', [(i, i + 1) for i in range(n_grp - 1)])  9.73 us
    ppermute x2, starting transfers between devices, shards(): lax.ppermute(planes, 'blk', partner)  4.57 us
    pallas_call x1, Pallas kernels, fix_edges(): pl.pallas_call(functools.partial(fix_kernel, low_w, side_w), out_shape=ja...  4.34 us
    ppermute x1, starting transfers between devices, shards(): gr = lax.ppermute(clo, 'blk', [((i + 1) % n_blk, i) for i in range(n_blk)])  4.15 us
    unnamed x30, local copies, waits for them, and re-layouts  3.08 us
    ppermute x1, waiting for transfers between devices, shards(): halo_hi = lax.ppermute(down, 'grp', [(i + 1, i) for i in range(n_grp - 1)])  2.9 us
    pallas_call x1, Pallas kernels, interpolate(): pl.pallas_call(functools.partial(interp_kernel, ks), out_shape=tuple((jax...  2.34 us
  transfers between devices with their start and end apart: 10, of which 2 were waited for; matrix products, arithmetic and copies ran while one was open for 13% of the time, Pallas kernels for 3%

profile of v21, /device:TPU:1, one launch (start us, length us, event | category | flops | bytes accessed | tf_op | source)
XLA Modules:
  0.0 70.4 jit_solution(6561506819937598265)
XLA Ops:
  0.0 0.0 copy-start.5
  0.0 0.0 copy-start.6
  0.0 0.0 copy-start.7
  0.0 0.0 copy-start.8
  0.0 0.8 %slice_bitcast_fusion.1 = f32[1,512]{1,0:T(1,128)S(1)} fusion(f32[14,128,512]{2,1,0:T(8,128)} %f_hbm.1), kind=kLoop, calls=%fused_computation.48 | loop fusion | bytes 4096 | tf_op jit(solution)/shard_map/slice | solution.py:316
  0.8 1.1 %fusion.15 = (f32[14,1,512]{2,1,0:T(1,128)S(1)}, f32[14,1,512]{2,1,0:T(1,128)S(1)}) fusion(f32[14,128,512]{2,1,0:T(8,128)} %f_hbm.1), kind=kLoop, calls=%fused_computation.51 | loop fusion | bytes 114688 | tf_op jit(solution)/shard_map/slice | solution.py:315
  1.9 0.0 copy-start
  1.9 3.2 %collective-permute-start = (f32[1,15,512]{2,1,0:T(8,128)S(1)}, f32[1,15,512]{2,1,0:T(8,128)S(1)}, u32[]{:S(2)}, u32[]{:S(2)}) collective-permute-start(f32[1,15,512]{2,1,0:T(8,128)S(1)} %maximum_bitcast_fusion.1), channel_id=1, source_target_pairs={{0,4},{1,5},{2,6},{3,7},{4,0},{5,1},{6,2},{7,3},{8,12},{9,13},{10,... | collective-permute-start | bytes 92168 | tf_op jit(solution)/shard_map/ppermute | solution.py:333
  5.1 1.8 %fusion.14 = (f32[14,128,1]{2,1,0:T(8,128)S(1)}, f32[14,128,1]{2,1,0:T(8,128)S(1)}) fusion(f32[14,128,512]{2,1,0:T(8,128)} %f_hbm.1), kind=kLoop, calls=%fused_computation.50 | loop fusion | bytes 28672 | tf_op jit(solution)/shard_map/slice | solution.py:321
  6.9 0.0 copy-done.5
  6.9 0.1 copy.20
  7.1 0.0 copy-done.6
  7.1 0.1 copy.21
  7.3 0.0 collective-permute-done
  7.3 1.4 %collective-permute-start.1 = (f32[2,15,512]{2,1,0:T(8,128)S(1)}, f32[2,15,512]{2,1,0:T(8,128)S(1)}, u32[]{:S(2)}, u32[]{:S(2)}) collective-permute-start(f32[2,15,512]{2,1,0:T(8,128)S(1)} %pad_maximum_fusion.2), channel_id=1, source_target_pairs={{0,2},{1,3},{2,0},{3,1},{4,6},{5,7},{6,4},{7,5},{8,10},{9,11},{10,... | collective-permute-start | bytes 184328 | tf_op jit(solution)/shard_map/ppermute | solution.py:333
  8.6 0.8 %add_select_fusion = (s32[4,512]{0,1:T(8,128)S(1)}, s32[4,512]{0,1:T(8,128)S(1)}) fusion(s32[4,512]{0,1:T(8,128)S(1)} %copy.20, s32[4,512]{0,1:T(8,128)S(1)} %copy.21, pred[]{:T(512)} %eq.17, s32[]{:T(128)S(6)} %axis_index.25), kind=kLoop, calls=%fused_computation | loop fusion | flops 157696 | bytes 32773 | tf_op jit(solution)/shard_map/jit(remainder)/select_n | solution.py:342
  9.5 0.6 copy.40
  10.1 0.0 copy-done.7
  10.1 0.1 copy.24
  10.2 0.0 copy-done.8
  10.2 0.1 copy.25
  10.4 0.3 copy.37
  10.7 0.3 copy.36
  11.0 0.0 copy-done
  11.1 0.0 collective-permute-done.1
  11.1 1.3 %collective-permute-start.2 = (f32[5,15,512]{2,1,0:T(8,128)S(1)}, f32[5,15,512]{2,1,0:T(8,128)S(1)}, u32[]{:S(2)}, u32[]{:S(2)}) collective-permute-start(f32[5,15,512]{2,1,0:T(8,128)S(1)} %pad_maximum_fusion), channel_id=1, source_target_pairs={{0,1},{1,0},{2,3},{3,2},{4,5},{5,4},{6,7},{7,6},{8,9},{9,8},{10,11... | collective-permute-start | bytes 460808 | tf_op jit(solution)/shard_map/ppermute | solution.py:329
  12.4 0.7 %select_bitcast_fusion.wt_ref = f32[512,4]{1,0:T(8,128)} fusion(f32[4,512]{0,1:T(8,128)S(1)} %copy.24, f32[4,512]{0,1:T(8,128)S(1)} %copy.25, pred[]{:T(512)} %eq.17), kind=kLoop, calls=%fused_computation.29 | loop fusion | flops 2048 | bytes 24577 | tf_op jit(solution)/shard_map/transpose | solution.py:343
  13.1 0.1 copy.23
  13.2 0.1 copy.22
  13.4 0.6 add.43.ids_s
  14.0 0.6 add_convert_fusion.flag_s
  14.6 2.1 %collective-permute-start.5 = (f32[14,128]{1,0:T(8,128)S(1)}, f32[14,128]{1,0:T(8,128)S(1)}, u32[]{:S(2)}, u32[]{:S(2)}) collective-permute-start(f32[14,128]{1,0:T(8,128)S(1)} %get-tuple-element.37), channel_id=1, source_target_pairs={{0,7},{1,2},{2,1},{3,4},{4,3},{5,6},{6,5},{7,0},{8,15},{9,10},{10,... | collective-permute-start | bytes 21512 | tf_op jit(solution)/shard_map/ppermute | solution.py:344
  16.7 0.0 collective-permute-done.2
  16.8 2.0 %copy.32 = f32[8,512,15]{2,1,0:T(8,128)} copy(f32[8,512,15]{1,2,0:T(8,128)S(1)} %maximum_bitcast_fusion) | data formatting | bytes 491520 | tf_op jit(solution)/shard_map/reshape | solution.py:335
  18.8 2.3 %shard_map.82 = (f32[14,512]{1,0:T(8,128)}, f32[14,512]{1,0:T(8,128)}) custom-call(f32[2]{0:T(128)} %add_convert_fusion.flag_s, s32[4,512]{1,0:T(4,128)} %add.43.ids_s, f32[512,4]{1,0:T(8,128)} %select_bitcast_fusion.wt_ref, f32[4096,15]{1,0:T(8,128)} %bitcast.27, f32[14,512]{1,0:T(8,128)} %bitcast.29, f32[14,512]{1,0:T(8,128)} %bitcast.30), custom_call_target="tpu_custom_call" | custom-call | tf_op jit(solution)/shard_map/pallas_call | solution.py:239
  21.1 9.7 %collective-permute-start.3 = (f32[14,512]{1,0:T(8,128)}, f32[14,512]{1,0:T(8,128)S(1)}, u32[]{:S(2)}, u32[]{:S(2)}) collective-permute-start(f32[14,512]{1,0:T(8,128)} %get-tuple-element.22), channel_id=1, source_target_pairs={{0,8},{8,16},{16,24},{1,9},{9,17},{17,25},{2,10},{10,18},{18,26},{... | collective-permute-start | bytes 86024 | tf_op jit(solution)/shard_map/ppermute | solution.py:353
  30.8 1.9 %collective-permute-start.4 = (f32[14,512]{1,0:T(8,128)}, f32[14,512]{1,0:T(8,128)S(1)}, u32[]{:S(2)}, u32[]{:S(2)}) collective-permute-start(f32[14,512]{1,0:T(8,128)} %get-tuple-element.23), channel_id=1, source_target_pairs={{8,0},{16,8},{24,16},{9,1},{17,9},{25,17},{10,2},{18,10},{26,18},{... | collective-permute-start | bytes 86024 | tf_op jit(solution)/shard_map/ppermute | solution.py:354
  32.8 0.0 collective-permute-done.5
  32.8 0.6 fusion.12
  33.4 0.0 collective-permute-done.3.hlo_ref
  33.4 0.0 copy-start.9
  33.4 2.9 %collective-permute-done.4.hhi_ref = f32[14,512]{1,0:T(8,128)S(1)} collective-permute-done((f32[14,512]{1,0:T(8,128)}, f32[14,512]{1,0:T(8,128)S(1)}, u32[]{:S(2)}, u32[]{:S(2)}) %collective-permute-start.4) | collective-permute-done | bytes 28704 | tf_op jit(solution)/shard_map/ppermute | solution.py:354
  36.3 0.0 copy-start.10
  36.3 0.0 copy-done.9
  36.3 0.6 copy-done.10
  36.9 18.6 %shard_map.83 = (f32[14,128,512]{2,1,0:T(8,128)}, f32[14,512]{1,0:T(8,128)}, f32[14,512]{1,0:T(8,128)}, f32[14,128]{1,0:T(8,128)}, f32[14,128]{1,0:T(8,128)}) custom-call(f32[14,14]{1,0:T(8,128)} %mix_s.1, f32[14]{0:T(128)} %act_s.1, f32[2]{0:T(128)} %add_convert_fusion.flag_s, f32[14,128,512]{2,1,0:T(8,128)} %f_hbm.1, f32[128,512]{1,0:T(8,128)} %rate_ref.1, ...), custom_call_target="tpu_custom_call" | custom-call | flops 95420416 | bytes 7602176 | tf_op jit(solution)/shard_map/pallas_call | solution.py:176
  55.5 2.0 %collective-permute-start.6 = (f32[14,512]{1,0:T(8,128)}, f32[14,512]{1,0:T(8,128)S(1)}, u32[]{:S(2)}, u32[]{:S(2)}) collective-permute-start(f32[14,512]{1,0:T(8,128)} %get-tuple-element.25), channel_id=1, source_target_pairs={{0,8},{8,16},{1,9},{9,17},{2,10},{10,18},{3,11},{11,19},{4,12},{12... | collective-permute-start | bytes 86024 | tf_op jit(solution)/shard_map/ppermute | solution.py:360
  57.5 2.3 %collective-permute-start.7 = (f32[14,512]{1,0:T(8,128)}, f32[14,512]{1,0:T(8,128)S(1)}, u32[]{:S(2)}, u32[]{:S(2)}) collective-permute-start(f32[14,512]{1,0:T(8,128)} %get-tuple-element.26), channel_id=1, source_target_pairs={{8,0},{16,8},{9,1},{17,9},{10,2},{18,10},{11,3},{19,11},{12,4},{20... | collective-permute-start | bytes 86024 | tf_op jit(solution)/shard_map/ppermute | solution.py:361
  59.8 0.1 collective-permute-start.8
  59.9 4.2 %collective-permute-start.9 = (f32[14,128]{1,0:T(8,128)}, f32[14,128]{1,0:T(8,128)S(1)}, u32[]{:S(2)}, u32[]{:S(2)}) collective-permute-start(f32[14,128]{1,0:T(8,128)} %get-tuple-element.28), channel_id=1, source_target_pairs={{1,0},{2,1},{3,2},{4,3},{5,4},{6,5},{7,6},{0,7},{9,8},{10,9},{11,1... | collective-permute-start | bytes 21512 | tf_op jit(solution)/shard_map/ppermute | solution.py:363
  64.0 1.4 %collective-permute-done.8.gl_ref = f32[14,128]{1,0:T(8,128)S(1)} collective-permute-done((f32[14,128]{1,0:T(8,128)}, f32[14,128]{1,0:T(8,128)S(1)}, u32[]{:S(2)}, u32[]{:S(2)}) %collective-permute-start.8) | collective-permute-done | bytes 7200 | tf_op jit(solution)/shard_map/ppermute | solution.py:362
  65.4 0.0 copy-start.3
  65.4 0.0 collective-permute-done.9.gr_ref
  65.4 0.0 copy-start.4
  65.4 0.0 collective-permute-done.6.g0_ref
  65.4 0.0 copy-start.1
  65.4 0.0 collective-permute-done.7.g1_ref
  65.4 0.0 copy-start.2
  65.5 0.5 copy-done.3
  66.0 0.0 copy-done.4
  66.0 0.0 copy-done.1
  66.0 0.0 copy-done.2
  66.0 4.3 %shard_map.84 = f32[14,128,512]{2,1,0:T(8,128)} custom-call(f32[14,128,512]{2,1,0:T(8,128)} %get-tuple-element.24.out_in, f32[14,512]{1,0:T(8,128)} %copy-done.1, f32[14,512]{1,0:T(8,128)} %copy-done.2, f32[14,128]{1,0:T(8,128)} %copy-done.3, f32[14,128]{1,0:T(8,128)} %copy-done.4), custom_call_target="tpu_custom_call", output_to_operand_aliasing={{}: (0, {})} | custom-call | tf_op jit(solution)/shard_map/pallas_call | solution.py:288
  (9 shorter events, 0.1 us)
Async XLA Ops:
  0.0 6.9 %copy-start.5 = (s32[4,512]{1,0:T(4,128)S(1)}, s32[4,512]{1,0:T(4,128)}, u32[]{:S(2)}) copy-start(s32[4,512]{1,0:T(4,128)} %param.12) | copy-start | bytes 24580
  0.0 7.1 %copy-start.6 = (s32[4,512]{1,0:T(4,128)S(1)}, s32[4,512]{1,0:T(4,128)}, u32[]{:S(2)}) copy-start(s32[4,512]{1,0:T(4,128)} %param.14) | copy-start | bytes 24580
  0.0 10.1 %copy-start.7 = (f32[4,512]{1,0:T(4,128)S(1)}, f32[4,512]{1,0:T(4,128)}, u32[]{:S(2)}) copy-start(f32[4,512]{1,0:T(4,128)} %param.13) | copy-start | bytes 24580
  0.0 10.2 %copy-start.8 = (f32[4,512]{1,0:T(4,128)S(1)}, f32[4,512]{1,0:T(4,128)}, u32[]{:S(2)}) copy-start(f32[4,512]{1,0:T(4,128)} %param.15) | copy-start | bytes 24580
  1.9 9.2 %copy-start = (f32[14,1,512]{2,0,1:T(8,128)}, f32[14,1,512]{2,0,1:T(8,128)S(1)}, u32[]{:S(2)}) copy-start(f32[14,1,512]{2,0,1:T(8,128)S(1)} %copy.41) | copy-start | bytes 86020
  1.9 5.3 %collective-permute-start = (f32[1,15,512]{2,1,0:T(8,128)S(1)}, f32[1,15,512]{2,1,0:T(8,128)S(1)}, u32[]{:S(2)}, u32[]{:S(2)}) collective-permute-start(f32[1,15,512]{2,1,0:T(8,128)S(1)} %maximum_bitcast_fusion.1), channel_id=1, source_target_pairs={{0,4},{1,5},{2,6},{3,7},{4,0},{5,1},{6,2},{7,3},{8,12},{9,13},{10,... | collective-permute-start | bytes 92168 | tf_op jit(solution)/shard_map/ppermute | solution.py:333
  7.3 3.8 %collective-permute-start.1 = (f32[2,15,512]{2,1,0:T(8,128)S(1)}, f32[2,15,512]{2,1,0:T(8,128)S(1)}, u32[]{:S(2)}, u32[]{:S(2)}) collective-permute-start(f32[2,15,512]{2,1,0:T(8,128)S(1)} %pad_maximum_fusion.2), channel_id=1, source_target_pairs={{0,2},{1,3},{2,0},{3,1},{4,6},{5,7},{6,4},{7,5},{8,10},{9,11},{10,... | collective-permute-start | bytes 184328 | tf_op jit(solution)/shard_map/ppermute | solution.py:333
  11.1 5.6 %collective-permute-start.2 = (f32[5,15,512]{2,1,0:T(8,128)S(1)}, f32[5,15,512]{2,1,0:T(8,128)S(1)}, u32[]{:S(2)}, u32[]{:S(2)}) collective-permute-start(f32[5,15,512]{2,1,0:T(8,128)S(1)} %pad_maximum_fusion), channel_id=1, source_target_pairs={{0,1},{1,0},{2,3},{3,2},{4,5},{5,4},{6,7},{7,6},{8,9},{9,8},{10,11... | collective-permute-start | bytes 460808 | tf_op jit(solution)/shard_map/ppermute | solution.py:329
  14.6 18.1 %collective-permute-start.5 = (f32[14,128]{1,0:T(8,128)S(1)}, f32[14,128]{1,0:T(8,128)S(1)}, u32[]{:S(2)}, u32[]{:S(2)}) collective-permute-start(f32[14,128]{1,0:T(8,128)S(1)} %get-tuple-element.37), channel_id=1, source_target_pairs={{0,7},{1,2},{2,1},{3,4},{4,3},{5,6},{6,5},{7,0},{8,15},{9,10},{10,... | collective-permute-start | bytes 21512 | tf_op jit(solution)/shard_map/ppermute | solution.py:344
  21.1 12.3 %collective-permute-start.3 = (f32[14,512]{1,0:T(8,128)}, f32[14,512]{1,0:T(8,128)S(1)}, u32[]{:S(2)}, u32[]{:S(2)}) collective-permute-start(f32[14,512]{1,0:T(8,128)} %get-tuple-element.22), channel_id=1, source_target_pairs={{0,8},{8,16},{16,24},{1,9},{9,17},{17,25},{2,10},{10,18},{18,26},{... | collective-permute-start | bytes 86024 | tf_op jit(solution)/shard_map/ppermute | solution.py:353
  30.8 5.4 %collective-permute-start.4 = (f32[14,512]{1,0:T(8,128)}, f32[14,512]{1,0:T(8,128)S(1)}, u32[]{:S(2)}, u32[]{:S(2)}) collective-permute-start(f32[14,512]{1,0:T(8,128)} %get-tuple-element.23), channel_id=1, source_target_pairs={{8,0},{16,8},{24,16},{9,1},{17,9},{25,17},{10,2},{18,10},{26,18},{... | collective-permute-start | bytes 86024 | tf_op jit(solution)/shard_map/ppermute | solution.py:354
  33.4 2.9 %copy-start.9 = (f32[14,512]{1,0:T(8,128)}, f32[14,512]{1,0:T(8,128)S(1)}, u32[]{:S(2)}) copy-start(f32[14,512]{1,0:T(8,128)S(1)} %collective-permute-done.3.hlo_ref) | copy-start | bytes 86020
  36.3 0.6 copy-start.10
  55.5 9.9 %collective-permute-start.6 = (f32[14,512]{1,0:T(8,128)}, f32[14,512]{1,0:T(8,128)S(1)}, u32[]{:S(2)}, u32[]{:S(2)}) collective-permute-start(f32[14,512]{1,0:T(8,128)} %get-tuple-element.25), channel_id=1, source_target_pairs={{0,8},{8,16},{1,9},{9,17},{2,10},{10,18},{3,11},{11,19},{4,12},{12... | collective-permute-start | bytes 86024 | tf_op jit(solution)/shard_map/ppermute | solution.py:360
  57.5 7.9 %collective-permute-start.7 = (f32[14,512]{1,0:T(8,128)}, f32[14,512]{1,0:T(8,128)S(1)}, u32[]{:S(2)}, u32[]{:S(2)}) collective-permute-start(f32[14,512]{1,0:T(8,128)} %get-tuple-element.26), channel_id=1, source_target_pairs={{8,0},{16,8},{9,1},{17,9},{10,2},{18,10},{11,3},{19,11},{12,4},{20... | collective-permute-start | bytes 86024 | tf_op jit(solution)/shard_map/ppermute | solution.py:361
  59.8 5.6 %collective-permute-start.8 = (f32[14,128]{1,0:T(8,128)}, f32[14,128]{1,0:T(8,128)S(1)}, u32[]{:S(2)}, u32[]{:S(2)}) collective-permute-start(f32[14,128]{1,0:T(8,128)} %get-tuple-element.27), channel_id=1, source_target_pairs={{0,1},{1,2},{2,3},{3,4},{4,5},{5,6},{6,7},{7,0},{8,9},{9,10},{10,1... | collective-permute-start | bytes 21512 | tf_op jit(solution)/shard_map/ppermute | solution.py:362
  59.9 5.5 %collective-permute-start.9 = (f32[14,128]{1,0:T(8,128)}, f32[14,128]{1,0:T(8,128)S(1)}, u32[]{:S(2)}, u32[]{:S(2)}) collective-permute-start(f32[14,128]{1,0:T(8,128)} %get-tuple-element.28), channel_id=1, source_target_pairs={{1,0},{2,1},{3,2},{4,3},{5,4},{6,5},{7,6},{0,7},{9,8},{10,9},{11,1... | collective-permute-start | bytes 21512 | tf_op jit(solution)/shard_map/ppermute | solution.py:363
  65.4 0.6 copy-start.3
  65.4 0.6 copy-start.4
  65.4 0.6 copy-start.1
  65.4 0.6 copy-start.2

commit v22 on v21

--- a/solution.py
+++ b/solution.py
@@ -30,6 +30,7 @@
     at_exit = flag_s[0] > 0.5
     at_turb = flag_s[1] > 0.5
     at_end = flag_s[0] + flag_s[1] > 0.5
+    even = flag_s[2] > 0.5
 
     copy = pltpu.make_async_copy(f_hbm, ext1.at[:, SUB:top, LANE:right], sem.at[0])
     copy.start()
@@ -38,8 +39,9 @@
         low = hlo_ref[f:f + 1, :]
         ext1[f, SUB - 1:SUB, LANE:right] = low
         ext2[f, SUB - 1:SUB, LANE:right] = jnp.where(at_turb, low, 0.0)
-        ext1[f, SUB:top, 0:LANE] = tile_t(lft_ref[f:f + 1, :])
-        ext1[f, SUB:top, right:right + LANE] = tile_t(rgt_ref[f:f + 1, :])
+        near, far = lft_ref[f:f + 1, :], rgt_ref[f:f + 1, :]
+        ext1[f, SUB:top, 0:LANE] = tile_t(jnp.where(even, far, near))
+        ext1[f, SUB:top, right:right + LANE] = tile_t(jnp.where(even, near, far))
         ext2[f, SUB:top, 0:LANE] = zeros
         ext2[f, SUB:top, right:right + LANE] = zeros
     for f in range(nf):
@@ -309,7 +311,7 @@
     b = lax.axis_index("blk")
     exit_grp = n_grp - 2
     turb_grp = n_grp - 1
-    flags = jnp.stack([g == exit_grp, g == turb_grp]).astype(jnp.float32)
+    flags = jnp.stack([g == exit_grp, g == turb_grp, b % 2 == 0]).astype(jnp.float32)
 
     last_row = fields[:, -1, :]
     first_row = fields[:, 0, :]
@@ -346,8 +348,7 @@
         "blk",
         [(i, (i + 1) % n_blk if i % 2 else (i - 1) % n_blk) for i in range(n_blk)],
     )
-    lft = jnp.where(even, other, side_got)
-    rgt = jnp.where(even, side_got, other)
+    lft, rgt = side_got, other
 
     up, down = interpolate(flags, ids, wt, table, (edges[0], edges[1]))
     halo_lo = lax.ppermute(up, "grp", [(i, i + 1) for i in range(n_grp - 1)])

time: 71.2 us -> 71.2 us (level)
    unnamed x30 -> x32, local copies, waits for them, and re-layouts: 3.08 us -> 3.09 us
where the time goes in v22:
time: 71.2 us; the launch traced here: 70.4 us
  starting transfers between devices  28.1 us (39%)
  Pallas kernels  25.3 us (36%)
  local copies, waits for them, and re-layouts  9.55 us (13%)
  waiting for transfers between devices  4.3 us (6%)
  other arithmetic  2.85 us (4%)
    pallas_call x1, Pallas kernels, fused_step(): pl.pallas_call(functools.partial(step_kernel, nf, rows, lanes), out_shape...  18.6 us
    ppermute x1, starting transfers between devices, shards(): halo_lo = lax.ppermute(up, 'grp', [(i, i + 1) for i in range(n_grp - 1)])  9.73 us
    ppermute x2, starting transfers between devices, shards(): lax.ppermute(planes, 'blk', partner)  4.57 us
    pallas_call x1, Pallas kernels, fix_edges(): pl.pallas_call(functools.partial(fix_kernel, low_w, side_w), out_shape=ja...  4.34 us
    ppermute x1, starting transfers between devices, shards(): gr = lax.ppermute(clo, 'blk', [((i + 1) % n_blk, i) for i in range(n_blk)])  4.15 us
    unnamed x32, local copies, waits for them, and re-layouts  3.09 us
    ppermute x1, waiting for transfers between devices, shards(): halo_hi = lax.ppermute(down, 'grp', [(i + 1, i) for i in range(n_grp - 1)])  2.9 us
    pallas_call x1, Pallas kernels, interpolate(): pl.pallas_call(functools.partial(interp_kernel, ks), out_shape=tuple((jax...  2.34 us
  transfers between devices with their start and end apart: 10, of which 2 were waited for; matrix products, arithmetic and copies ran while one was open for 13% of the time, Pallas kernels for 3%

profile of v22, /device:TPU:1, one launch (start us, length us, event | category | flops | bytes accessed | tf_op | source)
XLA Modules:
  0.0 70.4 jit_solution(18438824313055278778)
XLA Ops:
  0.0 0.0 copy-start.6
  0.0 0.0 copy-start.7
  0.0 0.0 copy-start.8
  0.0 0.8 %slice_bitcast_fusion.1 = f32[1,512]{1,0:T(1,128)S(1)} fusion(f32[14,128,512]{2,1,0:T(8,128)} %f_hbm.1), kind=kLoop, calls=%fused_computation.46 | loop fusion | bytes 4096 | tf_op jit(solution)/shard_map/slice | solution.py:318
  0.8 1.1 %fusion.13 = (f32[14,1,512]{2,1,0:T(1,128)S(1)}, f32[14,1,512]{2,1,0:T(1,128)S(1)}) fusion(f32[14,128,512]{2,1,0:T(8,128)} %f_hbm.1), kind=kLoop, calls=%fused_computation.49 | loop fusion | bytes 114688 | tf_op jit(solution)/shard_map/slice | solution.py:317
  1.9 0.0 copy-start
  1.9 3.2 %collective-permute-start = (f32[1,15,512]{2,1,0:T(8,128)S(1)}, f32[1,15,512]{2,1,0:T(8,128)S(1)}, u32[]{:S(2)}, u32[]{:S(2)}) collective-permute-start(f32[1,15,512]{2,1,0:T(8,128)S(1)} %maximum_bitcast_fusion.1), channel_id=1, source_target_pairs={{0,4},{1,5},{2,6},{3,7},{4,0},{5,1},{6,2},{7,3},{8,12},{9,13},{10,... | collective-permute-start | bytes 92168 | tf_op jit(solution)/shard_map/ppermute | solution.py:335
  5.1 1.8 %fusion.12 = (f32[14,128,1]{2,1,0:T(8,128)S(1)}, f32[14,128,1]{2,1,0:T(8,128)S(1)}) fusion(f32[14,128,512]{2,1,0:T(8,128)} %f_hbm.1), kind=kLoop, calls=%fused_computation.48 | loop fusion | bytes 28672 | tf_op jit(solution)/shard_map/slice | solution.py:323
  6.9 0.0 copy-done.5
  6.9 0.1 copy.20
  7.1 0.0 copy-done.6
  7.1 0.1 copy.21
  7.3 0.0 collective-permute-done
  7.3 1.4 %collective-permute-start.1 = (f32[2,15,512]{2,1,0:T(8,128)S(1)}, f32[2,15,512]{2,1,0:T(8,128)S(1)}, u32[]{:S(2)}, u32[]{:S(2)}) collective-permute-start(f32[2,15,512]{2,1,0:T(8,128)S(1)} %pad_maximum_fusion.2), channel_id=1, source_target_pairs={{0,2},{1,3},{2,0},{3,1},{4,6},{5,7},{6,4},{7,5},{8,10},{9,11},{10,... | collective-permute-start | bytes 184328 | tf_op jit(solution)/shard_map/ppermute | solution.py:335
  8.6 0.8 %add_select_fusion = (s32[4,512]{0,1:T(8,128)S(1)}, s32[4,512]{0,1:T(8,128)S(1)}) fusion(s32[4,512]{0,1:T(8,128)S(1)} %copy.20, s32[4,512]{0,1:T(8,128)S(1)} %copy.21, pred[]{:T(512)} %eq.19, s32[]{:T(128)S(6)} %axis_index.25), kind=kLoop, calls=%fused_computation | loop fusion | flops 157696 | bytes 32773 | tf_op jit(solution)/shard_map/jit(remainder)/select_n | solution.py:344
  9.5 0.6 copy.40
  10.1 0.0 copy-done.7
  10.1 0.1 copy.24
  10.2 0.0 copy-done.8
  10.2 0.1 copy.25
  10.4 0.3 copy.37
  10.7 0.3 copy.36
  11.0 0.0 copy-done
  11.1 0.0 collective-permute-done.1
  11.1 1.3 %collective-permute-start.2 = (f32[5,15,512]{2,1,0:T(8,128)S(1)}, f32[5,15,512]{2,1,0:T(8,128)S(1)}, u32[]{:S(2)}, u32[]{:S(2)}) collective-permute-start(f32[5,15,512]{2,1,0:T(8,128)S(1)} %pad_maximum_fusion), channel_id=1, source_target_pairs={{0,1},{1,0},{2,3},{3,2},{4,5},{5,4},{6,7},{7,6},{8,9},{9,8},{10,11... | collective-permute-start | bytes 460808 | tf_op jit(solution)/shard_map/ppermute | solution.py:331
  12.4 0.7 %select_bitcast_fusion.wt_ref = f32[512,4]{1,0:T(8,128)} fusion(f32[4,512]{0,1:T(8,128)S(1)} %copy.24, f32[4,512]{0,1:T(8,128)S(1)} %copy.25, pred[]{:T(512)} %eq.19), kind=kLoop, calls=%fused_computation.29 | loop fusion | flops 2048 | bytes 24577 | tf_op jit(solution)/shard_map/transpose | solution.py:345
  13.1 0.1 copy.23
  13.2 0.1 copy.22
  13.4 0.6 add.45.ids_s
  14.0 0.6 add_convert_fusion.flag_s
  14.6 2.1 %collective-permute-start.5 = (f32[14,128]{1,0:T(8,128)S(1)}, f32[14,128]{1,0:T(8,128)S(1)}, u32[]{:S(2)}, u32[]{:S(2)}) collective-permute-start(f32[14,128]{1,0:T(8,128)S(1)} %get-tuple-element.35), channel_id=1, source_target_pairs={{0,7},{1,2},{2,1},{3,4},{4,3},{5,6},{6,5},{7,0},{8,15},{9,10},{10,... | collective-permute-start | bytes 21512 | tf_op jit(solution)/shard_map/ppermute | solution.py:346
  16.7 0.0 collective-permute-done.2
  16.8 2.0 %copy.32 = f32[8,512,15]{2,1,0:T(8,128)} copy(f32[8,512,15]{1,2,0:T(8,128)S(1)} %maximum_bitcast_fusion) | data formatting | bytes 491520 | tf_op jit(solution)/shard_map/reshape | solution.py:337
  18.8 2.3 %shard_map.82 = (f32[14,512]{1,0:T(8,128)}, f32[14,512]{1,0:T(8,128)}) custom-call(f32[3]{0:T(128)} %add_convert_fusion.flag_s, s32[4,512]{1,0:T(4,128)} %add.45.ids_s, f32[512,4]{1,0:T(8,128)} %select_bitcast_fusion.wt_ref, f32[4096,15]{1,0:T(8,128)} %bitcast.24, f32[14,512]{1,0:T(8,128)} %bitcast.26, f32[14,512]{1,0:T(8,128)} %bitcast.27), custom_call_target="tpu_custom_call" | custom-call | tf_op jit(solution)/shard_map/pallas_call | solution.py:241
  21.1 9.7 %collective-permute-start.3 = (f32[14,512]{1,0:T(8,128)}, f32[14,512]{1,0:T(8,128)S(1)}, u32[]{:S(2)}, u32[]{:S(2)}) collective-permute-start(f32[14,512]{1,0:T(8,128)} %get-tuple-element.22), channel_id=1, source_target_pairs={{0,8},{8,16},{16,24},{1,9},{9,17},{17,25},{2,10},{10,18},{18,26},{... | collective-permute-start | bytes 86024 | tf_op jit(solution)/shard_map/ppermute | solution.py:354
  30.8 1.9 %collective-permute-start.4 = (f32[14,512]{1,0:T(8,128)}, f32[14,512]{1,0:T(8,128)S(1)}, u32[]{:S(2)}, u32[]{:S(2)}) collective-permute-start(f32[14,512]{1,0:T(8,128)} %get-tuple-element.23), channel_id=1, source_target_pairs={{8,0},{16,8},{24,16},{9,1},{17,9},{25,17},{10,2},{18,10},{26,18},{... | collective-permute-start | bytes 86024 | tf_op jit(solution)/shard_map/ppermute | solution.py:355
  32.8 0.6 slice_bitcast_fusion.lft_ref
  33.4 0.0 collective-permute-done.5.rgt_ref
  33.4 0.0 copy-start.11
  33.4 0.0 collective-permute-done.3.hlo_ref
  33.4 0.0 copy-start.9
  33.4 2.9 %collective-permute-done.4.hhi_ref = f32[14,512]{1,0:T(8,128)S(1)} collective-permute-done((f32[14,512]{1,0:T(8,128)}, f32[14,512]{1,0:T(8,128)S(1)}, u32[]{:S(2)}, u32[]{:S(2)}) %collective-permute-start.4) | collective-permute-done | bytes 28704 | tf_op jit(solution)/shard_map/ppermute | solution.py:355
  36.3 0.0 copy-done.11
  36.3 0.0 copy-done.9
  36.3 0.0 copy-start.10
  36.3 0.6 copy-done.10
  36.9 18.6 %shard_map.83 = (f32[14,128,512]{2,1,0:T(8,128)}, f32[14,512]{1,0:T(8,128)}, f32[14,512]{1,0:T(8,128)}, f32[14,128]{1,0:T(8,128)}, f32[14,128]{1,0:T(8,128)}) custom-call(f32[14,14]{1,0:T(8,128)} %mix_s.1, f32[14]{0:T(128)} %act_s.1, f32[3]{0:T(128)} %add_convert_fusion.flag_s, f32[14,128,512]{2,1,0:T(8,128)} %f_hbm.1, f32[128,512]{1,0:T(8,128)} %rate_ref.1, ...), custom_call_target="tpu_custom_call" | custom-call | flops 95420416 | bytes 7602176 | tf_op jit(solution)/shard_map/pallas_call | solution.py:178
  55.5 2.0 %collective-permute-start.6 = (f32[14,512]{1,0:T(8,128)}, f32[14,512]{1,0:T(8,128)S(1)}, u32[]{:S(2)}, u32[]{:S(2)}) collective-permute-start(f32[14,512]{1,0:T(8,128)} %get-tuple-element.25), channel_id=1, source_target_pairs={{0,8},{8,16},{1,9},{9,17},{2,10},{10,18},{3,11},{11,19},{4,12},{12... | collective-permute-start | bytes 86024 | tf_op jit(solution)/shard_map/ppermute | solution.py:361
  57.5 2.3 %collective-permute-start.7 = (f32[14,512]{1,0:T(8,128)}, f32[14,512]{1,0:T(8,128)S(1)}, u32[]{:S(2)}, u32[]{:S(2)}) collective-permute-start(f32[14,512]{1,0:T(8,128)} %get-tuple-element.26), channel_id=1, source_target_pairs={{8,0},{16,8},{9,1},{17,9},{10,2},{18,10},{11,3},{19,11},{12,4},{20... | collective-permute-start | bytes 86024 | tf_op jit(solution)/shard_map/ppermute | solution.py:362
  59.8 0.1 collective-permute-start.8
  59.9 4.2 %collective-permute-start.9 = (f32[14,128]{1,0:T(8,128)}, f32[14,128]{1,0:T(8,128)S(1)}, u32[]{:S(2)}, u32[]{:S(2)}) collective-permute-start(f32[14,128]{1,0:T(8,128)} %get-tuple-element.28), channel_id=1, source_target_pairs={{1,0},{2,1},{3,2},{4,3},{5,4},{6,5},{7,6},{0,7},{9,8},{10,9},{11,1... | collective-permute-start | bytes 21512 | tf_op jit(solution)/shard_map/ppermute | solution.py:364
  64.0 1.4 %collective-permute-done.8.gl_ref = f32[14,128]{1,0:T(8,128)S(1)} collective-permute-done((f32[14,128]{1,0:T(8,128)}, f32[14,128]{1,0:T(8,128)S(1)}, u32[]{:S(2)}, u32[]{:S(2)}) %collective-permute-start.8) | collective-permute-done | bytes 7200 | tf_op jit(solution)/shard_map/ppermute | solution.py:363
  65.4 0.0 copy-start.3
  65.4 0.0 collective-permute-done.9.gr_ref
  65.4 0.0 copy-start.4
  65.4 0.0 collective-permute-done.6.g0_ref
  65.4 0.0 copy-start.1
  65.4 0.0 collective-permute-done.7.g1_ref
  65.5 0.0 copy-start.2
  65.5 0.5 copy-done.3
  66.0 0.0 copy-done.4
  66.0 0.0 copy-done.1
  66.0 0.0 copy-done.2
  66.1 4.3 %shard_map.84 = f32[14,128,512]{2,1,0:T(8,128)} custom-call(f32[14,128,512]{2,1,0:T(8,128)} %get-tuple-element.24.out_in, f32[14,512]{1,0:T(8,128)} %copy-done.1, f32[14,512]{1,0:T(8,128)} %copy-done.2, f32[14,128]{1,0:T(8,128)} %copy-done.3, f32[14,128]{1,0:T(8,128)} %copy-done.4), custom_call_target="tpu_custom_call", output_to_operand_aliasing={{}: (0, {})} | custom-call | tf_op jit(solution)/shard_map/pallas_call | solution.py:290
  (10 shorter events, 0.1 us)
Async XLA Ops:
  0.0 6.9 %copy-start.5 = (s32[4,512]{1,0:T(4,128)S(1)}, s32[4,512]{1,0:T(4,128)}, u32[]{:S(2)}) copy-start(s32[4,512]{1,0:T(4,128)} %param.12) | copy-start | bytes 24580
  0.0 7.1 %copy-start.6 = (s32[4,512]{1,0:T(4,128)S(1)}, s32[4,512]{1,0:T(4,128)}, u32[]{:S(2)}) copy-start(s32[4,512]{1,0:T(4,128)} %param.14) | copy-start | bytes 24580
  0.0 10.1 %copy-start.7 = (f32[4,512]{1,0:T(4,128)S(1)}, f32[4,512]{1,0:T(4,128)}, u32[]{:S(2)}) copy-start(f32[4,512]{1,0:T(4,128)} %param.13) | copy-start | bytes 24580
  0.0 10.2 %copy-start.8 = (f32[4,512]{1,0:T(4,128)S(1)}, f32[4,512]{1,0:T(4,128)}, u32[]{:S(2)}) copy-start(f32[4,512]{1,0:T(4,128)} %param.15) | copy-start | bytes 24580
  1.9 9.2 %copy-start = (f32[14,1,512]{2,0,1:T(8,128)}, f32[14,1,512]{2,0,1:T(8,128)S(1)}, u32[]{:S(2)}) copy-start(f32[14,1,512]{2,0,1:T(8,128)S(1)} %copy.41) | copy-start | bytes 86020
  1.9 5.3 %collective-permute-start = (f32[1,15,512]{2,1,0:T(8,128)S(1)}, f32[1,15,512]{2,1,0:T(8,128)S(1)}, u32[]{:S(2)}, u32[]{:S(2)}) collective-permute-start(f32[1,15,512]{2,1,0:T(8,128)S(1)} %maximum_bitcast_fusion.1), channel_id=1, source_target_pairs={{0,4},{1,5},{2,6},{3,7},{4,0},{5,1},{6,2},{7,3},{8,12},{9,13},{10,... | collective-permute-start | bytes 92168 | tf_op jit(solution)/shard_map/ppermute | solution.py:335
  7.3 3.8 %collective-permute-start.1 = (f32[2,15,512]{2,1,0:T(8,128)S(1)}, f32[2,15,512]{2,1,0:T(8,128)S(1)}, u32[]{:S(2)}, u32[]{:S(2)}) collective-permute-start(f32[2,15,512]{2,1,0:T(8,128)S(1)} %pad_maximum_fusion.2), channel_id=1, source_target_pairs={{0,2},{1,3},{2,0},{3,1},{4,6},{5,7},{6,4},{7,5},{8,10},{9,11},{10,... | collective-permute-start | bytes 184328 | tf_op jit(solution)/shard_map/ppermute | solution.py:335
  11.1 5.6 %collective-permute-start.2 = (f32[5,15,512]{2,1,0:T(8,128)S(1)}, f32[5,15,512]{2,1,0:T(8,128)S(1)}, u32[]{:S(2)}, u32[]{:S(2)}) collective-permute-start(f32[5,15,512]{2,1,0:T(8,128)S(1)} %pad_maximum_fusion), channel_id=1, source_target_pairs={{0,1},{1,0},{2,3},{3,2},{4,5},{5,4},{6,7},{7,6},{8,9},{9,8},{10,11... | collective-permute-start | bytes 460808 | tf_op jit(solution)/shard_map/ppermute | solution.py:331
  14.6 18.7 %collective-permute-start.5 = (f32[14,128]{1,0:T(8,128)S(1)}, f32[14,128]{1,0:T(8,128)S(1)}, u32[]{:S(2)}, u32[]{:S(2)}) collective-permute-start(f32[14,128]{1,0:T(8,128)S(1)} %get-tuple-element.35), channel_id=1, source_target_pairs={{0,7},{1,2},{2,1},{3,4},{4,3},{5,6},{6,5},{7,0},{8,15},{9,10},{10,... | collective-permute-start | bytes 21512 | tf_op jit(solution)/shard_map/ppermute | solution.py:346
  21.1 12.3 %collective-permute-start.3 = (f32[14,512]{1,0:T(8,128)}, f32[14,512]{1,0:T(8,128)S(1)}, u32[]{:S(2)}, u32[]{:S(2)}) collective-permute-start(f32[14,512]{1,0:T(8,128)} %get-tuple-element.22), channel_id=1, source_target_pairs={{0,8},{8,16},{16,24},{1,9},{9,17},{17,25},{2,10},{10,18},{18,26},{... | collective-permute-start | bytes 86024 | tf_op jit(solution)/shard_map/ppermute | solution.py:354
  30.8 5.4 %collective-permute-start.4 = (f32[14,512]{1,0:T(8,128)}, f32[14,512]{1,0:T(8,128)S(1)}, u32[]{:S(2)}, u32[]{:S(2)}) collective-permute-start(f32[14,512]{1,0:T(8,128)} %get-tuple-element.23), channel_id=1, source_target_pairs={{8,0},{16,8},{24,16},{9,1},{17,9},{25,17},{10,2},{18,10},{26,18},{... | collective-permute-start | bytes 86024 | tf_op jit(solution)/shard_map/ppermute | solution.py:355
  33.4 2.9 %copy-start.11 = (f32[14,128]{1,0:T(8,128)}, f32[14,128]{1,0:T(8,128)S(1)}, u32[]{:S(2)}) copy-start(f32[14,128]{1,0:T(8,128)S(1)} %collective-permute-done.5.rgt_ref) | copy-start | bytes 21508
  33.4 2.9 %copy-start.9 = (f32[14,512]{1,0:T(8,128)}, f32[14,512]{1,0:T(8,128)S(1)}, u32[]{:S(2)}) copy-start(f32[14,512]{1,0:T(8,128)S(1)} %collective-permute-done.3.hlo_ref) | copy-start | bytes 86020
  36.3 0.6 copy-start.10
  55.5 9.9 %collective-permute-start.6 = (f32[14,512]{1,0:T(8,128)}, f32[14,512]{1,0:T(8,128)S(1)}, u32[]{:S(2)}, u32[]{:S(2)}) collective-permute-start(f32[14,512]{1,0:T(8,128)} %get-tuple-element.25), channel_id=1, source_target_pairs={{0,8},{8,16},{1,9},{9,17},{2,10},{10,18},{3,11},{11,19},{4,12},{12... | collective-permute-start | bytes 86024 | tf_op jit(solution)/shard_map/ppermute | solution.py:361
  57.5 7.9 %collective-permute-start.7 = (f32[14,512]{1,0:T(8,128)}, f32[14,512]{1,0:T(8,128)S(1)}, u32[]{:S(2)}, u32[]{:S(2)}) collective-permute-start(f32[14,512]{1,0:T(8,128)} %get-tuple-element.26), channel_id=1, source_target_pairs={{8,0},{16,8},{9,1},{17,9},{10,2},{18,10},{11,3},{19,11},{12,4},{20... | collective-permute-start | bytes 86024 | tf_op jit(solution)/shard_map/ppermute | solution.py:362
  59.8 5.6 %collective-permute-start.8 = (f32[14,128]{1,0:T(8,128)}, f32[14,128]{1,0:T(8,128)S(1)}, u32[]{:S(2)}, u32[]{:S(2)}) collective-permute-start(f32[14,128]{1,0:T(8,128)} %get-tuple-element.27), channel_id=1, source_target_pairs={{0,1},{1,2},{2,3},{3,4},{4,5},{5,6},{6,7},{7,0},{8,9},{9,10},{10,1... | collective-permute-start | bytes 21512 | tf_op jit(solution)/shard_map/ppermute | solution.py:363
  59.9 5.5 %collective-permute-start.9 = (f32[14,128]{1,0:T(8,128)}, f32[14,128]{1,0:T(8,128)S(1)}, u32[]{:S(2)}, u32[]{:S(2)}) collective-permute-start(f32[14,128]{1,0:T(8,128)} %get-tuple-element.28), channel_id=1, source_target_pairs={{1,0},{2,1},{3,2},{4,3},{5,4},{6,5},{7,6},{0,7},{9,8},{10,9},{11,1... | collective-permute-start | bytes 21512 | tf_op jit(solution)/shard_map/ppermute | solution.py:364
  65.4 0.6 copy-start.3
  65.4 0.6 copy-start.4
  65.4 0.6 copy-start.1
  65.5 0.6 copy-start.2
